TPU v7x, 32 devices: a whole 2x2x4 slice. The times are simulated.
32 devices in a mesh: cfg: 2 (over x), space: 16 (over z, y, core).
Axes of the slice: x: 2, y: 2, z: 4, core: 2. Of those that a mesh axis runs over, the one named last changes fastest.
Arguments:
- eigenvectors: bfloat16 [12, 2, 3, 256, 2048], P('cfg', None, None, None, 'space'), parts along dimension 0, may hold values from -6 to 6
- gauge_links: float32 [12, 3, 2, 3, 3, 2048], P('cfg', None, None, None, None, 'space'), parts along dimension 0, may hold values from -3.5 to 3.5
- perambulators: bfloat16 [32, 2, 256, 1024], P(('cfg', 'space')), parts along dimension 0, may hold values from -0.375 to 0.375
- directions: int32 [3], replicated, may hold values from 0 to 2, each once
- momenta: int32 [1, 3], replicated, may hold values from -2 to 2
- pair_times: int32 [4, 2], replicated, may hold values from 0 to 5, as said below
Outputs:
- elementals: bfloat16 [12, 1536, 256], P('cfg', 'space'), parts along dimension 0
- correlators: float32 [32, 3, 2], P(('cfg', 'space')), parts along dimension 0
There are 2 independent parts, one for each index of `cfg`. A program takes and returns all parts, laid end to end along the dimension named above; an argument that names none is the same for every part. Nothing has to cross between parts.
Inputs may be any that keep to these rules, and one draw needn't show every extreme that they name: `directions`: each direction appears exactly once. `pair_times`: no two time pairs have the same source and sink timeslice.
All inputs are finite; a program needn't handle non-finite values.
Results may differ from a plain program's by a relative error of at most 0.03.
Values may be sent and summed in bfloat16 or wider, within the bound.
No kernel may reach another device: no remote copies, remote signals or barrier semaphores. Data moves between devices by JAX's collectives and lax.ppermute only.
A program may use at most 128 MiB of HBM per device.

v0:
```python
import math

import jax
import jax.numpy as jnp
from jax import lax
from jax.sharding import PartitionSpec as P

NSPIN = 4
LY = 32
LZ = 8


def shifted(block, axis, distance):
    devices = range(lax.axis_size(axis))
    route = [((i - distance) % len(devices), i) for i in devices]
    return lax.ppermute(block, axis, route)


def swapped(value, axis, bit):
    return lax.ppermute(value, axis, [(i, i ^ 1 << bit) for i in range(lax.axis_size(axis))])


def phase_angles(momenta, coords, extents):
    fraction = 0.0
    for course in range(3):
        turns = momenta[:, course : course + 1] * coords[course][None, :] % extents[course]
        fraction = fraction + turns.astype(jnp.float32) / extents[course]
    return 2.0 * math.pi * fraction


def to_rows(field):
    count_t, _, _, count_ev, sites = field.shape
    return field.transpose(0, 3, 1, 2, 4).reshape(count_t, count_ev, 6 * sites)


def carried(link, field):
    field = field.astype(jnp.float32)
    real_part = 0.0
    imag_part = 0.0
    for inner in range(3):
        link_real = link[:, 0, :, inner][:, :, None, :]
        link_imag = link[:, 1, :, inner][:, :, None, :]
        field_real = field[:, 0, inner][:, None]
        field_imag = field[:, 1, inner][:, None]
        real_part = real_part + link_real * field_real - link_imag * field_imag
        imag_part = imag_part + link_real * field_imag + link_imag * field_real
    return jnp.stack([real_part, imag_part], 1).astype(jnp.bfloat16)


def local_sums(eigenvectors, gauge_links, far_tile, row_in, directions, angle):
    sites = eigenvectors.shape[-1]
    along_y = jnp.concatenate([eigenvectors[..., LZ:], row_in], axis=-1)
    column_pos = jnp.arange(sites, dtype=jnp.int32) % LZ
    along_z = jnp.where(
        column_pos == LZ - 1,
        jnp.roll(eigenvectors, LZ - 1, axis=-1),
        jnp.roll(eigenvectors, -1, axis=-1),
    )
    right = []
    for slot in range(directions.shape[0]):
        course = directions[slot]
        near = jnp.where(course == 0, far_tile, jnp.where(course == 1, along_y, along_z))
        link = lax.dynamic_index_in_dim(gauge_links, course, 1, keepdims=False)
        right.append(to_rows(carried(link, near)))
    right = jnp.stack(right, 1)
    cosine = jnp.cos(angle)[None, None, None, :]
    sine_part = jnp.sin(angle)[None, None, None, :]
    field_real = eigenvectors[:, 0].astype(jnp.float32)
    field_imag = eigenvectors[:, 1].astype(jnp.float32)
    phased_real = (cosine * field_real - sine_part * field_imag).astype(jnp.bfloat16)
    phased_imag = (sine_part * field_real + cosine * field_imag).astype(jnp.bfloat16)
    real_rows = to_rows(jnp.stack([phased_real, phased_imag], 1))
    imag_rows = to_rows(jnp.stack([-phased_imag, phased_real], 1))
    left = jnp.concatenate([real_rows, imag_rows], axis=1)
    joined = jnp.einsum("tPk,tajk->taPj", left, right, preferred_element_type=jnp.float32)
    return joined.reshape(joined.shape[0], -1, joined.shape[-1])


def contract_panel(sink, source, panel):
    count_ev = panel.shape[1]
    count_ops = sink.shape[0]
    sink_real = sink[:, 0]
    sink_imag = sink[:, 1]
    sink_wide = jnp.concatenate(
        [
            jnp.concatenate([sink_real, -sink_imag], axis=2),
            jnp.concatenate([sink_imag, sink_real], axis=2),
        ],
        axis=1,
    )
    panel_stack = panel.reshape(2 * count_ev, NSPIN * count_ev)
    left = jnp.einsum("amk,kn->amn", sink_wide, panel_stack, preferred_element_type=jnp.float32)
    left = left.reshape(count_ops, 2, count_ev, NSPIN, count_ev)
    blocks = panel.reshape(2, count_ev * NSPIN, count_ev)
    panel_wide = jnp.concatenate(
        [
            jnp.concatenate([blocks[0], -blocks[1]], axis=1),
            jnp.concatenate([blocks[1], blocks[0]], axis=1),
        ],
        axis=0,
    )
    source_stack = source.transpose(1, 2, 0, 3).reshape(2 * count_ev, count_ops * count_ev)
    right = jnp.einsum("mk,kn->mn", panel_wide, source_stack, preferred_element_type=jnp.float32)
    right = right.reshape(2, count_ev, NSPIN, count_ops, count_ev).transpose(3, 0, 1, 2, 4)
    left_real = left[:, 0]
    left_imag = left[:, 1]
    right_real = right[:, 0]
    right_imag = right[:, 1]
    trace_real = jnp.sum(left_real * right_real + left_imag * right_imag, axis=(1, 2, 3))
    trace_imag = jnp.sum(left_imag * right_real - left_real * right_imag, axis=(1, 2, 3))
    return jnp.stack([trace_real, trace_imag], -1) * (1.0 / (16.0 * count_ev))


def body(eigenvectors, gauge_links, perambulators, directions, momenta, pair_times):
    time_count = eigenvectors.shape[0]
    count_ev = eigenvectors.shape[3]
    local_sites = eigenvectors.shape[4]
    nspace = lax.axis_size("space")
    device = lax.axis_index("space")
    half_rows = LY // 2
    extent_x = nspace // 2
    column = jnp.arange(local_sites, dtype=jnp.int32)
    coord_x = device // 2 + 0 * column
    coord_y = device % 2 * half_rows + column // LZ
    coord_z = column % LZ
    angle = phase_angles(momenta, (coord_x, coord_y, coord_z), (extent_x, LY, LZ))[0]
    far_tile = shifted(eigenvectors, "space", -2)
    row_in = swapped(eigenvectors[..., :LZ], "space", 0)
    summands = local_sums(eigenvectors, gauge_links, far_tile, row_in, directions, angle)
    scale = 1.0 / math.sqrt(3.0 * extent_x * LY * LZ)
    shares = lax.psum_scatter(summands, "space", scatter_dimension=1, tiled=True)
    own_rows = (shares * scale).astype(jnp.bfloat16)
    rows = own_rows.shape[1]
    target = jnp.arange(nspace, dtype=jnp.int32) // NSPIN
    wanted = jnp.stack([pair_times[target, 1], pair_times[target, 0]], 1)
    outgoing = jnp.take(own_rows, wanted.reshape(-1), axis=0).reshape(nspace, 2, rows, count_ev)
    incoming = lax.all_to_all(outgoing, "space", 0, 0, tiled=True)
    count_ops = summands.shape[1] // (2 * count_ev)
    gathered = incoming.transpose(1, 0, 2, 3).reshape(2, count_ops, 2, count_ev, count_ev)
    correlators = contract_panel(gathered[0], gathered[1], perambulators[0])[None]
    return (own_rows, correlators)


def solution(mesh):
    placed = (
        P("cfg", None, None, None, "space"),
        P("cfg", None, None, None, None, "space"),
        P(("cfg", "space"), None, None, None),
        P(),
        P(),
        P(),
    )
    return jax.shard_map(
        body,
        mesh=mesh,
        in_specs=placed,
        out_specs=(P("cfg", "space", None), P(("cfg", "space"), None, None)),
        check_vma=False,
    )
```

profile of v0, /device:TPU:0, one launch (start us, length us, event | category | flops | bytes accessed | tf_op | source)
XLA Modules:
  0.0 325.3 jit_solution(4818696259189209072)
XLA Ops:
  7.3 6.1 %collective-permute-start = (bf16[6,2,3,256,128]{4,3,2,1,0:T(8,128)(2,1)}, bf16[6,2,3,256,128]{4,3,2,1,0:T(8,128)(2,1)}, u32[]{:S(2)}, u32[]{:S(2)}) collective-permute-start(bf16[6,2,3,256,128]{4,3,2,1,0:T(8,128)(2,1)} %param.6), channel_id=1, source_target_pairs={{2,0},{3,1},{4,2},{5,3},{6,4},{7,5},{8,6},{9,7},{10,8},{11,9},{12,... | collective-permute-start | bytes 7077896 | tf_op jit(solution)/shard_map/ppermute | solution.py:16
  13.3 2.6 copy.140
  27.4 2.4 copy.142
  37.9 2.4 pad_maximum_fusion.4
  51.1 4.3 %copy.106 = bf16[6,256,768]{2,1,0:T(8,128)(2,1)} copy(bf16[6,256,768]{1,2,0:T(8,128)(2,1)} %bitcast.196) | data formatting | bytes 4718592 | tf_op jit(solution)/shard_map/reshape | solution.py:33
  55.4 4.3 %copy.107 = bf16[6,256,768]{2,1,0:T(8,128)(2,1)} copy(bf16[6,256,768]{1,2,0:T(8,128)(2,1)} %bitcast.195) | data formatting | bytes 4718592 | tf_op jit(solution)/shard_map/reshape | solution.py:33
  59.7 2.7 copy.82
  64.1 8.8 %select_convert_fusion.2 = (f32[6,2,3,256,128]{4,3,2,1,0:T(8,128)S(1)}, bf16[6,2,3,256,128]{4,3,2,1,0:T(8,128)(2,1)}) fusion(bf16[6,2,3,256,128]{4,3,2,1,0:T(8,128)(2,1)} %collective-permute-done, pred[]{:T(512)S(6)} %eq.32, pred[]{:T(512)S(6)} %eq.31, bf16[6,2,3,256,8]{4,3,2,1,0:T(8,128)(2,1)} %copy.82, bf16[6,2,3,256,120]{4,3,2,1,0:T(8,128)(2,1)} %slice.192, ...), kind=kLoop, calls=%fused_computation.39 | loop fusion | flops 18874368 | bytes 16515202 | tf_op jit(solution)/shard_map/convert_element_type | solution.py:37
  74.4 2.4 copy.83
  83.0 4.8 %subtract_convert_fusion.2 = (bf16[6,1,3,256,128]{3,4,2,1,0:T(8,128)(2,1)S(1)}, bf16[6,1,3,256,128]{3,4,2,1,0:T(8,128)(2,1)S(1)}) fusion(f32[6,256,128]{1,2,0:T(8,128)S(1)} %copy.88, f32[6,3,128]{2,1,0:T(4,128)S(1)} %bitcast.213, f32[6,256,128]{1,2,0:T(8,128)} %copy.87, f32[6,3,128]{2,1,0:T(4,128)S(1)} %bitcast.214, f32[6,256,128]{1,2,0:T(8,128)} %copy.86, ...), kind=kLoop, calls=%fused_computation.38 | loop fusion | flops 14155776 | bytes 7133184 | tf_op jit(solution)/shard_map/convert.4
  89.4 4.4 %copy.101 = bf16[6,1,256,768]{3,2,1,0:T(8,128)(2,1)} copy(bf16[6,1,256,768]{2,3,0,1:T(8,128)(2,1)} %bitcast.192) | data formatting | bytes 4718592 | tf_op jit(solution)/shard_map/stack;reshape | solution.py:65
  93.9 4.3 %select_convert_fusion.1 = (f32[6,2,3,256,128]{4,3,2,1,0:T(8,128)S(1)}, f32[6,2,3,256,128]{4,3,2,1,0:T(8,128)S(1)}) fusion(bf16[6,2,3,256,128]{4,3,2,1,0:T(8,128)(2,1)} %collective-permute-done, bf16[6,2,3,256,128]{4,3,2,1,0:T(8,128)(2,1)} %get-tuple-element.5, pred[]{:T(512)S(6)} %eq.35, pred[]{:T(512)S(6)} %eq.34, bf16[6,2,3,256,8]{4,3,2,1,0:T(8,128)(2,1)} %copy.82, ...), kind=kLoop, calls=%fused_computation.36 | loop fusion | flops 11796480 | bytes 16515076 | tf_op jit(solution)/shard_map/convert_element_type | solution.py:37
  98.2 2.6 slice_bitcast_fusion.5
  110.4 5.0 %subtract_convert_fusion.1 = (bf16[6,1,3,256,128]{3,4,2,1,0:T(8,128)(2,1)S(1)}, bf16[6,1,3,256,128]{3,4,2,1,0:T(8,128)(2,1)S(1)}) fusion(f32[6,256,128]{1,2,0:T(8,128)S(1)} %copy.94, f32[6,3,128]{2,1,0:T(4,128)S(1)} %bitcast.207, f32[6,256,128]{1,2,0:T(8,128)} %copy.93, f32[6,3,128]{2,1,0:T(4,128)S(1)} %bitcast.208, f32[6,256,128]{1,2,0:T(8,128)} %copy.92, ...), kind=kLoop, calls=%fused_computation.35 | loop fusion | flops 14155776 | bytes 7133184 | tf_op jit(solution)/shard_map/convert.2
  115.6 2.4 copy.102
  118.0 2.4 copy.100
  120.4 2.4 copy.95
  126.6 4.8 %subtract_convert_fusion = (bf16[6,1,3,256,128]{3,4,2,1,0:T(8,128)(2,1)S(1)}, bf16[6,1,3,256,128]{3,4,2,1,0:T(8,128)(2,1)S(1)}) fusion(f32[6,256,128]{1,2,0:T(8,128)S(1)} %copy-done.10, f32[6,3,128]{2,1,0:T(4,128)S(1)} %get-tuple-element.87, f32[6,256,128]{1,2,0:T(8,128)S(1)} %copy.99, f32[6,3,128]{2,1,0:T(4,128)S(1)} %copy-done.16, ...), kind=kLoop, calls=%fused_computation.32 | loop fusion | flops 14155776 | bytes 7133184 | tf_op jit(solution)/shard_map/convert
  131.6 2.4 copy.103
  134.1 12.0 %fusion.8 = f32[6,3,512,256]{2,3,1,0:T(8,128)} fusion(bf16[6,256,768]{2,1,0:T(8,128)(2,1)} %copy.107, bf16[6,256,768]{2,1,0:T(8,128)(2,1)} %copy.106, bf16[6,1,256,768]{3,2,1,0:T(8,128)(2,1)} %copy.103, bf16[6,1,256,768]{3,2,1,0:T(8,128)(2,1)} %copy.102, bf16[6,1,256,768]{3,2,1,0:T(8,128)(2,1)} %copy.101), kind=kOutput, calls=%fused_computation.12 | convolution fusion | flops 3640393728 | bytes 21233664 | tf_op jit(solution)/shard_map/tPk,tajk->taPj/dot_general | solution.py:75
  146.0 9.6 %copy.108 = f32[6,3,512,256]{3,2,1,0:T(8,128)} copy(f32[6,3,512,256]{2,3,1,0:T(8,128)} %fusion.8) | data formatting | bytes 18874368 | tf_op jit(solution)/shard_map/tPk,tajk->taPj/transpose | solution.py:75
  157.4 111.7 %reduce-scatter.2.cloned.1.call-done = f32[6,96,256]{2,1,0:T(8,128)} async-done(((f32[6,1536,256]{2,1,0:T(8,128)}), f32[6,96,256]{2,1,0:T(8,128)}) %reduce-scatter.2.cloned.1.call-update) | async-done | bytes 589840 | tf_op jit(solution)/shard_map/reduce_scatter | solution.py:131
  272.2 4.8 %all-to-all-start = ((bf16[16,2,96,256]{3,2,1,0:T(8,128)(2,1)}), bf16[16,2,96,256]{3,2,1,0:T(8,128)(2,1)}, u32[]{:S(2)}, u32[]{:S(2)}) async-start(bf16[16,2,96,256]{3,2,1,0:T(8,128)(2,1)} %broadcast_select_fusion), calls=%async_computation.1 | async-start | bytes 3145728 | tf_op jit(solution)/shard_map/all_to_all | solution.py:137
  283.4 25.5 %all-to-all-done = bf16[16,2,96,256]{3,2,1,0:T(8,128)(2,1)} async-done(((bf16[16,2,96,256]{3,2,1,0:T(8,128)(2,1)}), bf16[16,2,96,256]{3,2,1,0:T(8,128)(2,1)}, u32[]{:S(2)}, u32[]{:S(2)}) %all-to-all-start) | async-done | bytes 1572896 | tf_op jit(solution)/shard_map/all_to_all | solution.py:137
  (151 shorter events, 65.3 us)
Async XLA Ops:
  7.2 148.5 %copy-start = (s32[4,2]{0,1:T(2,128)S(1)}, s32[4,2]{0,1:T(2,128)}, u32[]{:S(2)}) copy-start(s32[4,2]{0,1:T(2,128)} %param.11) | copy-start | bytes 100
  7.2 14.7 %copy-start.1 = (bf16[6,2,3,256,128]{4,3,2,1,0:T(8,128)(2,1)S(1)}, bf16[6,2,3,256,128]{4,3,2,1,0:T(8,128)(2,1)}, u32[]{:S(2)}) copy-start(bf16[6,2,3,256,128]{4,3,2,1,0:T(8,128)(2,1)} %param.6) | copy-start | bytes 7077892
  7.2 8.8 %copy-start.31 = (s32[3]{0:T(128)S(1)}, s32[3]{0:T(128)}, u32[]{:S(2)}) copy-start(s32[3]{0:T(128)} %param.9) | copy-start | bytes 40
  7.2 13.3 %copy-start.32 = (s32[1,3]{1,0:T(1,128)S(1)}, s32[1,3]{1,0:T(1,128)}, u32[]{:S(2)}) copy-start(s32[1,3]{1,0:T(1,128)} %param.10) | copy-start | bytes 40
  7.2 261.8 %reduce-scatter.2.cloned.1.call-start = ((), (), s32[]{:S(2)}) async-start(), calls=%async_computation.2 | async-start | bytes 10027008 | tf_op jit(solution)/shard_map/reduce_scatter | solution.py:131
  7.3 56.9 %collective-permute-start = (bf16[6,2,3,256,128]{4,3,2,1,0:T(8,128)(2,1)}, bf16[6,2,3,256,128]{4,3,2,1,0:T(8,128)(2,1)}, u32[]{:S(2)}, u32[]{:S(2)}) collective-permute-start(bf16[6,2,3,256,128]{4,3,2,1,0:T(8,128)(2,1)} %param.6), channel_id=1, source_target_pairs={{2,0},{3,1},{4,2},{5,3},{6,4},{7,5},{8,6},{9,7},{10,8},{11,9},{12,... | collective-permute-start | bytes 7077896 | tf_op jit(solution)/shard_map/ppermute | solution.py:16
  15.9 43.7 %collective-permute-start.1 = (bf16[6,2,3,256,8]{3,4,2,1,0:T(8,128)(2,1)}, bf16[6,2,3,256,8]{3,4,2,1,0:T(8,128)(2,1)}, u32[]{:S(2)}, u32[]{:S(2)}) collective-permute-start(bf16[6,2,3,256,8]{3,4,2,1,0:T(8,128)(2,1)} %copy.140), channel_id=1, source_target_pairs={{0,1},{1,0},{2,3},{3,2},{4,5},{5,4},{6,7},{7,6},{8,9},{9,8},{10,11... | collective-permute-start | bytes 442376 | tf_op jit(solution)/shard_map/ppermute | solution.py:20
  31.7 4.8 %copy-start.4 = (bf16[6,1,3,256,128]{3,4,2,1,0:T(8,128)(2,1)S(1)}, bf16[6,1,3,256,128]{3,4,2,1,0:T(8,128)(2,1)}, u32[]{:S(2)}) copy-start(bf16[6,1,3,256,128]{3,4,2,1,0:T(8,128)(2,1)} %copy.142) | copy-start | bytes 3538948
  45.7 5.1 %copy-start.30 = (f32[6,1,3,1,128]{4,1,3,2,0:T(1,128)S(1)}, f32[6,1,3,1,128]{4,1,3,2,0:T(1,128)}, u32[]{:S(2)}) copy-start(f32[6,1,3,1,128]{4,1,3,2,0:T(1,128)} %get-tuple-element.50) | copy-start | bytes 27652
  45.7 5.1 %copy-start.29 = (f32[6,1,3,1,128]{4,1,3,2,0:T(1,128)S(1)}, f32[6,1,3,1,128]{4,1,3,2,0:T(1,128)}, u32[]{:S(2)}) copy-start(f32[6,1,3,1,128]{4,1,3,2,0:T(1,128)} %get-tuple-element.51) | copy-start | bytes 27652
  45.7 5.1 %copy-start.28 = (f32[6,1,3,1,128]{4,1,3,2,0:T(1,128)S(1)}, f32[6,1,3,1,128]{4,1,3,2,0:T(1,128)}, u32[]{:S(2)}) copy-start(f32[6,1,3,1,128]{4,1,3,2,0:T(1,128)} %get-tuple-element.52) | copy-start | bytes 27652
  45.7 5.1 %copy-start.27 = (f32[6,1,3,1,128]{4,1,3,2,0:T(1,128)S(1)}, f32[6,1,3,1,128]{4,1,3,2,0:T(1,128)}, u32[]{:S(2)}) copy-start(f32[6,1,3,1,128]{4,1,3,2,0:T(1,128)} %get-tuple-element.53) | copy-start | bytes 27652
  45.7 5.2 %copy-start.26 = (f32[6,1,3,1,128]{4,1,3,2,0:T(1,128)S(1)}, f32[6,1,3,1,128]{4,1,3,2,0:T(1,128)}, u32[]{:S(2)}) copy-start(f32[6,1,3,1,128]{4,1,3,2,0:T(1,128)} %get-tuple-element.54) | copy-start | bytes 27652
  45.8 5.2 %copy-start.25 = (f32[6,1,3,1,128]{4,1,3,2,0:T(1,128)S(1)}, f32[6,1,3,1,128]{4,1,3,2,0:T(1,128)}, u32[]{:S(2)}) copy-start(f32[6,1,3,1,128]{4,1,3,2,0:T(1,128)} %get-tuple-element.49) | copy-start | bytes 27652
  45.8 5.2 %copy-start.24 = (f32[6,1,3,1,128]{4,1,3,2,0:T(1,128)S(1)}, f32[6,1,3,1,128]{4,1,3,2,0:T(1,128)}, u32[]{:S(2)}) copy-start(f32[6,1,3,1,128]{4,1,3,2,0:T(1,128)} %get-tuple-element.85) | copy-start | bytes 27652
  45.8 5.2 %copy-start.23 = (f32[6,1,3,1,128]{4,1,3,2,0:T(1,128)S(1)}, f32[6,1,3,1,128]{4,1,3,2,0:T(1,128)}, u32[]{:S(2)}) copy-start(f32[6,1,3,1,128]{4,1,3,2,0:T(1,128)} %get-tuple-element.84) | copy-start | bytes 27652
  45.8 5.2 %copy-start.22 = (f32[6,1,3,1,128]{4,1,3,2,0:T(1,128)S(1)}, f32[6,1,3,1,128]{4,1,3,2,0:T(1,128)}, u32[]{:S(2)}) copy-start(f32[6,1,3,1,128]{4,1,3,2,0:T(1,128)} %get-tuple-element.83) | copy-start | bytes 27652
  45.8 5.2 %copy-start.21 = (f32[6,1,3,1,128]{4,1,3,2,0:T(1,128)S(1)}, f32[6,1,3,1,128]{4,1,3,2,0:T(1,128)}, u32[]{:S(2)}) copy-start(f32[6,1,3,1,128]{4,1,3,2,0:T(1,128)} %get-tuple-element.82) | copy-start | bytes 27652
  45.8 5.2 %copy-start.20 = (f32[6,1,3,1,128]{4,1,3,2,0:T(1,128)S(1)}, f32[6,1,3,1,128]{4,1,3,2,0:T(1,128)}, u32[]{:S(2)}) copy-start(f32[6,1,3,1,128]{4,1,3,2,0:T(1,128)} %get-tuple-element.81) | copy-start | bytes 27652
  45.8 5.2 %copy-start.19 = (f32[6,1,3,1,128]{4,1,3,2,0:T(1,128)S(1)}, f32[6,1,3,1,128]{4,1,3,2,0:T(1,128)}, u32[]{:S(2)}) copy-start(f32[6,1,3,1,128]{4,1,3,2,0:T(1,128)} %get-tuple-element.86) | copy-start | bytes 27652
  118.0 4.8 %copy-start.9 = (f32[6,256,128]{2,1,0:T(8,128)S(1)}, f32[6,256,128]{2,1,0:T(8,128)}, u32[]{:S(2)}) copy-start(f32[6,256,128]{2,1,0:T(8,128)} %get-tuple-element.35) | copy-start | bytes 2359300
  118.0 6.0 %copy-start.8 = (f32[6,256,128]{2,1,0:T(8,128)S(1)}, f32[6,256,128]{2,1,0:T(8,128)}, u32[]{:S(2)}) copy-start(f32[6,256,128]{2,1,0:T(8,128)} %get-tuple-element.34) | copy-start | bytes 2359300
  272.2 4.8 %copy-start.6 = (bf16[1,2,256,1024]{3,2,1,0:T(8,128)(2,1)S(1)}, bf16[1,2,256,1024]{3,2,1,0:T(8,128)(2,1)}, u32[]{:S(2)}) copy-start(bf16[1,2,256,1024]{3,2,1,0:T(8,128)(2,1)} %param.8) | copy-start | bytes 3145732
  272.2 36.7 %all-to-all-start = ((bf16[16,2,96,256]{3,2,1,0:T(8,128)(2,1)}), bf16[16,2,96,256]{3,2,1,0:T(8,128)(2,1)}, u32[]{:S(2)}, u32[]{:S(2)}) async-start(bf16[16,2,96,256]{3,2,1,0:T(8,128)(2,1)} %broadcast_select_fusion), calls=%async_computation.1 | async-start | bytes 3145728 | tf_op jit(solution)/shard_map/all_to_all | solution.py:137
  (13 other events, 31.8 us)
Sparse Core Ops, SparseCore 0:
  155.7 113.2 reduce-scatter.1
where the time goes:
time: 330 us; the launch traced here: 325 us
  waiting for transfers between devices  139 us (42%)
  local copies, waits for them, and re-layouts  91.2 us (28%)
  other arithmetic  43.3 us (13%)
  between operations  25.1 us (8%)
  matrix products  15.9 us (5%)
  starting transfers between devices  10.9 us (3%)
    reduce_scatter x1, waiting for transfers between devices, body(): lax.psum_scatter(summands, 'space', scatter_dimension=1, tiled=True)  112 us
    mul x20, local copies, waits for them, and re-layouts, carried(): real_part = real_part + link_real * field_real - link_imag * field_imag  30.7 us
    all_to_all x1, waiting for transfers between devices, body(): incoming = lax.all_to_all(outgoing, 'space', 0, 0, tiled=True)  25.5 us
    another operation x3, other arithmetic  14.5 us
    convert_element_type x2, other arithmetic, carried(): field = field.astype(jnp.float32)  13.1 us
    dot_general x1, matrix products, local_sums(): jnp.einsum('tPk,tajk->taPj', left, right, preferred_element_type=jnp.floa...  12 us
    transpose x1, local copies, waits for them, and re-layouts, local_sums(): jnp.einsum('tPk,tajk->taPj', left, right, preferred_element_type=jnp.floa...  9.57 us
    another operation x3, local copies, waits for them, and re-layouts, local_sums(): right = jnp.stack(right, 1)  9.3 us
  transfers between devices with their start and end apart: 4, of which 3 were waited for; matrix products, arithmetic and copies ran while one was open for 14% of the time, Pallas kernels for 0%

commit v1 on v0

--- a/solution.py
+++ b/solution.py
@@ -128,8 +128,8 @@
     row_in = swapped(eigenvectors[..., :LZ], "space", 0)
     summands = local_sums(eigenvectors, gauge_links, far_tile, row_in, directions, angle)
     scale = 1.0 / math.sqrt(3.0 * extent_x * LY * LZ)
-    shares = lax.psum_scatter(summands, "space", scatter_dimension=1, tiled=True)
-    own_rows = (shares * scale).astype(jnp.bfloat16)
+    partial = (summands * scale).astype(jnp.bfloat16)
+    own_rows = lax.psum_scatter(partial, "space", scatter_dimension=1, tiled=True)
     rows = own_rows.shape[1]
     target = jnp.arange(nspace, dtype=jnp.int32) // NSPIN
     wanted = jnp.stack([pair_times[target, 1], pair_times[target, 0]], 1)

time: 330 us -> 288 us (0.87)
  waiting for transfers between devices: 139 us -> 103 us
    reduce_scatter x1, waiting for transfers between devices: 112 us -> 75.9 us  [body(): lax.psum_scatter(partial, 'space', scatter_dimension=1, tiled=True)]
    transpose x1 -> x0, local copies, waits for them, and re-layouts: 9.57 us -> none  [local_sums(): jnp.einsum('tPk,tajk->taPj', left, right, preferred_element_type=jnp.floa...]
    convert_element_type x0 -> x1, local copies, waits for them, and re-layouts: none -> 6.61 us  [body(): partial = (summands * scale).astype(jnp.bfloat16)]
    unnamed x85 -> x83, local copies, waits for them, and re-layouts: 9.04 us -> 9.03 us
  transfers between devices with their start and end apart: 4 -> 4, of which waited for: 3 -> 3; matrix products, arithmetic and copies ran while one was open for 14% -> 16% of each run, Pallas kernels for 0% -> 0%
where the time goes in v1:
time: 288 us; the launch traced here: 283 us
  waiting for transfers between devices  103 us (36%)
  local copies, waits for them, and re-layouts  89.1 us (31%)
  other arithmetic  42 us (15%)
  between operations  25 us (9%)
  matrix products  12.9 us (4%)
  starting transfers between devices  10.9 us (4%)
    reduce_scatter x1, waiting for transfers between devices, body(): lax.psum_scatter(partial, 'space', scatter_dimension=1, tiled=True)  75.9 us
    mul x20, local copies, waits for them, and re-layouts, carried(): real_part = real_part + link_real * field_real - link_imag * field_imag  30.6 us
    all_to_all x1, waiting for transfers between devices, body(): incoming = lax.all_to_all(outgoing, 'space', 0, 0, tiled=True)  25.4 us
    another operation x3, other arithmetic  14.5 us
    convert_element_type x2, other arithmetic, carried(): field = field.astype(jnp.float32)  13.1 us
    another operation x3, local copies, waits for them, and re-layouts, local_sums(): right = jnp.stack(right, 1)  9.46 us
    unnamed x83, local copies, waits for them, and re-layouts  9.03 us
    dot_general x1, matrix products, local_sums(): jnp.einsum('tPk,tajk->taPj', left, right, preferred_element_type=jnp.floa...  8.96 us
  transfers between devices with their start and end apart: 4, of which 3 were waited for; matrix products, arithmetic and copies ran while one was open for 16% of the time, Pallas kernels for 0%

profile of v1, /device:TPU:0, one launch (start us, length us, event | category | flops | bytes accessed | tf_op | source)
XLA Modules:
  0.0 283.2 jit_solution(897479932254643513)
XLA Ops:
  7.3 6.1 %collective-permute-start = (bf16[6,2,3,256,128]{4,3,2,1,0:T(8,128)(2,1)}, bf16[6,2,3,256,128]{4,3,2,1,0:T(8,128)(2,1)}, u32[]{:S(2)}, u32[]{:S(2)}) collective-permute-start(bf16[6,2,3,256,128]{4,3,2,1,0:T(8,128)(2,1)} %param.6), channel_id=1, source_target_pairs={{2,0},{3,1},{4,2},{5,3},{6,4},{7,5},{8,6},{9,7},{10,8},{11,9},{12,... | collective-permute-start | bytes 7077896 | tf_op jit(solution)/shard_map/ppermute | solution.py:16
  13.3 2.6 copy.140
  27.3 2.4 copy.142
  37.7 2.4 pad_maximum_fusion.4
  50.8 4.3 %copy.106 = bf16[6,256,768]{2,1,0:T(8,128)(2,1)} copy(bf16[6,256,768]{1,2,0:T(8,128)(2,1)} %bitcast.196) | data formatting | bytes 4718592 | tf_op jit(solution)/shard_map/reshape | solution.py:33
  55.1 4.3 %copy.107 = bf16[6,256,768]{2,1,0:T(8,128)(2,1)} copy(bf16[6,256,768]{1,2,0:T(8,128)(2,1)} %bitcast.195) | data formatting | bytes 4718592 | tf_op jit(solution)/shard_map/reshape | solution.py:33
  59.4 2.7 copy.82
  64.1 8.8 %select_convert_fusion.2 = (f32[6,2,3,256,128]{4,3,2,1,0:T(8,128)S(1)}, bf16[6,2,3,256,128]{4,3,2,1,0:T(8,128)(2,1)}) fusion(bf16[6,2,3,256,128]{4,3,2,1,0:T(8,128)(2,1)} %collective-permute-done, pred[]{:T(512)S(6)} %eq.32, pred[]{:T(512)S(6)} %eq.31, bf16[6,2,3,256,8]{4,3,2,1,0:T(8,128)(2,1)} %copy.82, bf16[6,2,3,256,120]{4,3,2,1,0:T(8,128)(2,1)} %slice.192, ...), kind=kLoop, calls=%fused_computation.40 | loop fusion | flops 18874368 | bytes 16515202 | tf_op jit(solution)/shard_map/convert_element_type | solution.py:37
  82.8 4.8 %subtract_convert_fusion.2 = (bf16[6,1,3,256,128]{3,4,2,1,0:T(8,128)(2,1)S(1)}, bf16[6,1,3,256,128]{3,4,2,1,0:T(8,128)(2,1)S(1)}) fusion(f32[6,256,128]{1,2,0:T(8,128)S(1)} %copy.88, f32[6,3,128]{2,1,0:T(4,128)S(1)} %bitcast.213, f32[6,256,128]{1,2,0:T(8,128)} %copy.87, f32[6,3,128]{2,1,0:T(4,128)S(1)} %bitcast.214, f32[6,256,128]{1,2,0:T(8,128)} %copy.86, ...), kind=kLoop, calls=%fused_computation.39 | loop fusion | flops 14155776 | bytes 7133184 | tf_op jit(solution)/shard_map/convert.4
  89.2 4.5 %copy.101 = bf16[6,1,256,768]{3,2,1,0:T(8,128)(2,1)} copy(bf16[6,1,256,768]{2,3,0,1:T(8,128)(2,1)} %bitcast.192) | data formatting | bytes 4718592 | tf_op jit(solution)/shard_map/stack;reshape | solution.py:65
  93.7 4.3 %select_convert_fusion.1 = (f32[6,2,3,256,128]{4,3,2,1,0:T(8,128)S(1)}, f32[6,2,3,256,128]{4,3,2,1,0:T(8,128)S(1)}) fusion(bf16[6,2,3,256,128]{4,3,2,1,0:T(8,128)(2,1)} %collective-permute-done, bf16[6,2,3,256,128]{4,3,2,1,0:T(8,128)(2,1)} %get-tuple-element.5, pred[]{:T(512)S(6)} %eq.35, pred[]{:T(512)S(6)} %eq.34, bf16[6,2,3,256,8]{4,3,2,1,0:T(8,128)(2,1)} %copy.82, ...), kind=kLoop, calls=%fused_computation.37 | loop fusion | flops 11796480 | bytes 16515076 | tf_op jit(solution)/shard_map/convert_element_type | solution.py:37
  98.0 2.6 slice_bitcast_fusion.5
  105.2 2.4 copy.91
  110.2 5.0 %subtract_convert_fusion.1 = (bf16[6,1,3,256,128]{3,4,2,1,0:T(8,128)(2,1)S(1)}, bf16[6,1,3,256,128]{3,4,2,1,0:T(8,128)(2,1)S(1)}) fusion(f32[6,256,128]{1,2,0:T(8,128)S(1)} %copy.94, f32[6,3,128]{2,1,0:T(4,128)S(1)} %bitcast.207, f32[6,256,128]{1,2,0:T(8,128)} %copy.93, f32[6,3,128]{2,1,0:T(4,128)S(1)} %bitcast.208, f32[6,256,128]{1,2,0:T(8,128)} %copy.92, ...), kind=kLoop, calls=%fused_computation.36 | loop fusion | flops 14155776 | bytes 7133184 | tf_op jit(solution)/shard_map/convert.2
  115.4 2.5 copy.102
  117.9 2.4 copy.100
  120.3 2.4 copy.95
  126.5 4.8 %subtract_convert_fusion = (bf16[6,1,3,256,128]{3,4,2,1,0:T(8,128)(2,1)S(1)}, bf16[6,1,3,256,128]{3,4,2,1,0:T(8,128)(2,1)S(1)}) fusion(f32[6,256,128]{1,2,0:T(8,128)S(1)} %copy-done.9, f32[6,3,128]{2,1,0:T(4,128)S(1)} %get-tuple-element.87, f32[6,256,128]{1,2,0:T(8,128)S(1)} %copy.99, f32[6,3,128]{2,1,0:T(4,128)S(1)} %copy-done.15, f32[6,256,128]{1,2,0:T(8,128)} %copy.98, ...), kind=kLoop, calls=%fused_computation.33 | loop fusion | flops 14155776 | bytes 7133184 | tf_op jit(solution)/shard_map/convert
  131.5 2.5 copy.103
  134.0 9.0 %fusion.6 = bf16[6,3,512,256]{2,3,1,0:T(8,128)(2,1)} fusion(bf16[6,256,768]{2,1,0:T(8,128)(2,1)} %copy.107, bf16[6,256,768]{2,1,0:T(8,128)(2,1)} %copy.106, bf16[6,1,256,768]{3,2,1,0:T(8,128)(2,1)} %copy.103, bf16[6,1,256,768]{3,2,1,0:T(8,128)(2,1)} %copy.102, bf16[6,1,256,768]{3,2,1,0:T(8,128)(2,1)} %copy.101), kind=kOutput, calls=%fused_computation.10 | convolution fusion | flops 3645112320 | bytes 16515072 | tf_op jit(solution)/shard_map/tPk,tajk->taPj/dot_general | solution.py:75
  143.0 6.6 %copy.108 = bf16[6,3,512,256]{3,2,1,0:T(8,128)(2,1)} copy(bf16[6,3,512,256]{2,3,1,0:T(8,128)(2,1)} %fusion.6) | data formatting | bytes 9437184 | tf_op jit(solution)/shard_map/convert_element_type | solution.py:131
  151.3 75.9 %reduce-scatter.2.cloned.1.call-done = bf16[6,96,256]{2,1,0:T(8,128)(2,1)} async-done(((bf16[6,1536,256]{2,1,0:T(8,128)(2,1)}), bf16[6,96,256]{2,1,0:T(8,128)(2,1)}) %reduce-scatter.2.cloned.1.call-update) | async-done | bytes 294928 | tf_op jit(solution)/shard_map/reduce_scatter | solution.py:132
  230.2 4.8 %all-to-all-start = ((bf16[16,2,96,256]{3,2,1,0:T(8,128)(2,1)}), bf16[16,2,96,256]{3,2,1,0:T(8,128)(2,1)}, u32[]{:S(2)}, u32[]{:S(2)}) async-start(bf16[16,2,96,256]{3,2,1,0:T(8,128)(2,1)} %broadcast_select_fusion), calls=%async_computation.1 | async-start | bytes 3145728 | tf_op jit(solution)/shard_map/all_to_all | solution.py:137
  241.4 25.4 %all-to-all-done = bf16[16,2,96,256]{3,2,1,0:T(8,128)(2,1)} async-done(((bf16[16,2,96,256]{3,2,1,0:T(8,128)(2,1)}), bf16[16,2,96,256]{3,2,1,0:T(8,128)(2,1)}, u32[]{:S(2)}, u32[]{:S(2)}) %all-to-all-start) | async-done | bytes 1572896 | tf_op jit(solution)/shard_map/all_to_all | solution.py:137
  (148 shorter events, 65.1 us)
Async XLA Ops:
  7.2 142.5 %copy-start = (s32[4,2]{0,1:T(2,128)S(1)}, s32[4,2]{0,1:T(2,128)}, u32[]{:S(2)}) copy-start(s32[4,2]{0,1:T(2,128)} %param.11) | copy-start | bytes 100
  7.2 14.6 %copy-start.1 = (bf16[6,2,3,256,128]{4,3,2,1,0:T(8,128)(2,1)S(1)}, bf16[6,2,3,256,128]{4,3,2,1,0:T(8,128)(2,1)}, u32[]{:S(2)}) copy-start(bf16[6,2,3,256,128]{4,3,2,1,0:T(8,128)(2,1)} %param.6) | copy-start | bytes 7077892
  7.2 8.8 %copy-start.30 = (s32[3]{0:T(128)S(1)}, s32[3]{0:T(128)}, u32[]{:S(2)}) copy-start(s32[3]{0:T(128)} %param.9) | copy-start | bytes 40
  7.2 13.3 %copy-start.31 = (s32[1,3]{1,0:T(1,128)S(1)}, s32[1,3]{1,0:T(1,128)}, u32[]{:S(2)}) copy-start(s32[1,3]{1,0:T(1,128)} %param.10) | copy-start | bytes 40
  7.2 220.0 %reduce-scatter.2.cloned.1.call-start = ((), (), s32[]{:S(2)}) async-start(), calls=%async_computation.2 | async-start | bytes 5013504 | tf_op jit(solution)/shard_map/reduce_scatter | solution.py:132
  7.3 56.9 %collective-permute-start = (bf16[6,2,3,256,128]{4,3,2,1,0:T(8,128)(2,1)}, bf16[6,2,3,256,128]{4,3,2,1,0:T(8,128)(2,1)}, u32[]{:S(2)}, u32[]{:S(2)}) collective-permute-start(bf16[6,2,3,256,128]{4,3,2,1,0:T(8,128)(2,1)} %param.6), channel_id=1, source_target_pairs={{2,0},{3,1},{4,2},{5,3},{6,4},{7,5},{8,6},{9,7},{10,8},{11,9},{12,... | collective-permute-start | bytes 7077896 | tf_op jit(solution)/shard_map/ppermute | solution.py:16
  15.9 43.4 %collective-permute-start.1 = (bf16[6,2,3,256,8]{3,4,2,1,0:T(8,128)(2,1)}, bf16[6,2,3,256,8]{3,4,2,1,0:T(8,128)(2,1)}, u32[]{:S(2)}, u32[]{:S(2)}) collective-permute-start(bf16[6,2,3,256,8]{3,4,2,1,0:T(8,128)(2,1)} %copy.140), channel_id=1, source_target_pairs={{0,1},{1,0},{2,3},{3,2},{4,5},{5,4},{6,7},{7,6},{8,9},{9,8},{10,11... | collective-permute-start | bytes 442376 | tf_op jit(solution)/shard_map/ppermute | solution.py:20
  31.6 4.8 %copy-start.3 = (bf16[6,1,3,256,128]{3,4,2,1,0:T(8,128)(2,1)S(1)}, bf16[6,1,3,256,128]{3,4,2,1,0:T(8,128)(2,1)}, u32[]{:S(2)}) copy-start(bf16[6,1,3,256,128]{3,4,2,1,0:T(8,128)(2,1)} %copy.142) | copy-start | bytes 3538948
  45.8 4.7 %copy-start.29 = (f32[6,1,3,1,128]{4,1,3,2,0:T(1,128)S(1)}, f32[6,1,3,1,128]{4,1,3,2,0:T(1,128)}, u32[]{:S(2)}) copy-start(f32[6,1,3,1,128]{4,1,3,2,0:T(1,128)} %get-tuple-element.50) | copy-start | bytes 27652
  45.8 4.8 %copy-start.28 = (f32[6,1,3,1,128]{4,1,3,2,0:T(1,128)S(1)}, f32[6,1,3,1,128]{4,1,3,2,0:T(1,128)}, u32[]{:S(2)}) copy-start(f32[6,1,3,1,128]{4,1,3,2,0:T(1,128)} %get-tuple-element.51) | copy-start | bytes 27652
  45.8 4.8 %copy-start.27 = (f32[6,1,3,1,128]{4,1,3,2,0:T(1,128)S(1)}, f32[6,1,3,1,128]{4,1,3,2,0:T(1,128)}, u32[]{:S(2)}) copy-start(f32[6,1,3,1,128]{4,1,3,2,0:T(1,128)} %get-tuple-element.52) | copy-start | bytes 27652
  45.8 4.8 %copy-start.26 = (f32[6,1,3,1,128]{4,1,3,2,0:T(1,128)S(1)}, f32[6,1,3,1,128]{4,1,3,2,0:T(1,128)}, u32[]{:S(2)}) copy-start(f32[6,1,3,1,128]{4,1,3,2,0:T(1,128)} %get-tuple-element.53) | copy-start | bytes 27652
  45.8 4.8 %copy-start.25 = (f32[6,1,3,1,128]{4,1,3,2,0:T(1,128)S(1)}, f32[6,1,3,1,128]{4,1,3,2,0:T(1,128)}, u32[]{:S(2)}) copy-start(f32[6,1,3,1,128]{4,1,3,2,0:T(1,128)} %get-tuple-element.54) | copy-start | bytes 27652
  45.8 4.8 %copy-start.24 = (f32[6,1,3,1,128]{4,1,3,2,0:T(1,128)S(1)}, f32[6,1,3,1,128]{4,1,3,2,0:T(1,128)}, u32[]{:S(2)}) copy-start(f32[6,1,3,1,128]{4,1,3,2,0:T(1,128)} %get-tuple-element.49) | copy-start | bytes 27652
  45.9 4.8 %copy-start.23 = (f32[6,1,3,1,128]{4,1,3,2,0:T(1,128)S(1)}, f32[6,1,3,1,128]{4,1,3,2,0:T(1,128)}, u32[]{:S(2)}) copy-start(f32[6,1,3,1,128]{4,1,3,2,0:T(1,128)} %get-tuple-element.85) | copy-start | bytes 27652
  45.9 4.8 %copy-start.22 = (f32[6,1,3,1,128]{4,1,3,2,0:T(1,128)S(1)}, f32[6,1,3,1,128]{4,1,3,2,0:T(1,128)}, u32[]{:S(2)}) copy-start(f32[6,1,3,1,128]{4,1,3,2,0:T(1,128)} %get-tuple-element.84) | copy-start | bytes 27652
  45.9 4.9 %copy-start.21 = (f32[6,1,3,1,128]{4,1,3,2,0:T(1,128)S(1)}, f32[6,1,3,1,128]{4,1,3,2,0:T(1,128)}, u32[]{:S(2)}) copy-start(f32[6,1,3,1,128]{4,1,3,2,0:T(1,128)} %get-tuple-element.83) | copy-start | bytes 27652
  45.9 4.9 %copy-start.20 = (f32[6,1,3,1,128]{4,1,3,2,0:T(1,128)S(1)}, f32[6,1,3,1,128]{4,1,3,2,0:T(1,128)}, u32[]{:S(2)}) copy-start(f32[6,1,3,1,128]{4,1,3,2,0:T(1,128)} %get-tuple-element.82) | copy-start | bytes 27652
  45.9 4.9 %copy-start.19 = (f32[6,1,3,1,128]{4,1,3,2,0:T(1,128)S(1)}, f32[6,1,3,1,128]{4,1,3,2,0:T(1,128)}, u32[]{:S(2)}) copy-start(f32[6,1,3,1,128]{4,1,3,2,0:T(1,128)} %get-tuple-element.81) | copy-start | bytes 27652
  45.9 4.9 %copy-start.18 = (f32[6,1,3,1,128]{4,1,3,2,0:T(1,128)S(1)}, f32[6,1,3,1,128]{4,1,3,2,0:T(1,128)}, u32[]{:S(2)}) copy-start(f32[6,1,3,1,128]{4,1,3,2,0:T(1,128)} %get-tuple-element.86) | copy-start | bytes 27652
  117.9 4.8 %copy-start.8 = (f32[6,256,128]{2,1,0:T(8,128)S(1)}, f32[6,256,128]{2,1,0:T(8,128)}, u32[]{:S(2)}) copy-start(f32[6,256,128]{2,1,0:T(8,128)} %get-tuple-element.35) | copy-start | bytes 2359300
  117.9 6.0 %copy-start.7 = (f32[6,256,128]{2,1,0:T(8,128)S(1)}, f32[6,256,128]{2,1,0:T(8,128)}, u32[]{:S(2)}) copy-start(f32[6,256,128]{2,1,0:T(8,128)} %get-tuple-element.34) | copy-start | bytes 2359300
  230.2 4.8 %copy-start.5 = (bf16[1,2,256,1024]{3,2,1,0:T(8,128)(2,1)S(1)}, bf16[1,2,256,1024]{3,2,1,0:T(8,128)(2,1)}, u32[]{:S(2)}) copy-start(bf16[1,2,256,1024]{3,2,1,0:T(8,128)(2,1)} %param.8) | copy-start | bytes 3145732
  230.2 36.5 %all-to-all-start = ((bf16[16,2,96,256]{3,2,1,0:T(8,128)(2,1)}), bf16[16,2,96,256]{3,2,1,0:T(8,128)(2,1)}, u32[]{:S(2)}, u32[]{:S(2)}) async-start(bf16[16,2,96,256]{3,2,1,0:T(8,128)(2,1)} %broadcast_select_fusion), calls=%async_computation.1 | async-start | bytes 3145728 | tf_op jit(solution)/shard_map/all_to_all | solution.py:137
  (12 other events, 29.8 us)
Sparse Core Ops, SparseCore 0:
  149.7 77.4 reduce-scatter.1

commit v2 on v1

--- a/solution.py
+++ b/solution.py
@@ -1,8 +1,11 @@
+import functools
 import math
 
 import jax
 import jax.numpy as jnp
 from jax import lax
+from jax.experimental import pallas as pl
+from jax.experimental.pallas import tpu as pltpu
 from jax.sharding import PartitionSpec as P
 
 NSPIN = 4
@@ -28,52 +31,78 @@
     return 2.0 * math.pi * fraction
 
 
-def to_rows(field):
-    count_t, _, _, count_ev, sites = field.shape
-    return field.transpose(0, 3, 1, 2, 4).reshape(count_t, count_ev, 6 * sites)
+def sums_kernel(slot_ref, field_ref, far_ref, row_ref, link_ref, trig_ref, out_ref, *, scale):
+    count_ev, sites = field_ref.shape[3], field_ref.shape[4]
+    lane = lax.broadcasted_iota(jnp.int32, (count_ev, sites), 1)
+    last_z = lane % LZ == LZ - 1
+    last_row = lane >= sites - LZ
+    cosine = trig_ref[0:1, :]
+    sine_part = trig_ref[1:2, :]
+    here = [[field_ref[0, part, colour].astype(jnp.float32) for colour in range(3)] for part in range(2)]
+    phased_real = [(cosine * here[0][c] - sine_part * here[1][c]).astype(jnp.bfloat16) for c in range(3)]
+    phased_imag = [(sine_part * here[0][c] + cosine * here[1][c]).astype(jnp.bfloat16) for c in range(3)]
+    real_rows = jnp.concatenate(phased_real + phased_imag, axis=1)
+    imag_rows = jnp.concatenate([-v for v in phased_imag] + phased_real, axis=1)
+    left = jnp.concatenate([real_rows, imag_rows], axis=0)
+    far = [[far_ref[0, part, colour].astype(jnp.float32) for colour in range(3)] for part in range(2)]
+    along_y = [
+        [
+            jnp.where(last_row, row_ref[0, part, colour].astype(jnp.float32), pltpu.roll(here[part][colour], sites - LZ, 1))
+            for colour in range(3)
+        ]
+        for part in range(2)
+    ]
+    along_z = [
+        [
+            jnp.where(last_z, pltpu.roll(here[part][colour], LZ - 1, 1), pltpu.roll(here[part][colour], sites - 1, 1))
+            for colour in range(3)
+        ]
+        for part in range(2)
+    ]
+    rows = 2 * count_ev
+    for course, near in enumerate((far, along_y, along_z)):
+        moved_real = []
+        moved_imag = []
+        for outer in range(3):
+            real_part = 0.0
+            imag_part = 0.0
+            for inner in range(3):
+                link_real = link_ref[0, course, 0, outer, inner : inner + 1, :]
+                link_imag = link_ref[0, course, 1, outer, inner : inner + 1, :]
+                real_part = real_part + link_real * near[0][inner] - link_imag * near[1][inner]
+                imag_part = imag_part + link_real * near[1][inner] + link_imag * near[0][inner]
+            moved_real.append(real_part.astype(jnp.bfloat16))
+            moved_imag.append(imag_part.astype(jnp.bfloat16))
+        right = jnp.concatenate(moved_real + moved_imag, axis=1)
+        joined = lax.dot_general(left, right, (((1,), (1,)), ((), ())), preferred_element_type=jnp.float32)
+        start = pl.multiple_of(slot_ref[course] * rows, rows)
+        out_ref[0, pl.ds(start, rows), :] = (joined * scale).astype(out_ref.dtype)
 
 
-def carried(link, field):
-    field = field.astype(jnp.float32)
-    real_part = 0.0
-    imag_part = 0.0
-    for inner in range(3):
-        link_real = link[:, 0, :, inner][:, :, None, :]
-        link_imag = link[:, 1, :, inner][:, :, None, :]
-        field_real = field[:, 0, inner][:, None]
-        field_imag = field[:, 1, inner][:, None]
-        real_part = real_part + link_real * field_real - link_imag * field_imag
-        imag_part = imag_part + link_real * field_imag + link_imag * field_real
-    return jnp.stack([real_part, imag_part], 1).astype(jnp.bfloat16)
-
-
-def local_sums(eigenvectors, gauge_links, far_tile, row_in, directions, angle):
-    sites = eigenvectors.shape[-1]
-    along_y = jnp.concatenate([eigenvectors[..., LZ:], row_in], axis=-1)
-    column_pos = jnp.arange(sites, dtype=jnp.int32) % LZ
-    along_z = jnp.where(
-        column_pos == LZ - 1,
-        jnp.roll(eigenvectors, LZ - 1, axis=-1),
-        jnp.roll(eigenvectors, -1, axis=-1),
+def local_sums(eigenvectors, gauge_links, far_tile, row_in, directions, angle, scale):
+    time_count, _, _, count_ev, sites = eigenvectors.shape
+    count_ops = directions.shape[0]
+    slot_of = jnp.sum(
+        (directions[None, :] == jnp.arange(count_ops, dtype=jnp.int32)[:, None]) * jnp.arange(count_ops, dtype=jnp.int32)[None, :],
+        axis=1,
+    ).astype(jnp.int32)
+    row_wide = jnp.pad(row_in, ((0, 0),) * 4 + ((sites - LZ, 0),))
+    trig = jnp.stack([jnp.cos(angle), jnp.sin(angle)], 0)
+    field_spec = pl.BlockSpec((1, 2, 3, count_ev, sites), lambda t, slot: (t, 0, 0, 0, 0))
+    link_spec = pl.BlockSpec((1,) + gauge_links.shape[1:], lambda t, slot: (t, 0, 0, 0, 0, 0))
+    trig_spec = pl.BlockSpec(trig.shape, lambda t, slot: (0, 0))
+    rows = count_ops * 2 * count_ev
+    grid_spec = pltpu.PrefetchScalarGridSpec(
+        num_scalar_prefetch=1,
+        grid=(time_count,),
+        in_specs=[field_spec, field_spec, field_spec, link_spec, trig_spec],
+        out_specs=pl.BlockSpec((1, rows, count_ev), lambda t, slot: (t, 0, 0)),
     )
-    right = []
-    for slot in range(directions.shape[0]):
-        course = directions[slot]
-        near = jnp.where(course == 0, far_tile, jnp.where(course == 1, along_y, along_z))
-        link = lax.dynamic_index_in_dim(gauge_links, course, 1, keepdims=False)
-        right.append(to_rows(carried(link, near)))
-    right = jnp.stack(right, 1)
-    cosine = jnp.cos(angle)[None, None, None, :]
-    sine_part = jnp.sin(angle)[None, None, None, :]
-    field_real = eigenvectors[:, 0].astype(jnp.float32)
-    field_imag = eigenvectors[:, 1].astype(jnp.float32)
-    phased_real = (cosine * field_real - sine_part * field_imag).astype(jnp.bfloat16)
-    phased_imag = (sine_part * field_real + cosine * field_imag).astype(jnp.bfloat16)
-    real_rows = to_rows(jnp.stack([phased_real, phased_imag], 1))
-    imag_rows = to_rows(jnp.stack([-phased_imag, phased_real], 1))
-    left = jnp.concatenate([real_rows, imag_rows], axis=1)
-    joined = jnp.einsum("tPk,tajk->taPj", left, right, preferred_element_type=jnp.float32)
-    return joined.reshape(joined.shape[0], -1, joined.shape[-1])
+    return pl.pallas_call(
+        functools.partial(sums_kernel, scale=scale),
+        grid_spec=grid_spec,
+        out_shape=jax.ShapeDtypeStruct((time_count, rows, count_ev), jnp.bfloat16),
+    )(slot_of, eigenvectors, far_tile, row_wide, gauge_links, trig)
 
 
 def contract_panel(sink, source, panel):
@@ -126,16 +155,15 @@
     angle = phase_angles(momenta, (coord_x, coord_y, coord_z), (extent_x, LY, LZ))[0]
     far_tile = shifted(eigenvectors, "space", -2)
     row_in = swapped(eigenvectors[..., :LZ], "space", 0)
-    summands = local_sums(eigenvectors, gauge_links, far_tile, row_in, directions, angle)
     scale = 1.0 / math.sqrt(3.0 * extent_x * LY * LZ)
-    partial = (summands * scale).astype(jnp.bfloat16)
+    partial = local_sums(eigenvectors, gauge_links, far_tile, row_in, directions, angle, scale)
     own_rows = lax.psum_scatter(partial, "space", scatter_dimension=1, tiled=True)
     rows = own_rows.shape[1]
     target = jnp.arange(nspace, dtype=jnp.int32) // NSPIN
     wanted = jnp.stack([pair_times[target, 1], pair_times[target, 0]], 1)
     outgoing = jnp.take(own_rows, wanted.reshape(-1), axis=0).reshape(nspace, 2, rows, count_ev)
     incoming = lax.all_to_all(outgoing, "space", 0, 0, tiled=True)
-    count_ops = summands.shape[1] // (2 * count_ev)
+    count_ops = partial.shape[1] // (2 * count_ev)
     gathered = incoming.transpose(1, 0, 2, 3).reshape(2, count_ops, 2, count_ev, count_ev)
     correlators = contract_panel(gathered[0], gathered[1], perambulators[0])[None]
     return (own_rows, correlators)

time: 288 us -> 218 us (0.76)
  local copies, waits for them, and re-layouts: 89.1 us -> 21.8 us
  waiting for transfers between devices: 103 us -> 142 us
  other arithmetic: 42 us -> 7.61 us
  Pallas kernels: 0 us -> 12.9 us
  between operations: 25 us -> 15 us
  matrix products: 12.9 us -> 3.9 us
    ppermute x1, waiting for transfers between devices: 2.06 us -> 40.6 us  [shifted(): return lax.ppermute(block, axis, route)]
    mul x20 -> x0, local copies, waits for them, and re-layouts: 30.6 us -> none  [carried(): real_part = real_part + link_real * field_real - link_imag * field_imag]
    another operation x7 -> x1, other arithmetic: 18.9 us -> 0.58 us  [local_sums(): trig = jnp.stack([jnp.cos(angle), jnp.sin(angle)], 0)]
    convert_element_type x3 -> x0, other arithmetic: 14.9 us -> none  [the longest x2 13.1 us: carried(): field = field.astype(jnp.float32)]
    pallas_call x0 -> x1, Pallas kernels: none -> 12.9 us  [local_sums(): pl.pallas_call(functools.partial(sums_kernel, scale=scale), grid_spec=gri...]
    slice x7 -> x0, local copies, waits for them, and re-layouts: 9.47 us -> none  [the longest x1 2.19 us: local_sums(): along_y = jnp.concatenate([eigenvectors[..., LZ:], row_in], axis=-1)]
    another operation x3 -> x0, local copies, waits for them, and re-layouts: 9.46 us -> none  [local_sums(): right = jnp.stack(right, 1)]
    dot_general x1 -> x0, matrix products: 8.96 us -> none  [local_sums(): jnp.einsum('tPk,tajk->taPj', left, right, preferred_element_type=jnp.floa...]
  transfers between devices with their start and end apart: 4 -> 4, of which waited for: 3 -> 3; matrix products, arithmetic and copies ran while one was open for 16% -> 8% of each run, Pallas kernels for 0% -> 0%
where the time goes in v2:
time: 218 us; the launch traced here: 214 us
  waiting for transfers between devices  142 us (65%)
  local copies, waits for them, and re-layouts  21.8 us (10%)
  between operations  15 us (7%)
  Pallas kernels  12.9 us (6%)
  starting transfers between devices  10.7 us (5%)
  other arithmetic  7.61 us (3%)
  matrix products  3.9 us (2%)
    reduce_scatter x1, waiting for transfers between devices, body(): lax.psum_scatter(partial, 'space', scatter_dimension=1, tiled=True)  75.8 us
    ppermute x1, waiting for transfers between devices, shifted(): return lax.ppermute(block, axis, route)  40.6 us
    all_to_all x1, waiting for transfers between devices, body(): incoming = lax.all_to_all(outgoing, 'space', 0, 0, tiled=True)  25.6 us
    pallas_call x1, Pallas kernels, local_sums(): pl.pallas_call(functools.partial(sums_kernel, scale=scale), grid_spec=gri...  12.9 us
    ppermute x1, starting transfers between devices, shifted(): return lax.ppermute(block, axis, route)  6.06 us
    all_to_all x1, starting transfers between devices, body(): incoming = lax.all_to_all(outgoing, 'space', 0, 0, tiled=True)  4.53 us
  transfers between devices with their start and end apart: 4, of which 3 were waited for; matrix products, arithmetic and copies ran while one was open for 8% of the time, Pallas kernels for 0%

profile of v2, /device:TPU:0, one launch (start us, length us, event | category | flops | bytes accessed | tf_op | source)
XLA Modules:
  0.0 214.0 jit_solution(16236659643630295406)
XLA Ops:
  7.3 6.1 %collective-permute-start = (bf16[6,2,3,256,128]{4,3,2,1,0:T(8,128)(2,1)}, bf16[6,2,3,256,128]{4,3,2,1,0:T(8,128)(2,1)}, u32[]{:S(2)}, u32[]{:S(2)}) collective-permute-start(bf16[6,2,3,256,128]{4,3,2,1,0:T(8,128)(2,1)} %field_ref.1), channel_id=1, source_target_pairs={{2,0},{3,1},{4,2},{5,3},{6,4},{7,5},{8,6},{9,7},{10,8},{11,9},{12,... | collective-permute-start | bytes 7077896 | tf_op jit(solution)/shard_map/ppermute | solution.py:19
  13.3 2.0 copy.51
  16.7 1.3 fusion.19
  18.7 0.7 copy.38.link_ref
  20.0 1.1 copy.37
  21.1 2.4 %pad.6.row_ref = bf16[6,2,3,256,128]{4,3,2,1,0:T(8,128)(2,1)} pad(bf16[6,2,3,256,8]{4,3,2,1,0:T(8,128)(2,1)S(1)} %copy.37, bf16[]{:T(256)} %constant.114.clone.1), padding=0_0x0_0x0_0x0_0x120_0 | pad | bytes 2506754 | tf_op jit(solution)/shard_map/jit(_pad)/pad | solution.py:89
  23.5 40.6 %collective-permute-done.far_ref = bf16[6,2,3,256,128]{4,3,2,1,0:T(8,128)(2,1)} collective-permute-done((bf16[6,2,3,256,128]{4,3,2,1,0:T(8,128)(2,1)}, bf16[6,2,3,256,128]{4,3,2,1,0:T(8,128)(2,1)}, u32[]{:S(2)}, u32[]{:S(2)}) %collective-permute-start) | collective-permute-done | bytes 2359328 | tf_op jit(solution)/shard_map/ppermute | solution.py:19
  64.1 12.9 %shard_map.77 = bf16[6,1536,256]{2,1,0:T(8,128)(2,1)} custom-call(s32[3]{0:T(128)} %select_reduce_fusion.slot_ref, bf16[6,2,3,256,128]{4,3,2,1,0:T(8,128)(2,1)} %field_ref.1, bf16[6,2,3,256,128]{4,3,2,1,0:T(8,128)(2,1)} %collective-permute-done.far_ref, bf16[6,2,3,256,128]{4,3,2,1,0:T(8,128)(2,1)} %pad.6.row_ref, f32[6,3,2,3,3,128]{5,4,3,2,1,0:T(4,128)} %copy.38.link_ref, ...), custom_call_target="tpu_custom_call" | custom-call | tf_op jit(solution)/shard_map/pallas_call | solution.py:101
  78.8 75.8 %reduce-scatter.2.cloned.1.call-done = bf16[6,96,256]{2,1,0:T(8,128)(2,1)} async-done(((bf16[6,1536,256]{2,1,0:T(8,128)(2,1)}), bf16[6,96,256]{2,1,0:T(8,128)(2,1)}) %reduce-scatter.2.cloned.1.call-update) | async-done | bytes 294928 | tf_op jit(solution)/shard_map/reduce_scatter | solution.py:160
  154.6 1.6 gather_fusion.2
  156.3 1.3 broadcast_select_fusion
  157.6 4.5 %all-to-all-start = ((bf16[16,2,96,256]{3,2,1,0:T(8,128)(2,1)}), bf16[16,2,96,256]{3,2,1,0:T(8,128)(2,1)}, u32[]{:S(2)}, u32[]{:S(2)}) async-start(bf16[16,2,96,256]{3,2,1,0:T(8,128)(2,1)} %broadcast_select_fusion), calls=%async_computation.1 | async-start | bytes 3145728 | tf_op jit(solution)/shard_map/all_to_all | solution.py:165
  162.2 1.3 copy.43
  164.0 1.1 squeeze.28
  165.1 1.4 maximum_maximum_fusion
  166.5 2.1 dot_general.22
  168.5 25.6 %all-to-all-done = bf16[16,2,96,256]{3,2,1,0:T(8,128)(2,1)} async-done(((bf16[16,2,96,256]{3,2,1,0:T(8,128)(2,1)}), bf16[16,2,96,256]{3,2,1,0:T(8,128)(2,1)}, u32[]{:S(2)}, u32[]{:S(2)}) %all-to-all-start) | async-done | bytes 1572896 | tf_op jit(solution)/shard_map/all_to_all | solution.py:165
  194.1 2.3 %fusion.21 = (bf16[1,16,96,256]{3,2,0,1:T(8,128)(2,1)S(1)}, bf16[1,16,96,256]{3,2,0,1:T(8,128)(2,1)}) fusion(bf16[2,16,96,256]{3,2,0,1:T(8,128)(2,1)} %bitcast.9), kind=kLoop, calls=%fused_computation.57 | loop fusion | bytes 3145728 | tf_op jit(solution)/shard_map/slice | solution.py:168
  196.5 0.9 slice_bitcast_fusion
  197.4 2.3 %copy.44 = bf16[2,256,3,256]{1,0,3,2:T(2,128)(2,1)S(1)} copy(bf16[2,256,3,256]{3,1,0,2:T(8,128)(2,1)} %bitcast.75) | data formatting | bytes 1572864 | tf_op jit(solution)/shard_map/transpose | solution.py:131
  199.9 2.1 convolution_bitcast_fusion
  202.2 1.1 copy-done.5
  203.2 1.8 fusion.24
  205.1 1.5 add_reduce_fusion
  (43 shorter events, 5.1 us)
Async XLA Ops:
  7.2 69.9 %copy-start = (s32[4,2]{0,1:T(2,128)S(1)}, s32[4,2]{0,1:T(2,128)}, u32[]{:S(2)}) copy-start(s32[4,2]{0,1:T(2,128)} %param.11) | copy-start | bytes 100
  7.2 8.2 %copy-start.7 = (s32[1,3]{1,0:T(1,128)S(1)}, s32[1,3]{1,0:T(1,128)}, u32[]{:S(2)}) copy-start(s32[1,3]{1,0:T(1,128)} %param.10) | copy-start | bytes 40
  7.2 11.5 %copy-start.6 = (f32[6,3,2,3,3,128]{5,2,4,3,1,0:T(2,128)S(1)}, f32[6,3,2,3,3,128]{5,2,4,3,1,0:T(2,128)}, u32[]{:S(2)}) copy-start(f32[6,3,2,3,3,128]{5,2,4,3,1,0:T(2,128)} %param.7) | copy-start | bytes 497668
  7.2 12.2 %copy-start.8 = (s32[3]{0:T(128)S(1)}, s32[3]{0:T(128)}, u32[]{:S(2)}) copy-start(s32[3]{0:T(128)} %param.9) | copy-start | bytes 40
  7.2 147.4 %reduce-scatter.2.cloned.1.call-start = ((), (), s32[]{:S(2)}) async-start(), calls=%async_computation.2 | async-start | bytes 5013504 | tf_op jit(solution)/shard_map/reduce_scatter | solution.py:160
  7.3 56.9 %collective-permute-start = (bf16[6,2,3,256,128]{4,3,2,1,0:T(8,128)(2,1)}, bf16[6,2,3,256,128]{4,3,2,1,0:T(8,128)(2,1)}, u32[]{:S(2)}, u32[]{:S(2)}) collective-permute-start(bf16[6,2,3,256,128]{4,3,2,1,0:T(8,128)(2,1)} %field_ref.1), channel_id=1, source_target_pairs={{2,0},{3,1},{4,2},{5,3},{6,4},{7,5},{8,6},{9,7},{10,8},{11,9},{12,... | collective-permute-start | bytes 7077896 | tf_op jit(solution)/shard_map/ppermute | solution.py:19
  15.3 4.7 %collective-permute-start.1 = (bf16[6,2,3,256,8]{3,4,2,1,0:T(8,128)(2,1)S(1)}, bf16[6,2,3,256,8]{3,4,2,1,0:T(8,128)(2,1)S(1)}, u32[]{:S(2)}, u32[]{:S(2)}) collective-permute-start(bf16[6,2,3,256,8]{3,4,2,1,0:T(8,128)(2,1)S(1)} %copy.51), channel_id=1, source_target_pairs={{0,1},{1,0},{2,3},{3,2},{4,5},{5,4},{6,7},{7,6},{8,9},{9,8},{10,11... | collective-permute-start | bytes 442376 | tf_op jit(solution)/shard_map/ppermute | solution.py:23
  157.6 4.5 %copy-start.2 = (bf16[1,2,256,1024]{3,2,1,0:T(8,128)(2,1)S(1)}, bf16[1,2,256,1024]{3,2,1,0:T(8,128)(2,1)}, u32[]{:S(2)}) copy-start(bf16[1,2,256,1024]{3,2,1,0:T(8,128)(2,1)} %param.8) | copy-start | bytes 3145732
  157.6 36.5 %all-to-all-start = ((bf16[16,2,96,256]{3,2,1,0:T(8,128)(2,1)}), bf16[16,2,96,256]{3,2,1,0:T(8,128)(2,1)}, u32[]{:S(2)}, u32[]{:S(2)}) async-start(bf16[16,2,96,256]{3,2,1,0:T(8,128)(2,1)} %broadcast_select_fusion), calls=%async_computation.1 | async-start | bytes 3145728 | tf_op jit(solution)/shard_map/all_to_all | solution.py:165
  196.5 3.4 %copy-start.1 = (bf16[2,256,4,512]{3,2,1,0:T(4,128)(2,1)S(1)}, bf16[2,256,4,512]{3,2,1,0:T(4,128)(2,1)}, u32[]{:S(2)}) copy-start(bf16[2,256,4,512]{3,2,1,0:T(4,128)(2,1)} %dot_general.22) | copy-start | bytes 6291460
  199.9 2.1 copy-start.3
  199.9 2.1 copy-start.4
  202.0 1.2 copy-start.5
Sparse Core Ops, SparseCore 0:
  77.2 77.4 reduce-scatter.1

commit v3 on v2

--- a/solution.py
+++ b/solution.py
@@ -6,7 +6,7 @@
 from jax import lax
 from jax.experimental import pallas as pl
 from jax.experimental.pallas import tpu as pltpu
-from jax.sharding import PartitionSpec as P
+from jax.sharding import Mesh, PartitionSpec as P
 
 NSPIN = 4
 LY = 32
@@ -101,7 +101,7 @@
     return pl.pallas_call(
         functools.partial(sums_kernel, scale=scale),
         grid_spec=grid_spec,
-        out_shape=jax.ShapeDtypeStruct((time_count, rows, count_ev), jnp.bfloat16),
+        out_shape=jax.ShapeDtypeStruct((time_count, rows, count_ev), jnp.float32),
     )(slot_of, eigenvectors, far_tile, row_wide, gauge_links, trig)
 
 
@@ -141,47 +141,56 @@
 
 
 def body(eigenvectors, gauge_links, perambulators, directions, momenta, pair_times):
-    time_count = eigenvectors.shape[0]
     count_ev = eigenvectors.shape[3]
     local_sites = eigenvectors.shape[4]
-    nspace = lax.axis_size("space")
-    device = lax.axis_index("space")
+    count_chips = lax.axis_size("chip")
+    nspace = 2 * count_chips
+    core = lax.axis_index("core")
+    device = lax.axis_index("chip") * 2 + core
     half_rows = LY // 2
-    extent_x = nspace // 2
+    extent_x = count_chips
     column = jnp.arange(local_sites, dtype=jnp.int32)
     coord_x = device // 2 + 0 * column
     coord_y = device % 2 * half_rows + column // LZ
     coord_z = column % LZ
     angle = phase_angles(momenta, (coord_x, coord_y, coord_z), (extent_x, LY, LZ))[0]
-    far_tile = shifted(eigenvectors, "space", -2)
-    row_in = swapped(eigenvectors[..., :LZ], "space", 0)
+    far_tile = shifted(eigenvectors, "chip", -1)
+    row_in = swapped(eigenvectors[..., :LZ], "core", 0)
     scale = 1.0 / math.sqrt(3.0 * extent_x * LY * LZ)
     partial = local_sums(eigenvectors, gauge_links, far_tile, row_in, directions, angle, scale)
-    own_rows = lax.psum_scatter(partial, "space", scatter_dimension=1, tiled=True)
-    rows = own_rows.shape[1]
+    time_count, all_rows = partial.shape[0], partial.shape[1]
+    rows = all_rows // nspace
+    blocks = partial.reshape(time_count, count_chips, 2, rows, count_ev)
+    chip_sums = lax.psum_scatter(blocks, "core", scatter_dimension=2, tiled=True)
+    own_rows = lax.psum_scatter(chip_sums.astype(jnp.bfloat16), "chip", scatter_dimension=1, tiled=True)
+    own_rows = own_rows.reshape(time_count, rows, count_ev)
     target = jnp.arange(nspace, dtype=jnp.int32) // NSPIN
     wanted = jnp.stack([pair_times[target, 1], pair_times[target, 0]], 1)
     outgoing = jnp.take(own_rows, wanted.reshape(-1), axis=0).reshape(nspace, 2, rows, count_ev)
-    incoming = lax.all_to_all(outgoing, "space", 0, 0, tiled=True)
-    count_ops = partial.shape[1] // (2 * count_ev)
+    incoming = lax.all_to_all(outgoing, ("chip", "core"), 0, 0, tiled=True)
+    count_ops = all_rows // (2 * count_ev)
     gathered = incoming.transpose(1, 0, 2, 3).reshape(2, count_ops, 2, count_ev, count_ev)
     correlators = contract_panel(gathered[0], gathered[1], perambulators[0])[None]
     return (own_rows, correlators)
 
 
 def solution(mesh):
+    count_cfg = mesh.shape["cfg"]
+    count_chips = mesh.shape["space"] // 2
+    split = Mesh(mesh.devices.reshape(count_cfg, count_chips, 2), ("cfg", "chip", "core"))
+    space = ("chip", "core")
     placed = (
-        P("cfg", None, None, None, "space"),
-        P("cfg", None, None, None, None, "space"),
-        P(("cfg", "space"), None, None, None),
+        P("cfg", None, None, None, space),
+        P("cfg", None, None, None, None, space),
+        P(("cfg",) + space, None, None, None),
         P(),
         P(),
         P(),
     )
     return jax.shard_map(
         body,
-        mesh=mesh,
+        mesh=split,
         in_specs=placed,
-        out_specs=(P("cfg", "space", None), P(("cfg", "space"), None, None)),
+        out_specs=(P("cfg", space, None), P(("cfg",) + space, None, None)),
         check_vma=False,
     )

time: 218 us -> 249 us (1.14)
  blocking collectives: 0 us -> 28.1 us
  local copies, waits for them, and re-layouts: 21.8 us -> 31.4 us
  waiting for transfers between devices: 142 us -> 135 us
    unnamed x0 -> x1, blocking collectives: none -> 28.1 us
    reshape x0 -> x1, local copies, waits for them, and re-layouts: none -> 8.53 us  [body(): blocks = partial.reshape(time_count, count_chips, 2, rows, count_ev)]
    reduce_scatter x1, waiting for transfers between devices: 75.8 us -> 69.4 us  [body(): lax.psum_scatter(chip_sums.astype(jnp.bfloat16), 'chip', scatter_dimensio...]
    convert_element_type x0 -> x1, local copies, waits for them, and re-layouts: none -> 3.94 us  [body(): chip_sums.astype(jnp.bfloat16)]
  transfers between devices with their start and end apart: 4 -> 4, of which waited for: 3 -> 3; matrix products, arithmetic and copies ran while one was open for 8% -> 7% of each run, Pallas kernels for 0% -> 0%
where the time goes in v3:
time: 249 us; the launch traced here: 245 us
  waiting for transfers between devices  135 us (54%)
  local copies, waits for them, and re-layouts  31.4 us (13%)
  blocking collectives  28.1 us (11%)
  between operations  15 us (6%)
  Pallas kernels  13.6 us (5%)
  starting transfers between devices  10.9 us (4%)
  other arithmetic  7.6 us (3%)
  matrix products  3.9 us (2%)
    reduce_scatter x1, waiting for transfers between devices, body(): lax.psum_scatter(chip_sums.astype(jnp.bfloat16), 'chip', scatter_dimensio...  69.4 us
    ppermute x1, waiting for transfers between devices, shifted(): return lax.ppermute(block, axis, route)  40.1 us
    unnamed x1, blocking collectives  28.1 us
    all_to_all x1, waiting for transfers between devices, body(): incoming = lax.all_to_all(outgoing, ('chip', 'core'), 0, 0, tiled=True)  25.4 us
    pallas_call x1, Pallas kernels, local_sums(): pl.pallas_call(functools.partial(sums_kernel, scale=scale), grid_spec=gri...  13.6 us
    reshape x1, local copies, waits for them, and re-layouts, body(): blocks = partial.reshape(time_count, count_chips, 2, rows, count_ev)  8.53 us
    ppermute x1, starting transfers between devices, shifted(): return lax.ppermute(block, axis, route)  6.06 us
  transfers between devices with their start and end apart: 4, of which 3 were waited for; matrix products, arithmetic and copies ran while one was open for 7% of the time, Pallas kernels for 0%

profile of v3, /device:TPU:0, one launch (start us, length us, event | category | flops | bytes accessed | tf_op | source)
XLA Modules:
  0.0 245.2 jit_solution(17643102878722424794)
XLA Ops:
  7.3 6.1 %collective-permute-start = (bf16[6,2,3,256,128]{4,3,2,1,0:T(8,128)(2,1)}, bf16[6,2,3,256,128]{4,3,2,1,0:T(8,128)(2,1)}, u32[]{:S(2)}, u32[]{:S(2)}) collective-permute-start(bf16[6,2,3,256,128]{4,3,2,1,0:T(8,128)(2,1)} %field_ref.1), channel_id=1, source_target_pairs={{2,0},{4,2},{6,4},{8,6},{10,8},{12,10},{14,12},{0,14},{3,1},{5,3},... | collective-permute-start | bytes 7077896 | tf_op jit(solution)/shard_map/ppermute | solution.py:19
  13.3 2.0 copy.60
  16.7 1.3 fusion.19
  20.6 1.1 copy.44
  21.7 2.4 pad.6.row_ref
  24.1 40.1 %collective-permute-done.far_ref = bf16[6,2,3,256,128]{4,3,2,1,0:T(8,128)(2,1)} collective-permute-done((bf16[6,2,3,256,128]{4,3,2,1,0:T(8,128)(2,1)}, bf16[6,2,3,256,128]{4,3,2,1,0:T(8,128)(2,1)}, u32[]{:S(2)}, u32[]{:S(2)}) %collective-permute-start) | collective-permute-done | bytes 2359328 | tf_op jit(solution)/shard_map/ppermute | solution.py:19
  64.1 13.6 %shard_map.77 = f32[6,1536,256]{2,1,0:T(8,128)} custom-call(s32[3]{0:T(128)} %select_reduce_fusion.slot_ref, bf16[6,2,3,256,128]{4,3,2,1,0:T(8,128)(2,1)} %field_ref.1, bf16[6,2,3,256,128]{4,3,2,1,0:T(8,128)(2,1)} %collective-permute-done.far_ref, bf16[6,2,3,256,128]{4,3,2,1,0:T(8,128)(2,1)} %pad.6.row_ref, f32[6,3,2,3,3,128]{5,4,3,2,1,0:T(4,128)} %copy.45.link_ref, ...), custom_call_target="tpu_custom_call" | custom-call | tf_op jit(solution)/shard_map/pallas_call | solution.py:101
  77.7 8.5 %copy.46 = f32[6,8,2,96,256]{4,3,0,2,1:T(8,128)} copy(f32[6,8,2,96,256]{4,3,2,1,0:T(8,128)} %bitcast.77) | data formatting | bytes 18874368 | tf_op jit(solution)/shard_map/reshape | solution.py:163
  86.3 28.1 %all-reduce.5 = bf16[6,8,2,96,256]{4,3,0,2,1:T(8,128)(2,1)} all-reduce(f32[6,8,2,96,256]{4,3,0,2,1:T(8,128)} %copy.46), channel_id=2, replica_groups=mesh['cfg'=2,'chip'=8,'core'=2] {'core'}, use_global_device_ids=true, to_apply=%region_1.2.clone | all-reduce | flops 2359296 | bytes 14155776
  114.3 3.9 %dynamic-slice_convert_fusion = bf16[6,8,1,96,256]{4,3,0,2,1:T(8,128)(2,1)} fusion(bf16[6,8,2,96,256]{4,3,0,2,1:T(8,128)(2,1)} %all-reduce.5, u32[]{:T(128)} %bitcast.41), kind=kLoop, calls=%fused_computation.3 | loop fusion | bytes 4718596 | tf_op jit(solution)/shard_map/convert_element_type | solution.py:165
  120.0 69.4 %reduce-scatter.5.cloned.1.call-done = bf16[6,1,1,96,256]{4,3,0,2,1:T(8,128)(2,1)} async-done(((bf16[6,8,1,96,256]{4,3,0,2,1:T(8,128)(2,1)}), bf16[6,1,1,96,256]{4,3,0,2,1:T(8,128)(2,1)}) %reduce-scatter.5.cloned.1.call-update) | async-done | bytes 294928 | tf_op jit(solution)/shard_map/reduce_scatter | solution.py:165
  189.4 1.6 gather_fusion.2
  191.0 1.4 broadcast_select_fusion
  192.4 4.7 %all-to-all-start = ((bf16[16,2,96,256]{3,2,1,0:T(8,128)(2,1)}), bf16[16,2,96,256]{3,2,1,0:T(8,128)(2,1)}, u32[]{:S(2)}, u32[]{:S(2)}) async-start(bf16[16,2,96,256]{3,2,1,0:T(8,128)(2,1)} %broadcast_select_fusion), calls=%async_computation.1 | async-start | bytes 3145728 | tf_op jit(solution)/shard_map/all_to_all | solution.py:170
  197.1 1.3 copy.50
  198.9 1.1 squeeze.28
  200.0 1.4 maximum_maximum_fusion
  201.4 2.1 dot_general.22
  203.5 25.4 %all-to-all-done = bf16[16,2,96,256]{3,2,1,0:T(8,128)(2,1)} async-done(((bf16[16,2,96,256]{3,2,1,0:T(8,128)(2,1)}), bf16[16,2,96,256]{3,2,1,0:T(8,128)(2,1)}, u32[]{:S(2)}, u32[]{:S(2)}) %all-to-all-start) | async-done | bytes 1572896 | tf_op jit(solution)/shard_map/all_to_all | solution.py:170
  228.9 1.5 fusion.21
  231.4 0.9 copy-done.4
  232.3 1.8 fusion.24
  234.2 2.1 convolution_bitcast_fusion
  236.3 1.5 add_reduce_fusion
  (47 shorter events, 7.2 us)
Async XLA Ops:
  7.2 111.2 %copy-start = (s32[4,2]{0,1:T(2,128)S(1)}, s32[4,2]{0,1:T(2,128)}, u32[]{:S(2)}) copy-start(s32[4,2]{0,1:T(2,128)} %param.11) | copy-start | bytes 100
  7.2 12.1 %copy-start.8 = (u32[32]{0:T(128)S(1)}, u32[32]{0:T(128)}, u32[]{:S(2)}) copy-start(u32[32]{0:T(128)} %constant.177) | copy-start | bytes 388
  7.2 8.2 %copy-start.6 = (s32[1,3]{1,0:T(1,128)S(1)}, s32[1,3]{1,0:T(1,128)}, u32[]{:S(2)}) copy-start(s32[1,3]{1,0:T(1,128)} %param.10) | copy-start | bytes 40
  7.2 11.4 %copy-start.5 = (f32[6,3,2,3,3,128]{5,2,4,3,1,0:T(2,128)S(1)}, f32[6,3,2,3,3,128]{5,2,4,3,1,0:T(2,128)}, u32[]{:S(2)}) copy-start(f32[6,3,2,3,3,128]{5,2,4,3,1,0:T(2,128)} %param.7) | copy-start | bytes 497668
  7.2 12.7 %copy-start.7 = (s32[3]{0:T(128)S(1)}, s32[3]{0:T(128)}, u32[]{:S(2)}) copy-start(s32[3]{0:T(128)} %param.9) | copy-start | bytes 40
  7.2 182.2 %reduce-scatter.5.cloned.1.call-start = ((), (), s32[]{:S(2)}) async-start(), calls=%async_computation.2 | async-start | bytes 2654208 | tf_op jit(solution)/shard_map/reduce_scatter | solution.py:165
  7.3 56.9 %collective-permute-start = (bf16[6,2,3,256,128]{4,3,2,1,0:T(8,128)(2,1)}, bf16[6,2,3,256,128]{4,3,2,1,0:T(8,128)(2,1)}, u32[]{:S(2)}, u32[]{:S(2)}) collective-permute-start(bf16[6,2,3,256,128]{4,3,2,1,0:T(8,128)(2,1)} %field_ref.1), channel_id=1, source_target_pairs={{2,0},{4,2},{6,4},{8,6},{10,8},{12,10},{14,12},{0,14},{3,1},{5,3},... | collective-permute-start | bytes 7077896 | tf_op jit(solution)/shard_map/ppermute | solution.py:19
  15.3 5.3 %collective-permute-start.1 = (bf16[6,2,3,256,8]{3,4,2,1,0:T(8,128)(2,1)S(1)}, bf16[6,2,3,256,8]{3,4,2,1,0:T(8,128)(2,1)S(1)}, u32[]{:S(2)}, u32[]{:S(2)}) collective-permute-start(bf16[6,2,3,256,8]{3,4,2,1,0:T(8,128)(2,1)S(1)} %copy.60), channel_id=1, source_target_pairs={{0,1},{1,0},{2,3},{3,2},{4,5},{5,4},{6,7},{7,6},{8,9},{9,8},{10,11... | collective-permute-start | bytes 442376 | tf_op jit(solution)/shard_map/ppermute | solution.py:23
  192.4 4.7 %copy-start.3 = (bf16[1,2,256,1024]{3,2,1,0:T(8,128)(2,1)S(1)}, bf16[1,2,256,1024]{3,2,1,0:T(8,128)(2,1)}, u32[]{:S(2)}) copy-start(bf16[1,2,256,1024]{3,2,1,0:T(8,128)(2,1)} %param.8) | copy-start | bytes 3145732
  192.4 36.5 %all-to-all-start = ((bf16[16,2,96,256]{3,2,1,0:T(8,128)(2,1)}), bf16[16,2,96,256]{3,2,1,0:T(8,128)(2,1)}, u32[]{:S(2)}, u32[]{:S(2)}) async-start(bf16[16,2,96,256]{3,2,1,0:T(8,128)(2,1)} %broadcast_select_fusion), calls=%async_computation.1 | async-start | bytes 3145728 | tf_op jit(solution)/shard_map/all_to_all | solution.py:170
  231.1 1.2 copy-start.4
  232.3 1.8 copy-start.2
  236.3 2.1 copy-start.1
Sparse Core Ops, SparseCore 0:
  118.4 70.9 reduce-scatter.4

commit v4 on v2

--- a/solution.py
+++ b/solution.py
@@ -31,7 +31,8 @@
     return 2.0 * math.pi * fraction
 
 
-def sums_kernel(slot_ref, field_ref, far_ref, row_ref, link_ref, trig_ref, out_ref, *, scale):
+def sums_kernel(slot_ref, field_ref, near_ref, link_ref, trig_ref, *rest, scale, course_list):
+    out_ref = rest[-1]
     count_ev, sites = field_ref.shape[3], field_ref.shape[4]
     lane = lax.broadcasted_iota(jnp.int32, (count_ev, sites), 1)
     last_z = lane % LZ == LZ - 1
@@ -44,23 +45,26 @@
     real_rows = jnp.concatenate(phased_real + phased_imag, axis=1)
     imag_rows = jnp.concatenate([-v for v in phased_imag] + phased_real, axis=1)
     left = jnp.concatenate([real_rows, imag_rows], axis=0)
-    far = [[far_ref[0, part, colour].astype(jnp.float32) for colour in range(3)] for part in range(2)]
-    along_y = [
-        [
-            jnp.where(last_row, row_ref[0, part, colour].astype(jnp.float32), pltpu.roll(here[part][colour], sites - LZ, 1))
-            for colour in range(3)
-        ]
-        for part in range(2)
-    ]
-    along_z = [
-        [
-            jnp.where(last_z, pltpu.roll(here[part][colour], LZ - 1, 1), pltpu.roll(here[part][colour], sites - 1, 1))
-            for colour in range(3)
-        ]
-        for part in range(2)
-    ]
     rows = 2 * count_ev
-    for course, near in enumerate((far, along_y, along_z)):
+    for course in course_list:
+        if course == 0:
+            near = [[near_ref[0, part, colour].astype(jnp.float32) for colour in range(3)] for part in range(2)]
+        elif course == 1:
+            near = [
+                [
+                    jnp.where(last_row, near_ref[0, part, colour].astype(jnp.float32), pltpu.roll(here[part][colour], sites - LZ, 1))
+                    for colour in range(3)
+                ]
+                for part in range(2)
+            ]
+        else:
+            near = [
+                [
+                    jnp.where(last_z, pltpu.roll(here[part][colour], LZ - 1, 1), pltpu.roll(here[part][colour], sites - 1, 1))
+                    for colour in range(3)
+                ]
+                for part in range(2)
+            ]
         moved_real = []
         moved_imag = []
         for outer in range(3):
@@ -75,8 +79,11 @@
             moved_imag.append(imag_part.astype(jnp.bfloat16))
         right = jnp.concatenate(moved_real + moved_imag, axis=1)
         joined = lax.dot_general(left, right, (((1,), (1,)), ((), ())), preferred_element_type=jnp.float32)
-        start = pl.multiple_of(slot_ref[course] * rows, rows)
-        out_ref[0, pl.ds(start, rows), :] = (joined * scale).astype(out_ref.dtype)
+        if len(course_list) == 1:
+            out_ref[0] = (joined * scale).astype(out_ref.dtype)
+        else:
+            start = pl.multiple_of(slot_ref[course] * rows, rows)
+            out_ref[0, pl.ds(start, rows), :] = (joined * scale).astype(out_ref.dtype)
 
 
 def local_sums(eigenvectors, gauge_links, far_tile, row_in, directions, angle, scale):
@@ -92,17 +99,30 @@
     link_spec = pl.BlockSpec((1,) + gauge_links.shape[1:], lambda t, slot: (t, 0, 0, 0, 0, 0))
     trig_spec = pl.BlockSpec(trig.shape, lambda t, slot: (0, 0))
     rows = count_ops * 2 * count_ev
-    grid_spec = pltpu.PrefetchScalarGridSpec(
+    near_courses = tuple(course for course in range(count_ops) if course != 0)
+    first_spec = pltpu.PrefetchScalarGridSpec(
         num_scalar_prefetch=1,
         grid=(time_count,),
-        in_specs=[field_spec, field_spec, field_spec, link_spec, trig_spec],
+        in_specs=[field_spec, field_spec, link_spec, trig_spec],
         out_specs=pl.BlockSpec((1, rows, count_ev), lambda t, slot: (t, 0, 0)),
     )
+    partial = pl.pallas_call(
+        functools.partial(sums_kernel, scale=scale, course_list=near_courses),
+        grid_spec=first_spec,
+        out_shape=jax.ShapeDtypeStruct((time_count, rows, count_ev), jnp.bfloat16),
+    )(slot_of, eigenvectors, row_wide, gauge_links, trig)
+    second_spec = pltpu.PrefetchScalarGridSpec(
+        num_scalar_prefetch=1,
+        grid=(time_count,),
+        in_specs=[field_spec, field_spec, link_spec, trig_spec, pl.BlockSpec(memory_space=pl.ANY)],
+        out_specs=pl.BlockSpec((1, 2 * count_ev, count_ev), lambda t, slot: (t, slot[0], 0)),
+    )
     return pl.pallas_call(
-        functools.partial(sums_kernel, scale=scale),
-        grid_spec=grid_spec,
+        functools.partial(sums_kernel, scale=scale, course_list=(0,)),
+        grid_spec=second_spec,
         out_shape=jax.ShapeDtypeStruct((time_count, rows, count_ev), jnp.bfloat16),
-    )(slot_of, eigenvectors, far_tile, row_wide, gauge_links, trig)
+        input_output_aliases={5: 0},
+    )(slot_of, eigenvectors, far_tile, gauge_links, trig, partial)
 
 
 def contract_panel(sink, source, panel):

time: 218 us -> 213 us (0.977)
  waiting for transfers between devices: 142 us -> 131 us
  Pallas kernels: 12.9 us -> 18.6 us
    ppermute x1, waiting for transfers between devices: 40.6 us -> 29.8 us  [shifted(): return lax.ppermute(block, axis, route)]
    pallas_call x1 -> x2, Pallas kernels: 12.9 us -> 18.6 us  [the longest x1 10.8 us: local_sums(): pl.pallas_call(functools.partial(sums_kernel, scale=scale, course_list=ne...]
  transfers between devices with their start and end apart: 4 -> 4, of which waited for: 3 -> 3; matrix products, arithmetic and copies ran while one was open for 8% -> 8% of each run, Pallas kernels for 0% -> 5%
where the time goes in v4:
time: 213 us; the launch traced here: 209 us
  waiting for transfers between devices  131 us (62%)
  local copies, waits for them, and re-layouts  21.8 us (10%)
  Pallas kernels  18.6 us (9%)
  between operations  15 us (7%)
  starting transfers between devices  10.7 us (5%)
  other arithmetic  7.61 us (4%)
  matrix products  3.9 us (2%)
    reduce_scatter x1, waiting for transfers between devices, body(): lax.psum_scatter(partial, 'space', scatter_dimension=1, tiled=True)  75.8 us
    ppermute x1, waiting for transfers between devices, shifted(): return lax.ppermute(block, axis, route)  29.8 us
    all_to_all x1, waiting for transfers between devices, body(): incoming = lax.all_to_all(outgoing, 'space', 0, 0, tiled=True)  25.6 us
    pallas_call x1, Pallas kernels, local_sums(): pl.pallas_call(functools.partial(sums_kernel, scale=scale, course_list=ne...  10.8 us
    pallas_call x1, Pallas kernels, local_sums(): pl.pallas_call(functools.partial(sums_kernel, scale=scale, course_list=(0...  7.85 us
    ppermute x1, starting transfers between devices, shifted(): return lax.ppermute(block, axis, route)  6.06 us
    all_to_all x1, starting transfers between devices, body(): incoming = lax.all_to_all(outgoing, 'space', 0, 0, tiled=True)  4.53 us
  transfers between devices with their start and end apart: 4, of which 3 were waited for; matrix products, arithmetic and copies ran while one was open for 8% of the time, Pallas kernels for 5%

profile of v4, /device:TPU:0, one launch (start us, length us, event | category | flops | bytes accessed | tf_op | source)
XLA Modules:
  0.0 208.9 jit_solution(16402294754851192944)
XLA Ops:
  7.3 6.1 %collective-permute-start = (bf16[6,2,3,256,128]{4,3,2,1,0:T(8,128)(2,1)}, bf16[6,2,3,256,128]{4,3,2,1,0:T(8,128)(2,1)}, u32[]{:S(2)}, u32[]{:S(2)}) collective-permute-start(bf16[6,2,3,256,128]{4,3,2,1,0:T(8,128)(2,1)} %field_ref.3), channel_id=1, source_target_pairs={{2,0},{3,1},{4,2},{5,3},{6,4},{7,5},{8,6},{9,7},{10,8},{11,9},{12,... | collective-permute-start | bytes 7077896 | tf_op jit(solution)/shard_map/ppermute | solution.py:19
  13.3 2.0 copy.56
  16.7 1.3 fusion.19
  20.0 1.1 copy.41
  21.1 2.4 %pad.6.near_ref = bf16[6,2,3,256,128]{4,3,2,1,0:T(8,128)(2,1)} pad(bf16[6,2,3,256,8]{4,3,2,1,0:T(8,128)(2,1)S(1)} %copy.41, bf16[]{:T(256)} %constant.127.clone.1), padding=0_0x0_0x0_0x0_0x120_0 | pad | bytes 2506754 | tf_op jit(solution)/shard_map/jit(_pad)/pad | solution.py:96
  23.5 10.8 %shard_map.77.rest_0_ = bf16[6,1536,256]{2,1,0:T(8,128)(2,1)} custom-call(s32[3]{0:T(128)} %select_reduce_fusion.slot_ref, bf16[6,2,3,256,128]{4,3,2,1,0:T(8,128)(2,1)} %field_ref.3, bf16[6,2,3,256,128]{4,3,2,1,0:T(8,128)(2,1)} %pad.6.near_ref, f32[6,3,2,3,3,128]{5,4,3,2,1,0:T(4,128)} %copy.43.link_ref, f32[2,128]{1,0:T(2,128)} %pad_maximum_fusion.trig_ref), custom_call_target="tpu_custom_call" | custom-call | tf_op jit(solution)/shard_map/pallas_call | solution.py:109
  34.3 29.8 %collective-permute-done.near_ref = bf16[6,2,3,256,128]{4,3,2,1,0:T(8,128)(2,1)} collective-permute-done((bf16[6,2,3,256,128]{4,3,2,1,0:T(8,128)(2,1)}, bf16[6,2,3,256,128]{4,3,2,1,0:T(8,128)(2,1)}, u32[]{:S(2)}, u32[]{:S(2)}) %collective-permute-start) | collective-permute-done | bytes 2359328 | tf_op jit(solution)/shard_map/ppermute | solution.py:19
  64.1 7.8 %shard_map.78 = bf16[6,1536,256]{2,1,0:T(8,128)(2,1)} custom-call(s32[3]{0:T(128)} %select_reduce_fusion.slot_ref, bf16[6,2,3,256,128]{4,3,2,1,0:T(8,128)(2,1)} %field_ref.3, bf16[6,2,3,256,128]{4,3,2,1,0:T(8,128)(2,1)} %collective-permute-done.near_ref, f32[6,3,2,3,3,128]{5,4,3,2,1,0:T(4,128)} %copy.43.link_ref, ...), custom_call_target="tpu_custom_call", output_to_operand_aliasing={{}: (5, {})} | custom-call | tf_op jit(solution)/shard_map/pallas_call | solution.py:120
  73.8 75.8 %reduce-scatter.2.cloned.1.call-done = bf16[6,96,256]{2,1,0:T(8,128)(2,1)} async-done(((bf16[6,1536,256]{2,1,0:T(8,128)(2,1)}), bf16[6,96,256]{2,1,0:T(8,128)(2,1)}) %reduce-scatter.2.cloned.1.call-update) | async-done | bytes 294928 | tf_op jit(solution)/shard_map/reduce_scatter | solution.py:180
  149.6 1.6 gather_fusion.2
  151.2 1.3 broadcast_select_fusion
  152.6 4.5 %all-to-all-start = ((bf16[16,2,96,256]{3,2,1,0:T(8,128)(2,1)}), bf16[16,2,96,256]{3,2,1,0:T(8,128)(2,1)}, u32[]{:S(2)}, u32[]{:S(2)}) async-start(bf16[16,2,96,256]{3,2,1,0:T(8,128)(2,1)} %broadcast_select_fusion), calls=%async_computation.1 | async-start | bytes 3145728 | tf_op jit(solution)/shard_map/all_to_all | solution.py:185
  157.1 1.3 copy.48
  158.9 1.1 squeeze.28
  160.0 1.4 maximum_maximum_fusion
  161.4 2.1 dot_general.22
  163.5 25.6 %all-to-all-done = bf16[16,2,96,256]{3,2,1,0:T(8,128)(2,1)} async-done(((bf16[16,2,96,256]{3,2,1,0:T(8,128)(2,1)}), bf16[16,2,96,256]{3,2,1,0:T(8,128)(2,1)}, u32[]{:S(2)}, u32[]{:S(2)}) %all-to-all-start) | async-done | bytes 1572896 | tf_op jit(solution)/shard_map/all_to_all | solution.py:185
  189.1 2.3 %fusion.21 = (bf16[1,16,96,256]{3,2,0,1:T(8,128)(2,1)S(1)}, bf16[1,16,96,256]{3,2,0,1:T(8,128)(2,1)}) fusion(bf16[2,16,96,256]{3,2,0,1:T(8,128)(2,1)} %bitcast.9), kind=kLoop, calls=%fused_computation.57 | loop fusion | bytes 3145728 | tf_op jit(solution)/shard_map/slice | solution.py:188
  191.4 0.9 slice_bitcast_fusion
  192.4 2.3 %copy.49 = bf16[2,256,3,256]{1,0,3,2:T(2,128)(2,1)S(1)} copy(bf16[2,256,3,256]{3,1,0,2:T(8,128)(2,1)} %bitcast.75) | data formatting | bytes 1572864 | tf_op jit(solution)/shard_map/transpose | solution.py:151
  194.9 2.1 convolution_bitcast_fusion
  197.1 1.1 copy-done.5
  198.2 1.8 fusion.24
  200.0 1.5 add_reduce_fusion
  (44 shorter events, 5.9 us)
Async XLA Ops:
  7.2 64.9 %copy-start = (s32[4,2]{0,1:T(2,128)S(1)}, s32[4,2]{0,1:T(2,128)}, u32[]{:S(2)}) copy-start(s32[4,2]{0,1:T(2,128)} %param.11) | copy-start | bytes 100
  7.2 8.2 %copy-start.7 = (s32[1,3]{1,0:T(1,128)S(1)}, s32[1,3]{1,0:T(1,128)}, u32[]{:S(2)}) copy-start(s32[1,3]{1,0:T(1,128)} %param.10) | copy-start | bytes 40
  7.2 11.5 %copy-start.6 = (f32[6,3,2,3,3,128]{5,2,4,3,1,0:T(2,128)S(1)}, f32[6,3,2,3,3,128]{5,2,4,3,1,0:T(2,128)}, u32[]{:S(2)}) copy-start(f32[6,3,2,3,3,128]{5,2,4,3,1,0:T(2,128)} %param.7) | copy-start | bytes 497668
  7.2 12.2 %copy-start.8 = (s32[3]{0:T(128)S(1)}, s32[3]{0:T(128)}, u32[]{:S(2)}) copy-start(s32[3]{0:T(128)} %param.9) | copy-start | bytes 40
  7.2 142.4 %reduce-scatter.2.cloned.1.call-start = ((), (), s32[]{:S(2)}) async-start(), calls=%async_computation.2 | async-start | bytes 5013504 | tf_op jit(solution)/shard_map/reduce_scatter | solution.py:180
  7.3 56.9 %collective-permute-start = (bf16[6,2,3,256,128]{4,3,2,1,0:T(8,128)(2,1)}, bf16[6,2,3,256,128]{4,3,2,1,0:T(8,128)(2,1)}, u32[]{:S(2)}, u32[]{:S(2)}) collective-permute-start(bf16[6,2,3,256,128]{4,3,2,1,0:T(8,128)(2,1)} %field_ref.3), channel_id=1, source_target_pairs={{2,0},{3,1},{4,2},{5,3},{6,4},{7,5},{8,6},{9,7},{10,8},{11,9},{12,... | collective-permute-start | bytes 7077896 | tf_op jit(solution)/shard_map/ppermute | solution.py:19
  15.3 4.7 %collective-permute-start.1 = (bf16[6,2,3,256,8]{3,4,2,1,0:T(8,128)(2,1)S(1)}, bf16[6,2,3,256,8]{3,4,2,1,0:T(8,128)(2,1)S(1)}, u32[]{:S(2)}, u32[]{:S(2)}) collective-permute-start(bf16[6,2,3,256,8]{3,4,2,1,0:T(8,128)(2,1)S(1)} %copy.56), channel_id=1, source_target_pairs={{0,1},{1,0},{2,3},{3,2},{4,5},{5,4},{6,7},{7,6},{8,9},{9,8},{10,11... | collective-permute-start | bytes 442376 | tf_op jit(solution)/shard_map/ppermute | solution.py:23
  152.6 4.5 %copy-start.2 = (bf16[1,2,256,1024]{3,2,1,0:T(8,128)(2,1)S(1)}, bf16[1,2,256,1024]{3,2,1,0:T(8,128)(2,1)}, u32[]{:S(2)}) copy-start(bf16[1,2,256,1024]{3,2,1,0:T(8,128)(2,1)} %param.8) | copy-start | bytes 3145732
  152.6 36.5 %all-to-all-start = ((bf16[16,2,96,256]{3,2,1,0:T(8,128)(2,1)}), bf16[16,2,96,256]{3,2,1,0:T(8,128)(2,1)}, u32[]{:S(2)}, u32[]{:S(2)}) async-start(bf16[16,2,96,256]{3,2,1,0:T(8,128)(2,1)} %broadcast_select_fusion), calls=%async_computation.1 | async-start | bytes 3145728 | tf_op jit(solution)/shard_map/all_to_all | solution.py:185
  191.4 3.4 %copy-start.1 = (bf16[2,256,4,512]{3,2,1,0:T(4,128)(2,1)S(1)}, bf16[2,256,4,512]{3,2,1,0:T(4,128)(2,1)}, u32[]{:S(2)}) copy-start(bf16[2,256,4,512]{3,2,1,0:T(4,128)(2,1)} %dot_general.22) | copy-start | bytes 6291460
  194.9 2.1 %copy-start.3 = (bf16[3,256,256]{2,1,0:T(8,128)(2,1)S(1)}, bf16[3,256,256]{2,1,0:T(8,128)(2,1)}, u32[]{:S(2)}) copy-start(bf16[3,256,256]{2,1,0:T(8,128)(2,1)} %get-tuple-element.10) | copy-start | bytes 1179652
  194.9 2.1 %copy-start.4 = (bf16[3,256,256]{2,1,0:T(8,128)(2,1)S(1)}, bf16[3,256,256]{2,1,0:T(8,128)(2,1)}, u32[]{:S(2)}) copy-start(bf16[3,256,256]{2,1,0:T(8,128)(2,1)} %get-tuple-element.11) | copy-start | bytes 1179652
  197.0 1.2 copy-start.5
Sparse Core Ops, SparseCore 0:
  72.1 77.4 reduce-scatter.1

commit v5 on v4

--- a/solution.py
+++ b/solution.py
@@ -6,11 +6,12 @@
 from jax import lax
 from jax.experimental import pallas as pl
 from jax.experimental.pallas import tpu as pltpu
-from jax.sharding import PartitionSpec as P
+from jax.sharding import Mesh, PartitionSpec as P
 
 NSPIN = 4
 LY = 32
 LZ = 8
+SPACE = ("slab", "member")
 
 
 def shifted(block, axis, distance):
@@ -164,8 +165,10 @@
     time_count = eigenvectors.shape[0]
     count_ev = eigenvectors.shape[3]
     local_sites = eigenvectors.shape[4]
-    nspace = lax.axis_size("space")
-    device = lax.axis_index("space")
+    count_slabs = lax.axis_size("slab")
+    nspace = NSPIN * count_slabs
+    member = lax.axis_index("member")
+    device = lax.axis_index("slab") * NSPIN + member
     half_rows = LY // 2
     extent_x = nspace // 2
     column = jnp.arange(local_sites, dtype=jnp.int32)
@@ -173,16 +176,19 @@
     coord_y = device % 2 * half_rows + column // LZ
     coord_z = column % LZ
     angle = phase_angles(momenta, (coord_x, coord_y, coord_z), (extent_x, LY, LZ))[0]
-    far_tile = shifted(eigenvectors, "space", -2)
-    row_in = swapped(eigenvectors[..., :LZ], "space", 0)
+    far_tile = shifted(eigenvectors, SPACE, -2)
+    row_in = swapped(eigenvectors[..., :LZ], SPACE, 0)
     scale = 1.0 / math.sqrt(3.0 * extent_x * LY * LZ)
     partial = local_sums(eigenvectors, gauge_links, far_tile, row_in, directions, angle, scale)
-    own_rows = lax.psum_scatter(partial, "space", scatter_dimension=1, tiled=True)
+    own_rows = lax.psum_scatter(partial, SPACE, scatter_dimension=1, tiled=True)
     rows = own_rows.shape[1]
-    target = jnp.arange(nspace, dtype=jnp.int32) // NSPIN
-    wanted = jnp.stack([pair_times[target, 1], pair_times[target, 0]], 1)
-    outgoing = jnp.take(own_rows, wanted.reshape(-1), axis=0).reshape(nspace, 2, rows, count_ev)
-    incoming = lax.all_to_all(outgoing, "space", 0, 0, tiled=True)
+    slabs = jnp.arange(count_slabs, dtype=jnp.int32)
+    wanted = jnp.stack([pair_times[slabs, 1], pair_times[slabs, 0]], 1)
+    outgoing = jnp.take(own_rows, wanted.reshape(-1), axis=0).reshape(count_slabs, 2, rows, count_ev)
+    across = lax.all_to_all(outgoing, "slab", 0, 0, tiled=True)
+    spread = jnp.broadcast_to(across[None], (NSPIN,) + across.shape)
+    within = lax.all_to_all(spread, "member", 0, 0, tiled=True)
+    incoming = within.transpose(1, 0, 2, 3, 4).reshape(nspace, 2, rows, count_ev)
     count_ops = partial.shape[1] // (2 * count_ev)
     gathered = incoming.transpose(1, 0, 2, 3).reshape(2, count_ops, 2, count_ev, count_ev)
     correlators = contract_panel(gathered[0], gathered[1], perambulators[0])[None]
@@ -190,18 +196,21 @@
 
 
 def solution(mesh):
+    count_cfg = mesh.shape["cfg"]
+    count_slabs = mesh.shape["space"] // NSPIN
+    split = Mesh(mesh.devices.reshape(count_cfg, count_slabs, NSPIN), ("cfg",) + SPACE)
     placed = (
-        P("cfg", None, None, None, "space"),
-        P("cfg", None, None, None, None, "space"),
-        P(("cfg", "space"), None, None, None),
+        P("cfg", None, None, None, SPACE),
+        P("cfg", None, None, None, None, SPACE),
+        P(("cfg",) + SPACE, None, None, None),
         P(),
         P(),
         P(),
     )
     return jax.shard_map(
         body,
-        mesh=mesh,
+        mesh=split,
         in_specs=placed,
-        out_specs=(P("cfg", "space", None), P(("cfg", "space"), None, None)),
+        out_specs=(P("cfg", SPACE, None), P(("cfg",) + SPACE, None, None)),
         check_vma=False,
     )

time: 213 us -> 210 us (0.986); the launches traced: 209 us -> 210 us
  waiting for transfers between devices: 131 us -> 116 us
  blocking collectives: 0 us -> 13.5 us
  local copies, waits for them, and re-layouts: 21.8 us -> 24.5 us
    all_to_all x0 -> x1, blocking collectives: none -> 13.5 us  [body(): across = lax.all_to_all(outgoing, 'slab', 0, 0, tiled=True)]
    all_to_all x1, waiting for transfers between devices: 25.6 us -> 13.7 us  [body(): within = lax.all_to_all(spread, 'member', 0, 0, tiled=True)]
    ppermute x1, waiting for transfers between devices: 29.8 us -> 27.4 us  [shifted(): return lax.ppermute(block, axis, route)]
    unnamed x21 -> x17, local copies, waits for them, and re-layouts: 3.99 us -> 4.46 us
  transfers between devices with their start and end apart: 4 -> 4, of which waited for: 3 -> 3; matrix products, arithmetic and copies ran while one was open for 8% -> 9% of each run, Pallas kernels for 5% -> 5%
where the time goes in v5:
time: 210 us
  waiting for transfers between devices  116 us (55%)
  local copies, waits for them, and re-layouts  24.5 us (12%)
  Pallas kernels  18.7 us (9%)
  between operations  14.9 us (7%)
  blocking collectives  13.5 us (6%)
  starting transfers between devices  10.5 us (5%)
  other arithmetic  7.13 us (3%)
  matrix products  3.9 us (2%)
    reduce_scatter x1, waiting for transfers between devices, body(): own_rows = lax.psum_scatter(partial, SPACE, scatter_dimension=1, tiled=True)  75.3 us
    ppermute x1, waiting for transfers between devices, shifted(): return lax.ppermute(block, axis, route)  27.4 us
    all_to_all x1, waiting for transfers between devices, body(): within = lax.all_to_all(spread, 'member', 0, 0, tiled=True)  13.7 us
    all_to_all x1, blocking collectives, body(): across = lax.all_to_all(outgoing, 'slab', 0, 0, tiled=True)  13.5 us
    pallas_call x1, Pallas kernels, local_sums(): pl.pallas_call(functools.partial(sums_kernel, scale=scale, course_list=ne...  10.8 us
    pallas_call x1, Pallas kernels, local_sums(): pl.pallas_call(functools.partial(sums_kernel, scale=scale, course_list=(0...  7.88 us
    ppermute x1, starting transfers between devices, shifted(): return lax.ppermute(block, axis, route)  6.06 us
    unnamed x17, local copies, waits for them, and re-layouts  4.46 us
  transfers between devices with their start and end apart: 4, of which 3 were waited for; matrix products, arithmetic and copies ran while one was open for 9% of the time, Pallas kernels for 5%

profile of v5, /device:TPU:0, one launch (start us, length us, event | category | flops | bytes accessed | tf_op | source)
XLA Modules:
  0.0 209.6 jit_solution(8751679477920061337)
XLA Ops:
  7.2 6.1 %collective-permute-start = (bf16[6,2,3,256,128]{4,3,2,1,0:T(8,128)(2,1)}, bf16[6,2,3,256,128]{4,3,2,1,0:T(8,128)(2,1)}, u32[]{:S(2)}, u32[]{:S(2)}) collective-permute-start(bf16[6,2,3,256,128]{4,3,2,1,0:T(8,128)(2,1)} %field_ref.3), channel_id=1, source_target_pairs={{2,0},{3,1},{4,2},{5,3},{6,4},{7,5},{8,6},{9,7},{10,8},{11,9},{12,... | collective-permute-start | bytes 7077896 | tf_op jit(solution)/shard_map/ppermute | solution.py:20
  13.3 2.0 copy.60
  15.4 1.4 fusion.20
  17.5 1.4 fusion.16
  19.5 1.7 copy.47.link_ref
  21.1 1.3 select_reduce_fusion.slot_ref
  23.6 2.3 %pad.6.near_ref = bf16[6,2,3,256,128]{4,3,2,1,0:T(8,128)(2,1)} pad(bf16[6,2,3,256,8]{4,3,2,1,0:T(8,128)(2,1)S(1)} %copy.45, bf16[]{:T(256)} %constant.122.clone.1), padding=0_0x0_0x0_0x0_0x120_0 | pad | bytes 2506754 | tf_op jit(solution)/shard_map/jit(_pad)/pad | solution.py:97
  25.9 10.8 %shard_map.77.rest_0_ = bf16[6,1536,256]{2,1,0:T(8,128)(2,1)} custom-call(s32[3]{0:T(128)} %select_reduce_fusion.slot_ref, bf16[6,2,3,256,128]{4,3,2,1,0:T(8,128)(2,1)} %field_ref.3, bf16[6,2,3,256,128]{4,3,2,1,0:T(8,128)(2,1)} %pad.6.near_ref, f32[6,3,2,3,3,128]{5,4,3,2,1,0:T(4,128)} %copy.47.link_ref, f32[2,128]{1,0:T(2,128)} %pad_maximum_fusion.trig_ref), custom_call_target="tpu_custom_call" | custom-call | tf_op jit(solution)/shard_map/pallas_call | solution.py:110
  36.7 27.4 %collective-permute-done.near_ref = bf16[6,2,3,256,128]{4,3,2,1,0:T(8,128)(2,1)} collective-permute-done((bf16[6,2,3,256,128]{4,3,2,1,0:T(8,128)(2,1)}, bf16[6,2,3,256,128]{4,3,2,1,0:T(8,128)(2,1)}, u32[]{:S(2)}, u32[]{:S(2)}) %collective-permute-start) | collective-permute-done | bytes 2359328 | tf_op jit(solution)/shard_map/ppermute | solution.py:20
  64.1 7.9 %shard_map.78 = bf16[6,1536,256]{2,1,0:T(8,128)(2,1)} custom-call(s32[3]{0:T(128)} %select_reduce_fusion.slot_ref, bf16[6,2,3,256,128]{4,3,2,1,0:T(8,128)(2,1)} %field_ref.3, bf16[6,2,3,256,128]{4,3,2,1,0:T(8,128)(2,1)} %collective-permute-done.near_ref, f32[6,3,2,3,3,128]{5,4,3,2,1,0:T(4,128)} %copy.47.link_ref, ...), custom_call_target="tpu_custom_call", output_to_operand_aliasing={{}: (5, {})} | custom-call | tf_op jit(solution)/shard_map/pallas_call | solution.py:121
  74.3 75.3 %reduce-scatter.2.cloned.1.call-done = bf16[6,96,256]{2,1,0:T(8,128)(2,1)} async-done(((bf16[6,1536,256]{2,1,0:T(8,128)(2,1)}), bf16[6,96,256]{2,1,0:T(8,128)(2,1)}) %reduce-scatter.2.cloned.1.call-update) | async-done | bytes 294928 | tf_op jit(solution)/shard_map/reduce_scatter | solution.py:183
  149.6 1.5 gather_fusion.2
  151.3 13.5 %all_to_all.10 = bf16[4,2,96,256]{3,2,1,0:T(8,128)(2,1)S(1)} all-to-all(bf16[4,2,96,256]{3,2,1,0:T(8,128)(2,1)S(1)} %broadcast_select_fusion), channel_id=1, replica_groups=mesh['cfg'=2,'slab'=4,'member'=4] {'slab'}, dimensions={0} | all-to-all | bytes 786432 | tf_op jit(solution)/shard_map/all_to_all | solution.py:188
  164.8 1.3 broadcast_in_dim.14
  166.1 4.4 %all-to-all-start.1 = ((bf16[4,4,2,96,256]{4,3,2,1,0:T(8,128)(2,1)}), bf16[4,4,2,96,256]{4,3,2,1,0:T(8,128)(2,1)}, u32[]{:S(2)}, u32[]{:S(2)}) async-start(bf16[4,4,2,96,256]{4,3,2,1,0:T(8,128)(2,1)} %broadcast_in_dim.14), calls=%async_computation.2 | async-start | bytes 3145728 | tf_op jit(solution)/shard_map/all_to_all | solution.py:190
  170.4 1.3 copy.52
  173.4 1.4 maximum_maximum_fusion
  174.8 2.1 %dot_general.22 = bf16[2,256,4,512]{3,2,1,0:T(4,128)(2,1)} reshape(bf16[2048,512]{1,0:T(8,128)(2,1)S(1)} %maximum_maximum_fusion) | data formatting | bytes 4194304 | tf_op jit(solution)/shard_map/mk,kn->mn/dot_general | solution.py:153
  176.9 13.7 %all-to-all-done.1 = bf16[4,4,2,96,256]{4,3,2,1,0:T(8,128)(2,1)} async-done(((bf16[4,4,2,96,256]{4,3,2,1,0:T(8,128)(2,1)}), bf16[4,4,2,96,256]{4,3,2,1,0:T(8,128)(2,1)}, u32[]{:S(2)}, u32[]{:S(2)}) %all-to-all-start.1) | async-done | bytes 1572896 | tf_op jit(solution)/shard_map/all_to_all | solution.py:190
  190.6 1.5 copy.50
  194.1 2.3 %copy.53 = bf16[2,256,3,256]{1,0,3,2:T(2,128)(2,1)S(1)} copy(bf16[2,256,3,256]{3,1,0,2:T(8,128)(2,1)} %bitcast.73) | data formatting | bytes 1572864 | tf_op jit(solution)/shard_map/transpose | solution.py:152
  196.6 2.1 convolution_bitcast_fusion
  198.8 1.8 fusion.21
  200.7 1.5 add_reduce_fusion
  (42 shorter events, 8.7 us)
Async XLA Ops:
  7.2 64.8 %copy-start = (s32[4,2]{0,1:T(2,128)S(1)}, s32[4,2]{0,1:T(2,128)}, u32[]{:S(2)}) copy-start(s32[4,2]{0,1:T(2,128)} %param.11) | copy-start | bytes 100
  7.2 142.4 %reduce-scatter.2.cloned.1.call-start = ((), (), s32[]{:S(2)}) async-start(), calls=%async_computation.3 | async-start | bytes 5013504 | tf_op jit(solution)/shard_map/reduce_scatter | solution.py:183
  7.2 56.9 %collective-permute-start = (bf16[6,2,3,256,128]{4,3,2,1,0:T(8,128)(2,1)}, bf16[6,2,3,256,128]{4,3,2,1,0:T(8,128)(2,1)}, u32[]{:S(2)}, u32[]{:S(2)}) collective-permute-start(bf16[6,2,3,256,128]{4,3,2,1,0:T(8,128)(2,1)} %field_ref.3), channel_id=1, source_target_pairs={{2,0},{3,1},{4,2},{5,3},{6,4},{7,5},{8,6},{9,7},{10,8},{11,9},{12,... | collective-permute-start | bytes 7077896 | tf_op jit(solution)/shard_map/ppermute | solution.py:20
  15.3 7.2 %collective-permute-start.1 = (bf16[6,2,3,256,8]{3,4,2,1,0:T(8,128)(2,1)S(1)}, bf16[6,2,3,256,8]{3,4,2,1,0:T(8,128)(2,1)S(1)}, u32[]{:S(2)}, u32[]{:S(2)}) collective-permute-start(bf16[6,2,3,256,8]{3,4,2,1,0:T(8,128)(2,1)S(1)} %copy.60), channel_id=1, source_target_pairs={{0,1},{1,0},{2,3},{3,2},{4,5},{5,4},{6,7},{7,6},{8,9},{9,8},{10,11... | collective-permute-start | bytes 442376 | tf_op jit(solution)/shard_map/ppermute | solution.py:24
  72.0 0.7 copy-start.6
  151.3 19.2 %copy-start.2 = (bf16[1,2,256,1024]{3,2,1,0:T(8,128)(2,1)S(1)}, bf16[1,2,256,1024]{3,2,1,0:T(8,128)(2,1)}, u32[]{:S(2)}) copy-start(bf16[1,2,256,1024]{3,2,1,0:T(8,128)(2,1)} %param.8) | copy-start | bytes 3145732
  166.1 24.5 %all-to-all-start.1 = ((bf16[4,4,2,96,256]{4,3,2,1,0:T(8,128)(2,1)}), bf16[4,4,2,96,256]{4,3,2,1,0:T(8,128)(2,1)}, u32[]{:S(2)}, u32[]{:S(2)}) async-start(bf16[4,4,2,96,256]{4,3,2,1,0:T(8,128)(2,1)} %broadcast_in_dim.14), calls=%async_computation.2 | async-start | bytes 3145728 | tf_op jit(solution)/shard_map/all_to_all | solution.py:190
  193.1 3.5 %copy-start.1 = (bf16[2,256,4,512]{3,2,1,0:T(4,128)(2,1)S(1)}, bf16[2,256,4,512]{3,2,1,0:T(4,128)(2,1)}, u32[]{:S(2)}) copy-start(bf16[2,256,4,512]{3,2,1,0:T(4,128)(2,1)} %dot_general.22) | copy-start | bytes 6291460
  196.6 2.1 %copy-start.3 = (bf16[3,256,256]{2,1,0:T(8,128)(2,1)S(1)}, bf16[3,256,256]{2,1,0:T(8,128)(2,1)}, u32[]{:S(2)}) copy-start(bf16[3,256,256]{2,1,0:T(8,128)(2,1)} %get-tuple-element.10) | copy-start | bytes 1179652
  196.6 2.1 %copy-start.4 = (bf16[3,256,256]{2,1,0:T(8,128)(2,1)S(1)}, bf16[3,256,256]{2,1,0:T(8,128)(2,1)}, u32[]{:S(2)}) copy-start(bf16[3,256,256]{2,1,0:T(8,128)(2,1)} %get-tuple-element.11) | copy-start | bytes 1179652
  196.6 2.2 %copy-start.5 = (bf16[1024,512]{1,0:T(8,128)(2,1)S(1)}, bf16[1024,512]{1,0:T(8,128)(2,1)}, u32[]{:S(2)}) copy-start(bf16[1024,512]{1,0:T(8,128)(2,1)} %copy.52) | copy-start | bytes 3145732
Sparse Core Ops, SparseCore 0:
  72.1 77.4 reduce-scatter.1

commit v6 on v5

--- a/solution.py
+++ b/solution.py
@@ -126,39 +126,58 @@
     )(slot_of, eigenvectors, far_tile, gauge_links, trig, partial)
 
 
-def contract_panel(sink, source, panel):
-    count_ev = panel.shape[1]
-    count_ops = sink.shape[0]
-    sink_real = sink[:, 0]
-    sink_imag = sink[:, 1]
+def panel_kernel(sink_ref, source_ref, stack_ref, wide_ref, out_ref):
+    count_ev = sink_ref.shape[3]
+    sink_real = sink_ref[0, 0, 0]
+    sink_imag = sink_ref[0, 0, 1]
     sink_wide = jnp.concatenate(
         [
-            jnp.concatenate([sink_real, -sink_imag], axis=2),
-            jnp.concatenate([sink_imag, sink_real], axis=2),
+            jnp.concatenate([sink_real, -sink_imag], axis=1),
+            jnp.concatenate([sink_imag, sink_real], axis=1),
         ],
-        axis=1,
-    )
-    panel_stack = panel.reshape(2 * count_ev, NSPIN * count_ev)
-    left = jnp.einsum("amk,kn->amn", sink_wide, panel_stack, preferred_element_type=jnp.float32)
-    left = left.reshape(count_ops, 2, count_ev, NSPIN, count_ev)
-    blocks = panel.reshape(2, count_ev * NSPIN, count_ev)
-    panel_wide = jnp.concatenate(
+        axis=0,
+    )
+    left = jnp.dot(sink_wide, stack_ref[...], preferred_element_type=jnp.float32)
+    source_stack = jnp.concatenate([source_ref[0, 0, 0], source_ref[0, 0, 1]], axis=0)
+    right = jnp.dot(wide_ref[...], source_stack, preferred_element_type=jnp.float32)
+    total_real = 0.0
+    total_imag = 0.0
+    half = NSPIN * count_ev
+    for spin in range(NSPIN):
+        left_real = left[:count_ev, spin * count_ev : (spin + 1) * count_ev]
+        left_imag = left[count_ev:, spin * count_ev : (spin + 1) * count_ev]
+        right_real = right[spin * count_ev : (spin + 1) * count_ev]
+        right_imag = right[half + spin * count_ev : half + (spin + 1) * count_ev]
+        total_real = total_real + left_real * right_real + left_imag * right_imag
+        total_imag = total_imag + left_imag * right_real - left_real * right_imag
+    out_ref[0, 0:1, :] = jnp.sum(total_real, axis=0, keepdims=True)
+    out_ref[0, 1:2, :] = jnp.sum(total_imag, axis=0, keepdims=True)
+
+
+def contract_panel(gathered, panel):
+    count_ops, count_ev = gathered.shape[1], panel.shape[1]
+    stack = panel.reshape(2 * count_ev, NSPIN * count_ev)
+    blocks = panel.reshape(2, count_ev, NSPIN, count_ev).transpose(0, 2, 1, 3).reshape(2, NSPIN * count_ev, count_ev)
+    wide = jnp.concatenate(
         [
             jnp.concatenate([blocks[0], -blocks[1]], axis=1),
             jnp.concatenate([blocks[1], blocks[0]], axis=1),
         ],
         axis=0,
     )
-    source_stack = source.transpose(1, 2, 0, 3).reshape(2 * count_ev, count_ops * count_ev)
-    right = jnp.einsum("mk,kn->mn", panel_wide, source_stack, preferred_element_type=jnp.float32)
-    right = right.reshape(2, count_ev, NSPIN, count_ops, count_ev).transpose(3, 0, 1, 2, 4)
-    left_real = left[:, 0]
-    left_imag = left[:, 1]
-    right_real = right[:, 0]
-    right_imag = right[:, 1]
-    trace_real = jnp.sum(left_real * right_real + left_imag * right_imag, axis=(1, 2, 3))
-    trace_imag = jnp.sum(left_imag * right_real - left_real * right_imag, axis=(1, 2, 3))
-    return jnp.stack([trace_real, trace_imag], -1) * (1.0 / (16.0 * count_ev))
+    sums = pl.pallas_call(
+        panel_kernel,
+        grid=(count_ops,),
+        in_specs=[
+            pl.BlockSpec((1, 1, 2, count_ev, count_ev), lambda a: (0, a, 0, 0, 0)),
+            pl.BlockSpec((1, 1, 2, count_ev, count_ev), lambda a: (1, a, 0, 0, 0)),
+            pl.BlockSpec(stack.shape, lambda a: (0, 0)),
+            pl.BlockSpec(wide.shape, lambda a: (0, 0)),
+        ],
+        out_specs=pl.BlockSpec((1, 2, count_ev), lambda a: (a, 0, 0)),
+        out_shape=jax.ShapeDtypeStruct((count_ops, 2, count_ev), jnp.float32),
+    )(gathered, gathered, stack, wide)
+    return jnp.sum(sums, axis=-1) * (1.0 / (16.0 * count_ev))
 
 
 def body(eigenvectors, gauge_links, perambulators, directions, momenta, pair_times):
@@ -191,7 +210,7 @@
     incoming = within.transpose(1, 0, 2, 3, 4).reshape(nspace, 2, rows, count_ev)
     count_ops = partial.shape[1] // (2 * count_ev)
     gathered = incoming.transpose(1, 0, 2, 3).reshape(2, count_ops, 2, count_ev, count_ev)
-    correlators = contract_panel(gathered[0], gathered[1], perambulators[0])[None]
+    correlators = contract_panel(gathered, perambulators[0])[None]
     return (own_rows, correlators)
 
 

time: 210 us -> 207 us (0.986)
  local copies, waits for them, and re-layouts: 24.5 us -> 16.4 us
  Pallas kernels: 18.7 us -> 25.3 us
  waiting for transfers between devices: 116 us -> 121 us
  matrix products: 3.9 us -> 0 us
    pallas_call x0 -> x1, Pallas kernels: none -> 6.63 us  [contract_panel(): pl.pallas_call(panel_kernel, grid=(count_ops,), in_specs=[pl.BlockSpec((1...]
    dot_general x2 -> x0, matrix products: 3.9 us -> none  [the longest x1 2.08 us: contract_panel(): jnp.einsum('mk,kn->mn', panel_wide, source_stack, preferred_element_type=...]
    dot_general x2 -> x0, local copies, waits for them, and re-layouts: 3.42 us -> none  [the longest x1 2.1 us: contract_panel(): jnp.einsum('mk,kn->mn', panel_wide, source_stack, preferred_element_type=...]
    another operation x1 -> x3, local copies, waits for them, and re-layouts: 0.01 us -> 2.94 us  [the longest x2 2.94 us: contract_panel(): panel.reshape(2, count_ev, NSPIN, count_ev).transpose(0, 2, 1, 3)]
    ppermute x1, waiting for transfers between devices: 27.4 us -> 29.8 us  [shifted(): return lax.ppermute(block, axis, route)]
    squeeze x3 -> x0, local copies, waits for them, and re-layouts: 2.39 us -> none  [the longest x1 1.12 us: contract_panel(): blocks[0]]
    unnamed x17 -> x14, local copies, waits for them, and re-layouts: 4.46 us -> 2.76 us
  transfers between devices with their start and end apart: 4 -> 4, of which waited for: 3 -> 3; matrix products, arithmetic and copies ran while one was open for 9% -> 8% of each run, Pallas kernels for 5% -> 5%
where the time goes in v6:
time: 207 us; the launch traced here: 206 us
  waiting for transfers between devices  121 us (58%)
  Pallas kernels  25.3 us (12%)
  local copies, waits for them, and re-layouts  16.4 us (8%)
  between operations  14.9 us (7%)
  blocking collectives  13.4 us (6%)
  starting transfers between devices  9.73 us (5%)
  other arithmetic  5.06 us (2%)
    reduce_scatter x1, waiting for transfers between devices, body(): own_rows = lax.psum_scatter(partial, SPACE, scatter_dimension=1, tiled=True)  75.9 us
    ppermute x1, waiting for transfers between devices, shifted(): return lax.ppermute(block, axis, route)  29.8 us
    all_to_all x1, waiting for transfers between devices, body(): within = lax.all_to_all(spread, 'member', 0, 0, tiled=True)  15.4 us
    all_to_all x1, blocking collectives, body(): across = lax.all_to_all(outgoing, 'slab', 0, 0, tiled=True)  13.4 us
    pallas_call x1, Pallas kernels, local_sums(): pl.pallas_call(functools.partial(sums_kernel, scale=scale, course_list=ne...  10.8 us
    pallas_call x1, Pallas kernels, local_sums(): pl.pallas_call(functools.partial(sums_kernel, scale=scale, course_list=(0...  7.86 us
    pallas_call x1, Pallas kernels, contract_panel(): pl.pallas_call(panel_kernel, grid=(count_ops,), in_specs=[pl.BlockSpec((1...  6.63 us
    ppermute x1, starting transfers between devices, shifted(): return lax.ppermute(block, axis, route)  6.06 us
  transfers between devices with their start and end apart: 4, of which 3 were waited for; matrix products, arithmetic and copies ran while one was open for 8% of the time, Pallas kernels for 5%

profile of v6, /device:TPU:0, one launch (start us, length us, event | category | flops | bytes accessed | tf_op | source)
XLA Modules:
  0.0 205.9 jit_solution(8203402753186216890)
XLA Ops:
  7.3 6.1 %collective-permute-start = (bf16[6,2,3,256,128]{4,3,2,1,0:T(8,128)(2,1)}, bf16[6,2,3,256,128]{4,3,2,1,0:T(8,128)(2,1)}, u32[]{:S(2)}, u32[]{:S(2)}) collective-permute-start(bf16[6,2,3,256,128]{4,3,2,1,0:T(8,128)(2,1)} %field_ref.3), channel_id=1, source_target_pairs={{2,0},{3,1},{4,2},{5,3},{6,4},{7,5},{8,6},{9,7},{10,8},{11,9},{12,... | collective-permute-start | bytes 7077896 | tf_op jit(solution)/shard_map/ppermute | solution.py:20
  13.3 2.0 copy.52
  16.7 1.3 fusion.13
  18.5 0.7 copy.44.link_ref
  19.3 0.7 select_reduce_fusion.slot_ref
  20.0 1.2 copy.42
  21.2 2.3 %pad.6.near_ref = bf16[6,2,3,256,128]{4,3,2,1,0:T(8,128)(2,1)} pad(bf16[6,2,3,256,8]{4,3,2,1,0:T(8,128)(2,1)S(1)} %copy.42, bf16[]{:T(256)} %constant.122.clone.1), padding=0_0x0_0x0_0x0_0x120_0 | pad | bytes 2506754 | tf_op jit(solution)/shard_map/jit(_pad)/pad | solution.py:97
  23.5 10.8 %shard_map.77.rest_0_ = bf16[6,1536,256]{2,1,0:T(8,128)(2,1)} custom-call(s32[3]{0:T(128)} %select_reduce_fusion.slot_ref, bf16[6,2,3,256,128]{4,3,2,1,0:T(8,128)(2,1)} %field_ref.3, bf16[6,2,3,256,128]{4,3,2,1,0:T(8,128)(2,1)} %pad.6.near_ref, f32[6,3,2,3,3,128]{5,4,3,2,1,0:T(4,128)} %copy.44.link_ref, f32[2,128]{1,0:T(2,128)} %pad_maximum_fusion.trig_ref), custom_call_target="tpu_custom_call" | custom-call | tf_op jit(solution)/shard_map/pallas_call | solution.py:110
  34.3 29.8 %collective-permute-done.near_ref = bf16[6,2,3,256,128]{4,3,2,1,0:T(8,128)(2,1)} collective-permute-done((bf16[6,2,3,256,128]{4,3,2,1,0:T(8,128)(2,1)}, bf16[6,2,3,256,128]{4,3,2,1,0:T(8,128)(2,1)}, u32[]{:S(2)}, u32[]{:S(2)}) %collective-permute-start) | collective-permute-done | bytes 2359328 | tf_op jit(solution)/shard_map/ppermute | solution.py:20
  64.1 7.9 %shard_map.78 = bf16[6,1536,256]{2,1,0:T(8,128)(2,1)} custom-call(s32[3]{0:T(128)} %select_reduce_fusion.slot_ref, bf16[6,2,3,256,128]{4,3,2,1,0:T(8,128)(2,1)} %field_ref.3, bf16[6,2,3,256,128]{4,3,2,1,0:T(8,128)(2,1)} %collective-permute-done.near_ref, f32[6,3,2,3,3,128]{5,4,3,2,1,0:T(4,128)} %copy.44.link_ref, ...), custom_call_target="tpu_custom_call", output_to_operand_aliasing={{}: (5, {})} | custom-call | tf_op jit(solution)/shard_map/pallas_call | solution.py:121
  72.7 0.6 gather_fusion
  73.7 75.9 %reduce-scatter.2.cloned.1.call-done = bf16[6,96,256]{2,1,0:T(8,128)(2,1)} async-done(((bf16[6,1536,256]{2,1,0:T(8,128)(2,1)}), bf16[6,96,256]{2,1,0:T(8,128)(2,1)}) %reduce-scatter.2.cloned.1.call-update) | async-done | bytes 294928 | tf_op jit(solution)/shard_map/reduce_scatter | solution.py:202
  149.6 1.5 gather_fusion.2
  151.3 13.4 %all_to_all.10 = bf16[4,2,96,256]{3,2,1,0:T(8,128)(2,1)S(1)} all-to-all(bf16[4,2,96,256]{3,2,1,0:T(8,128)(2,1)S(1)} %broadcast_select_fusion), channel_id=1, replica_groups=mesh['cfg'=2,'slab'=4,'member'=4] {'slab'}, dimensions={0} | all-to-all | bytes 786432 | tf_op jit(solution)/shard_map/all_to_all | solution.py:207
  164.7 1.3 broadcast_in_dim.14
  166.0 3.6 %all-to-all-start.1 = ((bf16[4,4,2,96,256]{4,3,1,2,0:T(8,128)(2,1)}), bf16[4,4,2,96,256]{4,3,1,2,0:T(8,128)(2,1)S(1)}, u32[]{:S(2)}, u32[]{:S(2)}) async-start(bf16[4,4,2,96,256]{4,3,1,2,0:T(8,128)(2,1)} %broadcast_in_dim.14), calls=%async_computation.2 | async-start | bytes 3145728 | tf_op jit(solution)/shard_map/all_to_all | solution.py:209
  169.6 1.6 reshape_squeeze.7
  171.2 1.4 copy.54
  172.7 1.5 maximum_maximum_fusion.wide_ref
  174.2 15.4 %all-to-all-done.1 = bf16[4,4,2,96,256]{4,3,1,2,0:T(8,128)(2,1)S(1)} async-done(((bf16[4,4,2,96,256]{4,3,1,2,0:T(8,128)(2,1)}), bf16[4,4,2,96,256]{4,3,1,2,0:T(8,128)(2,1)S(1)}, u32[]{:S(2)}, u32[]{:S(2)}) %all-to-all-start.1) | async-done | bytes 1572896 | tf_op jit(solution)/shard_map/all_to_all | solution.py:209
  189.7 1.3 copy.49
  191.0 6.6 %shard_map.79 = f32[3,2,256]{2,1,0:T(2,128)} custom-call(bf16[2,3,2,256,256]{4,3,2,1,0:T(8,128)(2,1)} %bitcast.26, bf16[2,3,2,256,256]{4,3,2,1,0:T(8,128)(2,1)} %bitcast.27, bf16[512,1024]{1,0:T(8,128)(2,1)} %bitcast.30, bf16[2048,512]{1,0:T(8,128)(2,1)} %maximum_maximum_fusion.wide_ref), custom_call_target="tpu_custom_call" | custom-call | tf_op jit(solution)/shard_map/pallas_call | solution.py:168
  197.6 0.8 reduce_sum.19
  198.4 0.7 copy.51
  (34 shorter events, 2.7 us)
Async XLA Ops:
  7.2 64.9 %copy-start = (s32[4,2]{0,1:T(2,128)S(1)}, s32[4,2]{0,1:T(2,128)}, u32[]{:S(2)}) copy-start(s32[4,2]{0,1:T(2,128)} %param.11) | copy-start | bytes 100
  7.2 8.2 %copy-start.4 = (s32[1,3]{1,0:T(1,128)S(1)}, s32[1,3]{1,0:T(1,128)}, u32[]{:S(2)}) copy-start(s32[1,3]{1,0:T(1,128)} %param.10) | copy-start | bytes 40
  7.2 11.4 %copy-start.2 = (f32[6,3,2,3,3,128]{5,2,4,3,1,0:T(2,128)S(1)}, f32[6,3,2,3,3,128]{5,2,4,3,1,0:T(2,128)}, u32[]{:S(2)}) copy-start(f32[6,3,2,3,3,128]{5,2,4,3,1,0:T(2,128)} %param.7) | copy-start | bytes 497668
  7.2 12.1 %copy-start.5 = (s32[3]{0:T(128)S(1)}, s32[3]{0:T(128)}, u32[]{:S(2)}) copy-start(s32[3]{0:T(128)} %param.9) | copy-start | bytes 40
  7.2 142.4 %reduce-scatter.2.cloned.1.call-start = ((), (), s32[]{:S(2)}) async-start(), calls=%async_computation.3 | async-start | bytes 5013504 | tf_op jit(solution)/shard_map/reduce_scatter | solution.py:202
  7.3 56.9 %collective-permute-start = (bf16[6,2,3,256,128]{4,3,2,1,0:T(8,128)(2,1)}, bf16[6,2,3,256,128]{4,3,2,1,0:T(8,128)(2,1)}, u32[]{:S(2)}, u32[]{:S(2)}) collective-permute-start(bf16[6,2,3,256,128]{4,3,2,1,0:T(8,128)(2,1)} %field_ref.3), channel_id=1, source_target_pairs={{2,0},{3,1},{4,2},{5,3},{6,4},{7,5},{8,6},{9,7},{10,8},{11,9},{12,... | collective-permute-start | bytes 7077896 | tf_op jit(solution)/shard_map/ppermute | solution.py:20
  15.3 4.7 %collective-permute-start.1 = (bf16[6,2,3,256,8]{3,4,2,1,0:T(8,128)(2,1)S(1)}, bf16[6,2,3,256,8]{3,4,2,1,0:T(8,128)(2,1)S(1)}, u32[]{:S(2)}, u32[]{:S(2)}) collective-permute-start(bf16[6,2,3,256,8]{3,4,2,1,0:T(8,128)(2,1)S(1)} %copy.52), channel_id=1, source_target_pairs={{0,1},{1,0},{2,3},{3,2},{4,5},{5,4},{6,7},{7,6},{8,9},{9,8},{10,11... | collective-permute-start | bytes 442376 | tf_op jit(solution)/shard_map/ppermute | solution.py:24
  72.0 0.7 copy-start.3
  164.7 4.9 %copy-start.1 = (bf16[1,2,256,1024]{3,2,1,0:T(8,128)(2,1)S(1)}, bf16[1,2,256,1024]{3,2,1,0:T(8,128)(2,1)}, u32[]{:S(2)}) copy-start(bf16[1,2,256,1024]{3,2,1,0:T(8,128)(2,1)} %param.8) | copy-start | bytes 3145732
  166.0 23.6 %all-to-all-start.1 = ((bf16[4,4,2,96,256]{4,3,1,2,0:T(8,128)(2,1)}), bf16[4,4,2,96,256]{4,3,1,2,0:T(8,128)(2,1)S(1)}, u32[]{:S(2)}, u32[]{:S(2)}) async-start(bf16[4,4,2,96,256]{4,3,1,2,0:T(8,128)(2,1)} %broadcast_in_dim.14), calls=%async_computation.2 | async-start | bytes 3145728 | tf_op jit(solution)/shard_map/all_to_all | solution.py:209
Sparse Core Ops, SparseCore 0:
  72.1 77.4 reduce-scatter.1

commit v7 on v6

--- a/solution.py
+++ b/solution.py
@@ -33,19 +33,23 @@
 
 
 def sums_kernel(slot_ref, field_ref, near_ref, link_ref, trig_ref, *rest, scale, course_list):
-    out_ref = rest[-1]
+    out_ref = rest[-1] if len(course_list) == 1 else rest[0]
     count_ev, sites = field_ref.shape[3], field_ref.shape[4]
     lane = lax.broadcasted_iota(jnp.int32, (count_ev, sites), 1)
     last_z = lane % LZ == LZ - 1
     last_row = lane >= sites - LZ
-    cosine = trig_ref[0:1, :]
-    sine_part = trig_ref[1:2, :]
-    here = [[field_ref[0, part, colour].astype(jnp.float32) for colour in range(3)] for part in range(2)]
-    phased_real = [(cosine * here[0][c] - sine_part * here[1][c]).astype(jnp.bfloat16) for c in range(3)]
-    phased_imag = [(sine_part * here[0][c] + cosine * here[1][c]).astype(jnp.bfloat16) for c in range(3)]
-    real_rows = jnp.concatenate(phased_real + phased_imag, axis=1)
-    imag_rows = jnp.concatenate([-v for v in phased_imag] + phased_real, axis=1)
-    left = jnp.concatenate([real_rows, imag_rows], axis=0)
+    if len(course_list) == 1:
+        left = trig_ref[0]
+    else:
+        cosine = trig_ref[0:1, :]
+        sine_part = trig_ref[1:2, :]
+        here = [[field_ref[0, part, colour].astype(jnp.float32) for colour in range(3)] for part in range(2)]
+        phased_real = [(cosine * here[0][c] - sine_part * here[1][c]).astype(jnp.bfloat16) for c in range(3)]
+        phased_imag = [(sine_part * here[0][c] + cosine * here[1][c]).astype(jnp.bfloat16) for c in range(3)]
+        real_rows = jnp.concatenate(phased_real + phased_imag, axis=1)
+        imag_rows = jnp.concatenate([-v for v in phased_imag] + phased_real, axis=1)
+        left = jnp.concatenate([real_rows, imag_rows], axis=0)
+        rest[1][0] = left
     rows = 2 * count_ev
     for course in course_list:
         if course == 0:
@@ -101,21 +105,26 @@
     trig_spec = pl.BlockSpec(trig.shape, lambda t, slot: (0, 0))
     rows = count_ops * 2 * count_ev
     near_courses = tuple(course for course in range(count_ops) if course != 0)
+    left_rows = 2 * count_ev
+    left_spec = pl.BlockSpec((1, left_rows, 6 * sites), lambda t, slot: (t, 0, 0))
     first_spec = pltpu.PrefetchScalarGridSpec(
         num_scalar_prefetch=1,
         grid=(time_count,),
         in_specs=[field_spec, field_spec, link_spec, trig_spec],
-        out_specs=pl.BlockSpec((1, rows, count_ev), lambda t, slot: (t, 0, 0)),
-    )
-    partial = pl.pallas_call(
+        out_specs=[pl.BlockSpec((1, rows, count_ev), lambda t, slot: (t, 0, 0)), left_spec],
+    )
+    partial, left = pl.pallas_call(
         functools.partial(sums_kernel, scale=scale, course_list=near_courses),
         grid_spec=first_spec,
-        out_shape=jax.ShapeDtypeStruct((time_count, rows, count_ev), jnp.bfloat16),
+        out_shape=(
+            jax.ShapeDtypeStruct((time_count, rows, count_ev), jnp.bfloat16),
+            jax.ShapeDtypeStruct((time_count, left_rows, 6 * sites), jnp.bfloat16),
+        ),
     )(slot_of, eigenvectors, row_wide, gauge_links, trig)
     second_spec = pltpu.PrefetchScalarGridSpec(
         num_scalar_prefetch=1,
         grid=(time_count,),
-        in_specs=[field_spec, field_spec, link_spec, trig_spec, pl.BlockSpec(memory_space=pl.ANY)],
+        in_specs=[pl.BlockSpec(memory_space=pl.ANY), field_spec, link_spec, left_spec, pl.BlockSpec(memory_space=pl.ANY)],
         out_specs=pl.BlockSpec((1, 2 * count_ev, count_ev), lambda t, slot: (t, slot[0], 0)),
     )
     return pl.pallas_call(
@@ -123,7 +132,7 @@
         grid_spec=second_spec,
         out_shape=jax.ShapeDtypeStruct((time_count, rows, count_ev), jnp.bfloat16),
         input_output_aliases={5: 0},
-    )(slot_of, eigenvectors, far_tile, gauge_links, trig, partial)
+    )(slot_of, eigenvectors, far_tile, gauge_links, left, partial)
 
 
 def panel_kernel(sink_ref, source_ref, stack_ref, wide_ref, out_ref):

time: 207 us -> 207 us (level)
  no operation moved by 1% of the time
where the time goes in v7:
time: 207 us; the launch traced here: 206 us
  waiting for transfers between devices  121 us (58%)
  Pallas kernels  25.7 us (12%)
  local copies, waits for them, and re-layouts  16.5 us (8%)
  between operations  14.9 us (7%)
  blocking collectives  13.4 us (6%)
  starting transfers between devices  9.73 us (5%)
  other arithmetic  5.16 us (2%)
    reduce_scatter x1, waiting for transfers between devices, body(): own_rows = lax.psum_scatter(partial, SPACE, scatter_dimension=1, tiled=True)  75.9 us
    ppermute x1, waiting for transfers between devices, shifted(): return lax.ppermute(block, axis, route)  29.4 us
    all_to_all x1, waiting for transfers between devices, body(): within = lax.all_to_all(spread, 'member', 0, 0, tiled=True)  15.4 us
    all_to_all x1, blocking collectives, body(): across = lax.all_to_all(outgoing, 'slab', 0, 0, tiled=True)  13.4 us
    pallas_call x1, Pallas kernels, local_sums(): pl.pallas_call(functools.partial(sums_kernel, scale=scale, course_list=ne...  11 us
    pallas_call x1, Pallas kernels, local_sums(): pl.pallas_call(functools.partial(sums_kernel, scale=scale, course_list=(0...  8.09 us
    pallas_call x1, Pallas kernels, contract_panel(): pl.pallas_call(panel_kernel, grid=(count_ops,), in_specs=[pl.BlockSpec((1...  6.63 us
    ppermute x1, starting transfers between devices, shifted(): return lax.ppermute(block, axis, route)  6.06 us
  transfers between devices with their start and end apart: 4, of which 3 were waited for; matrix products, arithmetic and copies ran while one was open for 8% of the time, Pallas kernels for 5%

profile of v7, /device:TPU:0, one launch (start us, length us, event | category | flops | bytes accessed | tf_op | source)
XLA Modules:
  0.0 206.1 jit_solution(6356930340247034148)
XLA Ops:
  7.3 6.1 %collective-permute-start = (bf16[6,2,3,256,128]{4,3,2,1,0:T(8,128)(2,1)}, bf16[6,2,3,256,128]{4,3,2,1,0:T(8,128)(2,1)}, u32[]{:S(2)}, u32[]{:S(2)}) collective-permute-start(bf16[6,2,3,256,128]{4,3,2,1,0:T(8,128)(2,1)} %field_ref.3), channel_id=1, source_target_pairs={{2,0},{3,1},{4,2},{5,3},{6,4},{7,5},{8,6},{9,7},{10,8},{11,9},{12,... | collective-permute-start | bytes 7077896 | tf_op jit(solution)/shard_map/ppermute | solution.py:20
  13.3 2.0 copy.52
  15.4 0.7 fusion.16
  16.7 1.4 fusion.13
  18.7 0.7 copy.44.link_ref
  19.5 0.7 select_reduce_fusion.slot_ref
  20.2 1.2 copy.42
  21.4 2.4 %pad.6.near_ref = bf16[6,2,3,256,128]{4,3,2,1,0:T(8,128)(2,1)} pad(bf16[6,2,3,256,8]{4,3,2,1,0:T(8,128)(2,1)S(1)} %copy.42, bf16[]{:T(256)} %constant.107.clone.1), padding=0_0x0_0x0_0x0_0x120_0 | pad | bytes 2506754 | tf_op jit(solution)/shard_map/jit(_pad)/pad | solution.py:101
  23.7 11.0 %shard_map.77 = (bf16[6,1536,256]{2,1,0:T(8,128)(2,1)}, bf16[6,512,768]{2,1,0:T(8,128)(2,1)}) custom-call(s32[3]{0:T(128)} %select_reduce_fusion.slot_ref, bf16[6,2,3,256,128]{4,3,2,1,0:T(8,128)(2,1)} %field_ref.3, bf16[6,2,3,256,128]{4,3,2,1,0:T(8,128)(2,1)} %pad.6.near_ref, f32[6,3,2,3,3,128]{5,4,3,2,1,0:T(4,128)} %copy.44.link_ref, ...), custom_call_target="tpu_custom_call" | custom-call | tf_op jit(solution)/shard_map/pallas_call | solution.py:116
  34.7 29.4 %collective-permute-done.near_ref = bf16[6,2,3,256,128]{4,3,2,1,0:T(8,128)(2,1)} collective-permute-done((bf16[6,2,3,256,128]{4,3,2,1,0:T(8,128)(2,1)}, bf16[6,2,3,256,128]{4,3,2,1,0:T(8,128)(2,1)}, u32[]{:S(2)}, u32[]{:S(2)}) %collective-permute-start) | collective-permute-done | bytes 2359328 | tf_op jit(solution)/shard_map/ppermute | solution.py:20
  64.1 8.1 %shard_map.78 = bf16[6,1536,256]{2,1,0:T(8,128)(2,1)} custom-call(s32[3]{0:T(128)} %select_reduce_fusion.slot_ref, bf16[6,2,3,256,128]{4,3,2,1,0:T(8,128)(2,1)} %field_ref.3, bf16[6,2,3,256,128]{4,3,2,1,0:T(8,128)(2,1)} %collective-permute-done.near_ref, f32[6,3,2,3,3,128]{5,4,3,2,1,0:T(4,128)} %copy.44.link_ref, ...), custom_call_target="tpu_custom_call", output_to_operand_aliasing={{}: (5, {})} | custom-call | tf_op jit(solution)/shard_map/pallas_call | solution.py:130
  73.9 75.9 %reduce-scatter.2.cloned.1.call-done = bf16[6,96,256]{2,1,0:T(8,128)(2,1)} async-done(((bf16[6,1536,256]{2,1,0:T(8,128)(2,1)}), bf16[6,96,256]{2,1,0:T(8,128)(2,1)}) %reduce-scatter.2.cloned.1.call-update) | async-done | bytes 294928 | tf_op jit(solution)/shard_map/reduce_scatter | solution.py:211
  149.8 1.5 gather_fusion.2
  151.5 13.4 %all_to_all.10 = bf16[4,2,96,256]{3,2,1,0:T(8,128)(2,1)S(1)} all-to-all(bf16[4,2,96,256]{3,2,1,0:T(8,128)(2,1)S(1)} %broadcast_select_fusion), channel_id=1, replica_groups=mesh['cfg'=2,'slab'=4,'member'=4] {'slab'}, dimensions={0} | all-to-all | bytes 786432 | tf_op jit(solution)/shard_map/all_to_all | solution.py:216
  164.9 1.3 broadcast_in_dim.14
  166.2 3.6 %all-to-all-start.1 = ((bf16[4,4,2,96,256]{4,3,1,2,0:T(8,128)(2,1)}), bf16[4,4,2,96,256]{4,3,1,2,0:T(8,128)(2,1)S(1)}, u32[]{:S(2)}, u32[]{:S(2)}) async-start(bf16[4,4,2,96,256]{4,3,1,2,0:T(8,128)(2,1)} %broadcast_in_dim.14), calls=%async_computation.2 | async-start | bytes 3145728 | tf_op jit(solution)/shard_map/all_to_all | solution.py:218
  169.8 1.6 reshape_squeeze.7
  171.4 1.4 copy.54
  172.9 1.5 maximum_maximum_fusion.wide_ref
  174.4 15.4 %all-to-all-done.1 = bf16[4,4,2,96,256]{4,3,1,2,0:T(8,128)(2,1)S(1)} async-done(((bf16[4,4,2,96,256]{4,3,1,2,0:T(8,128)(2,1)}), bf16[4,4,2,96,256]{4,3,1,2,0:T(8,128)(2,1)S(1)}, u32[]{:S(2)}, u32[]{:S(2)}) %all-to-all-start.1) | async-done | bytes 1572896 | tf_op jit(solution)/shard_map/all_to_all | solution.py:218
  190.0 1.3 copy.49
  191.2 6.6 %shard_map.79 = f32[3,2,256]{2,1,0:T(2,128)} custom-call(bf16[2,3,2,256,256]{4,3,2,1,0:T(8,128)(2,1)} %bitcast.26, bf16[2,3,2,256,256]{4,3,2,1,0:T(8,128)(2,1)} %bitcast.27, bf16[512,1024]{1,0:T(8,128)(2,1)} %bitcast.30, bf16[2048,512]{1,0:T(8,128)(2,1)} %maximum_maximum_fusion.wide_ref), custom_call_target="tpu_custom_call" | custom-call | tf_op jit(solution)/shard_map/pallas_call | solution.py:177
  197.8 0.8 reduce_sum.19
  198.6 0.7 copy.51
  (34 shorter events, 2.8 us)
Async XLA Ops:
  7.2 65.1 %copy-start = (s32[4,2]{0,1:T(2,128)S(1)}, s32[4,2]{0,1:T(2,128)}, u32[]{:S(2)}) copy-start(s32[4,2]{0,1:T(2,128)} %param.11) | copy-start | bytes 100
  7.2 8.2 %copy-start.4 = (s32[1,3]{1,0:T(1,128)S(1)}, s32[1,3]{1,0:T(1,128)}, u32[]{:S(2)}) copy-start(s32[1,3]{1,0:T(1,128)} %param.10) | copy-start | bytes 40
  7.2 11.6 %copy-start.2 = (f32[6,3,2,3,3,128]{5,2,4,3,1,0:T(2,128)S(1)}, f32[6,3,2,3,3,128]{5,2,4,3,1,0:T(2,128)}, u32[]{:S(2)}) copy-start(f32[6,3,2,3,3,128]{5,2,4,3,1,0:T(2,128)} %param.7) | copy-start | bytes 497668
  7.2 12.3 %copy-start.5 = (s32[3]{0:T(128)S(1)}, s32[3]{0:T(128)}, u32[]{:S(2)}) copy-start(s32[3]{0:T(128)} %param.9) | copy-start | bytes 40
  7.2 142.6 %reduce-scatter.2.cloned.1.call-start = ((), (), s32[]{:S(2)}) async-start(), calls=%async_computation.3 | async-start | bytes 5013504 | tf_op jit(solution)/shard_map/reduce_scatter | solution.py:211
  7.3 56.9 %collective-permute-start = (bf16[6,2,3,256,128]{4,3,2,1,0:T(8,128)(2,1)}, bf16[6,2,3,256,128]{4,3,2,1,0:T(8,128)(2,1)}, u32[]{:S(2)}, u32[]{:S(2)}) collective-permute-start(bf16[6,2,3,256,128]{4,3,2,1,0:T(8,128)(2,1)} %field_ref.3), channel_id=1, source_target_pairs={{2,0},{3,1},{4,2},{5,3},{6,4},{7,5},{8,6},{9,7},{10,8},{11,9},{12,... | collective-permute-start | bytes 7077896 | tf_op jit(solution)/shard_map/ppermute | solution.py:20
  15.3 4.9 %collective-permute-start.1 = (bf16[6,2,3,256,8]{3,4,2,1,0:T(8,128)(2,1)S(1)}, bf16[6,2,3,256,8]{3,4,2,1,0:T(8,128)(2,1)S(1)}, u32[]{:S(2)}, u32[]{:S(2)}) collective-permute-start(bf16[6,2,3,256,8]{3,4,2,1,0:T(8,128)(2,1)S(1)} %copy.52), channel_id=1, source_target_pairs={{0,1},{1,0},{2,3},{3,2},{4,5},{5,4},{6,7},{7,6},{8,9},{9,8},{10,11... | collective-permute-start | bytes 442376 | tf_op jit(solution)/shard_map/ppermute | solution.py:24
  72.2 0.7 copy-start.3
  164.9 4.9 %copy-start.1 = (bf16[1,2,256,1024]{3,2,1,0:T(8,128)(2,1)S(1)}, bf16[1,2,256,1024]{3,2,1,0:T(8,128)(2,1)}, u32[]{:S(2)}) copy-start(bf16[1,2,256,1024]{3,2,1,0:T(8,128)(2,1)} %param.8) | copy-start | bytes 3145732
  166.2 23.6 %all-to-all-start.1 = ((bf16[4,4,2,96,256]{4,3,1,2,0:T(8,128)(2,1)}), bf16[4,4,2,96,256]{4,3,1,2,0:T(8,128)(2,1)S(1)}, u32[]{:S(2)}, u32[]{:S(2)}) async-start(bf16[4,4,2,96,256]{4,3,1,2,0:T(8,128)(2,1)} %broadcast_in_dim.14), calls=%async_computation.2 | async-start | bytes 3145728 | tf_op jit(solution)/shard_map/all_to_all | solution.py:218
Sparse Core Ops, SparseCore 0:
  72.4 77.4 reduce-scatter.1

commit v8 on v7

--- a/solution.py
+++ b/solution.py
@@ -208,8 +208,11 @@
     row_in = swapped(eigenvectors[..., :LZ], SPACE, 0)
     scale = 1.0 / math.sqrt(3.0 * extent_x * LY * LZ)
     partial = local_sums(eigenvectors, gauge_links, far_tile, row_in, directions, angle, scale)
-    own_rows = lax.psum_scatter(partial, SPACE, scatter_dimension=1, tiled=True)
-    rows = own_rows.shape[1]
+    rows = partial.shape[1] // nspace
+    blocks = partial.reshape(time_count, count_slabs, NSPIN, rows, count_ev)
+    slab_sums = lax.psum_scatter(blocks, "slab", scatter_dimension=1, tiled=True)
+    own_rows = lax.psum_scatter(slab_sums, "member", scatter_dimension=2, tiled=True)
+    own_rows = own_rows.reshape(time_count, rows, count_ev)
     slabs = jnp.arange(count_slabs, dtype=jnp.int32)
     wanted = jnp.stack([pair_times[slabs, 1], pair_times[slabs, 0]], 1)
     outgoing = jnp.take(own_rows, wanted.reshape(-1), axis=0).reshape(count_slabs, 2, rows, count_ev)

time: 207 us -> 254 us (1.23)
  waiting for transfers between devices: 121 us -> 160 us
  local copies, waits for them, and re-layouts: 16.5 us -> 21.5 us
  blocking collectives: 13.4 us -> 16.1 us
    reduce_scatter x1 -> x2, waiting for transfers between devices: 75.9 us -> 115 us  [the longest x1 87.2 us: body(): lax.psum_scatter(blocks, 'slab', scatter_dimension=1, tiled=True)]
    reshape x0 -> x1, local copies, waits for them, and re-layouts: none -> 4.99 us  [body(): blocks = partial.reshape(time_count, count_slabs, NSPIN, rows, count_ev)]
    all_to_all x1, blocking collectives: 13.4 us -> 16.1 us  [body(): across = lax.all_to_all(outgoing, 'slab', 0, 0, tiled=True)]
  transfers between devices with their start and end apart: 4 -> 5, of which waited for: 3 -> 4; matrix products, arithmetic and copies ran while one was open for 8% -> 6% of each run, Pallas kernels for 5% -> 4%
where the time goes in v8:
time: 254 us; the launch traced here: 253 us
  waiting for transfers between devices  160 us (63%)
  Pallas kernels  25.7 us (10%)
  local copies, waits for them, and re-layouts  21.5 us (8%)
  blocking collectives  16.1 us (6%)
  between operations  14.9 us (6%)
  starting transfers between devices  9.77 us (4%)
  other arithmetic  5.16 us (2%)
    reduce_scatter x1, waiting for transfers between devices, body(): lax.psum_scatter(blocks, 'slab', scatter_dimension=1, tiled=True)  87.2 us
    ppermute x1, waiting for transfers between devices, shifted(): return lax.ppermute(block, axis, route)  29.4 us
    reduce_scatter x1, waiting for transfers between devices, body(): lax.psum_scatter(slab_sums, 'member', scatter_dimension=2, tiled=True)  27.7 us
    all_to_all x1, blocking collectives, body(): across = lax.all_to_all(outgoing, 'slab', 0, 0, tiled=True)  16.1 us
    all_to_all x1, waiting for transfers between devices, body(): within = lax.all_to_all(spread, 'member', 0, 0, tiled=True)  15.4 us
    pallas_call x1, Pallas kernels, local_sums(): pl.pallas_call(functools.partial(sums_kernel, scale=scale, course_list=ne...  11 us
    pallas_call x1, Pallas kernels, local_sums(): pl.pallas_call(functools.partial(sums_kernel, scale=scale, course_list=(0...  8.09 us
    pallas_call x1, Pallas kernels, contract_panel(): pl.pallas_call(panel_kernel, grid=(count_ops,), in_specs=[pl.BlockSpec((1...  6.63 us
  transfers between devices with their start and end apart: 5, of which 4 were waited for; matrix products, arithmetic and copies ran while one was open for 6% of the time, Pallas kernels for 4%

profile of v8, /device:TPU:0, one launch (start us, length us, event | category | flops | bytes accessed | tf_op | source)
XLA Modules:
  0.0 252.9 jit_solution(14404992375502370680)
XLA Ops:
  7.3 6.1 %collective-permute-start = (bf16[6,2,3,256,128]{4,3,2,1,0:T(8,128)(2,1)}, bf16[6,2,3,256,128]{4,3,2,1,0:T(8,128)(2,1)}, u32[]{:S(2)}, u32[]{:S(2)}) collective-permute-start(bf16[6,2,3,256,128]{4,3,2,1,0:T(8,128)(2,1)} %field_ref.3), channel_id=1, source_target_pairs={{2,0},{3,1},{4,2},{5,3},{6,4},{7,5},{8,6},{9,7},{10,8},{11,9},{12,... | collective-permute-start | bytes 7077896 | tf_op jit(solution)/shard_map/ppermute | solution.py:20
  13.3 2.0 copy.67
  16.7 1.4 fusion.13
  18.7 0.7 copy.58.link_ref
  19.5 0.7 select_reduce_fusion.slot_ref
  20.2 1.2 copy.56
  21.4 2.4 pad.6.near_ref
  23.7 11.0 %shard_map.77 = (bf16[6,1536,256]{2,1,0:T(8,128)(2,1)}, bf16[6,512,768]{2,1,0:T(8,128)(2,1)}) custom-call(s32[3]{0:T(128)} %select_reduce_fusion.slot_ref, bf16[6,2,3,256,128]{4,3,2,1,0:T(8,128)(2,1)} %field_ref.3, bf16[6,2,3,256,128]{4,3,2,1,0:T(8,128)(2,1)} %pad.6.near_ref, f32[6,3,2,3,3,128]{5,4,3,2,1,0:T(4,128)} %copy.58.link_ref, ...), custom_call_target="tpu_custom_call" | custom-call | tf_op jit(solution)/shard_map/pallas_call | solution.py:116
  34.7 29.4 %collective-permute-done.near_ref = bf16[6,2,3,256,128]{4,3,2,1,0:T(8,128)(2,1)} collective-permute-done((bf16[6,2,3,256,128]{4,3,2,1,0:T(8,128)(2,1)}, bf16[6,2,3,256,128]{4,3,2,1,0:T(8,128)(2,1)}, u32[]{:S(2)}, u32[]{:S(2)}) %collective-permute-start) | collective-permute-done | bytes 2359328 | tf_op jit(solution)/shard_map/ppermute | solution.py:20
  64.1 8.1 %shard_map.78 = bf16[6,1536,256]{2,1,0:T(8,128)(2,1)} custom-call(s32[3]{0:T(128)} %select_reduce_fusion.slot_ref, bf16[6,2,3,256,128]{4,3,2,1,0:T(8,128)(2,1)} %field_ref.3, bf16[6,2,3,256,128]{4,3,2,1,0:T(8,128)(2,1)} %collective-permute-done.near_ref, f32[6,3,2,3,3,128]{5,4,3,2,1,0:T(4,128)} %copy.58.link_ref, ...), custom_call_target="tpu_custom_call", output_to_operand_aliasing={{}: (5, {})} | custom-call | tf_op jit(solution)/shard_map/pallas_call | solution.py:130
  72.2 5.0 %copy.59 = bf16[6,4,4,96,256]{4,3,0,2,1:T(8,128)(2,1)} copy(bf16[6,4,4,96,256]{4,3,2,1,0:T(8,128)(2,1)} %bitcast.28) | data formatting | bytes 9437184 | tf_op jit(solution)/shard_map/reshape | solution.py:212
  77.3 87.2 %reduce-scatter.3.cloned.1.call-done = bf16[6,1,4,96,256]{4,3,0,2,1:T(8,128)(2,1)} async-done(((bf16[6,4,4,96,256]{4,3,0,2,1:T(8,128)(2,1)}), bf16[6,1,4,96,256]{4,3,0,2,1:T(8,128)(2,1)}) %reduce-scatter.3.cloned.1.call-update) | async-done | bytes 1179664 | tf_op jit(solution)/shard_map/reduce_scatter | solution.py:213
  166.2 27.7 %reduce-scatter.5.cloned.1.call-done = bf16[6,1,1,96,256]{4,3,0,2,1:T(8,128)(2,1)} async-done(((bf16[6,1,4,96,256]{4,3,0,2,1:T(8,128)(2,1)}), bf16[6,1,1,96,256]{4,3,0,2,1:T(8,128)(2,1)}) %reduce-scatter.5.cloned.1.call-update) | async-done | bytes 294928 | tf_op jit(solution)/shard_map/reduce_scatter | solution.py:214
  193.9 1.5 gather_fusion.2
  195.6 16.1 %all_to_all.10 = bf16[4,2,96,256]{3,2,1,0:T(8,128)(2,1)S(1)} all-to-all(bf16[4,2,96,256]{3,2,1,0:T(8,128)(2,1)S(1)} %broadcast_select_fusion), channel_id=1, replica_groups=mesh['cfg'=2,'slab'=4,'member'=4] {'slab'}, dimensions={0} | all-to-all | bytes 786432 | tf_op jit(solution)/shard_map/all_to_all | solution.py:219
  211.7 1.3 broadcast_in_dim.14
  213.0 3.6 %all-to-all-start.1 = ((bf16[4,4,2,96,256]{4,3,1,2,0:T(8,128)(2,1)}), bf16[4,4,2,96,256]{4,3,1,2,0:T(8,128)(2,1)S(1)}, u32[]{:S(2)}, u32[]{:S(2)}) async-start(bf16[4,4,2,96,256]{4,3,1,2,0:T(8,128)(2,1)} %broadcast_in_dim.14), calls=%async_computation.3 | async-start | bytes 3145728 | tf_op jit(solution)/shard_map/all_to_all | solution.py:221
  216.6 1.6 reshape_squeeze.7
  218.2 1.4 copy.69
  219.7 1.5 maximum_maximum_fusion.wide_ref
  221.2 15.4 %all-to-all-done.1 = bf16[4,4,2,96,256]{4,3,1,2,0:T(8,128)(2,1)S(1)} async-done(((bf16[4,4,2,96,256]{4,3,1,2,0:T(8,128)(2,1)}), bf16[4,4,2,96,256]{4,3,1,2,0:T(8,128)(2,1)S(1)}, u32[]{:S(2)}, u32[]{:S(2)}) %all-to-all-start.1) | async-done | bytes 1572896 | tf_op jit(solution)/shard_map/all_to_all | solution.py:221
  236.8 1.3 copy.64
  238.0 6.6 %shard_map.79 = f32[3,2,256]{2,1,0:T(2,128)} custom-call(bf16[2,3,2,256,256]{4,3,2,1,0:T(8,128)(2,1)} %bitcast.29, bf16[2,3,2,256,256]{4,3,2,1,0:T(8,128)(2,1)} %bitcast.30, bf16[512,1024]{1,0:T(8,128)(2,1)} %bitcast.33, bf16[2048,512]{1,0:T(8,128)(2,1)} %maximum_maximum_fusion.wide_ref), custom_call_target="tpu_custom_call" | custom-call | tf_op jit(solution)/shard_map/pallas_call | solution.py:177
  244.7 0.8 reduce_sum.19
  (38 shorter events, 4.2 us)
Async XLA Ops:
  7.2 157.4 %copy-start = (s32[4,2]{0,1:T(2,128)S(1)}, s32[4,2]{0,1:T(2,128)}, u32[]{:S(2)}) copy-start(s32[4,2]{0,1:T(2,128)} %param.11) | copy-start | bytes 100
  7.2 8.2 %copy-start.4 = (s32[1,3]{1,0:T(1,128)S(1)}, s32[1,3]{1,0:T(1,128)}, u32[]{:S(2)}) copy-start(s32[1,3]{1,0:T(1,128)} %param.10) | copy-start | bytes 40
  7.2 11.6 %copy-start.2 = (f32[6,3,2,3,3,128]{5,2,4,3,1,0:T(2,128)S(1)}, f32[6,3,2,3,3,128]{5,2,4,3,1,0:T(2,128)}, u32[]{:S(2)}) copy-start(f32[6,3,2,3,3,128]{5,2,4,3,1,0:T(2,128)} %param.7) | copy-start | bytes 497668
  7.2 12.3 %copy-start.5 = (s32[3]{0:T(128)S(1)}, s32[3]{0:T(128)}, u32[]{:S(2)}) copy-start(s32[3]{0:T(128)} %param.9) | copy-start | bytes 40
  7.2 157.3 %reduce-scatter.3.cloned.1.call-start = ((), (), s32[]{:S(2)}) async-start(), calls=%async_computation.4 | async-start | bytes 5898240 | tf_op jit(solution)/shard_map/reduce_scatter | solution.py:213
  7.3 56.9 %collective-permute-start = (bf16[6,2,3,256,128]{4,3,2,1,0:T(8,128)(2,1)}, bf16[6,2,3,256,128]{4,3,2,1,0:T(8,128)(2,1)}, u32[]{:S(2)}, u32[]{:S(2)}) collective-permute-start(bf16[6,2,3,256,128]{4,3,2,1,0:T(8,128)(2,1)} %field_ref.3), channel_id=1, source_target_pairs={{2,0},{3,1},{4,2},{5,3},{6,4},{7,5},{8,6},{9,7},{10,8},{11,9},{12,... | collective-permute-start | bytes 7077896 | tf_op jit(solution)/shard_map/ppermute | solution.py:20
  15.3 4.9 %collective-permute-start.1 = (bf16[6,2,3,256,8]{3,4,2,1,0:T(8,128)(2,1)S(1)}, bf16[6,2,3,256,8]{3,4,2,1,0:T(8,128)(2,1)S(1)}, u32[]{:S(2)}, u32[]{:S(2)}) collective-permute-start(bf16[6,2,3,256,8]{3,4,2,1,0:T(8,128)(2,1)S(1)} %copy.67), channel_id=1, source_target_pairs={{0,1},{1,0},{2,3},{3,2},{4,5},{5,4},{6,7},{7,6},{8,9},{9,8},{10,11... | collective-permute-start | bytes 442376 | tf_op jit(solution)/shard_map/ppermute | solution.py:24
  77.2 88.0 %copy-start.3 = (s32[4]{0:T(128)S(1)}, s32[4]{0:T(128)}, u32[]{:S(2)}) copy-start(s32[4]{0:T(128)} %constant.166) | copy-start | bytes 52
  77.2 116.7 %reduce-scatter.5.cloned.1.call-start = ((), (), s32[]{:S(2)}) async-start(), calls=%async_computation.5 | async-start | bytes 1474560 | tf_op jit(solution)/shard_map/reduce_scatter | solution.py:214
  211.7 4.9 %copy-start.1 = (bf16[1,2,256,1024]{3,2,1,0:T(8,128)(2,1)S(1)}, bf16[1,2,256,1024]{3,2,1,0:T(8,128)(2,1)}, u32[]{:S(2)}) copy-start(bf16[1,2,256,1024]{3,2,1,0:T(8,128)(2,1)} %param.8) | copy-start | bytes 3145732
  213.0 23.6 %all-to-all-start.1 = ((bf16[4,4,2,96,256]{4,3,1,2,0:T(8,128)(2,1)}), bf16[4,4,2,96,256]{4,3,1,2,0:T(8,128)(2,1)S(1)}, u32[]{:S(2)}, u32[]{:S(2)}) async-start(bf16[4,4,2,96,256]{4,3,1,2,0:T(8,128)(2,1)} %broadcast_in_dim.14), calls=%async_computation.3 | async-start | bytes 3145728 | tf_op jit(solution)/shard_map/all_to_all | solution.py:221
Sparse Core Ops, SparseCore 0:
  77.4 87.1 reduce-scatter.2
  167.7 26.2 reduce-scatter.4

commit v9 on v7

--- a/solution.py
+++ b/solution.py
@@ -121,18 +121,27 @@
             jax.ShapeDtypeStruct((time_count, left_rows, 6 * sites), jnp.bfloat16),
         ),
     )(slot_of, eigenvectors, row_wide, gauge_links, trig)
-    second_spec = pltpu.PrefetchScalarGridSpec(
-        num_scalar_prefetch=1,
-        grid=(time_count,),
-        in_specs=[pl.BlockSpec(memory_space=pl.ANY), field_spec, link_spec, left_spec, pl.BlockSpec(memory_space=pl.ANY)],
-        out_specs=pl.BlockSpec((1, 2 * count_ev, count_ev), lambda t, slot: (t, slot[0], 0)),
-    )
-    return pl.pallas_call(
-        functools.partial(sums_kernel, scale=scale, course_list=(0,)),
-        grid_spec=second_spec,
-        out_shape=jax.ShapeDtypeStruct((time_count, rows, count_ev), jnp.bfloat16),
-        input_output_aliases={5: 0},
-    )(slot_of, eigenvectors, far_tile, gauge_links, left, partial)
+    for first, far_part in far_tile:
+        span = far_part.shape[0]
+        second_spec = pltpu.PrefetchScalarGridSpec(
+            num_scalar_prefetch=1,
+            grid=(span,),
+            in_specs=[
+                pl.BlockSpec(memory_space=pl.ANY),
+                pl.BlockSpec((1, 2, 3, count_ev, sites), lambda t, slot: (t, 0, 0, 0, 0)),
+                pl.BlockSpec((1,) + gauge_links.shape[1:], lambda t, slot, first=first: (t + first, 0, 0, 0, 0, 0)),
+                pl.BlockSpec((1, left_rows, 6 * sites), lambda t, slot, first=first: (t + first, 0, 0)),
+                pl.BlockSpec(memory_space=pl.ANY),
+            ],
+            out_specs=pl.BlockSpec((1, 2 * count_ev, count_ev), lambda t, slot, first=first: (t + first, slot[0], 0)),
+        )
+        partial = pl.pallas_call(
+            functools.partial(sums_kernel, scale=scale, course_list=(0,)),
+            grid_spec=second_spec,
+            out_shape=jax.ShapeDtypeStruct((time_count, rows, count_ev), jnp.bfloat16),
+            input_output_aliases={5: 0},
+        )(slot_of, eigenvectors, far_part, gauge_links, left, partial)
+    return partial
 
 
 def panel_kernel(sink_ref, source_ref, stack_ref, wide_ref, out_ref):
@@ -204,7 +213,9 @@
     coord_y = device % 2 * half_rows + column // LZ
     coord_z = column % LZ
     angle = phase_angles(momenta, (coord_x, coord_y, coord_z), (extent_x, LY, LZ))[0]
-    far_tile = shifted(eigenvectors, SPACE, -2)
+    halves = 2 if time_count % 2 == 0 else 1
+    span = time_count // halves
+    far_tile = [(h * span, shifted(eigenvectors[h * span : (h + 1) * span], SPACE, -2)) for h in range(halves)]
     row_in = swapped(eigenvectors[..., :LZ], SPACE, 0)
     scale = 1.0 / math.sqrt(3.0 * extent_x * LY * LZ)
     partial = local_sums(eigenvectors, gauge_links, far_tile, row_in, directions, angle, scale)

time: 207 us -> 208 us (level)
  waiting for transfers between devices: 121 us -> 114 us
  local copies, waits for them, and re-layouts: 16.5 us -> 22.1 us
  Pallas kernels: 25.7 us -> 28.2 us
    ppermute x1 -> x2, waiting for transfers between devices: 29.4 us -> 22.7 us  [shifted(): return lax.ppermute(block, axis, route)]
    slice x0 -> x1, local copies, waits for them, and re-layouts: none -> 3.51 us  [body(): eigenvectors[h * span:(h + 1) * span]]
    pallas_call x1 -> x2, Pallas kernels: 8.09 us -> 10.5 us  [local_sums(): pl.pallas_call(functools.partial(sums_kernel, scale=scale, course_list=(0...]
    unnamed x14 -> x16, local copies, waits for them, and re-layouts: 2.76 us -> 4.19 us
    ppermute x1 -> x2, starting transfers between devices: 6.06 us -> 6.51 us  [shifted(): return lax.ppermute(block, axis, route)]
  transfers between devices with their start and end apart: 4 -> 5, of which waited for: 3 -> 4; matrix products, arithmetic and copies ran while one was open for 8% -> 8% of each run, Pallas kernels for 5% -> 8%
where the time goes in v9:
time: 208 us
  waiting for transfers between devices  114 us (55%)
  Pallas kernels  28.2 us (14%)
  local copies, waits for them, and re-layouts  22.1 us (11%)
  between operations  14.8 us (7%)
  blocking collectives  13.3 us (6%)
  starting transfers between devices  10.1 us (5%)
  other arithmetic  5.05 us (2%)
    reduce_scatter x1, waiting for transfers between devices, body(): own_rows = lax.psum_scatter(partial, SPACE, scatter_dimension=1, tiled=True)  75.8 us
    ppermute x2, waiting for transfers between devices, shifted(): return lax.ppermute(block, axis, route)  22.7 us
    all_to_all x1, waiting for transfers between devices, body(): within = lax.all_to_all(spread, 'member', 0, 0, tiled=True)  15.4 us
    all_to_all x1, blocking collectives, body(): across = lax.all_to_all(outgoing, 'slab', 0, 0, tiled=True)  13.3 us
    pallas_call x1, Pallas kernels, local_sums(): pl.pallas_call(functools.partial(sums_kernel, scale=scale, course_list=ne...  11 us
    pallas_call x2, Pallas kernels, local_sums(): pl.pallas_call(functools.partial(sums_kernel, scale=scale, course_list=(0...  10.5 us
    pallas_call x1, Pallas kernels, contract_panel(): pl.pallas_call(panel_kernel, grid=(count_ops,), in_specs=[pl.BlockSpec((1...  6.61 us
    ppermute x2, starting transfers between devices, shifted(): return lax.ppermute(block, axis, route)  6.51 us
  transfers between devices with their start and end apart: 5, of which 4 were waited for; matrix products, arithmetic and copies ran while one was open for 8% of the time, Pallas kernels for 8%

profile of v9, /device:TPU:0, one launch (start us, length us, event | category | flops | bytes accessed | tf_op | source)
XLA Modules:
  0.0 207.7 jit_solution(7788515809743592717)
XLA Ops:
  7.2 3.5 %fusion.15 = (bf16[3,2,3,256,128]{4,3,2,1,0:T(8,128)(2,1)}, bf16[3,2,3,256,128]{4,3,2,1,0:T(8,128)(2,1)}) fusion(bf16[6,2,3,256,128]{4,3,2,1,0:T(8,128)(2,1)} %field_ref.5), kind=kLoop, calls=%fused_computation.41 | loop fusion | bytes 4718592 | tf_op jit(solution)/shard_map/slice | solution.py:218
  10.7 6.0 %collective-permute-start.2 = (bf16[3,2,3,256,128]{4,3,2,1,0:T(8,128)(2,1)}, bf16[3,2,3,256,128]{4,3,2,1,0:T(8,128)(2,1)}, u32[]{:S(2)}, u32[]{:S(2)}) collective-permute-start(bf16[3,2,3,256,128]{4,3,2,1,0:T(8,128)(2,1)} %get-tuple-element.8), channel_id=1, source_target_pairs={{2,0},{3,1},{4,2},{5,3},{6,4},{7,5},{8,6},{9,7},{10,8},{11,9},{12,... | collective-permute-start | bytes 3538952 | tf_op jit(solution)/shard_map/ppermute | solution.py:20
  17.3 1.5 copy.58
  20.0 1.3 fusion.13
  22.0 1.7 copy.50.link_ref
  24.3 2.0 copy.47
  26.3 2.3 %pad.6.near_ref = bf16[6,2,3,256,128]{4,3,2,1,0:T(8,128)(2,1)} pad(bf16[6,2,3,256,8]{4,3,2,1,0:T(8,128)(2,1)S(1)} %copy.47, bf16[]{:T(256)} %constant.107.clone.1), padding=0_0x0_0x0_0x0_0x120_0 | pad | bytes 2506754 | tf_op jit(solution)/shard_map/jit(_pad)/pad | solution.py:101
  28.5 11.0 %shard_map.77 = (bf16[6,1536,256]{2,1,0:T(8,128)(2,1)}, bf16[6,512,768]{2,1,0:T(8,128)(2,1)}) custom-call(s32[3]{0:T(128)} %select_reduce_fusion.slot_ref, bf16[6,2,3,256,128]{4,3,2,1,0:T(8,128)(2,1)} %field_ref.5, bf16[6,2,3,256,128]{4,3,2,1,0:T(8,128)(2,1)} %pad.6.near_ref, f32[6,3,2,3,3,128]{5,4,3,2,1,0:T(4,128)} %copy.50.link_ref, ...), custom_call_target="tpu_custom_call" | custom-call | tf_op jit(solution)/shard_map/pallas_call | solution.py:116
  39.6 3.9 %collective-permute-done.2.near_ref = bf16[3,2,3,256,128]{4,3,2,1,0:T(8,128)(2,1)} collective-permute-done((bf16[3,2,3,256,128]{4,3,2,1,0:T(8,128)(2,1)}, bf16[3,2,3,256,128]{4,3,2,1,0:T(8,128)(2,1)}, u32[]{:S(2)}, u32[]{:S(2)}) %collective-permute-start.2) | collective-permute-done | bytes 1179680 | tf_op jit(solution)/shard_map/ppermute | solution.py:20
  43.4 5.3 %shard_map.78.rest_0_ = bf16[6,1536,256]{2,1,0:T(8,128)(2,1)} custom-call(s32[3]{0:T(128)} %select_reduce_fusion.slot_ref, bf16[6,2,3,256,128]{4,3,2,1,0:T(8,128)(2,1)} %field_ref.5, bf16[3,2,3,256,128]{4,3,2,1,0:T(8,128)(2,1)} %collective-permute-done.2.near_ref, f32[6,3,2,3,3,128]{5,4,3,2,1,0:T(4,128)} %copy.50.link_ref, ...), custom_call_target="tpu_custom_call", output_to_operand_aliasing={{}: (5, {})} | custom-call | tf_op jit(solution)/shard_map/pallas_call | solution.py:138
  48.7 18.9 %collective-permute-done.near_ref = bf16[3,2,3,256,128]{4,3,2,1,0:T(8,128)(2,1)S(1)} collective-permute-done((bf16[3,2,3,256,128]{4,3,2,1,0:T(8,128)(2,1)}, bf16[3,2,3,256,128]{4,3,2,1,0:T(8,128)(2,1)S(1)}, u32[]{:S(2)}, u32[]{:S(2)}) %collective-permute-start) | collective-permute-done | bytes 1179680 | tf_op jit(solution)/shard_map/ppermute | solution.py:20
  67.6 1.0 copy-done.3
  68.6 5.3 %shard_map.79 = bf16[6,1536,256]{2,1,0:T(8,128)(2,1)} custom-call(s32[3]{0:T(128)} %select_reduce_fusion.slot_ref, bf16[6,2,3,256,128]{4,3,2,1,0:T(8,128)(2,1)} %field_ref.5, bf16[3,2,3,256,128]{4,3,2,1,0:T(8,128)(2,1)} %copy-done.3, f32[6,3,2,3,3,128]{5,4,3,2,1,0:T(4,128)} %copy.50.link_ref, ...), custom_call_target="tpu_custom_call", output_to_operand_aliasing={{}: (5, {})} | custom-call | tf_op jit(solution)/shard_map/pallas_call | solution.py:138
  75.5 75.8 %reduce-scatter.2.cloned.1.call-done = bf16[6,96,256]{2,1,0:T(8,128)(2,1)} async-done(((bf16[6,1536,256]{2,1,0:T(8,128)(2,1)}), bf16[6,96,256]{2,1,0:T(8,128)(2,1)}) %reduce-scatter.2.cloned.1.call-update) | async-done | bytes 294928 | tf_op jit(solution)/shard_map/reduce_scatter | solution.py:222
  151.4 1.5 gather_fusion.2
  153.0 13.3 %all_to_all.10 = bf16[4,2,96,256]{3,2,1,0:T(8,128)(2,1)S(1)} all-to-all(bf16[4,2,96,256]{3,2,1,0:T(8,128)(2,1)S(1)} %broadcast_select_fusion), channel_id=1, replica_groups=mesh['cfg'=2,'slab'=4,'member'=4] {'slab'}, dimensions={0} | all-to-all | bytes 786432 | tf_op jit(solution)/shard_map/all_to_all | solution.py:227
  166.4 1.3 broadcast_in_dim.14
  167.7 3.6 %all-to-all-start.1 = ((bf16[4,4,2,96,256]{4,3,1,2,0:T(8,128)(2,1)}), bf16[4,4,2,96,256]{4,3,1,2,0:T(8,128)(2,1)S(1)}, u32[]{:S(2)}, u32[]{:S(2)}) async-start(bf16[4,4,2,96,256]{4,3,1,2,0:T(8,128)(2,1)} %broadcast_in_dim.14), calls=%async_computation.2 | async-start | bytes 3145728 | tf_op jit(solution)/shard_map/all_to_all | solution.py:229
  171.3 1.6 reshape_squeeze.7
  172.9 1.4 copy.60
  174.4 1.5 maximum_maximum_fusion.wide_ref
  175.9 15.4 %all-to-all-done.1 = bf16[4,4,2,96,256]{4,3,1,2,0:T(8,128)(2,1)S(1)} async-done(((bf16[4,4,2,96,256]{4,3,1,2,0:T(8,128)(2,1)}), bf16[4,4,2,96,256]{4,3,1,2,0:T(8,128)(2,1)S(1)}, u32[]{:S(2)}, u32[]{:S(2)}) %all-to-all-start.1) | async-done | bytes 1572896 | tf_op jit(solution)/shard_map/all_to_all | solution.py:229
  191.5 1.3 copy.55
  192.8 6.6 %shard_map.80 = f32[3,2,256]{2,1,0:T(2,128)} custom-call(bf16[2,3,2,256,256]{4,3,2,1,0:T(8,128)(2,1)} %bitcast.26, bf16[2,3,2,256,256]{4,3,2,1,0:T(8,128)(2,1)} %bitcast.27, bf16[512,1024]{1,0:T(8,128)(2,1)} %bitcast.30, bf16[2048,512]{1,0:T(8,128)(2,1)} %maximum_maximum_fusion.wide_ref), custom_call_target="tpu_custom_call" | custom-call | tf_op jit(solution)/shard_map/pallas_call | solution.py:186
  (40 shorter events, 5.9 us)
Async XLA Ops:
  7.2 66.7 %copy-start = (s32[4,2]{0,1:T(2,128)S(1)}, s32[4,2]{0,1:T(2,128)}, u32[]{:S(2)}) copy-start(s32[4,2]{0,1:T(2,128)} %param.11) | copy-start | bytes 100
  7.2 10.1 %copy-start.1 = (bf16[6,2,3,256,128]{4,3,2,1,0:T(8,128)(2,1)S(1)}, bf16[6,2,3,256,128]{4,3,2,1,0:T(8,128)(2,1)}, u32[]{:S(2)}) copy-start(bf16[6,2,3,256,128]{4,3,2,1,0:T(8,128)(2,1)} %field_ref.5) | copy-start | bytes 7077892
  7.2 144.2 %reduce-scatter.2.cloned.1.call-start = ((), (), s32[]{:S(2)}) async-start(), calls=%async_computation.3 | async-start | bytes 5013504 | tf_op jit(solution)/shard_map/reduce_scatter | solution.py:222
  10.7 8.0 %copy-start.5 = (s32[1,3]{1,0:T(1,128)S(1)}, s32[1,3]{1,0:T(1,128)}, u32[]{:S(2)}) copy-start(s32[1,3]{1,0:T(1,128)} %param.10) | copy-start | bytes 40
  10.7 12.9 %copy-start.6 = (s32[3]{0:T(128)S(1)}, s32[3]{0:T(128)}, u32[]{:S(2)}) copy-start(s32[3]{0:T(128)} %param.9) | copy-start | bytes 40
  10.7 32.7 %collective-permute-start.2 = (bf16[3,2,3,256,128]{4,3,2,1,0:T(8,128)(2,1)}, bf16[3,2,3,256,128]{4,3,2,1,0:T(8,128)(2,1)}, u32[]{:S(2)}, u32[]{:S(2)}) collective-permute-start(bf16[3,2,3,256,128]{4,3,2,1,0:T(8,128)(2,1)} %get-tuple-element.8), channel_id=1, source_target_pairs={{2,0},{3,1},{4,2},{5,3},{6,4},{7,5},{8,6},{9,7},{10,8},{11,9},{12,... | collective-permute-start | bytes 3538952 | tf_op jit(solution)/shard_map/ppermute | solution.py:20
  16.8 50.8 %collective-permute-start = (bf16[3,2,3,256,128]{4,3,2,1,0:T(8,128)(2,1)}, bf16[3,2,3,256,128]{4,3,2,1,0:T(8,128)(2,1)S(1)}, u32[]{:S(2)}, u32[]{:S(2)}) collective-permute-start(bf16[3,2,3,256,128]{4,3,2,1,0:T(8,128)(2,1)} %get-tuple-element.9), channel_id=1, source_target_pairs={{2,0},{3,1},{4,2},{5,3},{6,4},{7,5},{8,6},{9,7},{10,8},{11,9},{12,... | collective-permute-start | bytes 3538952 | tf_op jit(solution)/shard_map/ppermute | solution.py:20
  18.7 5.6 %collective-permute-start.1 = (bf16[6,2,3,256,8]{3,4,2,1,0:T(8,128)(2,1)}, bf16[6,2,3,256,8]{3,4,2,1,0:T(8,128)(2,1)}, u32[]{:S(2)}, u32[]{:S(2)}) collective-permute-start(bf16[6,2,3,256,8]{3,4,2,1,0:T(8,128)(2,1)} %copy.58), channel_id=1, source_target_pairs={{0,1},{1,0},{2,3},{3,2},{4,5},{5,4},{6,7},{7,6},{8,9},{9,8},{10,11... | collective-permute-start | bytes 442376 | tf_op jit(solution)/shard_map/ppermute | solution.py:24
  67.6 1.0 copy-start.3
  73.9 0.7 copy-start.4
  166.4 4.9 %copy-start.2 = (bf16[1,2,256,1024]{3,2,1,0:T(8,128)(2,1)S(1)}, bf16[1,2,256,1024]{3,2,1,0:T(8,128)(2,1)}, u32[]{:S(2)}) copy-start(bf16[1,2,256,1024]{3,2,1,0:T(8,128)(2,1)} %param.8) | copy-start | bytes 3145732
  167.7 23.6 %all-to-all-start.1 = ((bf16[4,4,2,96,256]{4,3,1,2,0:T(8,128)(2,1)}), bf16[4,4,2,96,256]{4,3,1,2,0:T(8,128)(2,1)S(1)}, u32[]{:S(2)}, u32[]{:S(2)}) async-start(bf16[4,4,2,96,256]{4,3,1,2,0:T(8,128)(2,1)} %broadcast_in_dim.14), calls=%async_computation.2 | async-start | bytes 3145728 | tf_op jit(solution)/shard_map/all_to_all | solution.py:229
Sparse Core Ops, SparseCore 0:
  74.0 77.3 reduce-scatter.1

commit v10 on v7

--- a/solution.py
+++ b/solution.py
@@ -208,8 +208,9 @@
     row_in = swapped(eigenvectors[..., :LZ], SPACE, 0)
     scale = 1.0 / math.sqrt(3.0 * extent_x * LY * LZ)
     partial = local_sums(eigenvectors, gauge_links, far_tile, row_in, directions, angle, scale)
-    own_rows = lax.psum_scatter(partial, SPACE, scatter_dimension=1, tiled=True)
-    rows = own_rows.shape[1]
+    rows = partial.shape[1] // nspace
+    blocks = partial.reshape(time_count, nspace, rows, count_ev).transpose(1, 0, 2, 3)
+    own_rows = lax.psum_scatter(blocks, SPACE, scatter_dimension=0, tiled=True)[0]
     slabs = jnp.arange(count_slabs, dtype=jnp.int32)
     wanted = jnp.stack([pair_times[slabs, 1], pair_times[slabs, 0]], 1)
     outgoing = jnp.take(own_rows, wanted.reshape(-1), axis=0).reshape(count_slabs, 2, rows, count_ev)

time: 207 us -> 212 us (1.024)
  local copies, waits for them, and re-layouts: 16.5 us -> 21.5 us
    reshape x0 -> x1, local copies, waits for them, and re-layouts: none -> 4.97 us  [body(): partial.reshape(time_count, nspace, rows, count_ev).transpose(1, 0, 2, 3)]
  transfers between devices with their start and end apart: 4 -> 4, of which waited for: 3 -> 3; matrix products, arithmetic and copies ran while one was open for 8% -> 7% of each run, Pallas kernels for 5% -> 5%
where the time goes in v10:
time: 212 us; the launch traced here: 211 us
  waiting for transfers between devices  121 us (57%)
  Pallas kernels  25.7 us (12%)
  local copies, waits for them, and re-layouts  21.5 us (10%)
  between operations  14.9 us (7%)
  blocking collectives  13.3 us (6%)
  starting transfers between devices  9.73 us (5%)
  other arithmetic  5.16 us (2%)
    reduce_scatter x1, waiting for transfers between devices, body(): lax.psum_scatter(blocks, SPACE, scatter_dimension=0, tiled=True)[0]  76 us
    ppermute x1, waiting for transfers between devices, shifted(): return lax.ppermute(block, axis, route)  29.4 us
    all_to_all x1, waiting for transfers between devices, body(): within = lax.all_to_all(spread, 'member', 0, 0, tiled=True)  15.4 us
    all_to_all x1, blocking collectives, body(): across = lax.all_to_all(outgoing, 'slab', 0, 0, tiled=True)  13.3 us
    pallas_call x1, Pallas kernels, local_sums(): pl.pallas_call(functools.partial(sums_kernel, scale=scale, course_list=ne...  11 us
    pallas_call x1, Pallas kernels, local_sums(): pl.pallas_call(functools.partial(sums_kernel, scale=scale, course_list=(0...  8.09 us
    pallas_call x1, Pallas kernels, contract_panel(): pl.pallas_call(panel_kernel, grid=(count_ops,), in_specs=[pl.BlockSpec((1...  6.63 us
    ppermute x1, starting transfers between devices, shifted(): return lax.ppermute(block, axis, route)  6.06 us
  transfers between devices with their start and end apart: 4, of which 3 were waited for; matrix products, arithmetic and copies ran while one was open for 7% of the time, Pallas kernels for 5%

profile of v10, /device:TPU:0, one launch (start us, length us, event | category | flops | bytes accessed | tf_op | source)
XLA Modules:
  0.0 211.1 jit_solution(10402347173122057492)
XLA Ops:
  7.3 6.1 %collective-permute-start = (bf16[6,2,3,256,128]{4,3,2,1,0:T(8,128)(2,1)}, bf16[6,2,3,256,128]{4,3,2,1,0:T(8,128)(2,1)}, u32[]{:S(2)}, u32[]{:S(2)}) collective-permute-start(bf16[6,2,3,256,128]{4,3,2,1,0:T(8,128)(2,1)} %field_ref.3), channel_id=1, source_target_pairs={{2,0},{3,1},{4,2},{5,3},{6,4},{7,5},{8,6},{9,7},{10,8},{11,9},{12,... | collective-permute-start | bytes 7077896 | tf_op jit(solution)/shard_map/ppermute | solution.py:20
  13.3 2.0 copy.67
  15.4 0.7 fusion.16
  16.7 1.4 fusion.13
  18.7 0.7 copy.58.link_ref
  19.5 0.7 select_reduce_fusion.slot_ref
  20.2 1.2 copy.56
  21.4 2.4 %pad.6.near_ref = bf16[6,2,3,256,128]{4,3,2,1,0:T(8,128)(2,1)} pad(bf16[6,2,3,256,8]{4,3,2,1,0:T(8,128)(2,1)S(1)} %copy.56, bf16[]{:T(256)} %constant.107.clone.1), padding=0_0x0_0x0_0x0_0x120_0 | pad | bytes 2506754 | tf_op jit(solution)/shard_map/jit(_pad)/pad | solution.py:101
  23.7 11.0 %shard_map.77 = (bf16[6,1536,256]{2,1,0:T(8,128)(2,1)}, bf16[6,512,768]{2,1,0:T(8,128)(2,1)}) custom-call(s32[3]{0:T(128)} %select_reduce_fusion.slot_ref, bf16[6,2,3,256,128]{4,3,2,1,0:T(8,128)(2,1)} %field_ref.3, bf16[6,2,3,256,128]{4,3,2,1,0:T(8,128)(2,1)} %pad.6.near_ref, f32[6,3,2,3,3,128]{5,4,3,2,1,0:T(4,128)} %copy.58.link_ref, ...), custom_call_target="tpu_custom_call" | custom-call | tf_op jit(solution)/shard_map/pallas_call | solution.py:116
  34.7 29.4 %collective-permute-done.near_ref = bf16[6,2,3,256,128]{4,3,2,1,0:T(8,128)(2,1)} collective-permute-done((bf16[6,2,3,256,128]{4,3,2,1,0:T(8,128)(2,1)}, bf16[6,2,3,256,128]{4,3,2,1,0:T(8,128)(2,1)}, u32[]{:S(2)}, u32[]{:S(2)}) %collective-permute-start) | collective-permute-done | bytes 2359328 | tf_op jit(solution)/shard_map/ppermute | solution.py:20
  64.1 8.1 %shard_map.78 = bf16[6,1536,256]{2,1,0:T(8,128)(2,1)} custom-call(s32[3]{0:T(128)} %select_reduce_fusion.slot_ref, bf16[6,2,3,256,128]{4,3,2,1,0:T(8,128)(2,1)} %field_ref.3, bf16[6,2,3,256,128]{4,3,2,1,0:T(8,128)(2,1)} %collective-permute-done.near_ref, f32[6,3,2,3,3,128]{5,4,3,2,1,0:T(4,128)} %copy.58.link_ref, ...), custom_call_target="tpu_custom_call", output_to_operand_aliasing={{}: (5, {})} | custom-call | tf_op jit(solution)/shard_map/pallas_call | solution.py:130
  72.2 5.0 %copy.70 = bf16[6,16,96,256]{3,2,0,1:T(8,128)(2,1)} copy(bf16[6,16,96,256]{3,2,1,0:T(8,128)(2,1)} %bitcast.32) | data formatting | bytes 9437184 | tf_op jit(solution)/shard_map/reshape | solution.py:212
  78.9 76.0 %reduce-scatter.2.cloned.1.call-done = bf16[1,6,96,256]{3,2,1,0:T(8,128)(2,1)} async-done(((bf16[16,6,96,256]{3,2,1,0:T(8,128)(2,1)}), bf16[1,6,96,256]{3,2,1,0:T(8,128)(2,1)}) %reduce-scatter.2.cloned.1.call-update) | async-done | bytes 294928 | tf_op jit(solution)/shard_map/reduce_scatter | solution.py:213
  154.8 1.5 gather_fusion.2
  156.5 13.3 %all_to_all.10 = bf16[4,2,96,256]{3,2,1,0:T(8,128)(2,1)S(1)} all-to-all(bf16[4,2,96,256]{3,2,1,0:T(8,128)(2,1)S(1)} %broadcast_select_fusion), channel_id=1, replica_groups=mesh['cfg'=2,'slab'=4,'member'=4] {'slab'}, dimensions={0} | all-to-all | bytes 786432 | tf_op jit(solution)/shard_map/all_to_all | solution.py:217
  169.9 1.3 broadcast_in_dim.14
  171.2 3.6 %all-to-all-start.1 = ((bf16[4,4,2,96,256]{4,3,1,2,0:T(8,128)(2,1)}), bf16[4,4,2,96,256]{4,3,1,2,0:T(8,128)(2,1)S(1)}, u32[]{:S(2)}, u32[]{:S(2)}) async-start(bf16[4,4,2,96,256]{4,3,1,2,0:T(8,128)(2,1)} %broadcast_in_dim.14), calls=%async_computation.2 | async-start | bytes 3145728 | tf_op jit(solution)/shard_map/all_to_all | solution.py:219
  174.8 1.6 reshape_squeeze.7
  176.3 1.4 copy.71
  177.9 1.5 maximum_maximum_fusion.wide_ref
  179.4 15.4 %all-to-all-done.1 = bf16[4,4,2,96,256]{4,3,1,2,0:T(8,128)(2,1)S(1)} async-done(((bf16[4,4,2,96,256]{4,3,1,2,0:T(8,128)(2,1)}), bf16[4,4,2,96,256]{4,3,1,2,0:T(8,128)(2,1)S(1)}, u32[]{:S(2)}, u32[]{:S(2)}) %all-to-all-start.1) | async-done | bytes 1572896 | tf_op jit(solution)/shard_map/all_to_all | solution.py:219
  194.9 1.3 copy.64
  196.2 6.6 %shard_map.79 = f32[3,2,256]{2,1,0:T(2,128)} custom-call(bf16[2,3,2,256,256]{4,3,2,1,0:T(8,128)(2,1)} %bitcast.33, bf16[2,3,2,256,256]{4,3,2,1,0:T(8,128)(2,1)} %bitcast.34, bf16[512,1024]{1,0:T(8,128)(2,1)} %bitcast.37, bf16[2048,512]{1,0:T(8,128)(2,1)} %maximum_maximum_fusion.wide_ref), custom_call_target="tpu_custom_call" | custom-call | tf_op jit(solution)/shard_map/pallas_call | solution.py:177
  202.8 0.8 reduce_sum.19
  (35 shorter events, 3.4 us)
Async XLA Ops:
  7.2 70.1 %copy-start = (s32[4,2]{0,1:T(2,128)S(1)}, s32[4,2]{0,1:T(2,128)}, u32[]{:S(2)}) copy-start(s32[4,2]{0,1:T(2,128)} %param.11) | copy-start | bytes 100
  7.2 8.2 %copy-start.4 = (s32[1,3]{1,0:T(1,128)S(1)}, s32[1,3]{1,0:T(1,128)}, u32[]{:S(2)}) copy-start(s32[1,3]{1,0:T(1,128)} %param.10) | copy-start | bytes 40
  7.2 11.6 %copy-start.2 = (f32[6,3,2,3,3,128]{5,2,4,3,1,0:T(2,128)S(1)}, f32[6,3,2,3,3,128]{5,2,4,3,1,0:T(2,128)}, u32[]{:S(2)}) copy-start(f32[6,3,2,3,3,128]{5,2,4,3,1,0:T(2,128)} %param.7) | copy-start | bytes 497668
  7.2 12.3 %copy-start.5 = (s32[3]{0:T(128)S(1)}, s32[3]{0:T(128)}, u32[]{:S(2)}) copy-start(s32[3]{0:T(128)} %param.9) | copy-start | bytes 40
  7.2 147.6 %reduce-scatter.2.cloned.1.call-start = ((), (), s32[]{:S(2)}) async-start(), calls=%async_computation.3 | async-start | bytes 5013504 | tf_op jit(solution)/shard_map/reduce_scatter | solution.py:213
  7.3 56.9 %collective-permute-start = (bf16[6,2,3,256,128]{4,3,2,1,0:T(8,128)(2,1)}, bf16[6,2,3,256,128]{4,3,2,1,0:T(8,128)(2,1)}, u32[]{:S(2)}, u32[]{:S(2)}) collective-permute-start(bf16[6,2,3,256,128]{4,3,2,1,0:T(8,128)(2,1)} %field_ref.3), channel_id=1, source_target_pairs={{2,0},{3,1},{4,2},{5,3},{6,4},{7,5},{8,6},{9,7},{10,8},{11,9},{12,... | collective-permute-start | bytes 7077896 | tf_op jit(solution)/shard_map/ppermute | solution.py:20
  15.3 4.9 %collective-permute-start.1 = (bf16[6,2,3,256,8]{3,4,2,1,0:T(8,128)(2,1)S(1)}, bf16[6,2,3,256,8]{3,4,2,1,0:T(8,128)(2,1)S(1)}, u32[]{:S(2)}, u32[]{:S(2)}) collective-permute-start(bf16[6,2,3,256,8]{3,4,2,1,0:T(8,128)(2,1)S(1)} %copy.67), channel_id=1, source_target_pairs={{0,1},{1,0},{2,3},{3,2},{4,5},{5,4},{6,7},{7,6},{8,9},{9,8},{10,11... | collective-permute-start | bytes 442376 | tf_op jit(solution)/shard_map/ppermute | solution.py:24
  77.2 0.7 copy-start.3
  169.8 4.9 %copy-start.1 = (bf16[1,2,256,1024]{3,2,1,0:T(8,128)(2,1)S(1)}, bf16[1,2,256,1024]{3,2,1,0:T(8,128)(2,1)}, u32[]{:S(2)}) copy-start(bf16[1,2,256,1024]{3,2,1,0:T(8,128)(2,1)} %param.8) | copy-start | bytes 3145732
  171.2 23.6 %all-to-all-start.1 = ((bf16[4,4,2,96,256]{4,3,1,2,0:T(8,128)(2,1)}), bf16[4,4,2,96,256]{4,3,1,2,0:T(8,128)(2,1)S(1)}, u32[]{:S(2)}, u32[]{:S(2)}) async-start(bf16[4,4,2,96,256]{4,3,1,2,0:T(8,128)(2,1)} %broadcast_in_dim.14), calls=%async_computation.2 | async-start | bytes 3145728 | tf_op jit(solution)/shard_map/all_to_all | solution.py:219
Sparse Core Ops, SparseCore 0:
  77.3 77.4 reduce-scatter.1

commit v11 on v7

--- a/solution.py
+++ b/solution.py
@@ -213,7 +213,14 @@
     slabs = jnp.arange(count_slabs, dtype=jnp.int32)
     wanted = jnp.stack([pair_times[slabs, 1], pair_times[slabs, 0]], 1)
     outgoing = jnp.take(own_rows, wanted.reshape(-1), axis=0).reshape(count_slabs, 2, rows, count_ev)
-    across = lax.all_to_all(outgoing, "slab", 0, 0, tiled=True)
+    if count_slabs <= 8:
+        slab = lax.axis_index("slab")
+        pieces = [jnp.take(outgoing, (slab + shift) % count_slabs, axis=0) for shift in range(count_slabs)]
+        arrived = [pieces[0]] + [shifted(pieces[shift], "slab", shift) for shift in range(1, count_slabs)]
+        arrived = jnp.stack(arrived, 0)
+        across = jnp.take(arrived, (slab - jnp.arange(count_slabs, dtype=jnp.int32)) % count_slabs, axis=0)
+    else:
+        across = lax.all_to_all(outgoing, "slab", 0, 0, tiled=True)
     spread = jnp.broadcast_to(across[None], (NSPIN,) + across.shape)
     within = lax.all_to_all(spread, "member", 0, 0, tiled=True)
     incoming = within.transpose(1, 0, 2, 3, 4).reshape(nspace, 2, rows, count_ev)

time: 207 us -> 204 us (0.986)
  blocking collectives: 13.4 us -> 0 us
  waiting for transfers between devices: 121 us -> 127 us
  starting transfers between devices: 9.73 us -> 13.2 us
    all_to_all x1 -> x0, blocking collectives: 13.4 us -> none  [body(): across = lax.all_to_all(outgoing, 'slab', 0, 0, tiled=True)]
    ppermute x1 -> x4, waiting for transfers between devices: 29.4 us -> 35.9 us  [shifted(): return lax.ppermute(block, axis, route)]
    ppermute x1 -> x4, starting transfers between devices: 6.06 us -> 9.52 us  [shifted(): return lax.ppermute(block, axis, route)]
  transfers between devices with their start and end apart: 4 -> 7, of which waited for: 3 -> 5; matrix products, arithmetic and copies ran while one was open for 8% -> 8% of each run, Pallas kernels for 5% -> 5%
where the time goes in v11:
time: 204 us
  waiting for transfers between devices  127 us (62%)
  Pallas kernels  25.7 us (13%)
  local copies, waits for them, and re-layouts  17 us (8%)
  between operations  15 us (7%)
  starting transfers between devices  13.2 us (6%)
  other arithmetic  5.3 us (3%)
    reduce_scatter x1, waiting for transfers between devices, body(): own_rows = lax.psum_scatter(partial, SPACE, scatter_dimension=1, tiled=True)  75.8 us
    ppermute x4, waiting for transfers between devices, shifted(): return lax.ppermute(block, axis, route)  35.9 us
    all_to_all x1, waiting for transfers between devices, body(): within = lax.all_to_all(spread, 'member', 0, 0, tiled=True)  15.4 us
    pallas_call x1, Pallas kernels, local_sums(): pl.pallas_call(functools.partial(sums_kernel, scale=scale, course_list=ne...  11 us
    ppermute x4, starting transfers between devices, shifted(): return lax.ppermute(block, axis, route)  9.52 us
    pallas_call x1, Pallas kernels, local_sums(): pl.pallas_call(functools.partial(sums_kernel, scale=scale, course_list=(0...  8.08 us
    pallas_call x1, Pallas kernels, contract_panel(): pl.pallas_call(panel_kernel, grid=(count_ops,), in_specs=[pl.BlockSpec((1...  6.62 us
  transfers between devices with their start and end apart: 7, of which 5 were waited for; matrix products, arithmetic and copies ran while one was open for 8% of the time, Pallas kernels for 5%

profile of v11, /device:TPU:0, one launch (start us, length us, event | category | flops | bytes accessed | tf_op | source)
XLA Modules:
  0.0 203.5 jit_solution(9914547466198519441)
XLA Ops:
  7.3 6.1 %collective-permute-start = (bf16[6,2,3,256,128]{4,3,2,1,0:T(8,128)(2,1)}, bf16[6,2,3,256,128]{4,3,2,1,0:T(8,128)(2,1)}, u32[]{:S(2)}, u32[]{:S(2)}) collective-permute-start(bf16[6,2,3,256,128]{4,3,2,1,0:T(8,128)(2,1)} %field_ref.3), channel_id=1, source_target_pairs={{2,0},{3,1},{4,2},{5,3},{6,4},{7,5},{8,6},{9,7},{10,8},{11,9},{12,... | collective-permute-start | bytes 7077896 | tf_op jit(solution)/shard_map/ppermute | solution.py:20
  13.3 2.0 copy.52
  16.7 1.3 fusion.16
  18.7 0.7 copy.44.link_ref
  20.1 1.2 copy.42
  21.2 2.4 %pad.6.near_ref = bf16[6,2,3,256,128]{4,3,2,1,0:T(8,128)(2,1)} pad(bf16[6,2,3,256,8]{4,3,2,1,0:T(8,128)(2,1)S(1)} %copy.42, bf16[]{:T(256)} %constant.161.clone.1), padding=0_0x0_0x0_0x0_0x120_0 | pad | bytes 2506754 | tf_op jit(solution)/shard_map/jit(_pad)/pad | solution.py:101
  23.6 11.0 %shard_map.77 = (bf16[6,1536,256]{2,1,0:T(8,128)(2,1)}, bf16[6,512,768]{2,1,0:T(8,128)(2,1)}) custom-call(s32[3]{0:T(128)} %select_reduce_fusion.slot_ref, bf16[6,2,3,256,128]{4,3,2,1,0:T(8,128)(2,1)} %field_ref.3, bf16[6,2,3,256,128]{4,3,2,1,0:T(8,128)(2,1)} %pad.6.near_ref, f32[6,3,2,3,3,128]{5,4,3,2,1,0:T(4,128)} %copy.44.link_ref, ...), custom_call_target="tpu_custom_call" | custom-call | tf_op jit(solution)/shard_map/pallas_call | solution.py:116
  34.6 29.5 %collective-permute-done.near_ref = bf16[6,2,3,256,128]{4,3,2,1,0:T(8,128)(2,1)} collective-permute-done((bf16[6,2,3,256,128]{4,3,2,1,0:T(8,128)(2,1)}, bf16[6,2,3,256,128]{4,3,2,1,0:T(8,128)(2,1)}, u32[]{:S(2)}, u32[]{:S(2)}) %collective-permute-start) | collective-permute-done | bytes 2359328 | tf_op jit(solution)/shard_map/ppermute | solution.py:20
  64.1 8.1 %shard_map.78 = bf16[6,1536,256]{2,1,0:T(8,128)(2,1)} custom-call(s32[3]{0:T(128)} %select_reduce_fusion.slot_ref, bf16[6,2,3,256,128]{4,3,2,1,0:T(8,128)(2,1)} %field_ref.3, bf16[6,2,3,256,128]{4,3,2,1,0:T(8,128)(2,1)} %collective-permute-done.near_ref, f32[6,3,2,3,3,128]{5,4,3,2,1,0:T(4,128)} %copy.44.link_ref, ...), custom_call_target="tpu_custom_call", output_to_operand_aliasing={{}: (5, {})} | custom-call | tf_op jit(solution)/shard_map/pallas_call | solution.py:130
  74.0 75.8 %reduce-scatter.2.cloned.1.call-done = bf16[6,96,256]{2,1,0:T(8,128)(2,1)} async-done(((bf16[6,1536,256]{2,1,0:T(8,128)(2,1)}), bf16[6,96,256]{2,1,0:T(8,128)(2,1)}) %reduce-scatter.2.cloned.1.call-update) | async-done | bytes 294928 | tf_op jit(solution)/shard_map/reduce_scatter | solution.py:211
  149.9 1.5 gather_fusion.2
  151.6 1.4 collective-permute-start.3
  153.0 1.9 collective-permute-start.4
  155.0 5.2 %collective-permute-done.3 = bf16[2,96,256]{2,1,0:T(8,128)(2,1)S(1)} collective-permute-done((bf16[2,96,256]{2,1,0:T(8,128)(2,1)S(1)}, bf16[2,96,256]{2,1,0:T(8,128)(2,1)S(1)}, u32[]{:S(2)}, u32[]{:S(2)}) %collective-permute-start.3) | collective-permute-done | bytes 98336 | tf_op jit(solution)/shard_map/ppermute | solution.py:20
  160.2 1.2 collective-permute-done.2
  162.2 1.3 broadcast_in_dim.45
  163.6 3.6 %all-to-all-start = ((bf16[4,4,2,96,256]{4,3,1,2,0:T(8,128)(2,1)}), bf16[4,4,2,96,256]{4,3,1,2,0:T(8,128)(2,1)S(1)}, u32[]{:S(2)}, u32[]{:S(2)}) async-start(bf16[4,4,2,96,256]{4,3,1,2,0:T(8,128)(2,1)} %broadcast_in_dim.45), calls=%async_computation.1 | async-start | bytes 3145728 | tf_op jit(solution)/shard_map/all_to_all | solution.py:225
  167.2 1.6 reshape_squeeze.7
  168.8 1.4 copy.54
  170.3 1.5 maximum_maximum_fusion.wide_ref
  171.8 15.4 %all-to-all-done = bf16[4,4,2,96,256]{4,3,1,2,0:T(8,128)(2,1)S(1)} async-done(((bf16[4,4,2,96,256]{4,3,1,2,0:T(8,128)(2,1)}), bf16[4,4,2,96,256]{4,3,1,2,0:T(8,128)(2,1)S(1)}, u32[]{:S(2)}, u32[]{:S(2)}) %all-to-all-start) | async-done | bytes 1572896 | tf_op jit(solution)/shard_map/all_to_all | solution.py:225
  187.3 1.3 copy.49
  188.6 6.6 %shard_map.79 = f32[3,2,256]{2,1,0:T(2,128)} custom-call(bf16[2,3,2,256,256]{4,3,2,1,0:T(8,128)(2,1)} %bitcast.38, bf16[2,3,2,256,256]{4,3,2,1,0:T(8,128)(2,1)} %bitcast.39, bf16[512,1024]{1,0:T(8,128)(2,1)} %bitcast.42, bf16[2048,512]{1,0:T(8,128)(2,1)} %maximum_maximum_fusion.wide_ref), custom_call_target="tpu_custom_call" | custom-call | tf_op jit(solution)/shard_map/pallas_call | solution.py:177
  195.2 0.8 reduce_sum.19
  (46 shorter events, 5.6 us)
Async XLA Ops:
  7.2 65.2 %copy-start = (s32[4,2]{0,1:T(2,128)S(1)}, s32[4,2]{0,1:T(2,128)}, u32[]{:S(2)}) copy-start(s32[4,2]{0,1:T(2,128)} %param.13) | copy-start | bytes 100
  7.2 8.2 %copy-start.4 = (s32[1,3]{1,0:T(1,128)S(1)}, s32[1,3]{1,0:T(1,128)}, u32[]{:S(2)}) copy-start(s32[1,3]{1,0:T(1,128)} %param.12) | copy-start | bytes 40
  7.2 11.5 %copy-start.2 = (f32[6,3,2,3,3,128]{5,2,4,3,1,0:T(2,128)S(1)}, f32[6,3,2,3,3,128]{5,2,4,3,1,0:T(2,128)}, u32[]{:S(2)}) copy-start(f32[6,3,2,3,3,128]{5,2,4,3,1,0:T(2,128)} %param.9) | copy-start | bytes 497668
  7.2 12.2 %copy-start.5 = (s32[3]{0:T(128)S(1)}, s32[3]{0:T(128)}, u32[]{:S(2)}) copy-start(s32[3]{0:T(128)} %param.11) | copy-start | bytes 40
  7.2 142.6 %reduce-scatter.2.cloned.1.call-start = ((), (), s32[]{:S(2)}) async-start(), calls=%async_computation.2 | async-start | bytes 5013504 | tf_op jit(solution)/shard_map/reduce_scatter | solution.py:211
  7.3 56.9 %collective-permute-start = (bf16[6,2,3,256,128]{4,3,2,1,0:T(8,128)(2,1)}, bf16[6,2,3,256,128]{4,3,2,1,0:T(8,128)(2,1)}, u32[]{:S(2)}, u32[]{:S(2)}) collective-permute-start(bf16[6,2,3,256,128]{4,3,2,1,0:T(8,128)(2,1)} %field_ref.3), channel_id=1, source_target_pairs={{2,0},{3,1},{4,2},{5,3},{6,4},{7,5},{8,6},{9,7},{10,8},{11,9},{12,... | collective-permute-start | bytes 7077896 | tf_op jit(solution)/shard_map/ppermute | solution.py:20
  15.3 4.8 %collective-permute-start.1 = (bf16[6,2,3,256,8]{3,4,2,1,0:T(8,128)(2,1)S(1)}, bf16[6,2,3,256,8]{3,4,2,1,0:T(8,128)(2,1)S(1)}, u32[]{:S(2)}, u32[]{:S(2)}) collective-permute-start(bf16[6,2,3,256,8]{3,4,2,1,0:T(8,128)(2,1)S(1)} %copy.52), channel_id=1, source_target_pairs={{0,1},{1,0},{2,3},{3,2},{4,5},{5,4},{6,7},{7,6},{8,9},{9,8},{10,11... | collective-permute-start | bytes 442376 | tf_op jit(solution)/shard_map/ppermute | solution.py:24
  72.2 0.8 copy-start.3
  151.6 8.7 %collective-permute-start.3 = (bf16[2,96,256]{2,1,0:T(8,128)(2,1)S(1)}, bf16[2,96,256]{2,1,0:T(8,128)(2,1)S(1)}, u32[]{:S(2)}, u32[]{:S(2)}) collective-permute-start(bf16[2,96,256]{2,1,0:T(8,128)(2,1)S(1)} %get-tuple-element.24), channel_id=1, source_target_pairs={{8,0},{12,4},{0,8},{4,12},{9,1},{13,5},{1,9},{5,13},{10,2},{14,6},... | collective-permute-start | bytes 294920 | tf_op jit(solution)/shard_map/ppermute | solution.py:20
  153.0 7.2 %collective-permute-start.4 = (bf16[2,96,256]{2,1,0:T(8,128)(2,1)S(1)}, bf16[2,96,256]{2,1,0:T(8,128)(2,1)S(1)}, u32[]{:S(2)}, u32[]{:S(2)}) collective-permute-start(bf16[2,96,256]{2,1,0:T(8,128)(2,1)S(1)} %get-tuple-element.23), channel_id=1, source_target_pairs={{4,0},{8,4},{12,8},{0,12},{5,1},{9,5},{13,9},{1,13},{6,2},{10,6},{... | collective-permute-start | bytes 294920 | tf_op jit(solution)/shard_map/ppermute | solution.py:20
  154.9 6.5 %collective-permute-start.2 = (bf16[2,96,256]{2,1,0:T(8,128)(2,1)S(1)}, bf16[2,96,256]{2,1,0:T(8,128)(2,1)S(1)}, u32[]{:S(2)}, u32[]{:S(2)}) collective-permute-start(bf16[2,96,256]{2,1,0:T(8,128)(2,1)S(1)} %get-tuple-element.25), channel_id=1, source_target_pairs={{12,0},{0,4},{4,8},{8,12},{13,1},{1,5},{5,9},{9,13},{14,2},{2,6},{... | collective-permute-start | bytes 294920 | tf_op jit(solution)/shard_map/ppermute | solution.py:20
  162.2 4.9 %copy-start.1 = (bf16[1,2,256,1024]{3,2,1,0:T(8,128)(2,1)S(1)}, bf16[1,2,256,1024]{3,2,1,0:T(8,128)(2,1)}, u32[]{:S(2)}) copy-start(bf16[1,2,256,1024]{3,2,1,0:T(8,128)(2,1)} %param.10) | copy-start | bytes 3145732
  163.6 23.6 %all-to-all-start = ((bf16[4,4,2,96,256]{4,3,1,2,0:T(8,128)(2,1)}), bf16[4,4,2,96,256]{4,3,1,2,0:T(8,128)(2,1)S(1)}, u32[]{:S(2)}, u32[]{:S(2)}) async-start(bf16[4,4,2,96,256]{4,3,1,2,0:T(8,128)(2,1)} %broadcast_in_dim.45), calls=%async_computation.1 | async-start | bytes 3145728 | tf_op jit(solution)/shard_map/all_to_all | solution.py:225
Sparse Core Ops, SparseCore 0:
  72.4 77.4 reduce-scatter.1

commit v12 on v11

--- a/solution.py
+++ b/solution.py
@@ -221,8 +221,9 @@
         across = jnp.take(arrived, (slab - jnp.arange(count_slabs, dtype=jnp.int32)) % count_slabs, axis=0)
     else:
         across = lax.all_to_all(outgoing, "slab", 0, 0, tiled=True)
-    spread = jnp.broadcast_to(across[None], (NSPIN,) + across.shape)
-    within = lax.all_to_all(spread, "member", 0, 0, tiled=True)
+    shared = [across] + [shifted(across, "member", shift) for shift in range(1, NSPIN)]
+    shared = jnp.stack(shared, 0)
+    within = jnp.take(shared, (member - jnp.arange(NSPIN, dtype=jnp.int32)) % NSPIN, axis=0)
     incoming = within.transpose(1, 0, 2, 3, 4).reshape(nspace, 2, rows, count_ev)
     count_ops = partial.shape[1] // (2 * count_ev)
     gathered = incoming.transpose(1, 0, 2, 3).reshape(2, count_ops, 2, count_ev, count_ev)

time: 204 us -> 199 us (0.975)
  local copies, waits for them, and re-layouts: 17 us -> 14.2 us
    ppermute x4 -> x7, waiting for transfers between devices: 35.9 us -> 51.8 us  [shifted(): return lax.ppermute(block, axis, route)]
    all_to_all x1 -> x0, waiting for transfers between devices: 15.4 us -> none  [body(): within = lax.all_to_all(spread, 'member', 0, 0, tiled=True)]
    all_to_all x1 -> x0, starting transfers between devices: 3.56 us -> none  [body(): within = lax.all_to_all(spread, 'member', 0, 0, tiled=True)]
    ppermute x4 -> x7, starting transfers between devices: 9.52 us -> 12.4 us  [shifted(): return lax.ppermute(block, axis, route)]
    reduce_scatter x1, waiting for transfers between devices: 75.8 us -> 73.2 us  [body(): own_rows = lax.psum_scatter(partial, SPACE, scatter_dimension=1, tiled=True)]
  transfers between devices with their start and end apart: 7 -> 9, of which waited for: 5 -> 7; matrix products, arithmetic and copies ran while one was open for 8% -> 7% of each run, Pallas kernels for 5% -> 6%
where the time goes in v12:
time: 199 us; the launch traced here: 198 us
  waiting for transfers between devices  125 us (63%)
  Pallas kernels  25.7 us (13%)
  between operations  15 us (8%)
  local copies, waits for them, and re-layouts  14.2 us (7%)
  starting transfers between devices  12.5 us (6%)
  other arithmetic  5.86 us (3%)
    reduce_scatter x1, waiting for transfers between devices, body(): own_rows = lax.psum_scatter(partial, SPACE, scatter_dimension=1, tiled=True)  73.2 us
    ppermute x7, waiting for transfers between devices, shifted(): return lax.ppermute(block, axis, route)  51.8 us
    ppermute x7, starting transfers between devices, shifted(): return lax.ppermute(block, axis, route)  12.4 us
    pallas_call x1, Pallas kernels, local_sums(): pl.pallas_call(functools.partial(sums_kernel, scale=scale, course_list=ne...  11 us
    pallas_call x1, Pallas kernels, local_sums(): pl.pallas_call(functools.partial(sums_kernel, scale=scale, course_list=(0...  8.06 us
    pallas_call x1, Pallas kernels, contract_panel(): pl.pallas_call(panel_kernel, grid=(count_ops,), in_specs=[pl.BlockSpec((1...  6.62 us
  transfers between devices with their start and end apart: 9, of which 7 were waited for; matrix products, arithmetic and copies ran while one was open for 7% of the time, Pallas kernels for 6%

profile of v12, /device:TPU:0, one launch (start us, length us, event | category | flops | bytes accessed | tf_op | source)
XLA Modules:
  0.0 198.2 jit_solution(5730211222754799185)
XLA Ops:
  7.3 6.1 %collective-permute-start = (bf16[6,2,3,256,128]{4,3,2,1,0:T(8,128)(2,1)}, bf16[6,2,3,256,128]{4,3,2,1,0:T(8,128)(2,1)}, u32[]{:S(2)}, u32[]{:S(2)}) collective-permute-start(bf16[6,2,3,256,128]{4,3,2,1,0:T(8,128)(2,1)} %field_ref.3), channel_id=1, source_target_pairs={{2,0},{3,1},{4,2},{5,3},{6,4},{7,5},{8,6},{9,7},{10,8},{11,9},{12,... | collective-permute-start | bytes 7077896 | tf_op jit(solution)/shard_map/ppermute | solution.py:20
  13.3 2.0 copy.39
  16.7 1.3 fusion.19
  20.0 1.2 copy.31
  21.2 2.3 %pad.6.near_ref = bf16[6,2,3,256,128]{4,3,2,1,0:T(8,128)(2,1)} pad(bf16[6,2,3,256,8]{4,3,2,1,0:T(8,128)(2,1)S(1)} %copy.31, bf16[]{:T(256)} %constant.180.clone.1), padding=0_0x0_0x0_0x0_0x120_0 | pad | bytes 2506754 | tf_op jit(solution)/shard_map/jit(_pad)/pad | solution.py:101
  23.6 11.0 %shard_map.77 = (bf16[6,1536,256]{2,1,0:T(8,128)(2,1)}, bf16[6,512,768]{2,1,0:T(8,128)(2,1)}) custom-call(s32[3]{0:T(128)} %select_reduce_fusion.slot_ref, bf16[6,2,3,256,128]{4,3,2,1,0:T(8,128)(2,1)} %field_ref.3, bf16[6,2,3,256,128]{4,3,2,1,0:T(8,128)(2,1)} %pad.6.near_ref, f32[6,3,2,3,3,128]{5,4,3,2,1,0:T(4,128)} %copy.33.link_ref, ...), custom_call_target="tpu_custom_call" | custom-call | tf_op jit(solution)/shard_map/pallas_call | solution.py:116
  34.6 29.6 %collective-permute-done.near_ref = bf16[6,2,3,256,128]{4,3,2,1,0:T(8,128)(2,1)} collective-permute-done((bf16[6,2,3,256,128]{4,3,2,1,0:T(8,128)(2,1)}, bf16[6,2,3,256,128]{4,3,2,1,0:T(8,128)(2,1)}, u32[]{:S(2)}, u32[]{:S(2)}) %collective-permute-start) | collective-permute-done | bytes 2359328 | tf_op jit(solution)/shard_map/ppermute | solution.py:20
  64.1 8.1 %shard_map.78 = bf16[6,1536,256]{2,1,0:T(8,128)(2,1)} custom-call(s32[3]{0:T(128)} %select_reduce_fusion.slot_ref, bf16[6,2,3,256,128]{4,3,2,1,0:T(8,128)(2,1)} %field_ref.3, bf16[6,2,3,256,128]{4,3,2,1,0:T(8,128)(2,1)} %collective-permute-done.near_ref, f32[6,3,2,3,3,128]{5,4,3,2,1,0:T(4,128)} %copy.33.link_ref, ...), custom_call_target="tpu_custom_call", output_to_operand_aliasing={{}: (5, {})} | custom-call | tf_op jit(solution)/shard_map/pallas_call | solution.py:130
  73.9 0.8 reshape_squeeze.7
  75.1 1.5 maximum_maximum_fusion.wide_ref
  76.7 73.2 %reduce-scatter.2.cloned.1.call-done = bf16[6,96,256]{2,1,0:T(8,128)(2,1)} async-done(((bf16[6,1536,256]{2,1,0:T(8,128)(2,1)}), bf16[6,96,256]{2,1,0:T(8,128)(2,1)}) %reduce-scatter.2.cloned.1.call-update) | async-done | bytes 294928 | tf_op jit(solution)/shard_map/reduce_scatter | solution.py:211
  149.8 1.5 gather_fusion.2
  151.5 1.4 collective-permute-start.3
  152.9 2.0 collective-permute-start.4
  154.9 5.3 %collective-permute-done.3 = bf16[2,96,256]{2,1,0:T(8,128)(2,1)S(1)} collective-permute-done((bf16[2,96,256]{2,1,0:T(8,128)(2,1)S(1)}, bf16[2,96,256]{2,1,0:T(8,128)(2,1)S(1)}, u32[]{:S(2)}, u32[]{:S(2)}) %collective-permute-start.3) | collective-permute-done | bytes 98336 | tf_op jit(solution)/shard_map/ppermute | solution.py:20
  160.3 1.1 collective-permute-done.2
  162.2 1.5 collective-permute-start.6
  163.7 1.4 collective-permute-start.7
  165.2 7.8 %collective-permute-done.5 = bf16[4,2,96,256]{3,2,1,0:T(8,128)(2,1)S(1)} collective-permute-done((bf16[4,2,96,256]{3,2,1,0:T(8,128)(2,1)S(1)}, bf16[4,2,96,256]{3,2,1,0:T(8,128)(2,1)S(1)}, u32[]{:S(2)}, u32[]{:S(2)}) %collective-permute-start.5) | collective-permute-done | bytes 393248 | tf_op jit(solution)/shard_map/ppermute | solution.py:20
  173.0 1.2 collective-permute-done.6
  174.2 6.8 %collective-permute-done.7 = bf16[4,2,96,256]{3,2,1,0:T(8,128)(2,1)S(1)} collective-permute-done((bf16[4,2,96,256]{3,2,1,0:T(8,128)(2,1)S(1)}, bf16[4,2,96,256]{3,2,1,0:T(8,128)(2,1)S(1)}, u32[]{:S(2)}, u32[]{:S(2)}) %collective-permute-start.7) | collective-permute-done | bytes 393248 | tf_op jit(solution)/shard_map/ppermute | solution.py:20
  182.0 1.3 copy.36
  183.3 6.6 %shard_map.79 = f32[3,2,256]{2,1,0:T(2,128)} custom-call(bf16[2,3,2,256,256]{4,3,2,1,0:T(8,128)(2,1)} %bitcast.46, bf16[2,3,2,256,256]{4,3,2,1,0:T(8,128)(2,1)} %bitcast.47, bf16[512,1024]{1,0:T(8,128)(2,1)} %bitcast.49, bf16[2048,512]{1,0:T(8,128)(2,1)} %maximum_maximum_fusion.wide_ref), custom_call_target="tpu_custom_call" | custom-call | tf_op jit(solution)/shard_map/pallas_call | solution.py:177
  190.0 0.8 reduce_sum.19
  (53 shorter events, 7.6 us)
Async XLA Ops:
  7.2 65.2 %copy-start = (s32[4,2]{0,1:T(2,128)S(1)}, s32[4,2]{0,1:T(2,128)}, u32[]{:S(2)}) copy-start(s32[4,2]{0,1:T(2,128)} %param.13) | copy-start | bytes 100
  7.2 8.2 %copy-start.4 = (s32[1,3]{1,0:T(1,128)S(1)}, s32[1,3]{1,0:T(1,128)}, u32[]{:S(2)}) copy-start(s32[1,3]{1,0:T(1,128)} %param.12) | copy-start | bytes 40
  7.2 11.5 %copy-start.2 = (f32[6,3,2,3,3,128]{5,2,4,3,1,0:T(2,128)S(1)}, f32[6,3,2,3,3,128]{5,2,4,3,1,0:T(2,128)}, u32[]{:S(2)}) copy-start(f32[6,3,2,3,3,128]{5,2,4,3,1,0:T(2,128)} %param.9) | copy-start | bytes 497668
  7.2 12.2 %copy-start.5 = (s32[3]{0:T(128)S(1)}, s32[3]{0:T(128)}, u32[]{:S(2)}) copy-start(s32[3]{0:T(128)} %param.11) | copy-start | bytes 40
  7.2 142.6 %reduce-scatter.2.cloned.1.call-start = ((), (), s32[]{:S(2)}) async-start(), calls=%async_computation.1 | async-start | bytes 5013504 | tf_op jit(solution)/shard_map/reduce_scatter | solution.py:211
  7.3 56.9 %collective-permute-start = (bf16[6,2,3,256,128]{4,3,2,1,0:T(8,128)(2,1)}, bf16[6,2,3,256,128]{4,3,2,1,0:T(8,128)(2,1)}, u32[]{:S(2)}, u32[]{:S(2)}) collective-permute-start(bf16[6,2,3,256,128]{4,3,2,1,0:T(8,128)(2,1)} %field_ref.3), channel_id=1, source_target_pairs={{2,0},{3,1},{4,2},{5,3},{6,4},{7,5},{8,6},{9,7},{10,8},{11,9},{12,... | collective-permute-start | bytes 7077896 | tf_op jit(solution)/shard_map/ppermute | solution.py:20
  15.3 4.7 %collective-permute-start.1 = (bf16[6,2,3,256,8]{3,4,2,1,0:T(8,128)(2,1)S(1)}, bf16[6,2,3,256,8]{3,4,2,1,0:T(8,128)(2,1)S(1)}, u32[]{:S(2)}, u32[]{:S(2)}) collective-permute-start(bf16[6,2,3,256,8]{3,4,2,1,0:T(8,128)(2,1)S(1)} %copy.39), channel_id=1, source_target_pairs={{0,1},{1,0},{2,3},{3,2},{4,5},{5,4},{6,7},{7,6},{8,9},{9,8},{10,11... | collective-permute-start | bytes 442376 | tf_op jit(solution)/shard_map/ppermute | solution.py:24
  72.2 0.8 copy-start.3
  72.2 1.7 copy-start.1
  151.5 8.7 %collective-permute-start.3 = (bf16[2,96,256]{2,1,0:T(8,128)(2,1)S(1)}, bf16[2,96,256]{2,1,0:T(8,128)(2,1)S(1)}, u32[]{:S(2)}, u32[]{:S(2)}) collective-permute-start(bf16[2,96,256]{2,1,0:T(8,128)(2,1)S(1)} %get-tuple-element.24), channel_id=1, source_target_pairs={{8,0},{12,4},{0,8},{4,12},{9,1},{13,5},{1,9},{5,13},{10,2},{14,6},... | collective-permute-start | bytes 294920 | tf_op jit(solution)/shard_map/ppermute | solution.py:20
  152.9 7.4 %collective-permute-start.4 = (bf16[2,96,256]{2,1,0:T(8,128)(2,1)S(1)}, bf16[2,96,256]{2,1,0:T(8,128)(2,1)S(1)}, u32[]{:S(2)}, u32[]{:S(2)}) collective-permute-start(bf16[2,96,256]{2,1,0:T(8,128)(2,1)S(1)} %get-tuple-element.23), channel_id=1, source_target_pairs={{4,0},{8,4},{12,8},{0,12},{5,1},{9,5},{13,9},{1,13},{6,2},{10,6},{... | collective-permute-start | bytes 294920 | tf_op jit(solution)/shard_map/ppermute | solution.py:20
  154.9 6.5 %collective-permute-start.2 = (bf16[2,96,256]{2,1,0:T(8,128)(2,1)S(1)}, bf16[2,96,256]{2,1,0:T(8,128)(2,1)S(1)}, u32[]{:S(2)}, u32[]{:S(2)}) collective-permute-start(bf16[2,96,256]{2,1,0:T(8,128)(2,1)S(1)} %get-tuple-element.25), channel_id=1, source_target_pairs={{12,0},{0,4},{4,8},{8,12},{13,1},{1,5},{5,9},{9,13},{14,2},{2,6},{... | collective-permute-start | bytes 294920 | tf_op jit(solution)/shard_map/ppermute | solution.py:20
  162.1 10.9 %collective-permute-start.5 = (bf16[4,2,96,256]{3,2,1,0:T(8,128)(2,1)S(1)}, bf16[4,2,96,256]{3,2,1,0:T(8,128)(2,1)S(1)}, u32[]{:S(2)}, u32[]{:S(2)}) collective-permute-start(bf16[4,2,96,256]{3,2,1,0:T(8,128)(2,1)S(1)} %broadcast_select_fusion), channel_id=1, source_target_pairs={{3,0},{0,1},{1,2},{2,3},{7,4},{4,5},{5,6},{6,7},{11,8},{8,9},{9,10... | collective-permute-start | bytes 1179656 | tf_op jit(solution)/shard_map/ppermute | solution.py:20
  162.2 12.0 %collective-permute-start.6 = (bf16[4,2,96,256]{3,2,1,0:T(8,128)(2,1)S(1)}, bf16[4,2,96,256]{3,2,1,0:T(8,128)(2,1)S(1)}, u32[]{:S(2)}, u32[]{:S(2)}) collective-permute-start(bf16[4,2,96,256]{3,2,1,0:T(8,128)(2,1)S(1)} %broadcast_select_fusion), channel_id=1, source_target_pairs={{2,0},{3,1},{0,2},{1,3},{6,4},{7,5},{4,6},{5,7},{10,8},{11,9},{8,1... | collective-permute-start | bytes 1179656 | tf_op jit(solution)/shard_map/ppermute | solution.py:20
  163.7 17.3 %collective-permute-start.7 = (bf16[4,2,96,256]{3,2,1,0:T(8,128)(2,1)S(1)}, bf16[4,2,96,256]{3,2,1,0:T(8,128)(2,1)S(1)}, u32[]{:S(2)}, u32[]{:S(2)}) collective-permute-start(bf16[4,2,96,256]{3,2,1,0:T(8,128)(2,1)S(1)} %broadcast_select_fusion), channel_id=1, source_target_pairs={{1,0},{2,1},{3,2},{0,3},{5,4},{6,5},{7,6},{4,7},{9,8},{10,9},{11,1... | collective-permute-start | bytes 1179656 | tf_op jit(solution)/shard_map/ppermute | solution.py:20
Sparse Core Ops, SparseCore 0:
  72.3 77.4 reduce-scatter.1

commit v13 on v12

--- a/solution.py
+++ b/solution.py
@@ -208,13 +208,26 @@
     row_in = swapped(eigenvectors[..., :LZ], SPACE, 0)
     scale = 1.0 / math.sqrt(3.0 * extent_x * LY * LZ)
     partial = local_sums(eigenvectors, gauge_links, far_tile, row_in, directions, angle, scale)
-    own_rows = lax.psum_scatter(partial, SPACE, scatter_dimension=1, tiled=True)
-    rows = own_rows.shape[1]
+    rows = partial.shape[1] // nspace
+    if count_slabs <= 8:
+        slab = lax.axis_index("slab")
+        blocks = partial.reshape(time_count, count_slabs, NSPIN, rows, count_ev)
+        slab_sum = lax.dynamic_index_in_dim(blocks, member, 2, keepdims=False).astype(jnp.float32)
+        for shift in range(1, NSPIN):
+            piece = lax.dynamic_index_in_dim(blocks, (member + shift) % NSPIN, 2, keepdims=False)
+            slab_sum = slab_sum + shifted(piece, "member", shift).astype(jnp.float32)
+        slab_part = slab_sum.astype(jnp.bfloat16)
+        total = lax.dynamic_index_in_dim(slab_sum, slab, 1, keepdims=False)
+        for shift in range(1, count_slabs):
+            piece = lax.dynamic_index_in_dim(slab_part, (slab + shift) % count_slabs, 1, keepdims=False)
+            total = total + shifted(piece, "slab", shift).astype(jnp.float32)
+        own_rows = total.astype(jnp.bfloat16)
+    else:
+        own_rows = lax.psum_scatter(partial, SPACE, scatter_dimension=1, tiled=True)
     slabs = jnp.arange(count_slabs, dtype=jnp.int32)
     wanted = jnp.stack([pair_times[slabs, 1], pair_times[slabs, 0]], 1)
     outgoing = jnp.take(own_rows, wanted.reshape(-1), axis=0).reshape(count_slabs, 2, rows, count_ev)
     if count_slabs <= 8:
-        slab = lax.axis_index("slab")
         pieces = [jnp.take(outgoing, (slab + shift) % count_slabs, axis=0) for shift in range(count_slabs)]
         arrived = [pieces[0]] + [shifted(pieces[shift], "slab", shift) for shift in range(1, count_slabs)]
         arrived = jnp.stack(arrived, 0)

time: 199 us -> 198 us (level)
  between operations: 15 us -> 1.61 us
  starting transfers between devices: 12.5 us -> 24.8 us
  waiting for transfers between devices: 125 us -> 113 us
  other arithmetic: 5.86 us -> 11.7 us
  local copies, waits for them, and re-layouts: 14.2 us -> 18.8 us
    reduce_scatter x1 -> x0, waiting for transfers between devices: 73.2 us -> none  [body(): own_rows = lax.psum_scatter(partial, SPACE, scatter_dimension=1, tiled=True)]
    ppermute x7 -> x13, waiting for transfers between devices: 51.8 us -> 113 us  [shifted(): return lax.ppermute(block, axis, route)]
    ppermute x7 -> x13, starting transfers between devices: 12.4 us -> 24.7 us  [shifted(): return lax.ppermute(block, axis, route)]
    squeeze x0 -> x2, local copies, waits for them, and re-layouts: none -> 4.93 us  [the longest x1 3.98 us: body(): lax.dynamic_index_in_dim(blocks, (member + shift) % NSPIN, 2, keepdims=Fa...]
    convert_element_type x0 -> x2, other arithmetic: none -> 4.52 us  [the longest x1 3.22 us: body(): slab_part = slab_sum.astype(jnp.bfloat16)]
  transfers between devices with their start and end apart: 9 -> 14, of which waited for: 7 -> 11; matrix products, arithmetic and copies ran while one was open for 7% -> 8% of each run, Pallas kernels for 6% -> 6%
where the time goes in v13:
time: 198 us; the launch traced here: 196 us
  waiting for transfers between devices  113 us (57%)
  Pallas kernels  25.7 us (13%)
  starting transfers between devices  24.8 us (13%)
  local copies, waits for them, and re-layouts  18.8 us (9%)
  other arithmetic  11.7 us (6%)
    ppermute x13, waiting for transfers between devices, shifted(): return lax.ppermute(block, axis, route)  113 us
    ppermute x13, starting transfers between devices, shifted(): return lax.ppermute(block, axis, route)  24.7 us
    pallas_call x1, Pallas kernels, local_sums(): pl.pallas_call(functools.partial(sums_kernel, scale=scale, course_list=ne...  11 us
    pallas_call x1, Pallas kernels, local_sums(): pl.pallas_call(functools.partial(sums_kernel, scale=scale, course_list=(0...  8.09 us
    pallas_call x1, Pallas kernels, contract_panel(): pl.pallas_call(panel_kernel, grid=(count_ops,), in_specs=[pl.BlockSpec((1...  6.62 us
    squeeze x1, local copies, waits for them, and re-layouts, body(): lax.dynamic_index_in_dim(blocks, (member + shift) % NSPIN, 2, keepdims=Fa...  3.98 us
  transfers between devices with their start and end apart: 14, of which 11 were waited for; matrix products, arithmetic and copies ran while one was open for 8% of the time, Pallas kernels for 6%

profile of v13, /device:TPU:0, one launch (start us, length us, event | category | flops | bytes accessed | tf_op | source)
XLA Modules:
  0.0 195.9 jit_solution(5164826567968613742)
XLA Ops:
  0.7 6.1 %collective-permute-start = (bf16[6,2,3,256,128]{4,3,2,1,0:T(8,128)(2,1)}, bf16[6,2,3,256,128]{4,3,2,1,0:T(8,128)(2,1)}, u32[]{:S(2)}, u32[]{:S(2)}) collective-permute-start(bf16[6,2,3,256,128]{4,3,2,1,0:T(8,128)(2,1)} %field_ref.3), channel_id=1, source_target_pairs={{2,0},{3,1},{4,2},{5,3},{6,4},{7,5},{8,6},{9,7},{10,8},{11,9},{12,... | collective-permute-start | bytes 7077896 | tf_op jit(solution)/shard_map/ppermute | solution.py:20
  6.7 2.0 %copy.39 = bf16[6,2,3,256,8]{3,4,2,1,0:T(8,128)(2,1)S(1)} copy(bf16[6,2,3,256,8]{4,3,2,1,0:T(8,128)(2,1)} %bitcast.70) | data formatting | bytes 294912
  10.1 1.3 fusion.26
  15.9 2.3 %pad.6.near_ref = bf16[6,2,3,256,128]{4,3,2,1,0:T(8,128)(2,1)} pad(bf16[6,2,3,256,8]{4,3,2,1,0:T(8,128)(2,1)S(1)} %copy.31, bf16[]{:T(256)} %constant.220.clone.1), padding=0_0x0_0x0_0x0_0x120_0 | pad | bytes 2506754 | tf_op jit(solution)/shard_map/jit(_pad)/pad | solution.py:101
  18.2 11.0 %shard_map.77 = (bf16[6,1536,256]{2,1,0:T(8,128)(2,1)}, bf16[6,512,768]{2,1,0:T(8,128)(2,1)}) custom-call(s32[3]{0:T(128)} %select_reduce_fusion.slot_ref, bf16[6,2,3,256,128]{4,3,2,1,0:T(8,128)(2,1)} %field_ref.3, bf16[6,2,3,256,128]{4,3,2,1,0:T(8,128)(2,1)} %pad.6.near_ref, f32[6,3,2,3,3,128]{5,4,3,2,1,0:T(4,128)} %copy.33.link_ref, ...), custom_call_target="tpu_custom_call" | custom-call | tf_op jit(solution)/shard_map/pallas_call | solution.py:116
  29.2 28.4 %collective-permute-done.near_ref = bf16[6,2,3,256,128]{4,3,2,1,0:T(8,128)(2,1)} collective-permute-done((bf16[6,2,3,256,128]{4,3,2,1,0:T(8,128)(2,1)}, bf16[6,2,3,256,128]{4,3,2,1,0:T(8,128)(2,1)}, u32[]{:S(2)}, u32[]{:S(2)}) %collective-permute-start) | collective-permute-done | bytes 2359328 | tf_op jit(solution)/shard_map/ppermute | solution.py:20
  57.5 8.1 %shard_map.78 = bf16[6,1536,256]{2,1,0:T(8,128)(2,1)} custom-call(s32[3]{0:T(128)} %select_reduce_fusion.slot_ref, bf16[6,2,3,256,128]{4,3,2,1,0:T(8,128)(2,1)} %field_ref.3, bf16[6,2,3,256,128]{4,3,2,1,0:T(8,128)(2,1)} %collective-permute-done.near_ref, f32[6,3,2,3,3,128]{5,4,3,2,1,0:T(4,128)} %copy.33.link_ref, ...), custom_call_target="tpu_custom_call", output_to_operand_aliasing={{}: (5, {})} | custom-call | tf_op jit(solution)/shard_map/pallas_call | solution.py:130
  65.6 4.0 %dynamic-slice_bitcast_fusion.2 = (bf16[6,4,96,256]{3,2,1,0:T(8,128)(2,1)}, bf16[6,4,96,256]{3,2,1,0:T(8,128)(2,1)}, bf16[6,4,96,256]{3,2,1,0:T(8,128)(2,1)}) fusion(bf16[6,4,4,96,256]{4,3,2,1,0:T(8,128)(2,1)} %bitcast.71, s32[]{:T(128)S(6)} %select_n.281, s32[]{:T(128)S(6)} %select_n.285, s32[]{:T(128)S(6)} %select_n.283), kind=kLoop, calls=%fused_computation.13 | loop fusion | bytes 7077900 | tf_op jit(solution)/shard_map/jit(dynamic_index_in_dim)/squeeze | solution.py:217
  70.0 1.4 collective-permute-start.4
  73.6 24.1 %collective-permute-done.2 = bf16[6,4,96,256]{3,2,1,0:T(8,128)(2,1)} collective-permute-done((bf16[6,4,96,256]{3,2,1,0:T(8,128)(2,1)}, bf16[6,4,96,256]{3,2,1,0:T(8,128)(2,1)}, u32[]{:S(2)}, u32[]{:S(2)}) %collective-permute-start.2) | collective-permute-done | bytes 1179680 | tf_op jit(solution)/shard_map/ppermute | solution.py:20
  98.8 22.6 %collective-permute-done.4 = bf16[6,4,96,256]{3,2,1,0:T(8,128)(2,1)} collective-permute-done((bf16[6,4,96,256]{3,2,1,0:T(8,128)(2,1)}, bf16[6,4,96,256]{3,2,1,0:T(8,128)(2,1)}, u32[]{:S(2)}, u32[]{:S(2)}) %collective-permute-start.4) | collective-permute-done | bytes 1179680 | tf_op jit(solution)/shard_map/ppermute | solution.py:20
  121.3 3.2 %fusion.24 = (bf16[6,4,96,256]{3,2,1,0:T(8,128)(2,1)S(1)}, f32[6,4,96,256]{3,2,1,0:T(8,128)S(1)}) fusion(bf16[6,4,96,256]{3,2,1,0:T(8,128)(2,1)} %collective-permute-done.4, bf16[6,4,96,256]{3,2,1,0:T(8,128)(2,1)} %collective-permute-done.3, bf16[6,4,96,256]{3,2,1,0:T(8,128)(2,1)} %collective-permute-done.2, bf16[6,4,4,96,256]{4,3,2,1,0:T(8,128)(2,1)} %bitcast.72, ...), kind=kLoop, calls=%fused_computation.90 | loop fusion | flops 4718592 | bytes 8257540 | tf_op jit(solution)/shard_map/convert_element_type | solution.py:219
  125.5 1.6 collective-permute-start.5
  127.1 4.4 %collective-permute-start.6 = (bf16[6,96,256]{2,1,0:T(8,128)(2,1)}, bf16[6,96,256]{2,1,0:T(8,128)(2,1)}, u32[]{:S(2)}, u32[]{:S(2)}) collective-permute-start(bf16[6,96,256]{2,1,0:T(8,128)(2,1)} %get-tuple-element.27), channel_id=1, source_target_pairs={{8,0},{12,4},{0,8},{4,12},{9,1},{13,5},{1,9},{5,13},{10,2},{14,6},... | collective-permute-start | bytes 884744 | tf_op jit(solution)/shard_map/ppermute | solution.py:20
  131.7 2.8 %maximum_maximum_fusion.wide_ref = bf16[2048,512]{1,0:T(8,128)(2,1)} fusion(bf16[1024,256]{1,0:T(8,128)(2,1)} %bitcast.78, bf16[1024,256]{1,0:T(8,128)(2,1)S(1)} %bitcast.75, bf16[1024,256]{1,0:T(8,128)(2,1)S(1)} %bitcast_negate_fusion), kind=kLoop, calls=%fused_computation.8 | loop fusion | flops 8388608 | bytes 3670016 | tf_op jit(solution)/shard_map/concatenate | solution.py:170
  134.4 4.8 %collective-permute-done.5 = bf16[6,96,256]{2,1,0:T(8,128)(2,1)} collective-permute-done((bf16[6,96,256]{2,1,0:T(8,128)(2,1)}, bf16[6,96,256]{2,1,0:T(8,128)(2,1)}, u32[]{:S(2)}, u32[]{:S(2)}) %collective-permute-start.5) | collective-permute-done | bytes 294944 | tf_op jit(solution)/shard_map/ppermute | solution.py:20
  139.2 12.1 %collective-permute-done.6 = bf16[6,96,256]{2,1,0:T(8,128)(2,1)} collective-permute-done((bf16[6,96,256]{2,1,0:T(8,128)(2,1)}, bf16[6,96,256]{2,1,0:T(8,128)(2,1)}, u32[]{:S(2)}, u32[]{:S(2)}) %collective-permute-start.6) | collective-permute-done | bytes 294944 | tf_op jit(solution)/shard_map/ppermute | solution.py:20
  153.4 6.6 %collective-permute-start.8 = (bf16[2,96,256]{2,1,0:T(8,128)(2,1)S(1)}, bf16[2,96,256]{2,1,0:T(8,128)(2,1)S(1)}, u32[]{:S(2)}, u32[]{:S(2)}) collective-permute-start(bf16[2,96,256]{2,1,0:T(8,128)(2,1)S(1)} %get-tuple-element.33), channel_id=1, source_target_pairs={{12,0},{0,4},{4,8},{8,12},{13,1},{1,5},{5,9},{9,13},{14,2},{2,6},{... | collective-permute-start | bytes 294920 | tf_op jit(solution)/shard_map/ppermute | solution.py:20
  160.0 2.4 %collective-permute-start.10 = (bf16[2,96,256]{2,1,0:T(8,128)(2,1)S(1)}, bf16[2,96,256]{2,1,0:T(8,128)(2,1)S(1)}, u32[]{:S(2)}, u32[]{:S(2)}) collective-permute-start(bf16[2,96,256]{2,1,0:T(8,128)(2,1)S(1)} %get-tuple-element.31), channel_id=1, source_target_pairs={{4,0},{8,4},{12,8},{0,12},{5,1},{9,5},{13,9},{1,13},{6,2},{10,6},{... | collective-permute-start | bytes 294920 | tf_op jit(solution)/shard_map/ppermute | solution.py:20
  163.2 4.1 %collective-permute-done.9 = bf16[2,96,256]{2,1,0:T(8,128)(2,1)S(1)} collective-permute-done((bf16[2,96,256]{2,1,0:T(8,128)(2,1)S(1)}, bf16[2,96,256]{2,1,0:T(8,128)(2,1)S(1)}, u32[]{:S(2)}, u32[]{:S(2)}) %collective-permute-start.9) | collective-permute-done | bytes 98336 | tf_op jit(solution)/shard_map/ppermute | solution.py:20
  168.2 1.6 collective-permute-start.13
  170.0 8.9 %collective-permute-done.11 = bf16[4,2,96,256]{3,2,1,0:T(8,128)(2,1)S(1)} collective-permute-done((bf16[4,2,96,256]{3,2,1,0:T(8,128)(2,1)S(1)}, bf16[4,2,96,256]{3,2,1,0:T(8,128)(2,1)S(1)}, u32[]{:S(2)}, u32[]{:S(2)}) %collective-permute-start.11) | collective-permute-done | bytes 393248 | tf_op jit(solution)/shard_map/ppermute | solution.py:20
  180.1 5.4 %collective-permute-done.13 = bf16[4,2,96,256]{3,2,1,0:T(8,128)(2,1)S(1)} collective-permute-done((bf16[4,2,96,256]{3,2,1,0:T(8,128)(2,1)S(1)}, bf16[4,2,96,256]{3,2,1,0:T(8,128)(2,1)S(1)}, u32[]{:S(2)}, u32[]{:S(2)}) %collective-permute-start.13) | collective-permute-done | bytes 393248 | tf_op jit(solution)/shard_map/ppermute | solution.py:20
  187.8 6.6 %shard_map.79 = f32[3,2,256]{2,1,0:T(2,128)} custom-call(bf16[2,3,2,256,256]{4,3,2,1,0:T(8,128)(2,1)} %bitcast.73, bf16[2,3,2,256,256]{4,3,2,1,0:T(8,128)(2,1)} %bitcast.74, bf16[512,1024]{1,0:T(8,128)(2,1)} %bitcast.76, bf16[2048,512]{1,0:T(8,128)(2,1)} %maximum_maximum_fusion.wide_ref), custom_call_target="tpu_custom_call" | custom-call | tf_op jit(solution)/shard_map/pallas_call | solution.py:177
  (68 shorter events, 18.6 us)
Async XLA Ops:
  0.6 12.2 %copy-start = (s32[4,2]{0,1:T(2,128)S(1)}, s32[4,2]{0,1:T(2,128)}, u32[]{:S(2)}) copy-start(s32[4,2]{0,1:T(2,128)} %param.13) | copy-start | bytes 100
  0.6 8.2 %copy-start.5 = (s32[1,3]{1,0:T(1,128)S(1)}, s32[1,3]{1,0:T(1,128)}, u32[]{:S(2)}) copy-start(s32[1,3]{1,0:T(1,128)} %param.12) | copy-start | bytes 40
  0.7 11.4 %copy-start.3 = (f32[6,3,2,3,3,128]{5,2,4,3,1,0:T(2,128)S(1)}, f32[6,3,2,3,3,128]{5,2,4,3,1,0:T(2,128)}, u32[]{:S(2)}) copy-start(f32[6,3,2,3,3,128]{5,2,4,3,1,0:T(2,128)} %param.9) | copy-start | bytes 497668
  0.7 56.9 %collective-permute-start = (bf16[6,2,3,256,128]{4,3,2,1,0:T(8,128)(2,1)}, bf16[6,2,3,256,128]{4,3,2,1,0:T(8,128)(2,1)}, u32[]{:S(2)}, u32[]{:S(2)}) collective-permute-start(bf16[6,2,3,256,128]{4,3,2,1,0:T(8,128)(2,1)} %field_ref.3), channel_id=1, source_target_pairs={{2,0},{3,1},{4,2},{5,3},{6,4},{7,5},{8,6},{9,7},{10,8},{11,9},{12,... | collective-permute-start | bytes 7077896 | tf_op jit(solution)/shard_map/ppermute | solution.py:20
  6.7 6.7 %copy-start.4 = (s32[4]{0:T(128)S(1)}, s32[4]{0:T(128)}, u32[]{:S(2)}) copy-start(s32[4]{0:T(128)} %constant.306) | copy-start | bytes 52
  6.7 7.4 %copy-start.6 = (s32[3]{0:T(128)S(1)}, s32[3]{0:T(128)}, u32[]{:S(2)}) copy-start(s32[3]{0:T(128)} %param.11) | copy-start | bytes 40
  8.7 6.1 %collective-permute-start.1 = (bf16[6,2,3,256,8]{3,4,2,1,0:T(8,128)(2,1)S(1)}, bf16[6,2,3,256,8]{3,4,2,1,0:T(8,128)(2,1)S(1)}, u32[]{:S(2)}, u32[]{:S(2)}) collective-permute-start(bf16[6,2,3,256,8]{3,4,2,1,0:T(8,128)(2,1)S(1)} %copy.39), channel_id=1, source_target_pairs={{0,1},{1,0},{2,3},{3,2},{4,5},{5,4},{6,7},{7,6},{8,9},{9,8},{10,11... | collective-permute-start | bytes 442376 | tf_op jit(solution)/shard_map/ppermute | solution.py:24
  65.6 6.0 %copy-start.1 = (bf16[1,2,256,1024]{3,2,1,0:T(8,128)(2,1)S(1)}, bf16[1,2,256,1024]{3,2,1,0:T(8,128)(2,1)}, u32[]{:S(2)}) copy-start(bf16[1,2,256,1024]{3,2,1,0:T(8,128)(2,1)} %param.10) | copy-start | bytes 3145732
  69.6 28.0 %collective-permute-start.2 = (bf16[6,4,96,256]{3,2,1,0:T(8,128)(2,1)}, bf16[6,4,96,256]{3,2,1,0:T(8,128)(2,1)}, u32[]{:S(2)}, u32[]{:S(2)}) collective-permute-start(bf16[6,4,96,256]{3,2,1,0:T(8,128)(2,1)} %get-tuple-element.22), channel_id=1, source_target_pairs={{3,0},{0,1},{1,2},{2,3},{7,4},{4,5},{5,6},{6,7},{11,8},{8,9},{9,10... | collective-permute-start | bytes 3538952 | tf_op jit(solution)/shard_map/ppermute | solution.py:20
  69.6 29.1 %collective-permute-start.3 = (bf16[6,4,96,256]{3,2,1,0:T(8,128)(2,1)}, bf16[6,4,96,256]{3,2,1,0:T(8,128)(2,1)}, u32[]{:S(2)}, u32[]{:S(2)}) collective-permute-start(bf16[6,4,96,256]{3,2,1,0:T(8,128)(2,1)} %get-tuple-element.24), channel_id=1, source_target_pairs={{2,0},{3,1},{0,2},{1,3},{6,4},{7,5},{4,6},{5,7},{10,8},{11,9},{8,1... | collective-permute-start | bytes 3538952 | tf_op jit(solution)/shard_map/ppermute | solution.py:20
  70.0 51.3 %collective-permute-start.4 = (bf16[6,4,96,256]{3,2,1,0:T(8,128)(2,1)}, bf16[6,4,96,256]{3,2,1,0:T(8,128)(2,1)}, u32[]{:S(2)}, u32[]{:S(2)}) collective-permute-start(bf16[6,4,96,256]{3,2,1,0:T(8,128)(2,1)} %get-tuple-element.23), channel_id=1, source_target_pairs={{1,0},{2,1},{3,2},{0,3},{5,4},{6,5},{7,6},{4,7},{9,8},{10,9},{11,1... | collective-permute-start | bytes 3538952 | tf_op jit(solution)/shard_map/ppermute | solution.py:20
  125.5 13.7 %collective-permute-start.5 = (bf16[6,96,256]{2,1,0:T(8,128)(2,1)}, bf16[6,96,256]{2,1,0:T(8,128)(2,1)}, u32[]{:S(2)}, u32[]{:S(2)}) collective-permute-start(bf16[6,96,256]{2,1,0:T(8,128)(2,1)} %get-tuple-element.25), channel_id=1, source_target_pairs={{12,0},{0,4},{4,8},{8,12},{13,1},{1,5},{5,9},{9,13},{14,2},{2,6},{... | collective-permute-start | bytes 884744 | tf_op jit(solution)/shard_map/ppermute | solution.py:20
  127.1 24.2 %collective-permute-start.6 = (bf16[6,96,256]{2,1,0:T(8,128)(2,1)}, bf16[6,96,256]{2,1,0:T(8,128)(2,1)}, u32[]{:S(2)}, u32[]{:S(2)}) collective-permute-start(bf16[6,96,256]{2,1,0:T(8,128)(2,1)} %get-tuple-element.27), channel_id=1, source_target_pairs={{8,0},{12,4},{0,8},{4,12},{9,1},{13,5},{1,9},{5,13},{10,2},{14,6},... | collective-permute-start | bytes 884744 | tf_op jit(solution)/shard_map/ppermute | solution.py:20
  131.5 19.8 %collective-permute-start.7 = (bf16[6,96,256]{2,1,0:T(8,128)(2,1)}, bf16[6,96,256]{2,1,0:T(8,128)(2,1)}, u32[]{:S(2)}, u32[]{:S(2)}) collective-permute-start(bf16[6,96,256]{2,1,0:T(8,128)(2,1)} %get-tuple-element.26), channel_id=1, source_target_pairs={{4,0},{8,4},{12,8},{0,12},{5,1},{9,5},{13,9},{1,13},{6,2},{10,6},{... | collective-permute-start | bytes 884744 | tf_op jit(solution)/shard_map/ppermute | solution.py:20
  152.6 14.7 %copy-start.2 = (bf16[6,96,256]{2,1,0:T(8,128)(2,1)}, bf16[6,96,256]{2,1,0:T(8,128)(2,1)S(1)}, u32[]{:S(2)}) copy-start(bf16[6,96,256]{2,1,0:T(8,128)(2,1)S(1)} %fusion.4) | copy-start | bytes 884740
  153.4 9.8 %collective-permute-start.8 = (bf16[2,96,256]{2,1,0:T(8,128)(2,1)S(1)}, bf16[2,96,256]{2,1,0:T(8,128)(2,1)S(1)}, u32[]{:S(2)}, u32[]{:S(2)}) collective-permute-start(bf16[2,96,256]{2,1,0:T(8,128)(2,1)S(1)} %get-tuple-element.33), channel_id=1, source_target_pairs={{12,0},{0,4},{4,8},{8,12},{13,1},{1,5},{5,9},{9,13},{14,2},{2,6},{... | collective-permute-start | bytes 294920 | tf_op jit(solution)/shard_map/ppermute | solution.py:20
  159.9 7.3 %collective-permute-start.9 = (bf16[2,96,256]{2,1,0:T(8,128)(2,1)S(1)}, bf16[2,96,256]{2,1,0:T(8,128)(2,1)S(1)}, u32[]{:S(2)}, u32[]{:S(2)}) collective-permute-start(bf16[2,96,256]{2,1,0:T(8,128)(2,1)S(1)} %get-tuple-element.32), channel_id=1, source_target_pairs={{8,0},{12,4},{0,8},{4,12},{9,1},{13,5},{1,9},{5,13},{10,2},{14,6},... | collective-permute-start | bytes 294920 | tf_op jit(solution)/shard_map/ppermute | solution.py:20
  160.0 7.3 %collective-permute-start.10 = (bf16[2,96,256]{2,1,0:T(8,128)(2,1)S(1)}, bf16[2,96,256]{2,1,0:T(8,128)(2,1)S(1)}, u32[]{:S(2)}, u32[]{:S(2)}) collective-permute-start(bf16[2,96,256]{2,1,0:T(8,128)(2,1)S(1)} %get-tuple-element.31), channel_id=1, source_target_pairs={{4,0},{8,4},{12,8},{0,12},{5,1},{9,5},{13,9},{1,13},{6,2},{10,6},{... | collective-permute-start | bytes 294920 | tf_op jit(solution)/shard_map/ppermute | solution.py:20
  168.0 10.9 %collective-permute-start.11 = (bf16[4,2,96,256]{3,2,1,0:T(8,128)(2,1)S(1)}, bf16[4,2,96,256]{3,2,1,0:T(8,128)(2,1)S(1)}, u32[]{:S(2)}, u32[]{:S(2)}) collective-permute-start(bf16[4,2,96,256]{3,2,1,0:T(8,128)(2,1)S(1)} %broadcast_select_fusion), channel_id=1, source_target_pairs={{3,0},{0,1},{1,2},{2,3},{7,4},{4,5},{5,6},{6,7},{11,8},{8,9},{9,10... | collective-permute-start | bytes 1179656 | tf_op jit(solution)/shard_map/ppermute | solution.py:20
  168.1 12.0 %collective-permute-start.12 = (bf16[4,2,96,256]{3,2,1,0:T(8,128)(2,1)S(1)}, bf16[4,2,96,256]{3,2,1,0:T(8,128)(2,1)S(1)}, u32[]{:S(2)}, u32[]{:S(2)}) collective-permute-start(bf16[4,2,96,256]{3,2,1,0:T(8,128)(2,1)S(1)} %broadcast_select_fusion), channel_id=1, source_target_pairs={{2,0},{3,1},{0,2},{1,3},{6,4},{7,5},{4,6},{5,7},{10,8},{11,9},{8,1... | collective-permute-start | bytes 1179656 | tf_op jit(solution)/shard_map/ppermute | solution.py:20
  168.2 17.3 %collective-permute-start.13 = (bf16[4,2,96,256]{3,2,1,0:T(8,128)(2,1)S(1)}, bf16[4,2,96,256]{3,2,1,0:T(8,128)(2,1)S(1)}, u32[]{:S(2)}, u32[]{:S(2)}) collective-permute-start(bf16[4,2,96,256]{3,2,1,0:T(8,128)(2,1)S(1)} %broadcast_select_fusion), channel_id=1, source_target_pairs={{1,0},{2,1},{3,2},{0,3},{5,4},{6,5},{7,6},{4,7},{9,8},{10,9},{11,1... | collective-permute-start | bytes 1179656 | tf_op jit(solution)/shard_map/ppermute | solution.py:20

commit v14 on v13

--- a/solution.py
+++ b/solution.py
@@ -211,11 +211,15 @@
     rows = partial.shape[1] // nspace
     if count_slabs <= 8:
         slab = lax.axis_index("slab")
-        blocks = partial.reshape(time_count, count_slabs, NSPIN, rows, count_ev)
-        slab_sum = lax.dynamic_index_in_dim(blocks, member, 2, keepdims=False).astype(jnp.float32)
-        for shift in range(1, NSPIN):
-            piece = lax.dynamic_index_in_dim(blocks, (member + shift) % NSPIN, 2, keepdims=False)
-            slab_sum = slab_sum + shifted(piece, "member", shift).astype(jnp.float32)
+        core = member % 2
+        side = member // 2
+        blocks = partial.reshape(time_count, count_slabs, 2, 2, rows, count_ev)
+        keep = lax.dynamic_index_in_dim(blocks, core, 3, keepdims=False).astype(jnp.float32)
+        send = lax.dynamic_index_in_dim(blocks, 1 - core, 3, keepdims=False)
+        chip_sum = keep + swapped(send, "member", 0).astype(jnp.float32)
+        keep = lax.dynamic_index_in_dim(chip_sum, side, 2, keepdims=False)
+        send = lax.dynamic_index_in_dim(chip_sum, 1 - side, 2, keepdims=False).astype(jnp.bfloat16)
+        slab_sum = keep + swapped(send, "member", 1).astype(jnp.float32)
         slab_part = slab_sum.astype(jnp.bfloat16)
         total = lax.dynamic_index_in_dim(slab_sum, slab, 1, keepdims=False)
         for shift in range(1, count_slabs):

time: 198 us -> 182 us (0.919)
  waiting for transfers between devices: 113 us -> 95.9 us
  other arithmetic: 11.7 us -> 14.1 us
    ppermute x13 -> x10, waiting for transfers between devices: 113 us -> 66.7 us  [shifted(): return lax.ppermute(block, axis, route)]
    ppermute x1 -> x3, waiting for transfers between devices: 0.01 us -> 29.1 us  [swapped(): lax.ppermute(value, axis, [(i, i ^ 1 << bit) for i in range(lax.axis_size...]
    add x0 -> x1, other arithmetic: none -> 3.3 us  [body(): chip_sum = keep + swapped(send, 'member', 0).astype(jnp.float32)]
    unnamed x16 -> x18, local copies, waits for them, and re-layouts: 2.76 us -> 4.9 us
    squeeze x1, local copies, waits for them, and re-layouts: 3.98 us -> 1.86 us  [body(): send = lax.dynamic_index_in_dim(blocks, 1 - core, 3, keepdims=False)]
    ppermute x13 -> x10, starting transfers between devices: 24.7 us -> 22.8 us  [shifted(): return lax.ppermute(block, axis, route)]
  transfers between devices with their start and end apart: 14 -> 13, of which waited for: 11 -> 10; matrix products, arithmetic and copies ran while one was open for 8% -> 9% of each run, Pallas kernels for 6% -> 6%
where the time goes in v14:
time: 182 us; the launch traced here: 181 us
  waiting for transfers between devices  95.9 us (53%)
  Pallas kernels  25.7 us (14%)
  starting transfers between devices  23.3 us (13%)
  local copies, waits for them, and re-layouts  20.1 us (11%)
  other arithmetic  14.1 us (8%)
    ppermute x10, waiting for transfers between devices, shifted(): return lax.ppermute(block, axis, route)  66.7 us
    ppermute x3, waiting for transfers between devices, swapped(): lax.ppermute(value, axis, [(i, i ^ 1 << bit) for i in range(lax.axis_size...  29.1 us
    ppermute x10, starting transfers between devices, shifted(): return lax.ppermute(block, axis, route)  22.8 us
    pallas_call x1, Pallas kernels, local_sums(): pl.pallas_call(functools.partial(sums_kernel, scale=scale, course_list=ne...  11 us
    pallas_call x1, Pallas kernels, local_sums(): pl.pallas_call(functools.partial(sums_kernel, scale=scale, course_list=(0...  8.08 us
    pallas_call x1, Pallas kernels, contract_panel(): pl.pallas_call(panel_kernel, grid=(count_ops,), in_specs=[pl.BlockSpec((1...  6.64 us
    unnamed x18, local copies, waits for them, and re-layouts  4.9 us
  transfers between devices with their start and end apart: 13, of which 10 were waited for; matrix products, arithmetic and copies ran while one was open for 9% of the time, Pallas kernels for 6%

profile of v14, /device:TPU:0, one launch (start us, length us, event | category | flops | bytes accessed | tf_op | source)
XLA Modules:
  0.0 180.8 jit_solution(13375819090148670031)
XLA Ops:
  0.7 6.1 %collective-permute-start = (bf16[6,2,3,256,128]{4,3,2,1,0:T(8,128)(2,1)}, bf16[6,2,3,256,128]{4,3,2,1,0:T(8,128)(2,1)}, u32[]{:S(2)}, u32[]{:S(2)}) collective-permute-start(bf16[6,2,3,256,128]{4,3,2,1,0:T(8,128)(2,1)} %field_ref.3), channel_id=1, source_target_pairs={{2,0},{3,1},{4,2},{5,3},{6,4},{7,5},{8,6},{9,7},{10,8},{11,9},{12,... | collective-permute-start | bytes 7077896 | tf_op jit(solution)/shard_map/ppermute | solution.py:20
  6.7 2.0 %copy.39 = bf16[6,2,3,256,8]{3,4,2,1,0:T(8,128)(2,1)S(1)} copy(bf16[6,2,3,256,8]{4,3,2,1,0:T(8,128)(2,1)} %bitcast.70) | data formatting | bytes 294912
  14.6 2.3 %pad.6.near_ref = bf16[6,2,3,256,128]{4,3,2,1,0:T(8,128)(2,1)} pad(bf16[6,2,3,256,8]{4,3,2,1,0:T(8,128)(2,1)S(1)} %copy.31, bf16[]{:T(256)} %constant.223.clone.1), padding=0_0x0_0x0_0x0_0x120_0 | pad | bytes 2506754 | tf_op jit(solution)/shard_map/jit(_pad)/pad | solution.py:101
  16.9 11.0 %shard_map.77 = (bf16[6,1536,256]{2,1,0:T(8,128)(2,1)}, bf16[6,512,768]{2,1,0:T(8,128)(2,1)}) custom-call(s32[3]{0:T(128)} %select_reduce_fusion.slot_ref, bf16[6,2,3,256,128]{4,3,2,1,0:T(8,128)(2,1)} %field_ref.3, bf16[6,2,3,256,128]{4,3,2,1,0:T(8,128)(2,1)} %pad.6.near_ref, f32[6,3,2,3,3,128]{5,4,3,2,1,0:T(4,128)} %copy.33.link_ref, ...), custom_call_target="tpu_custom_call" | custom-call | tf_op jit(solution)/shard_map/pallas_call | solution.py:116
  27.9 29.7 %collective-permute-done.near_ref = bf16[6,2,3,256,128]{4,3,2,1,0:T(8,128)(2,1)} collective-permute-done((bf16[6,2,3,256,128]{4,3,2,1,0:T(8,128)(2,1)}, bf16[6,2,3,256,128]{4,3,2,1,0:T(8,128)(2,1)}, u32[]{:S(2)}, u32[]{:S(2)}) %collective-permute-start) | collective-permute-done | bytes 2359328 | tf_op jit(solution)/shard_map/ppermute | solution.py:20
  57.6 8.1 %shard_map.78 = bf16[6,1536,256]{2,1,0:T(8,128)(2,1)} custom-call(s32[3]{0:T(128)} %select_reduce_fusion.slot_ref, bf16[6,2,3,256,128]{4,3,2,1,0:T(8,128)(2,1)} %field_ref.3, bf16[6,2,3,256,128]{4,3,2,1,0:T(8,128)(2,1)} %collective-permute-done.near_ref, f32[6,3,2,3,3,128]{5,4,3,2,1,0:T(4,128)} %copy.33.link_ref, ...), custom_call_target="tpu_custom_call", output_to_operand_aliasing={{}: (5, {})} | custom-call | tf_op jit(solution)/shard_map/pallas_call | solution.py:130
  65.6 1.9 %dynamic-slice_bitcast_fusion = bf16[6,4,2,96,256]{4,3,2,1,0:T(8,128)(2,1)S(1)} fusion(bf16[6,4,2,2,96,256]{5,4,3,2,1,0:T(8,128)(2,1)} %bitcast.71, s32[]{:T(128)S(6)} %select_n.277), kind=kLoop, calls=%fused_computation.8 | loop fusion | bytes 4718596 | tf_op jit(solution)/shard_map/jit(dynamic_index_in_dim)/squeeze | solution.py:218
  69.0 3.3 %collective-permute-done.2 = bf16[6,4,2,96,256]{4,3,2,1,0:T(8,128)(2,1)} collective-permute-done((bf16[6,4,2,96,256]{4,3,2,1,0:T(8,128)(2,1)S(1)}, bf16[6,4,2,96,256]{4,3,2,1,0:T(8,128)(2,1)}, u32[]{:S(2)}, u32[]{:S(2)}) %collective-permute-start.2) | collective-permute-done | bytes 2359328 | tf_op jit(solution)/shard_map/ppermute | solution.py:24
  72.2 3.3 %convert_add_fusion = f32[6,4,2,96,256]{4,3,2,1,0:T(8,128)S(1)} fusion(bf16[6,4,2,96,256]{4,3,2,1,0:T(8,128)(2,1)} %collective-permute-done.2, bf16[6,4,2,2,96,256]{5,4,3,2,1,0:T(8,128)(2,1)} %bitcast.72, s32[]{:T(128)S(6)} %select_n.276), kind=kLoop, calls=%fused_computation.5 | loop fusion | flops 3538944 | bytes 9437188 | tf_op jit(solution)/shard_map/add | solution.py:219
  75.6 2.1 %copy-done.1 = f32[6,4,2,96,256]{4,3,2,1,0:T(8,128)} copy-done((f32[6,4,2,96,256]{4,3,2,1,0:T(8,128)}, f32[6,4,2,96,256]{4,3,2,1,0:T(8,128)S(1)}, u32[]{:S(2)}) %copy-start.1) | copy-done | bytes 4718616
  81.4 25.8 %collective-permute-done.3 = bf16[6,4,96,256]{3,2,1,0:T(8,128)(2,1)} collective-permute-done((bf16[6,4,96,256]{3,2,1,0:T(8,128)(2,1)}, bf16[6,4,96,256]{3,2,1,0:T(8,128)(2,1)}, u32[]{:S(2)}, u32[]{:S(2)}) %collective-permute-start.3) | collective-permute-done | bytes 1179680 | tf_op jit(solution)/shard_map/ppermute | solution.py:24
  107.2 2.4 %fusion.23 = (bf16[6,4,96,256]{3,2,1,0:T(8,128)(2,1)S(1)}, f32[6,4,96,256]{3,2,1,0:T(8,128)S(1)}) fusion(bf16[6,4,96,256]{3,2,1,0:T(8,128)(2,1)} %collective-permute-done.3, f32[6,4,2,96,256]{4,3,2,1,0:T(8,128)} %copy-done.1, s32[]{:T(128)S(6)} %select_n.279), kind=kLoop, calls=%fused_computation.89 | loop fusion | flops 1769472 | bytes 7077892 | tf_op jit(solution)/shard_map/convert_element_type | solution.py:223
  110.8 4.4 %collective-permute-start.5 = (bf16[6,96,256]{2,1,0:T(8,128)(2,1)}, bf16[6,96,256]{2,1,0:T(8,128)(2,1)}, u32[]{:S(2)}, u32[]{:S(2)}) collective-permute-start(bf16[6,96,256]{2,1,0:T(8,128)(2,1)} %get-tuple-element.24), channel_id=1, source_target_pairs={{8,0},{12,4},{0,8},{4,12},{9,1},{13,5},{1,9},{5,13},{10,2},{14,6},... | collective-permute-start | bytes 884744 | tf_op jit(solution)/shard_map/ppermute | solution.py:20
  115.3 2.7 %maximum_maximum_fusion.wide_ref = bf16[2048,512]{1,0:T(8,128)(2,1)} fusion(bf16[1024,256]{1,0:T(8,128)(2,1)} %bitcast.78, bf16[1024,256]{1,0:T(8,128)(2,1)S(1)} %bitcast.75, bf16[1024,256]{1,0:T(8,128)(2,1)S(1)} %bitcast_negate_fusion), kind=kLoop, calls=%fused_computation.9 | loop fusion | flops 8388608 | bytes 3670016 | tf_op jit(solution)/shard_map/concatenate | solution.py:170
  118.1 4.9 %collective-permute-done.4 = bf16[6,96,256]{2,1,0:T(8,128)(2,1)} collective-permute-done((bf16[6,96,256]{2,1,0:T(8,128)(2,1)}, bf16[6,96,256]{2,1,0:T(8,128)(2,1)}, u32[]{:S(2)}, u32[]{:S(2)}) %collective-permute-start.4) | collective-permute-done | bytes 294944 | tf_op jit(solution)/shard_map/ppermute | solution.py:20
  122.9 11.6 %collective-permute-done.5 = bf16[6,96,256]{2,1,0:T(8,128)(2,1)} collective-permute-done((bf16[6,96,256]{2,1,0:T(8,128)(2,1)}, bf16[6,96,256]{2,1,0:T(8,128)(2,1)}, u32[]{:S(2)}, u32[]{:S(2)}) %collective-permute-start.5) | collective-permute-done | bytes 294944 | tf_op jit(solution)/shard_map/ppermute | solution.py:20
  136.6 6.8 %collective-permute-start.7 = (bf16[2,96,256]{2,1,0:T(8,128)(2,1)S(1)}, bf16[2,96,256]{2,1,0:T(8,128)(2,1)S(1)}, u32[]{:S(2)}, u32[]{:S(2)}) collective-permute-start(bf16[2,96,256]{2,1,0:T(8,128)(2,1)S(1)} %get-tuple-element.30), channel_id=1, source_target_pairs={{12,0},{0,4},{4,8},{8,12},{13,1},{1,5},{5,9},{9,13},{14,2},{2,6},{... | collective-permute-start | bytes 294920 | tf_op jit(solution)/shard_map/ppermute | solution.py:20
  143.4 2.4 %collective-permute-start.9 = (bf16[2,96,256]{2,1,0:T(8,128)(2,1)S(1)}, bf16[2,96,256]{2,1,0:T(8,128)(2,1)S(1)}, u32[]{:S(2)}, u32[]{:S(2)}) collective-permute-start(bf16[2,96,256]{2,1,0:T(8,128)(2,1)S(1)} %get-tuple-element.28), channel_id=1, source_target_pairs={{4,0},{8,4},{12,8},{0,12},{5,1},{9,5},{13,9},{1,13},{6,2},{10,6},{... | collective-permute-start | bytes 294920 | tf_op jit(solution)/shard_map/ppermute | solution.py:20
  146.6 4.2 %collective-permute-done.8 = bf16[2,96,256]{2,1,0:T(8,128)(2,1)S(1)} collective-permute-done((bf16[2,96,256]{2,1,0:T(8,128)(2,1)S(1)}, bf16[2,96,256]{2,1,0:T(8,128)(2,1)S(1)}, u32[]{:S(2)}, u32[]{:S(2)}) %collective-permute-start.8) | collective-permute-done | bytes 98336 | tf_op jit(solution)/shard_map/ppermute | solution.py:20
  151.6 1.5 collective-permute-start.11
  153.1 1.4 collective-permute-start.12
  154.6 7.8 %collective-permute-done.10 = bf16[4,2,96,256]{3,2,1,0:T(8,128)(2,1)S(1)} collective-permute-done((bf16[4,2,96,256]{3,2,1,0:T(8,128)(2,1)S(1)}, bf16[4,2,96,256]{3,2,1,0:T(8,128)(2,1)S(1)}, u32[]{:S(2)}, u32[]{:S(2)}) %collective-permute-start.10) | collective-permute-done | bytes 393248 | tf_op jit(solution)/shard_map/ppermute | solution.py:20
  163.6 6.8 %collective-permute-done.12 = bf16[4,2,96,256]{3,2,1,0:T(8,128)(2,1)S(1)} collective-permute-done((bf16[4,2,96,256]{3,2,1,0:T(8,128)(2,1)S(1)}, bf16[4,2,96,256]{3,2,1,0:T(8,128)(2,1)S(1)}, u32[]{:S(2)}, u32[]{:S(2)}) %collective-permute-start.12) | collective-permute-done | bytes 393248 | tf_op jit(solution)/shard_map/ppermute | solution.py:20
  172.7 6.6 %shard_map.79 = f32[3,2,256]{2,1,0:T(2,128)} custom-call(bf16[2,3,2,256,256]{4,3,2,1,0:T(8,128)(2,1)} %bitcast.73, bf16[2,3,2,256,256]{4,3,2,1,0:T(8,128)(2,1)} %bitcast.74, bf16[512,1024]{1,0:T(8,128)(2,1)} %bitcast.76, bf16[2048,512]{1,0:T(8,128)(2,1)} %maximum_maximum_fusion.wide_ref), custom_call_target="tpu_custom_call" | custom-call | tf_op jit(solution)/shard_map/pallas_call | solution.py:177
  (70 shorter events, 20.1 us)
Async XLA Ops:
  0.6 67.0 %copy-start = (s32[4,2]{0,1:T(2,128)S(1)}, s32[4,2]{0,1:T(2,128)}, u32[]{:S(2)}) copy-start(s32[4,2]{0,1:T(2,128)} %param.13) | copy-start | bytes 100
  0.6 8.2 %copy-start.6 = (s32[1,3]{1,0:T(1,128)S(1)}, s32[1,3]{1,0:T(1,128)}, u32[]{:S(2)}) copy-start(s32[1,3]{1,0:T(1,128)} %param.12) | copy-start | bytes 40
  0.7 11.4 %copy-start.4 = (f32[6,3,2,3,3,128]{5,2,4,3,1,0:T(2,128)S(1)}, f32[6,3,2,3,3,128]{5,2,4,3,1,0:T(2,128)}, u32[]{:S(2)}) copy-start(f32[6,3,2,3,3,128]{5,2,4,3,1,0:T(2,128)} %param.9) | copy-start | bytes 497668
  0.7 12.2 %copy-start.7 = (s32[3]{0:T(128)S(1)}, s32[3]{0:T(128)}, u32[]{:S(2)}) copy-start(s32[3]{0:T(128)} %param.11) | copy-start | bytes 40
  0.7 56.9 %collective-permute-start = (bf16[6,2,3,256,128]{4,3,2,1,0:T(8,128)(2,1)}, bf16[6,2,3,256,128]{4,3,2,1,0:T(8,128)(2,1)}, u32[]{:S(2)}, u32[]{:S(2)}) collective-permute-start(bf16[6,2,3,256,128]{4,3,2,1,0:T(8,128)(2,1)} %field_ref.3), channel_id=1, source_target_pairs={{2,0},{3,1},{4,2},{5,3},{6,4},{7,5},{8,6},{9,7},{10,8},{11,9},{12,... | collective-permute-start | bytes 7077896 | tf_op jit(solution)/shard_map/ppermute | solution.py:20
  8.7 4.8 %collective-permute-start.1 = (bf16[6,2,3,256,8]{3,4,2,1,0:T(8,128)(2,1)S(1)}, bf16[6,2,3,256,8]{3,4,2,1,0:T(8,128)(2,1)S(1)}, u32[]{:S(2)}, u32[]{:S(2)}) collective-permute-start(bf16[6,2,3,256,8]{3,4,2,1,0:T(8,128)(2,1)S(1)} %copy.39), channel_id=1, source_target_pairs={{0,1},{1,0},{2,3},{3,2},{4,5},{5,4},{6,7},{7,6},{8,9},{9,8},{10,11... | collective-permute-start | bytes 442376 | tf_op jit(solution)/shard_map/ppermute | solution.py:24
  65.6 2.7 %copy-start.5 = (s32[4]{0:T(128)S(1)}, s32[4]{0:T(128)}, u32[]{:S(2)}) copy-start(s32[4]{0:T(128)} %constant.309) | copy-start | bytes 52
  67.5 4.7 %collective-permute-start.2 = (bf16[6,4,2,96,256]{4,3,2,1,0:T(8,128)(2,1)S(1)}, bf16[6,4,2,96,256]{4,3,2,1,0:T(8,128)(2,1)}, u32[]{:S(2)}, u32[]{:S(2)}) collective-permute-start(bf16[6,4,2,96,256]{4,3,2,1,0:T(8,128)(2,1)S(1)} %dynamic-slice_bitcast_fusion), channel_id=1, source_target_pairs={{0,1},{1,0},{2,3},{3,2},{4,5},{5,4},{6,7},{7,6},{8,9},{9,8},{10,11... | collective-permute-start | bytes 7077896 | tf_op jit(solution)/shard_map/ppermute | solution.py:24
  75.5 2.1 %copy-start.1 = (f32[6,4,2,96,256]{4,3,2,1,0:T(8,128)}, f32[6,4,2,96,256]{4,3,2,1,0:T(8,128)S(1)}, u32[]{:S(2)}) copy-start(f32[6,4,2,96,256]{4,3,2,1,0:T(8,128)S(1)} %convert_add_fusion) | copy-start | bytes 14155780
  77.7 1.7 copy-start.2
  78.9 28.3 %collective-permute-start.3 = (bf16[6,4,96,256]{3,2,1,0:T(8,128)(2,1)}, bf16[6,4,96,256]{3,2,1,0:T(8,128)(2,1)}, u32[]{:S(2)}, u32[]{:S(2)}) collective-permute-start(bf16[6,4,96,256]{3,2,1,0:T(8,128)(2,1)} %fusion), channel_id=1, source_target_pairs={{0,2},{1,3},{2,0},{3,1},{4,6},{5,7},{6,4},{7,5},{8,10},{9,11},{10,... | collective-permute-start | bytes 3538952 | tf_op jit(solution)/shard_map/ppermute | solution.py:24
  110.6 12.3 %collective-permute-start.4 = (bf16[6,96,256]{2,1,0:T(8,128)(2,1)}, bf16[6,96,256]{2,1,0:T(8,128)(2,1)}, u32[]{:S(2)}, u32[]{:S(2)}) collective-permute-start(bf16[6,96,256]{2,1,0:T(8,128)(2,1)} %get-tuple-element.22), channel_id=1, source_target_pairs={{12,0},{0,4},{4,8},{8,12},{13,1},{1,5},{5,9},{9,13},{14,2},{2,6},{... | collective-permute-start | bytes 884744 | tf_op jit(solution)/shard_map/ppermute | solution.py:20
  110.8 23.7 %collective-permute-start.5 = (bf16[6,96,256]{2,1,0:T(8,128)(2,1)}, bf16[6,96,256]{2,1,0:T(8,128)(2,1)}, u32[]{:S(2)}, u32[]{:S(2)}) collective-permute-start(bf16[6,96,256]{2,1,0:T(8,128)(2,1)} %get-tuple-element.24), channel_id=1, source_target_pairs={{8,0},{12,4},{0,8},{4,12},{9,1},{13,5},{1,9},{5,13},{10,2},{14,6},... | collective-permute-start | bytes 884744 | tf_op jit(solution)/shard_map/ppermute | solution.py:20
  115.2 19.3 %collective-permute-start.6 = (bf16[6,96,256]{2,1,0:T(8,128)(2,1)}, bf16[6,96,256]{2,1,0:T(8,128)(2,1)}, u32[]{:S(2)}, u32[]{:S(2)}) collective-permute-start(bf16[6,96,256]{2,1,0:T(8,128)(2,1)} %get-tuple-element.23), channel_id=1, source_target_pairs={{4,0},{8,4},{12,8},{0,12},{5,1},{9,5},{13,9},{1,13},{6,2},{10,6},{... | collective-permute-start | bytes 884744 | tf_op jit(solution)/shard_map/ppermute | solution.py:20
  135.8 15.7 %copy-start.3 = (bf16[6,96,256]{2,1,0:T(8,128)(2,1)}, bf16[6,96,256]{2,1,0:T(8,128)(2,1)S(1)}, u32[]{:S(2)}) copy-start(bf16[6,96,256]{2,1,0:T(8,128)(2,1)S(1)} %fusion.3) | copy-start | bytes 884740
  136.6 10.0 %collective-permute-start.7 = (bf16[2,96,256]{2,1,0:T(8,128)(2,1)S(1)}, bf16[2,96,256]{2,1,0:T(8,128)(2,1)S(1)}, u32[]{:S(2)}, u32[]{:S(2)}) collective-permute-start(bf16[2,96,256]{2,1,0:T(8,128)(2,1)S(1)} %get-tuple-element.30), channel_id=1, source_target_pairs={{12,0},{0,4},{4,8},{8,12},{13,1},{1,5},{5,9},{9,13},{14,2},{2,6},{... | collective-permute-start | bytes 294920 | tf_op jit(solution)/shard_map/ppermute | solution.py:20
  143.4 7.3 %collective-permute-start.8 = (bf16[2,96,256]{2,1,0:T(8,128)(2,1)S(1)}, bf16[2,96,256]{2,1,0:T(8,128)(2,1)S(1)}, u32[]{:S(2)}, u32[]{:S(2)}) collective-permute-start(bf16[2,96,256]{2,1,0:T(8,128)(2,1)S(1)} %get-tuple-element.29), channel_id=1, source_target_pairs={{8,0},{12,4},{0,8},{4,12},{9,1},{13,5},{1,9},{5,13},{10,2},{14,6},... | collective-permute-start | bytes 294920 | tf_op jit(solution)/shard_map/ppermute | solution.py:20
  143.4 7.3 %collective-permute-start.9 = (bf16[2,96,256]{2,1,0:T(8,128)(2,1)S(1)}, bf16[2,96,256]{2,1,0:T(8,128)(2,1)S(1)}, u32[]{:S(2)}, u32[]{:S(2)}) collective-permute-start(bf16[2,96,256]{2,1,0:T(8,128)(2,1)S(1)} %get-tuple-element.28), channel_id=1, source_target_pairs={{4,0},{8,4},{12,8},{0,12},{5,1},{9,5},{13,9},{1,13},{6,2},{10,6},{... | collective-permute-start | bytes 294920 | tf_op jit(solution)/shard_map/ppermute | solution.py:20
  151.5 10.9 %collective-permute-start.10 = (bf16[4,2,96,256]{3,2,1,0:T(8,128)(2,1)S(1)}, bf16[4,2,96,256]{3,2,1,0:T(8,128)(2,1)S(1)}, u32[]{:S(2)}, u32[]{:S(2)}) collective-permute-start(bf16[4,2,96,256]{3,2,1,0:T(8,128)(2,1)S(1)} %broadcast_select_fusion), channel_id=1, source_target_pairs={{3,0},{0,1},{1,2},{2,3},{7,4},{4,5},{5,6},{6,7},{11,8},{8,9},{9,10... | collective-permute-start | bytes 1179656 | tf_op jit(solution)/shard_map/ppermute | solution.py:20
  151.6 12.0 %collective-permute-start.11 = (bf16[4,2,96,256]{3,2,1,0:T(8,128)(2,1)S(1)}, bf16[4,2,96,256]{3,2,1,0:T(8,128)(2,1)S(1)}, u32[]{:S(2)}, u32[]{:S(2)}) collective-permute-start(bf16[4,2,96,256]{3,2,1,0:T(8,128)(2,1)S(1)} %broadcast_select_fusion), channel_id=1, source_target_pairs={{2,0},{3,1},{0,2},{1,3},{6,4},{7,5},{4,6},{5,7},{10,8},{11,9},{8,1... | collective-permute-start | bytes 1179656 | tf_op jit(solution)/shard_map/ppermute | solution.py:20
  153.1 17.3 %collective-permute-start.12 = (bf16[4,2,96,256]{3,2,1,0:T(8,128)(2,1)S(1)}, bf16[4,2,96,256]{3,2,1,0:T(8,128)(2,1)S(1)}, u32[]{:S(2)}, u32[]{:S(2)}) collective-permute-start(bf16[4,2,96,256]{3,2,1,0:T(8,128)(2,1)S(1)} %broadcast_select_fusion), channel_id=1, source_target_pairs={{1,0},{2,1},{3,2},{0,3},{5,4},{6,5},{7,6},{4,7},{9,8},{10,9},{11,1... | collective-permute-start | bytes 1179656 | tf_op jit(solution)/shard_map/ppermute | solution.py:20

commit v15 on v14

--- a/solution.py
+++ b/solution.py
@@ -217,15 +217,21 @@
         keep = lax.dynamic_index_in_dim(blocks, core, 3, keepdims=False).astype(jnp.float32)
         send = lax.dynamic_index_in_dim(blocks, 1 - core, 3, keepdims=False)
         chip_sum = keep + swapped(send, "member", 0).astype(jnp.float32)
-        keep = lax.dynamic_index_in_dim(chip_sum, side, 2, keepdims=False)
-        send = lax.dynamic_index_in_dim(chip_sum, 1 - side, 2, keepdims=False).astype(jnp.bfloat16)
-        slab_sum = keep + swapped(send, "member", 1).astype(jnp.float32)
-        slab_part = slab_sum.astype(jnp.bfloat16)
-        total = lax.dynamic_index_in_dim(slab_sum, slab, 1, keepdims=False)
-        for shift in range(1, count_slabs):
-            piece = lax.dynamic_index_in_dim(slab_part, (slab + shift) % count_slabs, 1, keepdims=False)
-            total = total + shifted(piece, "slab", shift).astype(jnp.float32)
-        own_rows = total.astype(jnp.bfloat16)
+        halves = 2 if time_count % 2 == 0 else 1
+        span = time_count // halves
+        own_parts = []
+        for half in range(halves):
+            chunk = chip_sum[half * span : (half + 1) * span]
+            keep = lax.dynamic_index_in_dim(chunk, side, 2, keepdims=False)
+            send = lax.dynamic_index_in_dim(chunk, 1 - side, 2, keepdims=False).astype(jnp.bfloat16)
+            slab_sum = keep + swapped(send, "member", 1).astype(jnp.float32)
+            slab_part = slab_sum.astype(jnp.bfloat16)
+            total = lax.dynamic_index_in_dim(slab_sum, slab, 1, keepdims=False)
+            for shift in range(1, count_slabs):
+                piece = lax.dynamic_index_in_dim(slab_part, (slab + shift) % count_slabs, 1, keepdims=False)
+                total = total + shifted(piece, "slab", shift).astype(jnp.float32)
+            own_parts.append(total.astype(jnp.bfloat16))
+        own_rows = jnp.concatenate(own_parts, 0)
     else:
         own_rows = lax.psum_scatter(partial, SPACE, scatter_dimension=1, tiled=True)
     slabs = jnp.arange(count_slabs, dtype=jnp.int32)

time: 182 us -> 166 us (0.912)
  waiting for transfers between devices: 95.9 us -> 86.6 us
  other arithmetic: 14.1 us -> 9.68 us
  local copies, waits for them, and re-layouts: 20.1 us -> 17.3 us
    ppermute x3 -> x4, waiting for transfers between devices: 29.1 us -> 21.9 us  [swapped(): lax.ppermute(value, axis, [(i, i ^ 1 << bit) for i in range(lax.axis_size...]
    unnamed x18 -> x16, local copies, waits for them, and re-layouts: 4.9 us -> 2.76 us
    convert_element_type x1 -> x2, other arithmetic: 2.44 us -> 0.38 us  [body(): slab_part = slab_sum.astype(jnp.bfloat16)]
    ppermute x10 -> x13, waiting for transfers between devices: 66.7 us -> 64.7 us  [shifted(): return lax.ppermute(block, axis, route)]
    ppermute x10 -> x13, starting transfers between devices: 22.8 us -> 21.8 us  [shifted(): return lax.ppermute(block, axis, route)]
  transfers between devices with their start and end apart: 13 -> 17, of which waited for: 10 -> 12; matrix products, arithmetic and copies ran while one was open for 9% -> 9% of each run, Pallas kernels for 6% -> 7%
where the time goes in v15:
time: 166 us; the launch traced here: 165 us
  waiting for transfers between devices  86.6 us (52%)
  Pallas kernels  25.6 us (15%)
  starting transfers between devices  24.1 us (15%)
  local copies, waits for them, and re-layouts  17.3 us (10%)
  other arithmetic  9.68 us (6%)
  between operations  1.69 us (1%)
    ppermute x13, waiting for transfers between devices, shifted(): return lax.ppermute(block, axis, route)  64.7 us
    ppermute x4, waiting for transfers between devices, swapped(): lax.ppermute(value, axis, [(i, i ^ 1 << bit) for i in range(lax.axis_size...  21.9 us
    ppermute x13, starting transfers between devices, shifted(): return lax.ppermute(block, axis, route)  21.8 us
    pallas_call x1, Pallas kernels, local_sums(): pl.pallas_call(functools.partial(sums_kernel, scale=scale, course_list=ne...  10.9 us
    pallas_call x1, Pallas kernels, local_sums(): pl.pallas_call(functools.partial(sums_kernel, scale=scale, course_list=(0...  8.07 us
    pallas_call x1, Pallas kernels, contract_panel(): pl.pallas_call(panel_kernel, grid=(count_ops,), in_specs=[pl.BlockSpec((1...  6.62 us
    squeeze x1, local copies, waits for them, and re-layouts, body(): send = lax.dynamic_index_in_dim(blocks, 1 - core, 3, keepdims=False)  3.47 us
  transfers between devices with their start and end apart: 17, of which 12 were waited for; matrix products, arithmetic and copies ran while one was open for 9% of the time, Pallas kernels for 7%

profile of v15, /device:TPU:0, one launch (start us, length us, event | category | flops | bytes accessed | tf_op | source)
XLA Modules:
  0.0 165.0 jit_solution(16939362676993276446)
XLA Ops:
  0.7 6.1 %collective-permute-start = (bf16[6,2,3,256,128]{4,3,2,1,0:T(8,128)(2,1)}, bf16[6,2,3,256,128]{4,3,2,1,0:T(8,128)(2,1)}, u32[]{:S(2)}, u32[]{:S(2)}) collective-permute-start(bf16[6,2,3,256,128]{4,3,2,1,0:T(8,128)(2,1)} %field_ref.3), channel_id=1, source_target_pairs={{2,0},{3,1},{4,2},{5,3},{6,4},{7,5},{8,6},{9,7},{10,8},{11,9},{12,... | collective-permute-start | bytes 7077896 | tf_op jit(solution)/shard_map/ppermute | solution.py:20
  6.7 2.0 %copy.39 = bf16[6,2,3,256,8]{3,4,2,1,0:T(8,128)(2,1)S(1)} copy(bf16[6,2,3,256,8]{4,3,2,1,0:T(8,128)(2,1)} %bitcast.89) | data formatting | bytes 294912
  14.5 2.3 %pad.6.near_ref = bf16[6,2,3,256,128]{4,3,2,1,0:T(8,128)(2,1)} pad(bf16[6,2,3,256,8]{4,3,2,1,0:T(8,128)(2,1)S(1)} %copy.31, bf16[]{:T(256)} %constant.241.clone.1), padding=0_0x0_0x0_0x0_0x120_0 | pad | bytes 2506754 | tf_op jit(solution)/shard_map/jit(_pad)/pad | solution.py:101
  16.9 10.9 %shard_map.77 = (bf16[6,1536,256]{2,1,0:T(8,128)(2,1)}, bf16[6,512,768]{2,1,0:T(8,128)(2,1)}) custom-call(s32[3]{0:T(128)} %select_reduce_fusion.slot_ref, bf16[6,2,3,256,128]{4,3,2,1,0:T(8,128)(2,1)} %field_ref.3, bf16[6,2,3,256,128]{4,3,2,1,0:T(8,128)(2,1)} %pad.6.near_ref, f32[6,3,2,3,3,128]{5,4,3,2,1,0:T(4,128)} %copy.33.link_ref, ...), custom_call_target="tpu_custom_call" | custom-call | tf_op jit(solution)/shard_map/pallas_call | solution.py:116
  27.8 29.7 %collective-permute-done.near_ref = bf16[6,2,3,256,128]{4,3,2,1,0:T(8,128)(2,1)} collective-permute-done((bf16[6,2,3,256,128]{4,3,2,1,0:T(8,128)(2,1)}, bf16[6,2,3,256,128]{4,3,2,1,0:T(8,128)(2,1)}, u32[]{:S(2)}, u32[]{:S(2)}) %collective-permute-start) | collective-permute-done | bytes 2359328 | tf_op jit(solution)/shard_map/ppermute | solution.py:20
  57.6 8.1 %shard_map.78 = bf16[6,1536,256]{2,1,0:T(8,128)(2,1)} custom-call(s32[3]{0:T(128)} %select_reduce_fusion.slot_ref, bf16[6,2,3,256,128]{4,3,2,1,0:T(8,128)(2,1)} %field_ref.3, bf16[6,2,3,256,128]{4,3,2,1,0:T(8,128)(2,1)} %collective-permute-done.near_ref, f32[6,3,2,3,3,128]{5,4,3,2,1,0:T(4,128)} %copy.33.link_ref, ...), custom_call_target="tpu_custom_call", output_to_operand_aliasing={{}: (5, {})} | custom-call | tf_op jit(solution)/shard_map/pallas_call | solution.py:130
  65.6 3.5 %dynamic-slice_bitcast_fusion = bf16[6,4,2,96,256]{4,3,2,1,0:T(8,128)(2,1)} fusion(bf16[6,4,2,2,96,256]{5,4,3,2,1,0:T(8,128)(2,1)} %bitcast.90, s32[]{:T(128)S(6)} %select_n.289), kind=kLoop, calls=%fused_computation.6 | loop fusion | bytes 4718596 | tf_op jit(solution)/shard_map/jit(dynamic_index_in_dim)/squeeze | solution.py:218
  71.9 2.1 %collective-permute-done.2 = bf16[6,4,2,96,256]{4,3,2,1,0:T(8,128)(2,1)} collective-permute-done((bf16[6,4,2,96,256]{4,3,2,1,0:T(8,128)(2,1)}, bf16[6,4,2,96,256]{4,3,2,1,0:T(8,128)(2,1)}, u32[]{:S(2)}, u32[]{:S(2)}) %collective-permute-start.2) | collective-permute-done | bytes 2359328 | tf_op jit(solution)/shard_map/ppermute | solution.py:24
  74.0 3.3 %convert_add_fusion = f32[6,4,2,96,256]{4,3,2,1,0:T(8,128)S(1)} fusion(bf16[6,4,2,96,256]{4,3,2,1,0:T(8,128)(2,1)} %collective-permute-done.2, bf16[6,4,2,2,96,256]{5,4,3,2,1,0:T(8,128)(2,1)} %bitcast.91, s32[]{:T(128)S(6)} %select_n.288), kind=kLoop, calls=%fused_computation.5 | loop fusion | flops 3538944 | bytes 9437188 | tf_op jit(solution)/shard_map/add | solution.py:219
  79.9 1.8 %collective-permute-start.7 = (bf16[3,4,96,256]{3,2,1,0:T(8,128)(2,1)S(1)}, bf16[3,4,96,256]{3,2,1,0:T(8,128)(2,1)S(1)}, u32[]{:S(2)}, u32[]{:S(2)}) collective-permute-start(bf16[3,4,96,256]{3,2,1,0:T(8,128)(2,1)S(1)} %fusion.1), channel_id=1, source_target_pairs={{0,2},{1,3},{2,0},{3,1},{4,6},{5,7},{6,4},{7,5},{8,10},{9,11},{10,... | collective-permute-start | bytes 1769480 | tf_op jit(solution)/shard_map/ppermute | solution.py:24
  81.7 12.5 %collective-permute-done.3 = bf16[3,4,96,256]{3,2,1,0:T(8,128)(2,1)S(1)} collective-permute-done((bf16[3,4,96,256]{3,2,1,0:T(8,128)(2,1)S(1)}, bf16[3,4,96,256]{3,2,1,0:T(8,128)(2,1)S(1)}, u32[]{:S(2)}, u32[]{:S(2)}) %collective-permute-start.3) | collective-permute-done | bytes 589856 | tf_op jit(solution)/shard_map/ppermute | solution.py:24
  94.5 4.2 %collective-permute-start.5 = (bf16[3,96,256]{2,1,0:T(8,128)(2,1)S(1)}, bf16[3,96,256]{2,1,0:T(8,128)(2,1)S(1)}, u32[]{:S(2)}, u32[]{:S(2)}) collective-permute-start(bf16[3,96,256]{2,1,0:T(8,128)(2,1)S(1)} %get-tuple-element.30), channel_id=1, source_target_pairs={{8,0},{12,4},{0,8},{4,12},{9,1},{13,5},{1,9},{5,13},{10,2},{14,6},... | collective-permute-start | bytes 442376 | tf_op jit(solution)/shard_map/ppermute | solution.py:20
  98.7 7.3 %collective-permute-done.7 = bf16[3,4,96,256]{3,2,1,0:T(8,128)(2,1)S(1)} collective-permute-done((bf16[3,4,96,256]{3,2,1,0:T(8,128)(2,1)S(1)}, bf16[3,4,96,256]{3,2,1,0:T(8,128)(2,1)S(1)}, u32[]{:S(2)}, u32[]{:S(2)}) %collective-permute-start.7) | collective-permute-done | bytes 589856 | tf_op jit(solution)/shard_map/ppermute | solution.py:24
  106.2 4.1 %collective-permute-start.10 = (bf16[3,96,256]{2,1,0:T(8,128)(2,1)S(1)}, bf16[3,96,256]{2,1,0:T(8,128)(2,1)S(1)}, u32[]{:S(2)}, u32[]{:S(2)}) collective-permute-start(bf16[3,96,256]{2,1,0:T(8,128)(2,1)S(1)} %get-tuple-element.32), channel_id=1, source_target_pairs={{4,0},{8,4},{12,8},{0,12},{5,1},{9,5},{13,9},{1,13},{6,2},{10,6},{... | collective-permute-start | bytes 442376 | tf_op jit(solution)/shard_map/ppermute | solution.py:20
  111.0 3.6 %collective-permute-done.10 = bf16[3,96,256]{2,1,0:T(8,128)(2,1)S(1)} collective-permute-done((bf16[3,96,256]{2,1,0:T(8,128)(2,1)S(1)}, bf16[3,96,256]{2,1,0:T(8,128)(2,1)S(1)}, u32[]{:S(2)}, u32[]{:S(2)}) %collective-permute-start.10) | collective-permute-done | bytes 147488 | tf_op jit(solution)/shard_map/ppermute | solution.py:20
  114.6 4.3 %collective-permute-done.8 = bf16[3,96,256]{2,1,0:T(8,128)(2,1)S(1)} collective-permute-done((bf16[3,96,256]{2,1,0:T(8,128)(2,1)S(1)}, bf16[3,96,256]{2,1,0:T(8,128)(2,1)S(1)}, u32[]{:S(2)}, u32[]{:S(2)}) %collective-permute-start.8) | collective-permute-done | bytes 147488 | tf_op jit(solution)/shard_map/ppermute | solution.py:20
  118.9 4.5 %collective-permute-done.9 = bf16[3,96,256]{2,1,0:T(8,128)(2,1)S(1)} collective-permute-done((bf16[3,96,256]{2,1,0:T(8,128)(2,1)S(1)}, bf16[3,96,256]{2,1,0:T(8,128)(2,1)S(1)}, u32[]{:S(2)}, u32[]{:S(2)}) %collective-permute-start.9) | collective-permute-done | bytes 147488 | tf_op jit(solution)/shard_map/ppermute | solution.py:20
  125.6 2.6 %collective-permute-start.13 = (bf16[2,96,256]{2,1,0:T(8,128)(2,1)S(1)}, bf16[2,96,256]{2,1,0:T(8,128)(2,1)S(1)}, u32[]{:S(2)}, u32[]{:S(2)}) collective-permute-start(bf16[2,96,256]{2,1,0:T(8,128)(2,1)S(1)} %get-tuple-element.35), channel_id=1, source_target_pairs={{4,0},{8,4},{12,8},{0,12},{5,1},{9,5},{13,9},{1,13},{6,2},{10,6},{... | collective-permute-start | bytes 294920 | tf_op jit(solution)/shard_map/ppermute | solution.py:20
  128.2 3.7 %collective-permute-done.11 = bf16[2,96,256]{2,1,0:T(8,128)(2,1)S(1)} collective-permute-done((bf16[2,96,256]{2,1,0:T(8,128)(2,1)S(1)}, bf16[2,96,256]{2,1,0:T(8,128)(2,1)S(1)}, u32[]{:S(2)}, u32[]{:S(2)}) %collective-permute-start.11) | collective-permute-done | bytes 98336 | tf_op jit(solution)/shard_map/ppermute | solution.py:20
  131.8 3.2 %collective-permute-done.12 = bf16[2,96,256]{2,1,0:T(8,128)(2,1)S(1)} collective-permute-done((bf16[2,96,256]{2,1,0:T(8,128)(2,1)S(1)}, bf16[2,96,256]{2,1,0:T(8,128)(2,1)S(1)}, u32[]{:S(2)}, u32[]{:S(2)}) %collective-permute-start.12) | collective-permute-done | bytes 98336 | tf_op jit(solution)/shard_map/ppermute | solution.py:20
  135.8 1.5 collective-permute-start.15
  138.9 7.8 %collective-permute-done.14 = bf16[4,2,96,256]{3,2,1,0:T(8,128)(2,1)S(1)} collective-permute-done((bf16[4,2,96,256]{3,2,1,0:T(8,128)(2,1)S(1)}, bf16[4,2,96,256]{3,2,1,0:T(8,128)(2,1)S(1)}, u32[]{:S(2)}, u32[]{:S(2)}) %collective-permute-start.14) | collective-permute-done | bytes 393248 | tf_op jit(solution)/shard_map/ppermute | solution.py:20
  147.8 6.8 %collective-permute-done.16 = bf16[4,2,96,256]{3,2,1,0:T(8,128)(2,1)S(1)} collective-permute-done((bf16[4,2,96,256]{3,2,1,0:T(8,128)(2,1)S(1)}, bf16[4,2,96,256]{3,2,1,0:T(8,128)(2,1)S(1)}, u32[]{:S(2)}, u32[]{:S(2)}) %collective-permute-start.16) | collective-permute-done | bytes 393248 | tf_op jit(solution)/shard_map/ppermute | solution.py:20
  157.0 6.6 %shard_map.79 = f32[3,2,256]{2,1,0:T(2,128)} custom-call(bf16[2,3,2,256,256]{4,3,2,1,0:T(8,128)(2,1)} %bitcast.92, bf16[2,3,2,256,256]{4,3,2,1,0:T(8,128)(2,1)} %bitcast.93, bf16[512,1024]{1,0:T(8,128)(2,1)} %bitcast.95, bf16[2048,512]{1,0:T(8,128)(2,1)} %maximum_maximum_fusion.wide_ref), custom_call_target="tpu_custom_call" | custom-call | tf_op jit(solution)/shard_map/pallas_call | solution.py:177
  (82 shorter events, 21.1 us)
Async XLA Ops:
  0.6 68.5 %copy-start = (s32[4,2]{0,1:T(2,128)S(1)}, s32[4,2]{0,1:T(2,128)}, u32[]{:S(2)}) copy-start(s32[4,2]{0,1:T(2,128)} %param.13) | copy-start | bytes 100
  0.6 8.2 %copy-start.5 = (s32[1,3]{1,0:T(1,128)S(1)}, s32[1,3]{1,0:T(1,128)}, u32[]{:S(2)}) copy-start(s32[1,3]{1,0:T(1,128)} %param.12) | copy-start | bytes 40
  0.7 11.4 %copy-start.3 = (f32[6,3,2,3,3,128]{5,2,4,3,1,0:T(2,128)S(1)}, f32[6,3,2,3,3,128]{5,2,4,3,1,0:T(2,128)}, u32[]{:S(2)}) copy-start(f32[6,3,2,3,3,128]{5,2,4,3,1,0:T(2,128)} %param.9) | copy-start | bytes 497668
  0.7 12.1 %copy-start.6 = (s32[3]{0:T(128)S(1)}, s32[3]{0:T(128)}, u32[]{:S(2)}) copy-start(s32[3]{0:T(128)} %param.11) | copy-start | bytes 40
  0.7 56.9 %collective-permute-start = (bf16[6,2,3,256,128]{4,3,2,1,0:T(8,128)(2,1)}, bf16[6,2,3,256,128]{4,3,2,1,0:T(8,128)(2,1)}, u32[]{:S(2)}, u32[]{:S(2)}) collective-permute-start(bf16[6,2,3,256,128]{4,3,2,1,0:T(8,128)(2,1)} %field_ref.3), channel_id=1, source_target_pairs={{2,0},{3,1},{4,2},{5,3},{6,4},{7,5},{8,6},{9,7},{10,8},{11,9},{12,... | collective-permute-start | bytes 7077896 | tf_op jit(solution)/shard_map/ppermute | solution.py:20
  8.7 4.7 %collective-permute-start.1 = (bf16[6,2,3,256,8]{3,4,2,1,0:T(8,128)(2,1)S(1)}, bf16[6,2,3,256,8]{3,4,2,1,0:T(8,128)(2,1)S(1)}, u32[]{:S(2)}, u32[]{:S(2)}) collective-permute-start(bf16[6,2,3,256,8]{3,4,2,1,0:T(8,128)(2,1)S(1)} %copy.39), channel_id=1, source_target_pairs={{0,1},{1,0},{2,3},{3,2},{4,5},{5,4},{6,7},{7,6},{8,9},{9,8},{10,11... | collective-permute-start | bytes 442376 | tf_op jit(solution)/shard_map/ppermute | solution.py:24
  65.6 4.1 %copy-start.4 = (s32[4]{0:T(128)S(1)}, s32[4]{0:T(128)}, u32[]{:S(2)}) copy-start(s32[4]{0:T(128)} %constant.327) | copy-start | bytes 52
  65.6 5.1 %copy-start.1 = (bf16[1,2,256,1024]{3,2,1,0:T(8,128)(2,1)S(1)}, bf16[1,2,256,1024]{3,2,1,0:T(8,128)(2,1)}, u32[]{:S(2)}) copy-start(bf16[1,2,256,1024]{3,2,1,0:T(8,128)(2,1)} %param.10) | copy-start | bytes 3145732
  69.1 4.9 %collective-permute-start.2 = (bf16[6,4,2,96,256]{4,3,2,1,0:T(8,128)(2,1)}, bf16[6,4,2,96,256]{4,3,2,1,0:T(8,128)(2,1)}, u32[]{:S(2)}, u32[]{:S(2)}) collective-permute-start(bf16[6,4,2,96,256]{4,3,2,1,0:T(8,128)(2,1)} %dynamic-slice_bitcast_fusion), channel_id=1, source_target_pairs={{0,1},{1,0},{2,3},{3,2},{4,5},{5,4},{6,7},{7,6},{8,9},{9,8},{10,11... | collective-permute-start | bytes 7077896 | tf_op jit(solution)/shard_map/ppermute | solution.py:24
  77.9 16.2 %collective-permute-start.3 = (bf16[3,4,96,256]{3,2,1,0:T(8,128)(2,1)S(1)}, bf16[3,4,96,256]{3,2,1,0:T(8,128)(2,1)S(1)}, u32[]{:S(2)}, u32[]{:S(2)}) collective-permute-start(bf16[3,4,96,256]{3,2,1,0:T(8,128)(2,1)S(1)} %fusion), channel_id=1, source_target_pairs={{0,2},{1,3},{2,0},{3,1},{4,6},{5,7},{6,4},{7,5},{8,10},{9,11},{10,... | collective-permute-start | bytes 1769480 | tf_op jit(solution)/shard_map/ppermute | solution.py:24
  79.9 26.1 %collective-permute-start.7 = (bf16[3,4,96,256]{3,2,1,0:T(8,128)(2,1)S(1)}, bf16[3,4,96,256]{3,2,1,0:T(8,128)(2,1)S(1)}, u32[]{:S(2)}, u32[]{:S(2)}) collective-permute-start(bf16[3,4,96,256]{3,2,1,0:T(8,128)(2,1)S(1)} %fusion.1), channel_id=1, source_target_pairs={{0,2},{1,3},{2,0},{3,1},{4,6},{5,7},{6,4},{7,5},{8,10},{9,11},{10,... | collective-permute-start | bytes 1769480 | tf_op jit(solution)/shard_map/ppermute | solution.py:24
  94.4 15.9 %collective-permute-start.4 = (bf16[3,96,256]{2,1,0:T(8,128)(2,1)S(1)}, bf16[3,96,256]{2,1,0:T(8,128)(2,1)S(1)}, u32[]{:S(2)}, u32[]{:S(2)}) collective-permute-start(bf16[3,96,256]{2,1,0:T(8,128)(2,1)S(1)} %get-tuple-element.28), channel_id=1, source_target_pairs={{12,0},{0,4},{4,8},{8,12},{13,1},{1,5},{5,9},{9,13},{14,2},{2,6},{... | collective-permute-start | bytes 442376 | tf_op jit(solution)/shard_map/ppermute | solution.py:20
  94.5 16.5 %collective-permute-start.5 = (bf16[3,96,256]{2,1,0:T(8,128)(2,1)S(1)}, bf16[3,96,256]{2,1,0:T(8,128)(2,1)S(1)}, u32[]{:S(2)}, u32[]{:S(2)}) collective-permute-start(bf16[3,96,256]{2,1,0:T(8,128)(2,1)S(1)} %get-tuple-element.30), channel_id=1, source_target_pairs={{8,0},{12,4},{0,8},{4,12},{9,1},{13,5},{1,9},{5,13},{10,2},{14,6},... | collective-permute-start | bytes 442376 | tf_op jit(solution)/shard_map/ppermute | solution.py:20
  98.7 12.2 %collective-permute-start.6 = (bf16[3,96,256]{2,1,0:T(8,128)(2,1)S(1)}, bf16[3,96,256]{2,1,0:T(8,128)(2,1)S(1)}, u32[]{:S(2)}, u32[]{:S(2)}) collective-permute-start(bf16[3,96,256]{2,1,0:T(8,128)(2,1)S(1)} %get-tuple-element.29), channel_id=1, source_target_pairs={{4,0},{8,4},{12,8},{0,12},{5,1},{9,5},{13,9},{1,13},{6,2},{10,6},{... | collective-permute-start | bytes 442376 | tf_op jit(solution)/shard_map/ppermute | solution.py:20
  106.2 8.3 %collective-permute-start.10 = (bf16[3,96,256]{2,1,0:T(8,128)(2,1)S(1)}, bf16[3,96,256]{2,1,0:T(8,128)(2,1)S(1)}, u32[]{:S(2)}, u32[]{:S(2)}) collective-permute-start(bf16[3,96,256]{2,1,0:T(8,128)(2,1)S(1)} %get-tuple-element.32), channel_id=1, source_target_pairs={{4,0},{8,4},{12,8},{0,12},{5,1},{9,5},{13,9},{1,13},{6,2},{10,6},{... | collective-permute-start | bytes 442376 | tf_op jit(solution)/shard_map/ppermute | solution.py:20
  110.3 8.6 %collective-permute-start.8 = (bf16[3,96,256]{2,1,0:T(8,128)(2,1)S(1)}, bf16[3,96,256]{2,1,0:T(8,128)(2,1)S(1)}, u32[]{:S(2)}, u32[]{:S(2)}) collective-permute-start(bf16[3,96,256]{2,1,0:T(8,128)(2,1)S(1)} %get-tuple-element.31), channel_id=1, source_target_pairs={{12,0},{0,4},{4,8},{8,12},{13,1},{1,5},{5,9},{9,13},{14,2},{2,6},{... | collective-permute-start | bytes 442376 | tf_op jit(solution)/shard_map/ppermute | solution.py:20
  110.3 13.1 %collective-permute-start.9 = (bf16[3,96,256]{2,1,0:T(8,128)(2,1)S(1)}, bf16[3,96,256]{2,1,0:T(8,128)(2,1)S(1)}, u32[]{:S(2)}, u32[]{:S(2)}) collective-permute-start(bf16[3,96,256]{2,1,0:T(8,128)(2,1)S(1)} %get-tuple-element.33), channel_id=1, source_target_pairs={{8,0},{12,4},{0,8},{4,12},{9,1},{13,5},{1,9},{5,13},{10,2},{14,6},... | collective-permute-start | bytes 442376 | tf_op jit(solution)/shard_map/ppermute | solution.py:20
  123.5 12.2 %copy-start.2 = (bf16[6,96,256]{2,1,0:T(8,128)(2,1)}, bf16[6,96,256]{2,1,0:T(8,128)(2,1)S(1)}, u32[]{:S(2)}) copy-start(bf16[6,96,256]{2,1,0:T(8,128)(2,1)S(1)} %pad_maximum_fusion.2) | copy-start | bytes 884740
  124.3 7.6 %collective-permute-start.11 = (bf16[2,96,256]{2,1,0:T(8,128)(2,1)S(1)}, bf16[2,96,256]{2,1,0:T(8,128)(2,1)S(1)}, u32[]{:S(2)}, u32[]{:S(2)}) collective-permute-start(bf16[2,96,256]{2,1,0:T(8,128)(2,1)S(1)} %get-tuple-element.37), channel_id=1, source_target_pairs={{12,0},{0,4},{4,8},{8,12},{13,1},{1,5},{5,9},{9,13},{14,2},{2,6},{... | collective-permute-start | bytes 294920 | tf_op jit(solution)/shard_map/ppermute | solution.py:20
  124.3 10.7 %collective-permute-start.12 = (bf16[2,96,256]{2,1,0:T(8,128)(2,1)S(1)}, bf16[2,96,256]{2,1,0:T(8,128)(2,1)S(1)}, u32[]{:S(2)}, u32[]{:S(2)}) collective-permute-start(bf16[2,96,256]{2,1,0:T(8,128)(2,1)S(1)} %get-tuple-element.36), channel_id=1, source_target_pairs={{8,0},{12,4},{0,8},{4,12},{9,1},{13,5},{1,9},{5,13},{10,2},{14,6},... | collective-permute-start | bytes 294920 | tf_op jit(solution)/shard_map/ppermute | solution.py:20
  125.6 9.4 %collective-permute-start.13 = (bf16[2,96,256]{2,1,0:T(8,128)(2,1)S(1)}, bf16[2,96,256]{2,1,0:T(8,128)(2,1)S(1)}, u32[]{:S(2)}, u32[]{:S(2)}) collective-permute-start(bf16[2,96,256]{2,1,0:T(8,128)(2,1)S(1)} %get-tuple-element.35), channel_id=1, source_target_pairs={{4,0},{8,4},{12,8},{0,12},{5,1},{9,5},{13,9},{1,13},{6,2},{10,6},{... | collective-permute-start | bytes 294920 | tf_op jit(solution)/shard_map/ppermute | solution.py:20
  135.8 10.9 %collective-permute-start.14 = (bf16[4,2,96,256]{3,2,1,0:T(8,128)(2,1)S(1)}, bf16[4,2,96,256]{3,2,1,0:T(8,128)(2,1)S(1)}, u32[]{:S(2)}, u32[]{:S(2)}) collective-permute-start(bf16[4,2,96,256]{3,2,1,0:T(8,128)(2,1)S(1)} %broadcast_select_fusion), channel_id=1, source_target_pairs={{3,0},{0,1},{1,2},{2,3},{7,4},{4,5},{5,6},{6,7},{11,8},{8,9},{9,10... | collective-permute-start | bytes 1179656 | tf_op jit(solution)/shard_map/ppermute | solution.py:20
  135.8 12.0 %collective-permute-start.15 = (bf16[4,2,96,256]{3,2,1,0:T(8,128)(2,1)S(1)}, bf16[4,2,96,256]{3,2,1,0:T(8,128)(2,1)S(1)}, u32[]{:S(2)}, u32[]{:S(2)}) collective-permute-start(bf16[4,2,96,256]{3,2,1,0:T(8,128)(2,1)S(1)} %broadcast_select_fusion), channel_id=1, source_target_pairs={{2,0},{3,1},{0,2},{1,3},{6,4},{7,5},{4,6},{5,7},{10,8},{11,9},{8,1... | collective-permute-start | bytes 1179656 | tf_op jit(solution)/shard_map/ppermute | solution.py:20
  137.3 17.3 %collective-permute-start.16 = (bf16[4,2,96,256]{3,2,1,0:T(8,128)(2,1)S(1)}, bf16[4,2,96,256]{3,2,1,0:T(8,128)(2,1)S(1)}, u32[]{:S(2)}, u32[]{:S(2)}) collective-permute-start(bf16[4,2,96,256]{3,2,1,0:T(8,128)(2,1)S(1)} %broadcast_select_fusion), channel_id=1, source_target_pairs={{1,0},{2,1},{3,2},{0,3},{5,4},{6,5},{7,6},{4,7},{9,8},{10,9},{11,1... | collective-permute-start | bytes 1179656 | tf_op jit(solution)/shard_map/ppermute | solution.py:20

commit v16 on v15

--- a/solution.py
+++ b/solution.py
@@ -214,14 +214,14 @@
         core = member % 2
         side = member // 2
         blocks = partial.reshape(time_count, count_slabs, 2, 2, rows, count_ev)
-        keep = lax.dynamic_index_in_dim(blocks, core, 3, keepdims=False).astype(jnp.float32)
-        send = lax.dynamic_index_in_dim(blocks, 1 - core, 3, keepdims=False)
-        chip_sum = keep + swapped(send, "member", 0).astype(jnp.float32)
-        halves = 2 if time_count % 2 == 0 else 1
+        halves = 3 if time_count % 3 == 0 else (2 if time_count % 2 == 0 else 1)
         span = time_count // halves
         own_parts = []
         for half in range(halves):
-            chunk = chip_sum[half * span : (half + 1) * span]
+            part_blocks = blocks[half * span : (half + 1) * span]
+            keep = lax.dynamic_index_in_dim(part_blocks, core, 3, keepdims=False).astype(jnp.float32)
+            send = lax.dynamic_index_in_dim(part_blocks, 1 - core, 3, keepdims=False)
+            chunk = keep + swapped(send, "member", 0).astype(jnp.float32)
             keep = lax.dynamic_index_in_dim(chunk, side, 2, keepdims=False)
             send = lax.dynamic_index_in_dim(chunk, 1 - side, 2, keepdims=False).astype(jnp.bfloat16)
             slab_sum = keep + swapped(send, "member", 1).astype(jnp.float32)

time: 166 us -> 159 us (0.958)
  waiting for transfers between devices: 86.6 us -> 74.9 us
  starting transfers between devices: 24.1 us -> 31.4 us
  other arithmetic: 9.68 us -> 6.96 us
    ppermute x13 -> x16, waiting for transfers between devices: 64.7 us -> 55.4 us  [shifted(): return lax.ppermute(block, axis, route)]
    ppermute x13 -> x16, starting transfers between devices: 21.8 us -> 28.1 us  [shifted(): return lax.ppermute(block, axis, route)]
    squeeze x1 -> x3, local copies, waits for them, and re-layouts: 3.47 us -> 0.18 us  [body(): send = lax.dynamic_index_in_dim(part_blocks, 1 - core, 3, keepdims=False)]
    add x1 -> x3, other arithmetic: 3.3 us -> 0.6 us  [body(): chunk = keep + swapped(send, 'member', 0).astype(jnp.float32)]
    ppermute x4 -> x7, waiting for transfers between devices: 21.9 us -> 19.5 us  [swapped(): lax.ppermute(value, axis, [(i, i ^ 1 << bit) for i in range(lax.axis_size...]
    slice x1, local copies, waits for them, and re-layouts: 0.53 us -> 2.66 us  [body(): part_blocks = blocks[half * span:(half + 1) * span]]
    ppermute x4 -> x7, starting transfers between devices: 2.23 us -> 3.34 us  [swapped(): lax.ppermute(value, axis, [(i, i ^ 1 << bit) for i in range(lax.axis_size...]
  transfers between devices with their start and end apart: 17 -> 23, of which waited for: 12 -> 13; matrix products, arithmetic and copies ran while one was open for 9% -> 10% of each run, Pallas kernels for 7% -> 7%
where the time goes in v16:
time: 159 us; the launch traced here: 158 us
  waiting for transfers between devices  74.9 us (47%)
  starting transfers between devices  31.4 us (20%)
  Pallas kernels  25.6 us (16%)
  local copies, waits for them, and re-layouts  17.2 us (11%)
  other arithmetic  6.96 us (4%)
  between operations  1.91 us (1%)
    ppermute x16, waiting for transfers between devices, shifted(): return lax.ppermute(block, axis, route)  55.4 us
    ppermute x16, starting transfers between devices, shifted(): return lax.ppermute(block, axis, route)  28.1 us
    ppermute x7, waiting for transfers between devices, swapped(): lax.ppermute(value, axis, [(i, i ^ 1 << bit) for i in range(lax.axis_size...  19.5 us
    pallas_call x1, Pallas kernels, local_sums(): pl.pallas_call(functools.partial(sums_kernel, scale=scale, course_list=ne...  10.9 us
    pallas_call x1, Pallas kernels, local_sums(): pl.pallas_call(functools.partial(sums_kernel, scale=scale, course_list=(0...  8.08 us
    pallas_call x1, Pallas kernels, contract_panel(): pl.pallas_call(panel_kernel, grid=(count_ops,), in_specs=[pl.BlockSpec((1...  6.61 us
    ppermute x7, starting transfers between devices, swapped(): lax.ppermute(value, axis, [(i, i ^ 1 << bit) for i in range(lax.axis_size...  3.34 us
  transfers between devices with their start and end apart: 23, of which 13 were waited for; matrix products, arithmetic and copies ran while one was open for 10% of the time, Pallas kernels for 7%

profile of v16, /device:TPU:0, one launch (start us, length us, event | category | flops | bytes accessed | tf_op | source)
XLA Modules:
  0.0 158.0 jit_solution(16950739331972359530)
XLA Ops:
  0.7 6.1 %collective-permute-start = (bf16[6,2,3,256,128]{4,3,2,1,0:T(8,128)(2,1)}, bf16[6,2,3,256,128]{4,3,2,1,0:T(8,128)(2,1)}, u32[]{:S(2)}, u32[]{:S(2)}) collective-permute-start(bf16[6,2,3,256,128]{4,3,2,1,0:T(8,128)(2,1)} %field_ref.3), channel_id=1, source_target_pairs={{2,0},{3,1},{4,2},{5,3},{6,4},{7,5},{8,6},{9,7},{10,8},{11,9},{12,... | collective-permute-start | bytes 7077896 | tf_op jit(solution)/shard_map/ppermute | solution.py:20
  6.7 2.0 %copy.39 = bf16[6,2,3,256,8]{3,4,2,1,0:T(8,128)(2,1)S(1)} copy(bf16[6,2,3,256,8]{4,3,2,1,0:T(8,128)(2,1)} %bitcast.120) | data formatting | bytes 294912
  16.4 2.0 %copy.31 = bf16[6,2,3,256,8]{4,3,2,1,0:T(8,128)(2,1)S(1)} copy(bf16[6,2,3,256,8]{3,4,2,1,0:T(8,128)(2,1)} %collective-permute-done.1) | data formatting | bytes 294912 | tf_op jit(solution)/shard_map/ppermute | solution.py:24
  18.3 2.3 %pad.6.near_ref = bf16[6,2,3,256,128]{4,3,2,1,0:T(8,128)(2,1)} pad(bf16[6,2,3,256,8]{4,3,2,1,0:T(8,128)(2,1)S(1)} %copy.31, bf16[]{:T(256)} %constant.267.clone.1), padding=0_0x0_0x0_0x0_0x120_0 | pad | bytes 2506754 | tf_op jit(solution)/shard_map/jit(_pad)/pad | solution.py:101
  20.7 10.9 %shard_map.77 = (bf16[6,1536,256]{2,1,0:T(8,128)(2,1)}, bf16[6,512,768]{2,1,0:T(8,128)(2,1)}) custom-call(s32[3]{0:T(128)} %select_reduce_fusion.slot_ref, bf16[6,2,3,256,128]{4,3,2,1,0:T(8,128)(2,1)} %field_ref.3, bf16[6,2,3,256,128]{4,3,2,1,0:T(8,128)(2,1)} %pad.6.near_ref, f32[6,3,2,3,3,128]{5,4,3,2,1,0:T(4,128)} %copy.33.link_ref, ...), custom_call_target="tpu_custom_call" | custom-call | tf_op jit(solution)/shard_map/pallas_call | solution.py:116
  31.6 25.9 %collective-permute-done.near_ref = bf16[6,2,3,256,128]{4,3,2,1,0:T(8,128)(2,1)} collective-permute-done((bf16[6,2,3,256,128]{4,3,2,1,0:T(8,128)(2,1)}, bf16[6,2,3,256,128]{4,3,2,1,0:T(8,128)(2,1)}, u32[]{:S(2)}, u32[]{:S(2)}) %collective-permute-start) | collective-permute-done | bytes 2359328 | tf_op jit(solution)/shard_map/ppermute | solution.py:20
  57.5 8.1 %shard_map.78 = bf16[6,1536,256]{2,1,0:T(8,128)(2,1)} custom-call(s32[3]{0:T(128)} %select_reduce_fusion.slot_ref, bf16[6,2,3,256,128]{4,3,2,1,0:T(8,128)(2,1)} %field_ref.3, bf16[6,2,3,256,128]{4,3,2,1,0:T(8,128)(2,1)} %collective-permute-done.near_ref, f32[6,3,2,3,3,128]{5,4,3,2,1,0:T(4,128)} %copy.33.link_ref, ...), custom_call_target="tpu_custom_call", output_to_operand_aliasing={{}: (5, {})} | custom-call | tf_op jit(solution)/shard_map/pallas_call | solution.py:130
  65.6 2.7 %fusion.36 = (bf16[2,1536,256]{2,1,0:T(8,128)(2,1)S(1)}, bf16[2,1536,256]{2,1,0:T(8,128)(2,1)S(1)}, bf16[2,1536,256]{2,1,0:T(8,128)(2,1)S(1)}) fusion(bf16[6,1536,256]{2,1,0:T(8,128)(2,1)} %shard_map.78), kind=kLoop, calls=%fused_computation.118 | loop fusion | bytes 9437184 | tf_op jit(solution)/shard_map/slice | solution.py:221
  74.5 8.6 %collective-permute-done.3 = bf16[2,4,96,256]{3,2,1,0:T(8,128)(2,1)S(1)} collective-permute-done((bf16[2,4,96,256]{3,2,1,0:T(8,128)(2,1)S(1)}, bf16[2,4,96,256]{3,2,1,0:T(8,128)(2,1)S(1)}, u32[]{:S(2)}, u32[]{:S(2)}) %collective-permute-start.3) | collective-permute-done | bytes 393248 | tf_op jit(solution)/shard_map/ppermute | solution.py:24
  83.3 4.3 %collective-permute-start.5 = (bf16[2,96,256]{2,1,0:T(8,128)(2,1)S(1)}, bf16[2,96,256]{2,1,0:T(8,128)(2,1)S(1)}, u32[]{:S(2)}, u32[]{:S(2)}) collective-permute-start(bf16[2,96,256]{2,1,0:T(8,128)(2,1)S(1)} %get-tuple-element.37), channel_id=1, source_target_pairs={{8,0},{12,4},{0,8},{4,12},{9,1},{13,5},{1,9},{5,13},{10,2},{14,6},... | collective-permute-start | bytes 294920 | tf_op jit(solution)/shard_map/ppermute | solution.py:20
  87.7 3.8 %collective-permute-done.8 = bf16[2,4,96,256]{3,2,1,0:T(8,128)(2,1)S(1)} collective-permute-done((bf16[2,4,96,256]{3,2,1,0:T(8,128)(2,1)S(1)}, bf16[2,4,96,256]{3,2,1,0:T(8,128)(2,1)S(1)}, u32[]{:S(2)}, u32[]{:S(2)}) %collective-permute-start.8) | collective-permute-done | bytes 393248 | tf_op jit(solution)/shard_map/ppermute | solution.py:24
  92.7 6.8 %collective-permute-done.13 = bf16[2,4,96,256]{3,2,1,0:T(8,128)(2,1)S(1)} collective-permute-done((bf16[2,4,96,256]{3,2,1,0:T(8,128)(2,1)S(1)}, bf16[2,4,96,256]{3,2,1,0:T(8,128)(2,1)S(1)}, u32[]{:S(2)}, u32[]{:S(2)}) %collective-permute-start.13) | collective-permute-done | bytes 393248 | tf_op jit(solution)/shard_map/ppermute | solution.py:24
  99.5 4.0 %collective-permute-start.11 = (bf16[2,96,256]{2,1,0:T(8,128)(2,1)S(1)}, bf16[2,96,256]{2,1,0:T(8,128)(2,1)S(1)}, u32[]{:S(2)}, u32[]{:S(2)}) collective-permute-start(bf16[2,96,256]{2,1,0:T(8,128)(2,1)S(1)} %get-tuple-element.39), channel_id=1, source_target_pairs={{4,0},{8,4},{12,8},{0,12},{5,1},{9,5},{13,9},{1,13},{6,2},{10,6},{... | collective-permute-start | bytes 294920 | tf_op jit(solution)/shard_map/ppermute | solution.py:20
  103.8 4.3 %collective-permute-start.15 = (bf16[2,96,256]{2,1,0:T(8,128)(2,1)S(1)}, bf16[2,96,256]{2,1,0:T(8,128)(2,1)S(1)}, u32[]{:S(2)}, u32[]{:S(2)}) collective-permute-start(bf16[2,96,256]{2,1,0:T(8,128)(2,1)S(1)} %get-tuple-element.43), channel_id=1, source_target_pairs={{8,0},{12,4},{0,8},{4,12},{9,1},{13,5},{1,9},{5,13},{10,2},{14,6},... | collective-permute-start | bytes 294920 | tf_op jit(solution)/shard_map/ppermute | solution.py:20
  108.3 3.1 %collective-permute-done.9 = bf16[2,96,256]{2,1,0:T(8,128)(2,1)S(1)} collective-permute-done((bf16[2,96,256]{2,1,0:T(8,128)(2,1)S(1)}, bf16[2,96,256]{2,1,0:T(8,128)(2,1)S(1)}, u32[]{:S(2)}, u32[]{:S(2)}) %collective-permute-start.9) | collective-permute-done | bytes 98336 | tf_op jit(solution)/shard_map/ppermute | solution.py:20
  111.4 2.0 %collective-permute-done.14 = bf16[2,96,256]{2,1,0:T(8,128)(2,1)S(1)} collective-permute-done((bf16[2,96,256]{2,1,0:T(8,128)(2,1)S(1)}, bf16[2,96,256]{2,1,0:T(8,128)(2,1)S(1)}, u32[]{:S(2)}, u32[]{:S(2)}) %collective-permute-start.14) | collective-permute-done | bytes 98336 | tf_op jit(solution)/shard_map/ppermute | solution.py:20
  113.5 2.8 %collective-permute-done.15 = bf16[2,96,256]{2,1,0:T(8,128)(2,1)S(1)} collective-permute-done((bf16[2,96,256]{2,1,0:T(8,128)(2,1)S(1)}, bf16[2,96,256]{2,1,0:T(8,128)(2,1)S(1)}, u32[]{:S(2)}, u32[]{:S(2)}) %collective-permute-start.15) | collective-permute-done | bytes 98336 | tf_op jit(solution)/shard_map/ppermute | solution.py:20
  117.2 2.6 %collective-permute-start.17 = (bf16[2,96,256]{2,1,0:T(8,128)(2,1)S(1)}, bf16[2,96,256]{2,1,0:T(8,128)(2,1)S(1)}, u32[]{:S(2)}, u32[]{:S(2)}) collective-permute-start(bf16[2,96,256]{2,1,0:T(8,128)(2,1)S(1)} %get-tuple-element.34), channel_id=1, source_target_pairs={{12,0},{0,4},{4,8},{8,12},{13,1},{1,5},{5,9},{9,13},{14,2},{2,6},{... | collective-permute-start | bytes 294920 | tf_op jit(solution)/shard_map/ppermute | solution.py:20
  119.9 2.3 %collective-permute-start.19 = (bf16[2,96,256]{2,1,0:T(8,128)(2,1)S(1)}, bf16[2,96,256]{2,1,0:T(8,128)(2,1)S(1)}, u32[]{:S(2)}, u32[]{:S(2)}) collective-permute-start(bf16[2,96,256]{2,1,0:T(8,128)(2,1)S(1)} %get-tuple-element.32), channel_id=1, source_target_pairs={{4,0},{8,4},{12,8},{0,12},{5,1},{9,5},{13,9},{1,13},{6,2},{10,6},{... | collective-permute-start | bytes 294920 | tf_op jit(solution)/shard_map/ppermute | solution.py:20
  122.2 2.3 %collective-permute-done.17 = bf16[2,96,256]{2,1,0:T(8,128)(2,1)S(1)} collective-permute-done((bf16[2,96,256]{2,1,0:T(8,128)(2,1)S(1)}, bf16[2,96,256]{2,1,0:T(8,128)(2,1)S(1)}, u32[]{:S(2)}, u32[]{:S(2)}) %collective-permute-start.17) | collective-permute-done | bytes 98336 | tf_op jit(solution)/shard_map/ppermute | solution.py:20
  124.5 3.4 %collective-permute-done.18 = bf16[2,96,256]{2,1,0:T(8,128)(2,1)S(1)} collective-permute-done((bf16[2,96,256]{2,1,0:T(8,128)(2,1)S(1)}, bf16[2,96,256]{2,1,0:T(8,128)(2,1)S(1)}, u32[]{:S(2)}, u32[]{:S(2)}) %collective-permute-start.18) | collective-permute-done | bytes 98336 | tf_op jit(solution)/shard_map/ppermute | solution.py:20
  131.9 7.7 %collective-permute-done.20 = bf16[4,2,96,256]{3,2,1,0:T(8,128)(2,1)S(1)} collective-permute-done((bf16[4,2,96,256]{3,2,1,0:T(8,128)(2,1)S(1)}, bf16[4,2,96,256]{3,2,1,0:T(8,128)(2,1)S(1)}, u32[]{:S(2)}, u32[]{:S(2)}) %collective-permute-start.20) | collective-permute-done | bytes 393248 | tf_op jit(solution)/shard_map/ppermute | solution.py:20
  140.8 6.9 %collective-permute-done.22 = bf16[4,2,96,256]{3,2,1,0:T(8,128)(2,1)S(1)} collective-permute-done((bf16[4,2,96,256]{3,2,1,0:T(8,128)(2,1)S(1)}, bf16[4,2,96,256]{3,2,1,0:T(8,128)(2,1)S(1)}, u32[]{:S(2)}, u32[]{:S(2)}) %collective-permute-start.22) | collective-permute-done | bytes 393248 | tf_op jit(solution)/shard_map/ppermute | solution.py:20
  150.0 6.6 %shard_map.79 = f32[3,2,256]{2,1,0:T(2,128)} custom-call(bf16[2,3,2,256,256]{4,3,2,1,0:T(8,128)(2,1)} %bitcast.121, bf16[2,3,2,256,256]{4,3,2,1,0:T(8,128)(2,1)} %bitcast.122, bf16[512,1024]{1,0:T(8,128)(2,1)} %bitcast.130, bf16[2048,512]{1,0:T(8,128)(2,1)} %maximum_maximum_fusion.wide_ref), custom_call_target="tpu_custom_call" | custom-call | tf_op jit(solution)/shard_map/pallas_call | solution.py:177
  (102 shorter events, 24.5 us)
Async XLA Ops:
  0.7 56.9 %collective-permute-start = (bf16[6,2,3,256,128]{4,3,2,1,0:T(8,128)(2,1)}, bf16[6,2,3,256,128]{4,3,2,1,0:T(8,128)(2,1)}, u32[]{:S(2)}, u32[]{:S(2)}) collective-permute-start(bf16[6,2,3,256,128]{4,3,2,1,0:T(8,128)(2,1)} %field_ref.3), channel_id=1, source_target_pairs={{2,0},{3,1},{4,2},{5,3},{6,4},{7,5},{8,6},{9,7},{10,8},{11,9},{12,... | collective-permute-start | bytes 7077896 | tf_op jit(solution)/shard_map/ppermute | solution.py:20
  8.8 7.6 %collective-permute-start.1 = (bf16[6,2,3,256,8]{3,4,2,1,0:T(8,128)(2,1)S(1)}, bf16[6,2,3,256,8]{3,4,2,1,0:T(8,128)(2,1)}, u32[]{:S(2)}, u32[]{:S(2)}) collective-permute-start(bf16[6,2,3,256,8]{3,4,2,1,0:T(8,128)(2,1)S(1)} %copy.39), channel_id=1, source_target_pairs={{0,1},{1,0},{2,3},{3,2},{4,5},{5,4},{6,7},{7,6},{8,9},{9,8},{10,11... | collective-permute-start | bytes 442376 | tf_op jit(solution)/shard_map/ppermute | solution.py:24
  68.4 2.5 %collective-permute-start.2 = (bf16[2,4,2,96,256]{4,3,2,1,0:T(8,128)(2,1)S(1)}, bf16[2,4,2,96,256]{4,3,2,1,0:T(8,128)(2,1)S(1)}, u32[]{:S(2)}, u32[]{:S(2)}) collective-permute-start(bf16[2,4,2,96,256]{4,3,2,1,0:T(8,128)(2,1)S(1)} %dynamic-slice_bitcast_fusion.2), channel_id=1, source_target_pairs={{0,1},{1,0},{2,3},{3,2},{4,5},{5,4},{6,7},{7,6},{8,9},{9,8},{10,11... | collective-permute-start | bytes 2359304 | tf_op jit(solution)/shard_map/ppermute | solution.py:24
  68.6 3.2 %collective-permute-start.7 = (bf16[2,4,2,96,256]{4,3,2,1,0:T(8,128)(2,1)S(1)}, bf16[2,4,2,96,256]{4,3,2,1,0:T(8,128)(2,1)S(1)}, u32[]{:S(2)}, u32[]{:S(2)}) collective-permute-start(bf16[2,4,2,96,256]{4,3,2,1,0:T(8,128)(2,1)S(1)} %dynamic-slice_bitcast_fusion.1), channel_id=1, source_target_pairs={{0,1},{1,0},{2,3},{3,2},{4,5},{5,4},{6,7},{7,6},{8,9},{9,8},{10,11... | collective-permute-start | bytes 2359304 | tf_op jit(solution)/shard_map/ppermute | solution.py:24
  70.7 2.8 %collective-permute-start.12 = (bf16[2,4,2,96,256]{4,3,2,1,0:T(8,128)(2,1)S(1)}, bf16[2,4,2,96,256]{4,3,2,1,0:T(8,128)(2,1)S(1)}, u32[]{:S(2)}, u32[]{:S(2)}) collective-permute-start(bf16[2,4,2,96,256]{4,3,2,1,0:T(8,128)(2,1)S(1)} %dynamic-slice_bitcast_fusion), channel_id=1, source_target_pairs={{0,1},{1,0},{2,3},{3,2},{4,5},{5,4},{6,7},{7,6},{8,9},{9,8},{10,11... | collective-permute-start | bytes 2359304 | tf_op jit(solution)/shard_map/ppermute | solution.py:24
  71.1 12.0 %collective-permute-start.3 = (bf16[2,4,96,256]{3,2,1,0:T(8,128)(2,1)S(1)}, bf16[2,4,96,256]{3,2,1,0:T(8,128)(2,1)S(1)}, u32[]{:S(2)}, u32[]{:S(2)}) collective-permute-start(bf16[2,4,96,256]{3,2,1,0:T(8,128)(2,1)S(1)} %fusion), channel_id=1, source_target_pairs={{0,2},{1,3},{2,0},{3,1},{4,6},{5,7},{6,4},{7,5},{8,10},{9,11},{10,... | collective-permute-start | bytes 1179656 | tf_op jit(solution)/shard_map/ppermute | solution.py:24
  72.1 19.4 %collective-permute-start.8 = (bf16[2,4,96,256]{3,2,1,0:T(8,128)(2,1)S(1)}, bf16[2,4,96,256]{3,2,1,0:T(8,128)(2,1)S(1)}, u32[]{:S(2)}, u32[]{:S(2)}) collective-permute-start(bf16[2,4,96,256]{3,2,1,0:T(8,128)(2,1)S(1)} %fusion.1), channel_id=1, source_target_pairs={{0,2},{1,3},{2,0},{3,1},{4,6},{5,7},{6,4},{7,5},{8,10},{9,11},{10,... | collective-permute-start | bytes 1179656 | tf_op jit(solution)/shard_map/ppermute | solution.py:24
  73.8 25.7 %collective-permute-start.13 = (bf16[2,4,96,256]{3,2,1,0:T(8,128)(2,1)S(1)}, bf16[2,4,96,256]{3,2,1,0:T(8,128)(2,1)S(1)}, u32[]{:S(2)}, u32[]{:S(2)}) collective-permute-start(bf16[2,4,96,256]{3,2,1,0:T(8,128)(2,1)S(1)} %fusion.2), channel_id=1, source_target_pairs={{0,2},{1,3},{2,0},{3,1},{4,6},{5,7},{6,4},{7,5},{8,10},{9,11},{10,... | collective-permute-start | bytes 1179656 | tf_op jit(solution)/shard_map/ppermute | solution.py:24
  83.2 20.4 %collective-permute-start.4 = (bf16[2,96,256]{2,1,0:T(8,128)(2,1)S(1)}, bf16[2,96,256]{2,1,0:T(8,128)(2,1)S(1)}, u32[]{:S(2)}, u32[]{:S(2)}) collective-permute-start(bf16[2,96,256]{2,1,0:T(8,128)(2,1)S(1)} %get-tuple-element.35), channel_id=1, source_target_pairs={{12,0},{0,4},{4,8},{8,12},{13,1},{1,5},{5,9},{9,13},{14,2},{2,6},{... | collective-permute-start | bytes 294920 | tf_op jit(solution)/shard_map/ppermute | solution.py:20
  83.3 20.5 %collective-permute-start.5 = (bf16[2,96,256]{2,1,0:T(8,128)(2,1)S(1)}, bf16[2,96,256]{2,1,0:T(8,128)(2,1)S(1)}, u32[]{:S(2)}, u32[]{:S(2)}) collective-permute-start(bf16[2,96,256]{2,1,0:T(8,128)(2,1)S(1)} %get-tuple-element.37), channel_id=1, source_target_pairs={{8,0},{12,4},{0,8},{4,12},{9,1},{13,5},{1,9},{5,13},{10,2},{14,6},... | collective-permute-start | bytes 294920 | tf_op jit(solution)/shard_map/ppermute | solution.py:20
  87.7 16.2 %collective-permute-start.6 = (bf16[2,96,256]{2,1,0:T(8,128)(2,1)S(1)}, bf16[2,96,256]{2,1,0:T(8,128)(2,1)S(1)}, u32[]{:S(2)}, u32[]{:S(2)}) collective-permute-start(bf16[2,96,256]{2,1,0:T(8,128)(2,1)S(1)} %get-tuple-element.36), channel_id=1, source_target_pairs={{4,0},{8,4},{12,8},{0,12},{5,1},{9,5},{13,9},{1,13},{6,2},{10,6},{... | collective-permute-start | bytes 294920 | tf_op jit(solution)/shard_map/ppermute | solution.py:20
  91.7 16.5 %collective-permute-start.10 = (bf16[2,96,256]{2,1,0:T(8,128)(2,1)S(1)}, bf16[2,96,256]{2,1,0:T(8,128)(2,1)S(1)}, u32[]{:S(2)}, u32[]{:S(2)}) collective-permute-start(bf16[2,96,256]{2,1,0:T(8,128)(2,1)S(1)} %get-tuple-element.40), channel_id=1, source_target_pairs={{8,0},{12,4},{0,8},{4,12},{9,1},{13,5},{1,9},{5,13},{10,2},{14,6},... | collective-permute-start | bytes 294920 | tf_op jit(solution)/shard_map/ppermute | solution.py:20
  99.5 8.8 %collective-permute-start.11 = (bf16[2,96,256]{2,1,0:T(8,128)(2,1)S(1)}, bf16[2,96,256]{2,1,0:T(8,128)(2,1)S(1)}, u32[]{:S(2)}, u32[]{:S(2)}) collective-permute-start(bf16[2,96,256]{2,1,0:T(8,128)(2,1)S(1)} %get-tuple-element.39), channel_id=1, source_target_pairs={{4,0},{8,4},{12,8},{0,12},{5,1},{9,5},{13,9},{1,13},{6,2},{10,6},{... | collective-permute-start | bytes 294920 | tf_op jit(solution)/shard_map/ppermute | solution.py:20
  103.7 7.7 %collective-permute-start.9 = (bf16[2,96,256]{2,1,0:T(8,128)(2,1)S(1)}, bf16[2,96,256]{2,1,0:T(8,128)(2,1)S(1)}, u32[]{:S(2)}, u32[]{:S(2)}) collective-permute-start(bf16[2,96,256]{2,1,0:T(8,128)(2,1)S(1)} %get-tuple-element.38), channel_id=1, source_target_pairs={{12,0},{0,4},{4,8},{8,12},{13,1},{1,5},{5,9},{9,13},{14,2},{2,6},{... | collective-permute-start | bytes 294920 | tf_op jit(solution)/shard_map/ppermute | solution.py:20
  103.8 9.7 %collective-permute-start.14 = (bf16[2,96,256]{2,1,0:T(8,128)(2,1)S(1)}, bf16[2,96,256]{2,1,0:T(8,128)(2,1)S(1)}, u32[]{:S(2)}, u32[]{:S(2)}) collective-permute-start(bf16[2,96,256]{2,1,0:T(8,128)(2,1)S(1)} %get-tuple-element.41), channel_id=1, source_target_pairs={{12,0},{0,4},{4,8},{8,12},{13,1},{1,5},{5,9},{9,13},{14,2},{2,6},{... | collective-permute-start | bytes 294920 | tf_op jit(solution)/shard_map/ppermute | solution.py:20
  103.8 12.4 %collective-permute-start.15 = (bf16[2,96,256]{2,1,0:T(8,128)(2,1)S(1)}, bf16[2,96,256]{2,1,0:T(8,128)(2,1)S(1)}, u32[]{:S(2)}, u32[]{:S(2)}) collective-permute-start(bf16[2,96,256]{2,1,0:T(8,128)(2,1)S(1)} %get-tuple-element.43), channel_id=1, source_target_pairs={{8,0},{12,4},{0,8},{4,12},{9,1},{13,5},{1,9},{5,13},{10,2},{14,6},... | collective-permute-start | bytes 294920 | tf_op jit(solution)/shard_map/ppermute | solution.py:20
  108.2 8.1 %collective-permute-start.16 = (bf16[2,96,256]{2,1,0:T(8,128)(2,1)S(1)}, bf16[2,96,256]{2,1,0:T(8,128)(2,1)S(1)}, u32[]{:S(2)}, u32[]{:S(2)}) collective-permute-start(bf16[2,96,256]{2,1,0:T(8,128)(2,1)S(1)} %get-tuple-element.42), channel_id=1, source_target_pairs={{4,0},{8,4},{12,8},{0,12},{5,1},{9,5},{13,9},{1,13},{6,2},{10,6},{... | collective-permute-start | bytes 294920 | tf_op jit(solution)/shard_map/ppermute | solution.py:20
  116.4 11.6 %copy-start.2 = (bf16[6,96,256]{2,1,0:T(8,128)(2,1)}, bf16[6,96,256]{2,1,0:T(8,128)(2,1)S(1)}, u32[]{:S(2)}) copy-start(bf16[6,96,256]{2,1,0:T(8,128)(2,1)S(1)} %pad_maximum_fusion.2) | copy-start | bytes 884740
  117.2 7.4 %collective-permute-start.17 = (bf16[2,96,256]{2,1,0:T(8,128)(2,1)S(1)}, bf16[2,96,256]{2,1,0:T(8,128)(2,1)S(1)}, u32[]{:S(2)}, u32[]{:S(2)}) collective-permute-start(bf16[2,96,256]{2,1,0:T(8,128)(2,1)S(1)} %get-tuple-element.34), channel_id=1, source_target_pairs={{12,0},{0,4},{4,8},{8,12},{13,1},{1,5},{5,9},{9,13},{14,2},{2,6},{... | collective-permute-start | bytes 294920 | tf_op jit(solution)/shard_map/ppermute | solution.py:20
  119.8 8.2 %collective-permute-start.18 = (bf16[2,96,256]{2,1,0:T(8,128)(2,1)S(1)}, bf16[2,96,256]{2,1,0:T(8,128)(2,1)S(1)}, u32[]{:S(2)}, u32[]{:S(2)}) collective-permute-start(bf16[2,96,256]{2,1,0:T(8,128)(2,1)S(1)} %get-tuple-element.33), channel_id=1, source_target_pairs={{8,0},{12,4},{0,8},{4,12},{9,1},{13,5},{1,9},{5,13},{10,2},{14,6},... | collective-permute-start | bytes 294920 | tf_op jit(solution)/shard_map/ppermute | solution.py:20
  119.9 8.1 %collective-permute-start.19 = (bf16[2,96,256]{2,1,0:T(8,128)(2,1)S(1)}, bf16[2,96,256]{2,1,0:T(8,128)(2,1)S(1)}, u32[]{:S(2)}, u32[]{:S(2)}) collective-permute-start(bf16[2,96,256]{2,1,0:T(8,128)(2,1)S(1)} %get-tuple-element.32), channel_id=1, source_target_pairs={{4,0},{8,4},{12,8},{0,12},{5,1},{9,5},{13,9},{1,13},{6,2},{10,6},{... | collective-permute-start | bytes 294920 | tf_op jit(solution)/shard_map/ppermute | solution.py:20
  128.7 10.9 %collective-permute-start.20 = (bf16[4,2,96,256]{3,2,1,0:T(8,128)(2,1)S(1)}, bf16[4,2,96,256]{3,2,1,0:T(8,128)(2,1)S(1)}, u32[]{:S(2)}, u32[]{:S(2)}) collective-permute-start(bf16[4,2,96,256]{3,2,1,0:T(8,128)(2,1)S(1)} %broadcast_select_fusion), channel_id=1, source_target_pairs={{3,0},{0,1},{1,2},{2,3},{7,4},{4,5},{5,6},{6,7},{11,8},{8,9},{9,10... | collective-permute-start | bytes 1179656 | tf_op jit(solution)/shard_map/ppermute | solution.py:20
  128.8 12.0 %collective-permute-start.21 = (bf16[4,2,96,256]{3,2,1,0:T(8,128)(2,1)S(1)}, bf16[4,2,96,256]{3,2,1,0:T(8,128)(2,1)S(1)}, u32[]{:S(2)}, u32[]{:S(2)}) collective-permute-start(bf16[4,2,96,256]{3,2,1,0:T(8,128)(2,1)S(1)} %broadcast_select_fusion), channel_id=1, source_target_pairs={{2,0},{3,1},{0,2},{1,3},{6,4},{7,5},{4,6},{5,7},{10,8},{11,9},{8,1... | collective-permute-start | bytes 1179656 | tf_op jit(solution)/shard_map/ppermute | solution.py:20
  130.4 17.3 %collective-permute-start.22 = (bf16[4,2,96,256]{3,2,1,0:T(8,128)(2,1)S(1)}, bf16[4,2,96,256]{3,2,1,0:T(8,128)(2,1)S(1)}, u32[]{:S(2)}, u32[]{:S(2)}) collective-permute-start(bf16[4,2,96,256]{3,2,1,0:T(8,128)(2,1)S(1)} %broadcast_select_fusion), channel_id=1, source_target_pairs={{1,0},{2,1},{3,2},{0,3},{5,4},{6,5},{7,6},{4,7},{9,8},{10,9},{11,1... | collective-permute-start | bytes 1179656 | tf_op jit(solution)/shard_map/ppermute | solution.py:20
  (6 other events, 39.4 us)

commit v17 on v16

--- a/solution.py
+++ b/solution.py
@@ -85,7 +85,9 @@
         right = jnp.concatenate(moved_real + moved_imag, axis=1)
         joined = lax.dot_general(left, right, (((1,), (1,)), ((), ())), preferred_element_type=jnp.float32)
         if len(course_list) == 1:
-            out_ref[0] = (joined * scale).astype(out_ref.dtype)
+            out_ref[0] = rest[0][0]
+            start = pl.multiple_of(slot_ref[course] * rows, rows)
+            out_ref[0, pl.ds(start, rows), :] = (joined * scale).astype(out_ref.dtype)
         else:
             start = pl.multiple_of(slot_ref[course] * rows, rows)
             out_ref[0, pl.ds(start, rows), :] = (joined * scale).astype(out_ref.dtype)
@@ -121,18 +123,29 @@
             jax.ShapeDtypeStruct((time_count, left_rows, 6 * sites), jnp.bfloat16),
         ),
     )(slot_of, eigenvectors, row_wide, gauge_links, trig)
-    second_spec = pltpu.PrefetchScalarGridSpec(
-        num_scalar_prefetch=1,
-        grid=(time_count,),
-        in_specs=[pl.BlockSpec(memory_space=pl.ANY), field_spec, link_spec, left_spec, pl.BlockSpec(memory_space=pl.ANY)],
-        out_specs=pl.BlockSpec((1, 2 * count_ev, count_ev), lambda t, slot: (t, slot[0], 0)),
-    )
-    return pl.pallas_call(
-        functools.partial(sums_kernel, scale=scale, course_list=(0,)),
-        grid_spec=second_spec,
-        out_shape=jax.ShapeDtypeStruct((time_count, rows, count_ev), jnp.bfloat16),
-        input_output_aliases={5: 0},
-    )(slot_of, eigenvectors, far_tile, gauge_links, left, partial)
+    chunks = []
+    for first, far_part in far_tile:
+        span = far_part.shape[0]
+        second_spec = pltpu.PrefetchScalarGridSpec(
+            num_scalar_prefetch=1,
+            grid=(span,),
+            in_specs=[
+                pl.BlockSpec(memory_space=pl.ANY),
+                pl.BlockSpec((1, 2, 3, count_ev, sites), lambda t, slot: (t, 0, 0, 0, 0)),
+                pl.BlockSpec((1,) + gauge_links.shape[1:], lambda t, slot, first=first: (t + first, 0, 0, 0, 0, 0)),
+                pl.BlockSpec((1, left_rows, 6 * sites), lambda t, slot, first=first: (t + first, 0, 0)),
+                pl.BlockSpec((1, rows, count_ev), lambda t, slot, first=first: (t + first, 0, 0)),
+            ],
+            out_specs=pl.BlockSpec((1, rows, count_ev), lambda t, slot: (t, 0, 0)),
+        )
+        chunks.append(
+            pl.pallas_call(
+                functools.partial(sums_kernel, scale=scale, course_list=(0,)),
+                grid_spec=second_spec,
+                out_shape=jax.ShapeDtypeStruct((span, rows, count_ev), jnp.bfloat16),
+            )(slot_of, eigenvectors, far_part, gauge_links, left, partial)
+        )
+    return chunks
 
 
 def panel_kernel(sink_ref, source_ref, stack_ref, wide_ref, out_ref):
@@ -204,21 +217,21 @@
     coord_y = device % 2 * half_rows + column // LZ
     coord_z = column % LZ
     angle = phase_angles(momenta, (coord_x, coord_y, coord_z), (extent_x, LY, LZ))[0]
-    far_tile = shifted(eigenvectors, SPACE, -2)
+    halves = 3 if time_count % 3 == 0 else (2 if time_count % 2 == 0 else 1)
+    span = time_count // halves
+    far_tile = [(h * span, shifted(eigenvectors[h * span : (h + 1) * span], SPACE, -2)) for h in range(halves)]
     row_in = swapped(eigenvectors[..., :LZ], SPACE, 0)
     scale = 1.0 / math.sqrt(3.0 * extent_x * LY * LZ)
-    partial = local_sums(eigenvectors, gauge_links, far_tile, row_in, directions, angle, scale)
+    partial_chunks = local_sums(eigenvectors, gauge_links, far_tile, row_in, directions, angle, scale)
+    partial = jnp.concatenate(partial_chunks, 0)
     rows = partial.shape[1] // nspace
     if count_slabs <= 8:
         slab = lax.axis_index("slab")
         core = member % 2
         side = member // 2
-        blocks = partial.reshape(time_count, count_slabs, 2, 2, rows, count_ev)
-        halves = 3 if time_count % 3 == 0 else (2 if time_count % 2 == 0 else 1)
-        span = time_count // halves
         own_parts = []
         for half in range(halves):
-            part_blocks = blocks[half * span : (half + 1) * span]
+            part_blocks = partial_chunks[half].reshape(span, count_slabs, 2, 2, rows, count_ev)
             keep = lax.dynamic_index_in_dim(part_blocks, core, 3, keepdims=False).astype(jnp.float32)
             send = lax.dynamic_index_in_dim(part_blocks, 1 - core, 3, keepdims=False)
             chunk = keep + swapped(send, "member", 0).astype(jnp.float32)

time: 159 us -> 158 us (level)
  waiting for transfers between devices: 74.9 us -> 62.4 us
  Pallas kernels: 25.6 us -> 30.7 us
  local copies, waits for them, and re-layouts: 17.2 us -> 20.5 us
  other arithmetic: 6.96 us -> 9.37 us
    ppermute x16 -> x18, waiting for transfers between devices: 55.4 us -> 43.3 us  [shifted(): return lax.ppermute(block, axis, route)]
    pallas_call x1 -> x3, Pallas kernels: 8.08 us -> 13.1 us  [local_sums(): pl.pallas_call(functools.partial(sums_kernel, scale=scale, course_list=(0...]
    squeeze x3, local copies, waits for them, and re-layouts: 0.18 us -> 3.7 us  [body(): send = lax.dynamic_index_in_dim(part_blocks, 1 - core, 3, keepdims=False)]
    add x3, other arithmetic: 0.6 us -> 3.03 us  [body(): chunk = keep + swapped(send, 'member', 0).astype(jnp.float32)]
    unnamed x16 -> x24, local copies, waits for them, and re-layouts: 2.92 us -> 3.9 us
    ppermute x16 -> x18, starting transfers between devices: 28.1 us -> 28.6 us  [shifted(): return lax.ppermute(block, axis, route)]
  transfers between devices with their start and end apart: 23 -> 25, of which waited for: 13 -> 13; matrix products, arithmetic and copies ran while one was open for 10% -> 14% of each run, Pallas kernels for 7% -> 15%
where the time goes in v17:
time: 158 us; the launch traced here: 157 us
  waiting for transfers between devices  62.4 us (39%)
  starting transfers between devices  31.9 us (20%)
  Pallas kernels  30.7 us (19%)
  local copies, waits for them, and re-layouts  20.5 us (13%)
  other arithmetic  9.37 us (6%)
  between operations  1.85 us (1%)
    ppermute x18, waiting for transfers between devices, shifted(): return lax.ppermute(block, axis, route)  43.3 us
    ppermute x18, starting transfers between devices, shifted(): return lax.ppermute(block, axis, route)  28.6 us
    ppermute x7, waiting for transfers between devices, swapped(): lax.ppermute(value, axis, [(i, i ^ 1 << bit) for i in range(lax.axis_size...  19.1 us
    pallas_call x3, Pallas kernels, local_sums(): pl.pallas_call(functools.partial(sums_kernel, scale=scale, course_list=(0...  13.1 us
    pallas_call x1, Pallas kernels, local_sums(): pl.pallas_call(functools.partial(sums_kernel, scale=scale, course_list=ne...  11 us
    pallas_call x1, Pallas kernels, contract_panel(): pl.pallas_call(panel_kernel, grid=(count_ops,), in_specs=[pl.BlockSpec((1...  6.63 us
    unnamed x24, local copies, waits for them, and re-layouts  3.9 us
    squeeze x3, local copies, waits for them, and re-layouts, body(): send = lax.dynamic_index_in_dim(part_blocks, 1 - core, 3, keepdims=False)  3.7 us
  transfers between devices with their start and end apart: 25, of which 13 were waited for; matrix products, arithmetic and copies ran while one was open for 14% of the time, Pallas kernels for 15%

profile of v17, /device:TPU:0, one launch (start us, length us, event | category | flops | bytes accessed | tf_op | source)
XLA Modules:
  0.0 156.8 jit_solution(9969023267003988411)
XLA Ops:
  0.7 2.8 %copy.46 = bf16[6,2,3,256,8]{3,4,2,1,0:T(8,128)(2,1)} copy(bf16[6,2,3,256,8]{4,3,2,1,0:T(8,128)(2,1)} %bitcast.120) | data formatting | bytes 294912
  5.4 5.6 %collective-permute-start = (bf16[2,2,3,256,128]{4,3,2,1,0:T(8,128)(2,1)}, bf16[2,2,3,256,128]{4,3,2,1,0:T(8,128)(2,1)}, u32[]{:S(2)}, u32[]{:S(2)}) collective-permute-start(bf16[2,2,3,256,128]{4,3,2,1,0:T(8,128)(2,1)} %get-tuple-element.26), channel_id=1, source_target_pairs={{2,0},{3,1},{4,2},{5,3},{6,4},{7,5},{8,6},{9,7},{10,8},{11,9},{12,... | collective-permute-start | bytes 2359304 | tf_op jit(solution)/shard_map/ppermute | solution.py:20
  22.4 2.3 %pad.6.near_ref = bf16[6,2,3,256,128]{4,3,2,1,0:T(8,128)(2,1)} pad(bf16[6,2,3,256,8]{4,3,2,1,0:T(8,128)(2,1)S(1)} %copy.36, bf16[]{:T(256)} %constant.267.clone.1), padding=0_0x0_0x0_0x0_0x120_0 | pad | bytes 2506754 | tf_op jit(solution)/shard_map/jit(_pad)/pad | solution.py:103
  24.6 11.0 %shard_map.77 = (bf16[6,1536,256]{2,1,0:T(8,128)(2,1)}, bf16[6,512,768]{2,1,0:T(8,128)(2,1)}) custom-call(s32[3]{0:T(128)} %select_reduce_fusion.slot_ref, bf16[6,2,3,256,128]{4,3,2,1,0:T(8,128)(2,1)} %field_ref.7, bf16[6,2,3,256,128]{4,3,2,1,0:T(8,128)(2,1)} %pad.6.near_ref, f32[6,3,2,3,3,128]{5,4,3,2,1,0:T(4,128)} %copy.38.link_ref, ...), custom_call_target="tpu_custom_call" | custom-call | tf_op jit(solution)/shard_map/pallas_call | solution.py:118
  35.6 4.4 %shard_map.78 = bf16[2,1536,256]{2,1,0:T(8,128)(2,1)} custom-call(s32[3]{0:T(128)} %select_reduce_fusion.slot_ref, bf16[6,2,3,256,128]{4,3,2,1,0:T(8,128)(2,1)} %field_ref.7, bf16[2,2,3,256,128]{4,3,2,1,0:T(8,128)(2,1)} %collective-permute-done.near_ref, f32[6,3,2,3,3,128]{5,4,3,2,1,0:T(4,128)} %copy.38.link_ref, ...), custom_call_target="tpu_custom_call" | custom-call | tf_op jit(solution)/shard_map/pallas_call | solution.py:142
  41.4 4.6 %collective-permute-done.7.near_ref = bf16[2,2,3,256,128]{4,3,2,1,0:T(8,128)(2,1)} collective-permute-done((bf16[2,2,3,256,128]{4,3,2,1,0:T(8,128)(2,1)}, bf16[2,2,3,256,128]{4,3,2,1,0:T(8,128)(2,1)}, u32[]{:S(2)}, u32[]{:S(2)}) %collective-permute-start.7) | collective-permute-done | bytes 786464 | tf_op jit(solution)/shard_map/ppermute | solution.py:20
  46.0 4.3 %shard_map.79 = bf16[2,1536,256]{2,1,0:T(8,128)(2,1)} custom-call(s32[3]{0:T(128)} %select_reduce_fusion.slot_ref, bf16[6,2,3,256,128]{4,3,2,1,0:T(8,128)(2,1)} %field_ref.7, bf16[2,2,3,256,128]{4,3,2,1,0:T(8,128)(2,1)} %collective-permute-done.7.near_ref, f32[6,3,2,3,3,128]{5,4,3,2,1,0:T(4,128)} %copy.38.link_ref, ...), custom_call_target="tpu_custom_call" | custom-call | tf_op jit(solution)/shard_map/pallas_call | solution.py:142
  53.1 9.3 %collective-permute-done.13.near_ref = bf16[2,2,3,256,128]{4,3,2,1,0:T(8,128)(2,1)} collective-permute-done((bf16[2,2,3,256,128]{4,3,2,1,0:T(8,128)(2,1)}, bf16[2,2,3,256,128]{4,3,2,1,0:T(8,128)(2,1)}, u32[]{:S(2)}, u32[]{:S(2)}) %collective-permute-start.13) | collective-permute-done | bytes 786464 | tf_op jit(solution)/shard_map/ppermute | solution.py:20
  62.4 4.3 %shard_map.80 = bf16[2,1536,256]{2,1,0:T(8,128)(2,1)} custom-call(s32[3]{0:T(128)} %select_reduce_fusion.slot_ref, bf16[6,2,3,256,128]{4,3,2,1,0:T(8,128)(2,1)} %field_ref.7, bf16[2,2,3,256,128]{4,3,2,1,0:T(8,128)(2,1)} %collective-permute-done.13.near_ref, f32[6,3,2,3,3,128]{5,4,3,2,1,0:T(4,128)} %copy.38.link_ref, ...), custom_call_target="tpu_custom_call" | custom-call | tf_op jit(solution)/shard_map/pallas_call | solution.py:142
  74.2 7.8 %collective-permute-done.3 = bf16[2,4,96,256]{3,2,1,0:T(8,128)(2,1)S(1)} collective-permute-done((bf16[2,4,96,256]{3,2,1,0:T(8,128)(2,1)S(1)}, bf16[2,4,96,256]{3,2,1,0:T(8,128)(2,1)S(1)}, u32[]{:S(2)}, u32[]{:S(2)}) %collective-permute-start.3) | collective-permute-done | bytes 393248 | tf_op jit(solution)/shard_map/ppermute | solution.py:24
  82.2 4.2 %collective-permute-start.5 = (bf16[2,96,256]{2,1,0:T(8,128)(2,1)S(1)}, bf16[2,96,256]{2,1,0:T(8,128)(2,1)S(1)}, u32[]{:S(2)}, u32[]{:S(2)}) collective-permute-start(bf16[2,96,256]{2,1,0:T(8,128)(2,1)S(1)} %get-tuple-element.37), channel_id=1, source_target_pairs={{8,0},{12,4},{0,8},{4,12},{9,1},{13,5},{1,9},{5,13},{10,2},{14,6},... | collective-permute-start | bytes 294920 | tf_op jit(solution)/shard_map/ppermute | solution.py:20
  86.4 4.0 %collective-permute-done.9 = bf16[2,4,96,256]{3,2,1,0:T(8,128)(2,1)S(1)} collective-permute-done((bf16[2,4,96,256]{3,2,1,0:T(8,128)(2,1)S(1)}, bf16[2,4,96,256]{3,2,1,0:T(8,128)(2,1)S(1)}, u32[]{:S(2)}, u32[]{:S(2)}) %collective-permute-start.9) | collective-permute-done | bytes 393248 | tf_op jit(solution)/shard_map/ppermute | solution.py:24
  90.6 7.4 %collective-permute-done.15 = bf16[2,4,96,256]{3,2,1,0:T(8,128)(2,1)S(1)} collective-permute-done((bf16[2,4,96,256]{3,2,1,0:T(8,128)(2,1)S(1)}, bf16[2,4,96,256]{3,2,1,0:T(8,128)(2,1)S(1)}, u32[]{:S(2)}, u32[]{:S(2)}) %collective-permute-start.15) | collective-permute-done | bytes 393248 | tf_op jit(solution)/shard_map/ppermute | solution.py:24
  99.4 2.9 %collective-permute-start.12 = (bf16[2,96,256]{2,1,0:T(8,128)(2,1)S(1)}, bf16[2,96,256]{2,1,0:T(8,128)(2,1)S(1)}, u32[]{:S(2)}, u32[]{:S(2)}) collective-permute-start(bf16[2,96,256]{2,1,0:T(8,128)(2,1)S(1)} %get-tuple-element.39), channel_id=1, source_target_pairs={{4,0},{8,4},{12,8},{0,12},{5,1},{9,5},{13,9},{1,13},{6,2},{10,6},{... | collective-permute-start | bytes 294920 | tf_op jit(solution)/shard_map/ppermute | solution.py:20
  104.4 2.9 %collective-permute-start.18 = (bf16[2,96,256]{2,1,0:T(8,128)(2,1)S(1)}, bf16[2,96,256]{2,1,0:T(8,128)(2,1)S(1)}, u32[]{:S(2)}, u32[]{:S(2)}) collective-permute-start(bf16[2,96,256]{2,1,0:T(8,128)(2,1)S(1)} %get-tuple-element.42), channel_id=1, source_target_pairs={{4,0},{8,4},{12,8},{0,12},{5,1},{9,5},{13,9},{1,13},{6,2},{10,6},{... | collective-permute-start | bytes 294920 | tf_op jit(solution)/shard_map/ppermute | solution.py:20
  107.4 2.4 %collective-permute-done.16 = bf16[2,96,256]{2,1,0:T(8,128)(2,1)S(1)} collective-permute-done((bf16[2,96,256]{2,1,0:T(8,128)(2,1)S(1)}, bf16[2,96,256]{2,1,0:T(8,128)(2,1)S(1)}, u32[]{:S(2)}, u32[]{:S(2)}) %collective-permute-start.16) | collective-permute-done | bytes 98336 | tf_op jit(solution)/shard_map/ppermute | solution.py:20
  109.8 4.9 %collective-permute-done.17 = bf16[2,96,256]{2,1,0:T(8,128)(2,1)S(1)} collective-permute-done((bf16[2,96,256]{2,1,0:T(8,128)(2,1)S(1)}, bf16[2,96,256]{2,1,0:T(8,128)(2,1)S(1)}, u32[]{:S(2)}, u32[]{:S(2)}) %collective-permute-start.17) | collective-permute-done | bytes 98336 | tf_op jit(solution)/shard_map/ppermute | solution.py:20
  115.6 2.0 %collective-permute-start.19 = (bf16[2,96,256]{2,1,0:T(8,128)(2,1)S(1)}, bf16[2,96,256]{2,1,0:T(8,128)(2,1)S(1)}, u32[]{:S(2)}, u32[]{:S(2)}) collective-permute-start(bf16[2,96,256]{2,1,0:T(8,128)(2,1)S(1)} %get-tuple-element.34), channel_id=1, source_target_pairs={{12,0},{0,4},{4,8},{8,12},{13,1},{1,5},{5,9},{9,13},{14,2},{2,6},{... | collective-permute-start | bytes 294920 | tf_op jit(solution)/shard_map/ppermute | solution.py:20
  117.6 2.2 %collective-permute-start.20 = (bf16[2,96,256]{2,1,0:T(8,128)(2,1)S(1)}, bf16[2,96,256]{2,1,0:T(8,128)(2,1)S(1)}, u32[]{:S(2)}, u32[]{:S(2)}) collective-permute-start(bf16[2,96,256]{2,1,0:T(8,128)(2,1)S(1)} %get-tuple-element.33), channel_id=1, source_target_pairs={{8,0},{12,4},{0,8},{4,12},{9,1},{13,5},{1,9},{5,13},{10,2},{14,6},... | collective-permute-start | bytes 294920 | tf_op jit(solution)/shard_map/ppermute | solution.py:20
  120.1 3.2 %collective-permute-done.19 = bf16[2,96,256]{2,1,0:T(8,128)(2,1)S(1)} collective-permute-done((bf16[2,96,256]{2,1,0:T(8,128)(2,1)S(1)}, bf16[2,96,256]{2,1,0:T(8,128)(2,1)S(1)}, u32[]{:S(2)}, u32[]{:S(2)}) %collective-permute-start.19) | collective-permute-done | bytes 98336 | tf_op jit(solution)/shard_map/ppermute | solution.py:20
  123.3 2.6 %collective-permute-done.20 = bf16[2,96,256]{2,1,0:T(8,128)(2,1)S(1)} collective-permute-done((bf16[2,96,256]{2,1,0:T(8,128)(2,1)S(1)}, bf16[2,96,256]{2,1,0:T(8,128)(2,1)S(1)}, u32[]{:S(2)}, u32[]{:S(2)}) %collective-permute-start.20) | collective-permute-done | bytes 98336 | tf_op jit(solution)/shard_map/ppermute | solution.py:20
  130.6 7.4 %collective-permute-done.22 = bf16[4,2,96,256]{3,2,1,0:T(8,128)(2,1)S(1)} collective-permute-done((bf16[4,2,96,256]{3,2,1,0:T(8,128)(2,1)S(1)}, bf16[4,2,96,256]{3,2,1,0:T(8,128)(2,1)S(1)}, u32[]{:S(2)}, u32[]{:S(2)}) %collective-permute-start.22) | collective-permute-done | bytes 393248 | tf_op jit(solution)/shard_map/ppermute | solution.py:20
  139.2 7.1 %collective-permute-done.24 = bf16[4,2,96,256]{3,2,1,0:T(8,128)(2,1)S(1)} collective-permute-done((bf16[4,2,96,256]{3,2,1,0:T(8,128)(2,1)S(1)}, bf16[4,2,96,256]{3,2,1,0:T(8,128)(2,1)S(1)}, u32[]{:S(2)}, u32[]{:S(2)}) %collective-permute-start.24) | collective-permute-done | bytes 393248 | tf_op jit(solution)/shard_map/ppermute | solution.py:20
  148.7 6.6 %shard_map.81 = f32[3,2,256]{2,1,0:T(2,128)} custom-call(bf16[2,3,2,256,256]{4,3,2,1,0:T(8,128)(2,1)} %bitcast.121, bf16[2,3,2,256,256]{4,3,2,1,0:T(8,128)(2,1)} %bitcast.122, bf16[512,1024]{1,0:T(8,128)(2,1)} %bitcast.130, bf16[2048,512]{1,0:T(8,128)(2,1)} %maximum_maximum_fusion.wide_ref), custom_call_target="tpu_custom_call" | custom-call | tf_op jit(solution)/shard_map/pallas_call | solution.py:190
  (116 shorter events, 38.7 us)
Async XLA Ops:
  3.4 17.0 %collective-permute-start.1 = (bf16[6,2,3,256,8]{3,4,2,1,0:T(8,128)(2,1)}, bf16[6,2,3,256,8]{3,4,2,1,0:T(8,128)(2,1)}, u32[]{:S(2)}, u32[]{:S(2)}) collective-permute-start(bf16[6,2,3,256,8]{3,4,2,1,0:T(8,128)(2,1)} %copy.46), channel_id=1, source_target_pairs={{0,1},{1,0},{2,3},{3,2},{4,5},{5,4},{6,7},{7,6},{8,9},{9,8},{10,11... | collective-permute-start | bytes 442376 | tf_op jit(solution)/shard_map/ppermute | solution.py:24
  5.4 30.2 %collective-permute-start = (bf16[2,2,3,256,128]{4,3,2,1,0:T(8,128)(2,1)}, bf16[2,2,3,256,128]{4,3,2,1,0:T(8,128)(2,1)}, u32[]{:S(2)}, u32[]{:S(2)}) collective-permute-start(bf16[2,2,3,256,128]{4,3,2,1,0:T(8,128)(2,1)} %get-tuple-element.26), channel_id=1, source_target_pairs={{2,0},{3,1},{4,2},{5,3},{6,4},{7,5},{8,6},{9,7},{10,8},{11,9},{12,... | collective-permute-start | bytes 2359304 | tf_op jit(solution)/shard_map/ppermute | solution.py:20
  10.9 35.0 %collective-permute-start.7 = (bf16[2,2,3,256,128]{4,3,2,1,0:T(8,128)(2,1)}, bf16[2,2,3,256,128]{4,3,2,1,0:T(8,128)(2,1)}, u32[]{:S(2)}, u32[]{:S(2)}) collective-permute-start(bf16[2,2,3,256,128]{4,3,2,1,0:T(8,128)(2,1)} %get-tuple-element.27), channel_id=1, source_target_pairs={{2,0},{3,1},{4,2},{5,3},{6,4},{7,5},{8,6},{9,7},{10,8},{11,9},{12,... | collective-permute-start | bytes 2359304 | tf_op jit(solution)/shard_map/ppermute | solution.py:20
  11.4 51.0 %collective-permute-start.13 = (bf16[2,2,3,256,128]{4,3,2,1,0:T(8,128)(2,1)}, bf16[2,2,3,256,128]{4,3,2,1,0:T(8,128)(2,1)}, u32[]{:S(2)}, u32[]{:S(2)}) collective-permute-start(bf16[2,2,3,256,128]{4,3,2,1,0:T(8,128)(2,1)} %get-tuple-element.28), channel_id=1, source_target_pairs={{2,0},{3,1},{4,2},{5,3},{6,4},{7,5},{8,6},{9,7},{10,8},{11,9},{12,... | collective-permute-start | bytes 2359304 | tf_op jit(solution)/shard_map/ppermute | solution.py:20
  41.2 26.9 %collective-permute-start.2 = (bf16[2,4,2,96,256]{4,3,2,1,0:T(8,128)(2,1)S(1)}, bf16[2,4,2,96,256]{4,3,2,1,0:T(8,128)(2,1)}, u32[]{:S(2)}, u32[]{:S(2)}) collective-permute-start(bf16[2,4,2,96,256]{4,3,2,1,0:T(8,128)(2,1)S(1)} %dynamic-slice_bitcast_fusion.2), channel_id=1, source_target_pairs={{0,1},{1,0},{2,3},{3,2},{4,5},{5,4},{6,7},{7,6},{8,9},{9,8},{10,11... | collective-permute-start | bytes 2359304 | tf_op jit(solution)/shard_map/ppermute | solution.py:24
  51.5 18.8 %collective-permute-start.8 = (bf16[2,4,2,96,256]{4,3,2,1,0:T(8,128)(2,1)S(1)}, bf16[2,4,2,96,256]{4,3,2,1,0:T(8,128)(2,1)}, u32[]{:S(2)}, u32[]{:S(2)}) collective-permute-start(bf16[2,4,2,96,256]{4,3,2,1,0:T(8,128)(2,1)S(1)} %dynamic-slice_bitcast_fusion.1), channel_id=1, source_target_pairs={{0,1},{1,0},{2,3},{3,2},{4,5},{5,4},{6,7},{7,6},{8,9},{9,8},{10,11... | collective-permute-start | bytes 2359304 | tf_op jit(solution)/shard_map/ppermute | solution.py:24
  70.0 12.0 %collective-permute-start.3 = (bf16[2,4,96,256]{3,2,1,0:T(8,128)(2,1)S(1)}, bf16[2,4,96,256]{3,2,1,0:T(8,128)(2,1)S(1)}, u32[]{:S(2)}, u32[]{:S(2)}) collective-permute-start(bf16[2,4,96,256]{3,2,1,0:T(8,128)(2,1)S(1)} %fusion), channel_id=1, source_target_pairs={{0,2},{1,3},{2,0},{3,1},{4,6},{5,7},{6,4},{7,5},{8,10},{9,11},{10,... | collective-permute-start | bytes 1179656 | tf_op jit(solution)/shard_map/ppermute | solution.py:24
  71.8 18.6 %collective-permute-start.9 = (bf16[2,4,96,256]{3,2,1,0:T(8,128)(2,1)S(1)}, bf16[2,4,96,256]{3,2,1,0:T(8,128)(2,1)S(1)}, u32[]{:S(2)}, u32[]{:S(2)}) collective-permute-start(bf16[2,4,96,256]{3,2,1,0:T(8,128)(2,1)S(1)} %fusion.1), channel_id=1, source_target_pairs={{0,2},{1,3},{2,0},{3,1},{4,6},{5,7},{6,4},{7,5},{8,10},{9,11},{10,... | collective-permute-start | bytes 1179656 | tf_op jit(solution)/shard_map/ppermute | solution.py:24
  73.8 24.2 %collective-permute-start.15 = (bf16[2,4,96,256]{3,2,1,0:T(8,128)(2,1)S(1)}, bf16[2,4,96,256]{3,2,1,0:T(8,128)(2,1)S(1)}, u32[]{:S(2)}, u32[]{:S(2)}) collective-permute-start(bf16[2,4,96,256]{3,2,1,0:T(8,128)(2,1)S(1)} %fusion.2), channel_id=1, source_target_pairs={{0,2},{1,3},{2,0},{3,1},{4,6},{5,7},{6,4},{7,5},{8,10},{9,11},{10,... | collective-permute-start | bytes 1179656 | tf_op jit(solution)/shard_map/ppermute | solution.py:24
  82.1 17.2 %collective-permute-start.4 = (bf16[2,96,256]{2,1,0:T(8,128)(2,1)S(1)}, bf16[2,96,256]{2,1,0:T(8,128)(2,1)S(1)}, u32[]{:S(2)}, u32[]{:S(2)}) collective-permute-start(bf16[2,96,256]{2,1,0:T(8,128)(2,1)S(1)} %get-tuple-element.35), channel_id=1, source_target_pairs={{12,0},{0,4},{4,8},{8,12},{13,1},{1,5},{5,9},{9,13},{14,2},{2,6},{... | collective-permute-start | bytes 294920 | tf_op jit(solution)/shard_map/ppermute | solution.py:20
  82.2 20.0 %collective-permute-start.5 = (bf16[2,96,256]{2,1,0:T(8,128)(2,1)S(1)}, bf16[2,96,256]{2,1,0:T(8,128)(2,1)S(1)}, u32[]{:S(2)}, u32[]{:S(2)}) collective-permute-start(bf16[2,96,256]{2,1,0:T(8,128)(2,1)S(1)} %get-tuple-element.37), channel_id=1, source_target_pairs={{8,0},{12,4},{0,8},{4,12},{9,1},{13,5},{1,9},{5,13},{10,2},{14,6},... | collective-permute-start | bytes 294920 | tf_op jit(solution)/shard_map/ppermute | solution.py:20
  86.4 16.4 %collective-permute-start.6 = (bf16[2,96,256]{2,1,0:T(8,128)(2,1)S(1)}, bf16[2,96,256]{2,1,0:T(8,128)(2,1)S(1)}, u32[]{:S(2)}, u32[]{:S(2)}) collective-permute-start(bf16[2,96,256]{2,1,0:T(8,128)(2,1)S(1)} %get-tuple-element.36), channel_id=1, source_target_pairs={{4,0},{8,4},{12,8},{0,12},{5,1},{9,5},{13,9},{1,13},{6,2},{10,6},{... | collective-permute-start | bytes 294920 | tf_op jit(solution)/shard_map/ppermute | solution.py:20
  90.6 13.8 %collective-permute-start.10 = (bf16[2,96,256]{2,1,0:T(8,128)(2,1)S(1)}, bf16[2,96,256]{2,1,0:T(8,128)(2,1)S(1)}, u32[]{:S(2)}, u32[]{:S(2)}) collective-permute-start(bf16[2,96,256]{2,1,0:T(8,128)(2,1)S(1)} %get-tuple-element.38), channel_id=1, source_target_pairs={{12,0},{0,4},{4,8},{8,12},{13,1},{1,5},{5,9},{9,13},{14,2},{2,6},{... | collective-permute-start | bytes 294920 | tf_op jit(solution)/shard_map/ppermute | solution.py:20
  98.0 9.3 %collective-permute-start.11 = (bf16[2,96,256]{2,1,0:T(8,128)(2,1)S(1)}, bf16[2,96,256]{2,1,0:T(8,128)(2,1)S(1)}, u32[]{:S(2)}, u32[]{:S(2)}) collective-permute-start(bf16[2,96,256]{2,1,0:T(8,128)(2,1)S(1)} %get-tuple-element.40), channel_id=1, source_target_pairs={{8,0},{12,4},{0,8},{4,12},{9,1},{13,5},{1,9},{5,13},{10,2},{14,6},... | collective-permute-start | bytes 294920 | tf_op jit(solution)/shard_map/ppermute | solution.py:20
  99.4 7.9 %collective-permute-start.12 = (bf16[2,96,256]{2,1,0:T(8,128)(2,1)S(1)}, bf16[2,96,256]{2,1,0:T(8,128)(2,1)S(1)}, u32[]{:S(2)}, u32[]{:S(2)}) collective-permute-start(bf16[2,96,256]{2,1,0:T(8,128)(2,1)S(1)} %get-tuple-element.39), channel_id=1, source_target_pairs={{4,0},{8,4},{12,8},{0,12},{5,1},{9,5},{13,9},{1,13},{6,2},{10,6},{... | collective-permute-start | bytes 294920 | tf_op jit(solution)/shard_map/ppermute | solution.py:20
  102.2 7.6 %collective-permute-start.16 = (bf16[2,96,256]{2,1,0:T(8,128)(2,1)S(1)}, bf16[2,96,256]{2,1,0:T(8,128)(2,1)S(1)}, u32[]{:S(2)}, u32[]{:S(2)}) collective-permute-start(bf16[2,96,256]{2,1,0:T(8,128)(2,1)S(1)} %get-tuple-element.41), channel_id=1, source_target_pairs={{12,0},{0,4},{4,8},{8,12},{13,1},{1,5},{5,9},{9,13},{14,2},{2,6},{... | collective-permute-start | bytes 294920 | tf_op jit(solution)/shard_map/ppermute | solution.py:20
  102.9 11.9 %collective-permute-start.17 = (bf16[2,96,256]{2,1,0:T(8,128)(2,1)S(1)}, bf16[2,96,256]{2,1,0:T(8,128)(2,1)S(1)}, u32[]{:S(2)}, u32[]{:S(2)}) collective-permute-start(bf16[2,96,256]{2,1,0:T(8,128)(2,1)S(1)} %get-tuple-element.43), channel_id=1, source_target_pairs={{8,0},{12,4},{0,8},{4,12},{9,1},{13,5},{1,9},{5,13},{10,2},{14,6},... | collective-permute-start | bytes 294920 | tf_op jit(solution)/shard_map/ppermute | solution.py:20
  104.4 10.4 %collective-permute-start.18 = (bf16[2,96,256]{2,1,0:T(8,128)(2,1)S(1)}, bf16[2,96,256]{2,1,0:T(8,128)(2,1)S(1)}, u32[]{:S(2)}, u32[]{:S(2)}) collective-permute-start(bf16[2,96,256]{2,1,0:T(8,128)(2,1)S(1)} %get-tuple-element.42), channel_id=1, source_target_pairs={{4,0},{8,4},{12,8},{0,12},{5,1},{9,5},{13,9},{1,13},{6,2},{10,6},{... | collective-permute-start | bytes 294920 | tf_op jit(solution)/shard_map/ppermute | solution.py:20
  115.6 7.7 %collective-permute-start.19 = (bf16[2,96,256]{2,1,0:T(8,128)(2,1)S(1)}, bf16[2,96,256]{2,1,0:T(8,128)(2,1)S(1)}, u32[]{:S(2)}, u32[]{:S(2)}) collective-permute-start(bf16[2,96,256]{2,1,0:T(8,128)(2,1)S(1)} %get-tuple-element.34), channel_id=1, source_target_pairs={{12,0},{0,4},{4,8},{8,12},{13,1},{1,5},{5,9},{9,13},{14,2},{2,6},{... | collective-permute-start | bytes 294920 | tf_op jit(solution)/shard_map/ppermute | solution.py:20
  117.6 8.2 %collective-permute-start.20 = (bf16[2,96,256]{2,1,0:T(8,128)(2,1)S(1)}, bf16[2,96,256]{2,1,0:T(8,128)(2,1)S(1)}, u32[]{:S(2)}, u32[]{:S(2)}) collective-permute-start(bf16[2,96,256]{2,1,0:T(8,128)(2,1)S(1)} %get-tuple-element.33), channel_id=1, source_target_pairs={{8,0},{12,4},{0,8},{4,12},{9,1},{13,5},{1,9},{5,13},{10,2},{14,6},... | collective-permute-start | bytes 294920 | tf_op jit(solution)/shard_map/ppermute | solution.py:20
  119.8 6.6 %collective-permute-start.21 = (bf16[2,96,256]{2,1,0:T(8,128)(2,1)S(1)}, bf16[2,96,256]{2,1,0:T(8,128)(2,1)S(1)}, u32[]{:S(2)}, u32[]{:S(2)}) collective-permute-start(bf16[2,96,256]{2,1,0:T(8,128)(2,1)S(1)} %get-tuple-element.32), channel_id=1, source_target_pairs={{4,0},{8,4},{12,8},{0,12},{5,1},{9,5},{13,9},{1,13},{6,2},{10,6},{... | collective-permute-start | bytes 294920 | tf_op jit(solution)/shard_map/ppermute | solution.py:20
  127.1 10.9 %collective-permute-start.22 = (bf16[4,2,96,256]{3,2,1,0:T(8,128)(2,1)S(1)}, bf16[4,2,96,256]{3,2,1,0:T(8,128)(2,1)S(1)}, u32[]{:S(2)}, u32[]{:S(2)}) collective-permute-start(bf16[4,2,96,256]{3,2,1,0:T(8,128)(2,1)S(1)} %broadcast_select_fusion), channel_id=1, source_target_pairs={{3,0},{0,1},{1,2},{2,3},{7,4},{4,5},{5,6},{6,7},{11,8},{8,9},{9,10... | collective-permute-start | bytes 1179656 | tf_op jit(solution)/shard_map/ppermute | solution.py:20
  127.2 12.0 %collective-permute-start.23 = (bf16[4,2,96,256]{3,2,1,0:T(8,128)(2,1)S(1)}, bf16[4,2,96,256]{3,2,1,0:T(8,128)(2,1)S(1)}, u32[]{:S(2)}, u32[]{:S(2)}) collective-permute-start(bf16[4,2,96,256]{3,2,1,0:T(8,128)(2,1)S(1)} %broadcast_select_fusion), channel_id=1, source_target_pairs={{2,0},{3,1},{0,2},{1,3},{6,4},{7,5},{4,6},{5,7},{10,8},{11,9},{8,1... | collective-permute-start | bytes 1179656 | tf_op jit(solution)/shard_map/ppermute | solution.py:20
  129.0 17.3 %collective-permute-start.24 = (bf16[4,2,96,256]{3,2,1,0:T(8,128)(2,1)S(1)}, bf16[4,2,96,256]{3,2,1,0:T(8,128)(2,1)S(1)}, u32[]{:S(2)}, u32[]{:S(2)}) collective-permute-start(bf16[4,2,96,256]{3,2,1,0:T(8,128)(2,1)S(1)} %broadcast_select_fusion), channel_id=1, source_target_pairs={{1,0},{2,1},{3,2},{0,3},{5,4},{6,5},{7,6},{4,7},{9,8},{10,9},{11,1... | collective-permute-start | bytes 1179656 | tf_op jit(solution)/shard_map/ppermute | solution.py:20
  (12 other events, 79.1 us)

commit v18 on v17

--- a/solution.py
+++ b/solution.py
@@ -93,7 +93,7 @@
             out_ref[0, pl.ds(start, rows), :] = (joined * scale).astype(out_ref.dtype)
 
 
-def local_sums(eigenvectors, gauge_links, far_tile, row_in, directions, angle, scale):
+def local_sums(eigenvectors, gauge_links, row_in, directions, angle, scale):
     time_count, _, _, count_ev, sites = eigenvectors.shape
     count_ops = directions.shape[0]
     slot_of = jnp.sum(
@@ -123,8 +123,14 @@
             jax.ShapeDtypeStruct((time_count, left_rows, 6 * sites), jnp.bfloat16),
         ),
     )(slot_of, eigenvectors, row_wide, gauge_links, trig)
-    chunks = []
-    for first, far_part in far_tile:
+    return slot_of, left, partial
+
+
+def second_pass(slot_of, eigenvectors, gauge_links, left, partial, first, far_part, scale):
+    count_ev, sites = eigenvectors.shape[3], eigenvectors.shape[4]
+    rows = partial.shape[1]
+    left_rows = left.shape[1]
+    if True:
         span = far_part.shape[0]
         second_spec = pltpu.PrefetchScalarGridSpec(
             num_scalar_prefetch=1,
@@ -138,14 +144,11 @@
             ],
             out_specs=pl.BlockSpec((1, rows, count_ev), lambda t, slot: (t, 0, 0)),
         )
-        chunks.append(
-            pl.pallas_call(
-                functools.partial(sums_kernel, scale=scale, course_list=(0,)),
-                grid_spec=second_spec,
-                out_shape=jax.ShapeDtypeStruct((span, rows, count_ev), jnp.bfloat16),
-            )(slot_of, eigenvectors, far_part, gauge_links, left, partial)
-        )
-    return chunks
+        return pl.pallas_call(
+            functools.partial(sums_kernel, scale=scale, course_list=(0,)),
+            grid_spec=second_spec,
+            out_shape=jax.ShapeDtypeStruct((span, rows, count_ev), jnp.bfloat16),
+        )(slot_of, eigenvectors, far_part, gauge_links, left, partial)
 
 
 def panel_kernel(sink_ref, source_ref, stack_ref, wide_ref, out_ref):
@@ -222,19 +225,30 @@
     far_tile = [(h * span, shifted(eigenvectors[h * span : (h + 1) * span], SPACE, -2)) for h in range(halves)]
     row_in = swapped(eigenvectors[..., :LZ], SPACE, 0)
     scale = 1.0 / math.sqrt(3.0 * extent_x * LY * LZ)
-    partial_chunks = local_sums(eigenvectors, gauge_links, far_tile, row_in, directions, angle, scale)
+    slot_of, left, first_partial = local_sums(eigenvectors, gauge_links, row_in, directions, angle, scale)
+    partial_chunks = []
+    core = member % 2
+    swapped_chunks = []
+    for half in range(halves):
+        first, far_part = far_tile[half]
+        if swapped_chunks:
+            far_part = lax.optimization_barrier((far_part, swapped_chunks[-1]))[0]
+        chunk_partial = second_pass(slot_of, eigenvectors, gauge_links, left, first_partial, first, far_part, scale)
+        partial_chunks.append(chunk_partial)
+        if count_slabs <= 8:
+            part_blocks = chunk_partial.reshape(span, count_slabs, 2, 2, -1, count_ev)
+            send = lax.dynamic_index_in_dim(part_blocks, 1 - core, 3, keepdims=False)
+            swapped_chunks.append(swapped(send, "member", 0))
     partial = jnp.concatenate(partial_chunks, 0)
     rows = partial.shape[1] // nspace
     if count_slabs <= 8:
         slab = lax.axis_index("slab")
-        core = member % 2
         side = member // 2
         own_parts = []
         for half in range(halves):
             part_blocks = partial_chunks[half].reshape(span, count_slabs, 2, 2, rows, count_ev)
             keep = lax.dynamic_index_in_dim(part_blocks, core, 3, keepdims=False).astype(jnp.float32)
-            send = lax.dynamic_index_in_dim(part_blocks, 1 - core, 3, keepdims=False)
-            chunk = keep + swapped(send, "member", 0).astype(jnp.float32)
+            chunk = keep + swapped_chunks[half].astype(jnp.float32)
             keep = lax.dynamic_index_in_dim(chunk, side, 2, keepdims=False)
             send = lax.dynamic_index_in_dim(chunk, 1 - side, 2, keepdims=False).astype(jnp.bfloat16)
             slab_sum = keep + swapped(send, "member", 1).astype(jnp.float32)

time: 158 us -> 148 us (0.937)
  waiting for transfers between devices: 62.4 us -> 50.6 us
  starting transfers between devices: 31.9 us -> 33.6 us
    ppermute x7, waiting for transfers between devices: 19.1 us -> 10.4 us  [swapped(): lax.ppermute(value, axis, [(i, i ^ 1 << bit) for i in range(lax.axis_size...]
    ppermute x18, waiting for transfers between devices: 43.3 us -> 40.3 us  [shifted(): return lax.ppermute(block, axis, route)]
  transfers between devices with their start and end apart: 25 -> 25, of which waited for: 13 -> 13; matrix products, arithmetic and copies ran while one was open for 14% -> 15% of each run, Pallas kernels for 15% -> 16%
where the time goes in v18:
time: 148 us; the launch traced here: 147 us
  waiting for transfers between devices  50.6 us (34%)
  starting transfers between devices  33.6 us (23%)
  Pallas kernels  30.7 us (21%)
  local copies, waits for them, and re-layouts  21.2 us (14%)
  other arithmetic  9.33 us (6%)
  between operations  1.83 us (1%)
    ppermute x18, waiting for transfers between devices, shifted(): return lax.ppermute(block, axis, route)  40.3 us
    ppermute x18, starting transfers between devices, shifted(): return lax.ppermute(block, axis, route)  30.1 us
    pallas_call x3, Pallas kernels, second_pass(): pl.pallas_call(functools.partial(sums_kernel, scale=scale, course_list=(0...  13.1 us
    pallas_call x1, Pallas kernels, local_sums(): pl.pallas_call(functools.partial(sums_kernel, scale=scale, course_list=ne...  11 us
    ppermute x7, waiting for transfers between devices, swapped(): lax.ppermute(value, axis, [(i, i ^ 1 << bit) for i in range(lax.axis_size...  10.4 us
    pallas_call x1, Pallas kernels, contract_panel(): pl.pallas_call(panel_kernel, grid=(count_ops,), in_specs=[pl.BlockSpec((1...  6.63 us
    squeeze x3, local copies, waits for them, and re-layouts, body(): send = lax.dynamic_index_in_dim(part_blocks, 1 - core, 3, keepdims=False)  4.66 us
    unnamed x24, local copies, waits for them, and re-layouts  3.79 us
  transfers between devices with their start and end apart: 25, of which 13 were waited for; matrix products, arithmetic and copies ran while one was open for 15% of the time, Pallas kernels for 16%

profile of v18, /device:TPU:0, one launch (start us, length us, event | category | flops | bytes accessed | tf_op | source)
XLA Modules:
  0.0 147.3 jit_solution(18270707000894848941)
XLA Ops:
  0.7 2.8 %copy.46 = bf16[6,2,3,256,8]{3,4,2,1,0:T(8,128)(2,1)} copy(bf16[6,2,3,256,8]{4,3,2,1,0:T(8,128)(2,1)} %bitcast.120) | data formatting | bytes 294912
  5.3 5.6 %collective-permute-start = (bf16[2,2,3,256,128]{4,3,2,1,0:T(8,128)(2,1)S(1)}, bf16[2,2,3,256,128]{4,3,2,1,0:T(8,128)(2,1)}, u32[]{:S(2)}, u32[]{:S(2)}) collective-permute-start(bf16[2,2,3,256,128]{4,3,2,1,0:T(8,128)(2,1)S(1)} %get-tuple-element.30), channel_id=1, source_target_pairs={{2,0},{3,1},{4,2},{5,3},{6,4},{7,5},{8,6},{9,7},{10,8},{11,9},{12,... | collective-permute-start | bytes 2359304 | tf_op jit(solution)/shard_map/ppermute | solution.py:20
  20.1 2.3 %pad.6.near_ref = bf16[6,2,3,256,128]{4,3,2,1,0:T(8,128)(2,1)} pad(bf16[6,2,3,256,8]{4,3,2,1,0:T(8,128)(2,1)S(1)} %copy.36, bf16[]{:T(256)} %constant.267.clone.1), padding=0_0x0_0x0_0x0_0x120_0 | pad | bytes 2506754 | tf_op jit(solution)/shard_map/jit(_pad)/pad | solution.py:103
  22.4 11.0 %shard_map.77 = (bf16[6,1536,256]{2,1,0:T(8,128)(2,1)}, bf16[6,512,768]{2,1,0:T(8,128)(2,1)}) custom-call(s32[3]{0:T(128)} %select_reduce_fusion.slot_ref, bf16[6,2,3,256,128]{4,3,2,1,0:T(8,128)(2,1)} %field_ref.7, bf16[6,2,3,256,128]{4,3,2,1,0:T(8,128)(2,1)} %pad.6.near_ref, f32[6,3,2,3,3,128]{5,4,3,2,1,0:T(4,128)} %copy.38.link_ref, ...), custom_call_target="tpu_custom_call" | custom-call | tf_op jit(solution)/shard_map/pallas_call | solution.py:118
  33.3 4.3 %shard_map.78 = bf16[2,1536,256]{2,1,0:T(8,128)(2,1)} custom-call(s32[3]{0:T(128)} %select_reduce_fusion.slot_ref, bf16[6,2,3,256,128]{4,3,2,1,0:T(8,128)(2,1)} %field_ref.7, bf16[2,2,3,256,128]{4,3,2,1,0:T(8,128)(2,1)} %collective-permute-done.near_ref, f32[6,3,2,3,3,128]{5,4,3,2,1,0:T(4,128)} %copy.38.link_ref, ...), custom_call_target="tpu_custom_call" | custom-call | tf_op jit(solution)/shard_map/pallas_call | solution.py:147
  41.2 4.4 %collective-permute-done.7.near_ref = bf16[2,2,3,256,128]{4,3,2,1,0:T(8,128)(2,1)} collective-permute-done((bf16[2,2,3,256,128]{4,3,2,1,0:T(8,128)(2,1)}, bf16[2,2,3,256,128]{4,3,2,1,0:T(8,128)(2,1)}, u32[]{:S(2)}, u32[]{:S(2)}) %collective-permute-start.7) | collective-permute-done | bytes 786464 | tf_op jit(solution)/shard_map/ppermute | solution.py:20
  45.7 4.4 %shard_map.79 = bf16[2,1536,256]{2,1,0:T(8,128)(2,1)} custom-call(s32[3]{0:T(128)} %select_reduce_fusion.slot_ref, bf16[6,2,3,256,128]{4,3,2,1,0:T(8,128)(2,1)} %field_ref.7, bf16[2,2,3,256,128]{4,3,2,1,0:T(8,128)(2,1)} %collective-permute-done.7.near_ref, f32[6,3,2,3,3,128]{5,4,3,2,1,0:T(4,128)} %copy.38.link_ref, ...), custom_call_target="tpu_custom_call" | custom-call | tf_op jit(solution)/shard_map/pallas_call | solution.py:147
  55.7 6.4 %collective-permute-done.13.near_ref = bf16[2,2,3,256,128]{4,3,2,1,0:T(8,128)(2,1)} collective-permute-done((bf16[2,2,3,256,128]{4,3,2,1,0:T(8,128)(2,1)}, bf16[2,2,3,256,128]{4,3,2,1,0:T(8,128)(2,1)}, u32[]{:S(2)}, u32[]{:S(2)}) %collective-permute-start.13) | collective-permute-done | bytes 786464 | tf_op jit(solution)/shard_map/ppermute | solution.py:20
  62.2 4.4 %shard_map.80 = bf16[2,1536,256]{2,1,0:T(8,128)(2,1)} custom-call(s32[3]{0:T(128)} %select_reduce_fusion.slot_ref, bf16[6,2,3,256,128]{4,3,2,1,0:T(8,128)(2,1)} %field_ref.7, bf16[2,2,3,256,128]{4,3,2,1,0:T(8,128)(2,1)} %collective-permute-done.13.near_ref, f32[6,3,2,3,3,128]{5,4,3,2,1,0:T(4,128)} %copy.38.link_ref, ...), custom_call_target="tpu_custom_call" | custom-call | tf_op jit(solution)/shard_map/pallas_call | solution.py:147
  70.2 4.4 %collective-permute-start.5 = (bf16[2,96,256]{2,1,0:T(8,128)(2,1)S(1)}, bf16[2,96,256]{2,1,0:T(8,128)(2,1)S(1)}, u32[]{:S(2)}, u32[]{:S(2)}) collective-permute-start(bf16[2,96,256]{2,1,0:T(8,128)(2,1)S(1)} %get-tuple-element.41), channel_id=1, source_target_pairs={{8,0},{12,4},{0,8},{4,12},{9,1},{13,5},{1,9},{5,13},{10,2},{14,6},... | collective-permute-start | bytes 294920 | tf_op jit(solution)/shard_map/ppermute | solution.py:20
  76.1 2.4 %collective-permute-start.9 = (bf16[2,4,96,256]{3,2,1,0:T(8,128)(2,1)S(1)}, bf16[2,4,96,256]{3,2,1,0:T(8,128)(2,1)S(1)}, u32[]{:S(2)}, u32[]{:S(2)}) collective-permute-start(bf16[2,4,96,256]{3,2,1,0:T(8,128)(2,1)S(1)} %fusion.1), channel_id=1, source_target_pairs={{0,2},{1,3},{2,0},{3,1},{4,6},{5,7},{6,4},{7,5},{8,10},{9,11},{10,... | collective-permute-start | bytes 1179656 | tf_op jit(solution)/shard_map/ppermute | solution.py:24
  79.0 2.4 %collective-permute-done.5 = bf16[2,96,256]{2,1,0:T(8,128)(2,1)S(1)} collective-permute-done((bf16[2,96,256]{2,1,0:T(8,128)(2,1)S(1)}, bf16[2,96,256]{2,1,0:T(8,128)(2,1)S(1)}, u32[]{:S(2)}, u32[]{:S(2)}) %collective-permute-start.5) | collective-permute-done | bytes 98336 | tf_op jit(solution)/shard_map/ppermute | solution.py:20
  81.4 7.1 %collective-permute-done.9 = bf16[2,4,96,256]{3,2,1,0:T(8,128)(2,1)S(1)} collective-permute-done((bf16[2,4,96,256]{3,2,1,0:T(8,128)(2,1)S(1)}, bf16[2,4,96,256]{3,2,1,0:T(8,128)(2,1)S(1)}, u32[]{:S(2)}, u32[]{:S(2)}) %collective-permute-start.9) | collective-permute-done | bytes 393248 | tf_op jit(solution)/shard_map/ppermute | solution.py:24
  90.7 2.4 %collective-permute-start.12 = (bf16[2,96,256]{2,1,0:T(8,128)(2,1)S(1)}, bf16[2,96,256]{2,1,0:T(8,128)(2,1)S(1)}, u32[]{:S(2)}, u32[]{:S(2)}) collective-permute-start(bf16[2,96,256]{2,1,0:T(8,128)(2,1)S(1)} %get-tuple-element.43), channel_id=1, source_target_pairs={{4,0},{8,4},{12,8},{0,12},{5,1},{9,5},{13,9},{1,13},{6,2},{10,6},{... | collective-permute-start | bytes 294920 | tf_op jit(solution)/shard_map/ppermute | solution.py:20
  93.2 2.6 %collective-permute-done.15 = bf16[2,4,96,256]{3,2,1,0:T(8,128)(2,1)S(1)} collective-permute-done((bf16[2,4,96,256]{3,2,1,0:T(8,128)(2,1)S(1)}, bf16[2,4,96,256]{3,2,1,0:T(8,128)(2,1)S(1)}, u32[]{:S(2)}, u32[]{:S(2)}) %collective-permute-start.15) | collective-permute-done | bytes 393248 | tf_op jit(solution)/shard_map/ppermute | solution.py:24
  97.9 2.4 %collective-permute-start.18 = (bf16[2,96,256]{2,1,0:T(8,128)(2,1)S(1)}, bf16[2,96,256]{2,1,0:T(8,128)(2,1)S(1)}, u32[]{:S(2)}, u32[]{:S(2)}) collective-permute-start(bf16[2,96,256]{2,1,0:T(8,128)(2,1)S(1)} %get-tuple-element.46), channel_id=1, source_target_pairs={{4,0},{8,4},{12,8},{0,12},{5,1},{9,5},{13,9},{1,13},{6,2},{10,6},{... | collective-permute-start | bytes 294920 | tf_op jit(solution)/shard_map/ppermute | solution.py:20
  100.4 3.2 %collective-permute-done.16 = bf16[2,96,256]{2,1,0:T(8,128)(2,1)S(1)} collective-permute-done((bf16[2,96,256]{2,1,0:T(8,128)(2,1)S(1)}, bf16[2,96,256]{2,1,0:T(8,128)(2,1)S(1)}, u32[]{:S(2)}, u32[]{:S(2)}) %collective-permute-start.16) | collective-permute-done | bytes 98336 | tf_op jit(solution)/shard_map/ppermute | solution.py:20
  103.6 2.4 %collective-permute-done.17 = bf16[2,96,256]{2,1,0:T(8,128)(2,1)S(1)} collective-permute-done((bf16[2,96,256]{2,1,0:T(8,128)(2,1)S(1)}, bf16[2,96,256]{2,1,0:T(8,128)(2,1)S(1)}, u32[]{:S(2)}, u32[]{:S(2)}) %collective-permute-start.17) | collective-permute-done | bytes 98336 | tf_op jit(solution)/shard_map/ppermute | solution.py:20
  106.9 2.3 %collective-permute-start.19 = (bf16[2,96,256]{2,1,0:T(8,128)(2,1)S(1)}, bf16[2,96,256]{2,1,0:T(8,128)(2,1)S(1)}, u32[]{:S(2)}, u32[]{:S(2)}) collective-permute-start(bf16[2,96,256]{2,1,0:T(8,128)(2,1)S(1)} %get-tuple-element.38), channel_id=1, source_target_pairs={{12,0},{0,4},{4,8},{8,12},{13,1},{1,5},{5,9},{9,13},{14,2},{2,6},{... | collective-permute-start | bytes 294920 | tf_op jit(solution)/shard_map/ppermute | solution.py:20
  111.6 2.7 %collective-permute-done.19 = bf16[2,96,256]{2,1,0:T(8,128)(2,1)S(1)} collective-permute-done((bf16[2,96,256]{2,1,0:T(8,128)(2,1)S(1)}, bf16[2,96,256]{2,1,0:T(8,128)(2,1)S(1)}, u32[]{:S(2)}, u32[]{:S(2)}) %collective-permute-start.19) | collective-permute-done | bytes 98336 | tf_op jit(solution)/shard_map/ppermute | solution.py:20
  114.4 2.9 %collective-permute-done.20 = bf16[2,96,256]{2,1,0:T(8,128)(2,1)S(1)} collective-permute-done((bf16[2,96,256]{2,1,0:T(8,128)(2,1)S(1)}, bf16[2,96,256]{2,1,0:T(8,128)(2,1)S(1)}, u32[]{:S(2)}, u32[]{:S(2)}) %collective-permute-start.20) | collective-permute-done | bytes 98336 | tf_op jit(solution)/shard_map/ppermute | solution.py:20
  121.1 7.7 %collective-permute-done.22 = bf16[4,2,96,256]{3,2,1,0:T(8,128)(2,1)S(1)} collective-permute-done((bf16[4,2,96,256]{3,2,1,0:T(8,128)(2,1)S(1)}, bf16[4,2,96,256]{3,2,1,0:T(8,128)(2,1)S(1)}, u32[]{:S(2)}, u32[]{:S(2)}) %collective-permute-start.22) | collective-permute-done | bytes 393248 | tf_op jit(solution)/shard_map/ppermute | solution.py:20
  130.1 6.8 %collective-permute-done.24 = bf16[4,2,96,256]{3,2,1,0:T(8,128)(2,1)S(1)} collective-permute-done((bf16[4,2,96,256]{3,2,1,0:T(8,128)(2,1)S(1)}, bf16[4,2,96,256]{3,2,1,0:T(8,128)(2,1)S(1)}, u32[]{:S(2)}, u32[]{:S(2)}) %collective-permute-start.24) | collective-permute-done | bytes 393248 | tf_op jit(solution)/shard_map/ppermute | solution.py:20
  139.3 6.6 %shard_map.81 = f32[3,2,256]{2,1,0:T(2,128)} custom-call(bf16[2,3,2,256,256]{4,3,2,1,0:T(8,128)(2,1)} %bitcast.121, bf16[2,3,2,256,256]{4,3,2,1,0:T(8,128)(2,1)} %bitcast.122, bf16[512,1024]{1,0:T(8,128)(2,1)} %bitcast.130, bf16[2048,512]{1,0:T(8,128)(2,1)} %maximum_maximum_fusion.wide_ref), custom_call_target="tpu_custom_call" | custom-call | tf_op jit(solution)/shard_map/pallas_call | solution.py:193
  (116 shorter events, 41.5 us)
Async XLA Ops:
  3.4 15.6 %collective-permute-start.1 = (bf16[6,2,3,256,8]{3,4,2,1,0:T(8,128)(2,1)}, bf16[6,2,3,256,8]{3,4,2,1,0:T(8,128)(2,1)S(1)}, u32[]{:S(2)}, u32[]{:S(2)}) collective-permute-start(bf16[6,2,3,256,8]{3,4,2,1,0:T(8,128)(2,1)} %copy.46), channel_id=1, source_target_pairs={{0,1},{1,0},{2,3},{3,2},{4,5},{5,4},{6,7},{7,6},{8,9},{9,8},{10,11... | collective-permute-start | bytes 442376 | tf_op jit(solution)/shard_map/ppermute | solution.py:24
  5.3 28.0 %collective-permute-start = (bf16[2,2,3,256,128]{4,3,2,1,0:T(8,128)(2,1)S(1)}, bf16[2,2,3,256,128]{4,3,2,1,0:T(8,128)(2,1)}, u32[]{:S(2)}, u32[]{:S(2)}) collective-permute-start(bf16[2,2,3,256,128]{4,3,2,1,0:T(8,128)(2,1)S(1)} %get-tuple-element.30), channel_id=1, source_target_pairs={{2,0},{3,1},{4,2},{5,3},{6,4},{7,5},{8,6},{9,7},{10,8},{11,9},{12,... | collective-permute-start | bytes 2359304 | tf_op jit(solution)/shard_map/ppermute | solution.py:20
  10.9 34.8 %collective-permute-start.7 = (bf16[2,2,3,256,128]{4,3,2,1,0:T(8,128)(2,1)}, bf16[2,2,3,256,128]{4,3,2,1,0:T(8,128)(2,1)}, u32[]{:S(2)}, u32[]{:S(2)}) collective-permute-start(bf16[2,2,3,256,128]{4,3,2,1,0:T(8,128)(2,1)} %get-tuple-element.31), channel_id=1, source_target_pairs={{2,0},{3,1},{4,2},{5,3},{6,4},{7,5},{8,6},{9,7},{10,8},{11,9},{12,... | collective-permute-start | bytes 2359304 | tf_op jit(solution)/shard_map/ppermute | solution.py:20
  11.4 50.8 %collective-permute-start.13 = (bf16[2,2,3,256,128]{4,3,2,1,0:T(8,128)(2,1)}, bf16[2,2,3,256,128]{4,3,2,1,0:T(8,128)(2,1)}, u32[]{:S(2)}, u32[]{:S(2)}) collective-permute-start(bf16[2,2,3,256,128]{4,3,2,1,0:T(8,128)(2,1)} %get-tuple-element.32), channel_id=1, source_target_pairs={{2,0},{3,1},{4,2},{5,3},{6,4},{7,5},{8,6},{9,7},{10,8},{11,9},{12,... | collective-permute-start | bytes 2359304 | tf_op jit(solution)/shard_map/ppermute | solution.py:20
  51.4 10.7 %collective-permute-start.8 = (bf16[2,4,2,96,256]{4,3,2,1,0:T(8,128)(2,1)S(1)}, bf16[2,4,2,96,256]{4,3,2,1,0:T(8,128)(2,1)}, u32[]{:S(2)}, u32[]{:S(2)}) collective-permute-start(bf16[2,4,2,96,256]{4,3,2,1,0:T(8,128)(2,1)S(1)} %dynamic-slice_bitcast_fusion.1), channel_id=1, source_target_pairs={{0,1},{1,0},{2,3},{3,2},{4,5},{5,4},{6,7},{7,6},{8,9},{9,8},{10,11... | collective-permute-start | bytes 2359304 | tf_op jit(solution)/shard_map/ppermute | solution.py:24
  53.9 14.5 %collective-permute-start.3 = (bf16[2,4,96,256]{3,2,1,0:T(8,128)(2,1)}, bf16[2,4,96,256]{3,2,1,0:T(8,128)(2,1)S(1)}, u32[]{:S(2)}, u32[]{:S(2)}) collective-permute-start(bf16[2,4,96,256]{3,2,1,0:T(8,128)(2,1)} %fusion), channel_id=1, source_target_pairs={{0,2},{1,3},{2,0},{3,1},{4,6},{5,7},{6,4},{7,5},{8,10},{9,11},{10,... | collective-permute-start | bytes 1179656 | tf_op jit(solution)/shard_map/ppermute | solution.py:24
  67.7 10.9 %collective-permute-start.14 = (bf16[2,4,2,96,256]{4,3,2,1,0:T(8,128)(2,1)S(1)}, bf16[2,4,2,96,256]{4,3,2,1,0:T(8,128)(2,1)S(1)}, u32[]{:S(2)}, u32[]{:S(2)}) collective-permute-start(bf16[2,4,2,96,256]{4,3,2,1,0:T(8,128)(2,1)S(1)} %dynamic-slice_bitcast_fusion), channel_id=1, source_target_pairs={{0,1},{1,0},{2,3},{3,2},{4,5},{5,4},{6,7},{7,6},{8,9},{9,8},{10,11... | collective-permute-start | bytes 2359304 | tf_op jit(solution)/shard_map/ppermute | solution.py:24
  68.6 10.4 %collective-permute-start.4 = (bf16[2,96,256]{2,1,0:T(8,128)(2,1)S(1)}, bf16[2,96,256]{2,1,0:T(8,128)(2,1)S(1)}, u32[]{:S(2)}, u32[]{:S(2)}) collective-permute-start(bf16[2,96,256]{2,1,0:T(8,128)(2,1)S(1)} %get-tuple-element.39), channel_id=1, source_target_pairs={{12,0},{0,4},{4,8},{8,12},{13,1},{1,5},{5,9},{9,13},{14,2},{2,6},{... | collective-permute-start | bytes 294920 | tf_op jit(solution)/shard_map/ppermute | solution.py:20
  70.2 11.1 %collective-permute-start.5 = (bf16[2,96,256]{2,1,0:T(8,128)(2,1)S(1)}, bf16[2,96,256]{2,1,0:T(8,128)(2,1)S(1)}, u32[]{:S(2)}, u32[]{:S(2)}) collective-permute-start(bf16[2,96,256]{2,1,0:T(8,128)(2,1)S(1)} %get-tuple-element.41), channel_id=1, source_target_pairs={{8,0},{12,4},{0,8},{4,12},{9,1},{13,5},{1,9},{5,13},{10,2},{14,6},... | collective-permute-start | bytes 294920 | tf_op jit(solution)/shard_map/ppermute | solution.py:20
  74.6 6.7 %collective-permute-start.6 = (bf16[2,96,256]{2,1,0:T(8,128)(2,1)S(1)}, bf16[2,96,256]{2,1,0:T(8,128)(2,1)S(1)}, u32[]{:S(2)}, u32[]{:S(2)}) collective-permute-start(bf16[2,96,256]{2,1,0:T(8,128)(2,1)S(1)} %get-tuple-element.40), channel_id=1, source_target_pairs={{4,0},{8,4},{12,8},{0,12},{5,1},{9,5},{13,9},{1,13},{6,2},{10,6},{... | collective-permute-start | bytes 294920 | tf_op jit(solution)/shard_map/ppermute | solution.py:20
  76.1 12.4 %collective-permute-start.9 = (bf16[2,4,96,256]{3,2,1,0:T(8,128)(2,1)S(1)}, bf16[2,4,96,256]{3,2,1,0:T(8,128)(2,1)S(1)}, u32[]{:S(2)}, u32[]{:S(2)}) collective-permute-start(bf16[2,4,96,256]{3,2,1,0:T(8,128)(2,1)S(1)} %fusion.1), channel_id=1, source_target_pairs={{0,2},{1,3},{2,0},{3,1},{4,6},{5,7},{6,4},{7,5},{8,10},{9,11},{10,... | collective-permute-start | bytes 1179656 | tf_op jit(solution)/shard_map/ppermute | solution.py:24
  78.8 16.9 %collective-permute-start.15 = (bf16[2,4,96,256]{3,2,1,0:T(8,128)(2,1)S(1)}, bf16[2,4,96,256]{3,2,1,0:T(8,128)(2,1)S(1)}, u32[]{:S(2)}, u32[]{:S(2)}) collective-permute-start(bf16[2,4,96,256]{3,2,1,0:T(8,128)(2,1)S(1)} %fusion.2), channel_id=1, source_target_pairs={{0,2},{1,3},{2,0},{3,1},{4,6},{5,7},{6,4},{7,5},{8,10},{9,11},{10,... | collective-permute-start | bytes 1179656 | tf_op jit(solution)/shard_map/ppermute | solution.py:24
  88.7 9.2 %collective-permute-start.10 = (bf16[2,96,256]{2,1,0:T(8,128)(2,1)S(1)}, bf16[2,96,256]{2,1,0:T(8,128)(2,1)S(1)}, u32[]{:S(2)}, u32[]{:S(2)}) collective-permute-start(bf16[2,96,256]{2,1,0:T(8,128)(2,1)S(1)} %get-tuple-element.42), channel_id=1, source_target_pairs={{12,0},{0,4},{4,8},{8,12},{13,1},{1,5},{5,9},{9,13},{14,2},{2,6},{... | collective-permute-start | bytes 294920 | tf_op jit(solution)/shard_map/ppermute | solution.py:20
  90.7 9.6 %collective-permute-start.11 = (bf16[2,96,256]{2,1,0:T(8,128)(2,1)S(1)}, bf16[2,96,256]{2,1,0:T(8,128)(2,1)S(1)}, u32[]{:S(2)}, u32[]{:S(2)}) collective-permute-start(bf16[2,96,256]{2,1,0:T(8,128)(2,1)S(1)} %get-tuple-element.44), channel_id=1, source_target_pairs={{8,0},{12,4},{0,8},{4,12},{9,1},{13,5},{1,9},{5,13},{10,2},{14,6},... | collective-permute-start | bytes 294920 | tf_op jit(solution)/shard_map/ppermute | solution.py:20
  90.7 9.6 %collective-permute-start.12 = (bf16[2,96,256]{2,1,0:T(8,128)(2,1)S(1)}, bf16[2,96,256]{2,1,0:T(8,128)(2,1)S(1)}, u32[]{:S(2)}, u32[]{:S(2)}) collective-permute-start(bf16[2,96,256]{2,1,0:T(8,128)(2,1)S(1)} %get-tuple-element.43), channel_id=1, source_target_pairs={{4,0},{8,4},{12,8},{0,12},{5,1},{9,5},{13,9},{1,13},{6,2},{10,6},{... | collective-permute-start | bytes 294920 | tf_op jit(solution)/shard_map/ppermute | solution.py:20
  95.9 7.7 %collective-permute-start.16 = (bf16[2,96,256]{2,1,0:T(8,128)(2,1)S(1)}, bf16[2,96,256]{2,1,0:T(8,128)(2,1)S(1)}, u32[]{:S(2)}, u32[]{:S(2)}) collective-permute-start(bf16[2,96,256]{2,1,0:T(8,128)(2,1)S(1)} %get-tuple-element.45), channel_id=1, source_target_pairs={{12,0},{0,4},{4,8},{8,12},{13,1},{1,5},{5,9},{9,13},{14,2},{2,6},{... | collective-permute-start | bytes 294920 | tf_op jit(solution)/shard_map/ppermute | solution.py:20
  97.6 8.4 %collective-permute-start.17 = (bf16[2,96,256]{2,1,0:T(8,128)(2,1)S(1)}, bf16[2,96,256]{2,1,0:T(8,128)(2,1)S(1)}, u32[]{:S(2)}, u32[]{:S(2)}) collective-permute-start(bf16[2,96,256]{2,1,0:T(8,128)(2,1)S(1)} %get-tuple-element.47), channel_id=1, source_target_pairs={{8,0},{12,4},{0,8},{4,12},{9,1},{13,5},{1,9},{5,13},{10,2},{14,6},... | collective-permute-start | bytes 294920 | tf_op jit(solution)/shard_map/ppermute | solution.py:20
  97.9 8.1 %collective-permute-start.18 = (bf16[2,96,256]{2,1,0:T(8,128)(2,1)S(1)}, bf16[2,96,256]{2,1,0:T(8,128)(2,1)S(1)}, u32[]{:S(2)}, u32[]{:S(2)}) collective-permute-start(bf16[2,96,256]{2,1,0:T(8,128)(2,1)S(1)} %get-tuple-element.46), channel_id=1, source_target_pairs={{4,0},{8,4},{12,8},{0,12},{5,1},{9,5},{13,9},{1,13},{6,2},{10,6},{... | collective-permute-start | bytes 294920 | tf_op jit(solution)/shard_map/ppermute | solution.py:20
  106.9 7.5 %collective-permute-start.19 = (bf16[2,96,256]{2,1,0:T(8,128)(2,1)S(1)}, bf16[2,96,256]{2,1,0:T(8,128)(2,1)S(1)}, u32[]{:S(2)}, u32[]{:S(2)}) collective-permute-start(bf16[2,96,256]{2,1,0:T(8,128)(2,1)S(1)} %get-tuple-element.38), channel_id=1, source_target_pairs={{12,0},{0,4},{4,8},{8,12},{13,1},{1,5},{5,9},{9,13},{14,2},{2,6},{... | collective-permute-start | bytes 294920 | tf_op jit(solution)/shard_map/ppermute | solution.py:20
  109.2 8.0 %collective-permute-start.20 = (bf16[2,96,256]{2,1,0:T(8,128)(2,1)S(1)}, bf16[2,96,256]{2,1,0:T(8,128)(2,1)S(1)}, u32[]{:S(2)}, u32[]{:S(2)}) collective-permute-start(bf16[2,96,256]{2,1,0:T(8,128)(2,1)S(1)} %get-tuple-element.37), channel_id=1, source_target_pairs={{8,0},{12,4},{0,8},{4,12},{9,1},{13,5},{1,9},{5,13},{10,2},{14,6},... | collective-permute-start | bytes 294920 | tf_op jit(solution)/shard_map/ppermute | solution.py:20
  110.5 6.7 %collective-permute-start.21 = (bf16[2,96,256]{2,1,0:T(8,128)(2,1)S(1)}, bf16[2,96,256]{2,1,0:T(8,128)(2,1)S(1)}, u32[]{:S(2)}, u32[]{:S(2)}) collective-permute-start(bf16[2,96,256]{2,1,0:T(8,128)(2,1)S(1)} %get-tuple-element.36), channel_id=1, source_target_pairs={{4,0},{8,4},{12,8},{0,12},{5,1},{9,5},{13,9},{1,13},{6,2},{10,6},{... | collective-permute-start | bytes 294920 | tf_op jit(solution)/shard_map/ppermute | solution.py:20
  118.0 10.9 %collective-permute-start.22 = (bf16[4,2,96,256]{3,2,1,0:T(8,128)(2,1)S(1)}, bf16[4,2,96,256]{3,2,1,0:T(8,128)(2,1)S(1)}, u32[]{:S(2)}, u32[]{:S(2)}) collective-permute-start(bf16[4,2,96,256]{3,2,1,0:T(8,128)(2,1)S(1)} %broadcast_select_fusion), channel_id=1, source_target_pairs={{3,0},{0,1},{1,2},{2,3},{7,4},{4,5},{5,6},{6,7},{11,8},{8,9},{9,10... | collective-permute-start | bytes 1179656 | tf_op jit(solution)/shard_map/ppermute | solution.py:20
  118.1 12.0 %collective-permute-start.23 = (bf16[4,2,96,256]{3,2,1,0:T(8,128)(2,1)S(1)}, bf16[4,2,96,256]{3,2,1,0:T(8,128)(2,1)S(1)}, u32[]{:S(2)}, u32[]{:S(2)}) collective-permute-start(bf16[4,2,96,256]{3,2,1,0:T(8,128)(2,1)S(1)} %broadcast_select_fusion), channel_id=1, source_target_pairs={{2,0},{3,1},{0,2},{1,3},{6,4},{7,5},{4,6},{5,7},{10,8},{11,9},{8,1... | collective-permute-start | bytes 1179656 | tf_op jit(solution)/shard_map/ppermute | solution.py:20
  119.6 17.3 %collective-permute-start.24 = (bf16[4,2,96,256]{3,2,1,0:T(8,128)(2,1)S(1)}, bf16[4,2,96,256]{3,2,1,0:T(8,128)(2,1)S(1)}, u32[]{:S(2)}, u32[]{:S(2)}) collective-permute-start(bf16[4,2,96,256]{3,2,1,0:T(8,128)(2,1)S(1)} %broadcast_select_fusion), channel_id=1, source_target_pairs={{1,0},{2,1},{3,2},{0,3},{5,4},{6,5},{7,6},{4,7},{9,8},{10,9},{11,1... | collective-permute-start | bytes 1179656 | tf_op jit(solution)/shard_map/ppermute | solution.py:20
  (12 other events, 99.7 us)

commit v19 on v18

--- a/solution.py
+++ b/solution.py
@@ -228,30 +228,39 @@
     slot_of, left, first_partial = local_sums(eigenvectors, gauge_links, row_in, directions, angle, scale)
     partial_chunks = []
     core = member % 2
+    side = member // 2
     swapped_chunks = []
+    chunk_sums = []
+    side_chunks = []
     for half in range(halves):
         first, far_part = far_tile[half]
-        if swapped_chunks:
-            far_part = lax.optimization_barrier((far_part, swapped_chunks[-1]))[0]
+        ties = []
+        if half >= 1 and swapped_chunks:
+            ties.append(swapped_chunks[half - 1])
+        if half >= 2 and side_chunks:
+            ties.append(side_chunks[half - 2])
+        if ties:
+            far_part = lax.optimization_barrier((far_part,) + tuple(ties))[0]
         chunk_partial = second_pass(slot_of, eigenvectors, gauge_links, left, first_partial, first, far_part, scale)
         partial_chunks.append(chunk_partial)
         if count_slabs <= 8:
             part_blocks = chunk_partial.reshape(span, count_slabs, 2, 2, -1, count_ev)
             send = lax.dynamic_index_in_dim(part_blocks, 1 - core, 3, keepdims=False)
-            swapped_chunks.append(swapped(send, "member", 0))
+            received = swapped(send, "member", 0)
+            swapped_chunks.append(received)
+            keep = lax.dynamic_index_in_dim(part_blocks, core, 3, keepdims=False).astype(jnp.float32)
+            chunk = keep + received.astype(jnp.float32)
+            chunk_sums.append(chunk)
+            send = lax.dynamic_index_in_dim(chunk, 1 - side, 2, keepdims=False).astype(jnp.bfloat16)
+            side_chunks.append(swapped(send, "member", 1))
     partial = jnp.concatenate(partial_chunks, 0)
     rows = partial.shape[1] // nspace
     if count_slabs <= 8:
         slab = lax.axis_index("slab")
-        side = member // 2
         own_parts = []
         for half in range(halves):
-            part_blocks = partial_chunks[half].reshape(span, count_slabs, 2, 2, rows, count_ev)
-            keep = lax.dynamic_index_in_dim(part_blocks, core, 3, keepdims=False).astype(jnp.float32)
-            chunk = keep + swapped_chunks[half].astype(jnp.float32)
-            keep = lax.dynamic_index_in_dim(chunk, side, 2, keepdims=False)
-            send = lax.dynamic_index_in_dim(chunk, 1 - side, 2, keepdims=False).astype(jnp.bfloat16)
-            slab_sum = keep + swapped(send, "member", 1).astype(jnp.float32)
+            keep = lax.dynamic_index_in_dim(chunk_sums[half], side, 2, keepdims=False)
+            slab_sum = keep + side_chunks[half].astype(jnp.float32)
             slab_part = slab_sum.astype(jnp.bfloat16)
             total = lax.dynamic_index_in_dim(slab_sum, slab, 1, keepdims=False)
             for shift in range(1, count_slabs):

time: 148 us -> 155 us (1.047)
  waiting for transfers between devices: 50.6 us -> 55.6 us
    ppermute x7, waiting for transfers between devices: 10.4 us -> 16.1 us  [swapped(): lax.ppermute(value, axis, [(i, i ^ 1 << bit) for i in range(lax.axis_size...]
    unnamed x24 -> x28, local copies, waits for them, and re-layouts: 3.79 us -> 3.57 us
  transfers between devices with their start and end apart: 25 -> 25, of which waited for: 13 -> 13; matrix products, arithmetic and copies ran while one was open for 15% -> 15% of each run, Pallas kernels for 16% -> 13%
where the time goes in v19:
time: 155 us; the launch traced here: 154 us
  waiting for transfers between devices  55.6 us (36%)
  starting transfers between devices  33.9 us (22%)
  Pallas kernels  30.7 us (20%)
  local copies, waits for them, and re-layouts  22.3 us (14%)
  other arithmetic  9.83 us (6%)
  between operations  1.69 us (1%)
    ppermute x18, waiting for transfers between devices, shifted(): return lax.ppermute(block, axis, route)  39.5 us
    ppermute x18, starting transfers between devices, shifted(): return lax.ppermute(block, axis, route)  30.4 us
    ppermute x7, waiting for transfers between devices, swapped(): lax.ppermute(value, axis, [(i, i ^ 1 << bit) for i in range(lax.axis_size...  16.1 us
    pallas_call x3, Pallas kernels, second_pass(): pl.pallas_call(functools.partial(sums_kernel, scale=scale, course_list=(0...  13.1 us
    pallas_call x1, Pallas kernels, local_sums(): pl.pallas_call(functools.partial(sums_kernel, scale=scale, course_list=ne...  11 us
    pallas_call x1, Pallas kernels, contract_panel(): pl.pallas_call(panel_kernel, grid=(count_ops,), in_specs=[pl.BlockSpec((1...  6.62 us
    squeeze x3, local copies, waits for them, and re-layouts, body(): send = lax.dynamic_index_in_dim(part_blocks, 1 - core, 3, keepdims=False)  5.55 us
    unnamed x28, local copies, waits for them, and re-layouts  3.57 us
  transfers between devices with their start and end apart: 25, of which 13 were waited for; matrix products, arithmetic and copies ran while one was open for 15% of the time, Pallas kernels for 13%

profile of v19, /device:TPU:0, one launch (start us, length us, event | category | flops | bytes accessed | tf_op | source)
XLA Modules:
  0.0 154.0 jit_solution(17030617848221459419)
XLA Ops:
  0.7 2.8 %copy.46 = bf16[6,2,3,256,8]{3,4,2,1,0:T(8,128)(2,1)} copy(bf16[6,2,3,256,8]{4,3,2,1,0:T(8,128)(2,1)} %bitcast.120) | data formatting | bytes 294912
  5.3 5.6 %collective-permute-start = (bf16[2,2,3,256,128]{4,3,2,1,0:T(8,128)(2,1)S(1)}, bf16[2,2,3,256,128]{4,3,2,1,0:T(8,128)(2,1)}, u32[]{:S(2)}, u32[]{:S(2)}) collective-permute-start(bf16[2,2,3,256,128]{4,3,2,1,0:T(8,128)(2,1)S(1)} %get-tuple-element.30), channel_id=1, source_target_pairs={{2,0},{3,1},{4,2},{5,3},{6,4},{7,5},{8,6},{9,7},{10,8},{11,9},{12,... | collective-permute-start | bytes 2359304 | tf_op jit(solution)/shard_map/ppermute | solution.py:20
  22.3 11.0 %shard_map.77 = (bf16[6,1536,256]{2,1,0:T(8,128)(2,1)}, bf16[6,512,768]{2,1,0:T(8,128)(2,1)}) custom-call(s32[3]{0:T(128)} %select_reduce_fusion.slot_ref, bf16[6,2,3,256,128]{4,3,2,1,0:T(8,128)(2,1)} %field_ref.7, bf16[6,2,3,256,128]{4,3,2,1,0:T(8,128)(2,1)} %pad.6.near_ref, f32[6,3,2,3,3,128]{5,4,3,2,1,0:T(4,128)} %copy.38.link_ref, ...), custom_call_target="tpu_custom_call" | custom-call | tf_op jit(solution)/shard_map/pallas_call | solution.py:118
  33.3 4.4 %shard_map.78 = bf16[2,1536,256]{2,1,0:T(8,128)(2,1)} custom-call(s32[3]{0:T(128)} %select_reduce_fusion.slot_ref, bf16[6,2,3,256,128]{4,3,2,1,0:T(8,128)(2,1)} %field_ref.7, bf16[2,2,3,256,128]{4,3,2,1,0:T(8,128)(2,1)} %collective-permute-done.near_ref, f32[6,3,2,3,3,128]{5,4,3,2,1,0:T(4,128)} %copy.38.link_ref, ...), custom_call_target="tpu_custom_call" | custom-call | tf_op jit(solution)/shard_map/pallas_call | solution.py:147
  41.5 4.3 %collective-permute-done.7.near_ref = bf16[2,2,3,256,128]{4,3,2,1,0:T(8,128)(2,1)} collective-permute-done((bf16[2,2,3,256,128]{4,3,2,1,0:T(8,128)(2,1)}, bf16[2,2,3,256,128]{4,3,2,1,0:T(8,128)(2,1)}, u32[]{:S(2)}, u32[]{:S(2)}) %collective-permute-start.7) | collective-permute-done | bytes 786464 | tf_op jit(solution)/shard_map/ppermute | solution.py:20
  45.7 4.4 %shard_map.79 = bf16[2,1536,256]{2,1,0:T(8,128)(2,1)} custom-call(s32[3]{0:T(128)} %select_reduce_fusion.slot_ref, bf16[6,2,3,256,128]{4,3,2,1,0:T(8,128)(2,1)} %field_ref.7, bf16[2,2,3,256,128]{4,3,2,1,0:T(8,128)(2,1)} %collective-permute-done.7.near_ref, f32[6,3,2,3,3,128]{5,4,3,2,1,0:T(4,128)} %copy.38.link_ref, ...), custom_call_target="tpu_custom_call" | custom-call | tf_op jit(solution)/shard_map/pallas_call | solution.py:147
  56.9 5.2 %collective-permute-done.13.near_ref = bf16[2,2,3,256,128]{4,3,2,1,0:T(8,128)(2,1)} collective-permute-done((bf16[2,2,3,256,128]{4,3,2,1,0:T(8,128)(2,1)}, bf16[2,2,3,256,128]{4,3,2,1,0:T(8,128)(2,1)}, u32[]{:S(2)}, u32[]{:S(2)}) %collective-permute-start.13) | collective-permute-done | bytes 786464 | tf_op jit(solution)/shard_map/ppermute | solution.py:20
  62.2 6.3 %collective-permute-done.3 = bf16[2,4,96,256]{3,2,1,0:T(8,128)(2,1)S(1)} collective-permute-done((bf16[2,4,96,256]{3,2,1,0:T(8,128)(2,1)}, bf16[2,4,96,256]{3,2,1,0:T(8,128)(2,1)S(1)}, u32[]{:S(2)}, u32[]{:S(2)}) %collective-permute-start.3) | collective-permute-done | bytes 393248 | tf_op jit(solution)/shard_map/ppermute | solution.py:24
  68.5 4.3 %shard_map.80 = bf16[2,1536,256]{2,1,0:T(8,128)(2,1)} custom-call(s32[3]{0:T(128)} %select_reduce_fusion.slot_ref, bf16[6,2,3,256,128]{4,3,2,1,0:T(8,128)(2,1)} %field_ref.7, bf16[2,2,3,256,128]{4,3,2,1,0:T(8,128)(2,1)} %collective-permute-done.13.near_ref, f32[6,3,2,3,3,128]{5,4,3,2,1,0:T(4,128)} %copy.38.link_ref, ...), custom_call_target="tpu_custom_call" | custom-call | tf_op jit(solution)/shard_map/pallas_call | solution.py:147
  75.9 4.4 %collective-permute-start.5 = (bf16[2,96,256]{2,1,0:T(8,128)(2,1)S(1)}, bf16[2,96,256]{2,1,0:T(8,128)(2,1)S(1)}, u32[]{:S(2)}, u32[]{:S(2)}) collective-permute-start(bf16[2,96,256]{2,1,0:T(8,128)(2,1)S(1)} %get-tuple-element.41), channel_id=1, source_target_pairs={{8,0},{12,4},{0,8},{4,12},{9,1},{13,5},{1,9},{5,13},{10,2},{14,6},... | collective-permute-start | bytes 294920 | tf_op jit(solution)/shard_map/ppermute | solution.py:20
  81.8 2.4 %collective-permute-start.9 = (bf16[2,4,96,256]{3,2,1,0:T(8,128)(2,1)S(1)}, bf16[2,4,96,256]{3,2,1,0:T(8,128)(2,1)S(1)}, u32[]{:S(2)}, u32[]{:S(2)}) collective-permute-start(bf16[2,4,96,256]{3,2,1,0:T(8,128)(2,1)S(1)} %fusion.1), channel_id=1, source_target_pairs={{0,2},{1,3},{2,0},{3,1},{4,6},{5,7},{6,4},{7,5},{8,10},{9,11},{10,... | collective-permute-start | bytes 1179656 | tf_op jit(solution)/shard_map/ppermute | solution.py:24
  84.7 2.7 %collective-permute-done.5 = bf16[2,96,256]{2,1,0:T(8,128)(2,1)S(1)} collective-permute-done((bf16[2,96,256]{2,1,0:T(8,128)(2,1)S(1)}, bf16[2,96,256]{2,1,0:T(8,128)(2,1)S(1)}, u32[]{:S(2)}, u32[]{:S(2)}) %collective-permute-start.5) | collective-permute-done | bytes 98336 | tf_op jit(solution)/shard_map/ppermute | solution.py:20
  87.5 6.7 %collective-permute-done.9 = bf16[2,4,96,256]{3,2,1,0:T(8,128)(2,1)S(1)} collective-permute-done((bf16[2,4,96,256]{3,2,1,0:T(8,128)(2,1)S(1)}, bf16[2,4,96,256]{3,2,1,0:T(8,128)(2,1)S(1)}, u32[]{:S(2)}, u32[]{:S(2)}) %collective-permute-start.9) | collective-permute-done | bytes 393248 | tf_op jit(solution)/shard_map/ppermute | solution.py:24
  96.4 2.4 %collective-permute-start.12 = (bf16[2,96,256]{2,1,0:T(8,128)(2,1)S(1)}, bf16[2,96,256]{2,1,0:T(8,128)(2,1)S(1)}, u32[]{:S(2)}, u32[]{:S(2)}) collective-permute-start(bf16[2,96,256]{2,1,0:T(8,128)(2,1)S(1)} %get-tuple-element.43), channel_id=1, source_target_pairs={{4,0},{8,4},{12,8},{0,12},{5,1},{9,5},{13,9},{1,13},{6,2},{10,6},{... | collective-permute-start | bytes 294920 | tf_op jit(solution)/shard_map/ppermute | solution.py:20
  98.8 3.0 %collective-permute-done.15 = bf16[2,4,96,256]{3,2,1,0:T(8,128)(2,1)S(1)} collective-permute-done((bf16[2,4,96,256]{3,2,1,0:T(8,128)(2,1)S(1)}, bf16[2,4,96,256]{3,2,1,0:T(8,128)(2,1)S(1)}, u32[]{:S(2)}, u32[]{:S(2)}) %collective-permute-start.15) | collective-permute-done | bytes 393248 | tf_op jit(solution)/shard_map/ppermute | solution.py:24
  104.0 2.4 %collective-permute-start.18 = (bf16[2,96,256]{2,1,0:T(8,128)(2,1)S(1)}, bf16[2,96,256]{2,1,0:T(8,128)(2,1)S(1)}, u32[]{:S(2)}, u32[]{:S(2)}) collective-permute-start(bf16[2,96,256]{2,1,0:T(8,128)(2,1)S(1)} %get-tuple-element.46), channel_id=1, source_target_pairs={{4,0},{8,4},{12,8},{0,12},{5,1},{9,5},{13,9},{1,13},{6,2},{10,6},{... | collective-permute-start | bytes 294920 | tf_op jit(solution)/shard_map/ppermute | solution.py:20
  106.5 3.2 %collective-permute-done.16 = bf16[2,96,256]{2,1,0:T(8,128)(2,1)S(1)} collective-permute-done((bf16[2,96,256]{2,1,0:T(8,128)(2,1)S(1)}, bf16[2,96,256]{2,1,0:T(8,128)(2,1)S(1)}, u32[]{:S(2)}, u32[]{:S(2)}) %collective-permute-start.16) | collective-permute-done | bytes 98336 | tf_op jit(solution)/shard_map/ppermute | solution.py:20
  109.7 2.5 %collective-permute-done.17 = bf16[2,96,256]{2,1,0:T(8,128)(2,1)S(1)} collective-permute-done((bf16[2,96,256]{2,1,0:T(8,128)(2,1)S(1)}, bf16[2,96,256]{2,1,0:T(8,128)(2,1)S(1)}, u32[]{:S(2)}, u32[]{:S(2)}) %collective-permute-start.17) | collective-permute-done | bytes 98336 | tf_op jit(solution)/shard_map/ppermute | solution.py:20
  113.2 2.6 %collective-permute-start.19 = (bf16[2,96,256]{2,1,0:T(8,128)(2,1)S(1)}, bf16[2,96,256]{2,1,0:T(8,128)(2,1)S(1)}, u32[]{:S(2)}, u32[]{:S(2)}) collective-permute-start(bf16[2,96,256]{2,1,0:T(8,128)(2,1)S(1)} %get-tuple-element.38), channel_id=1, source_target_pairs={{12,0},{0,4},{4,8},{8,12},{13,1},{1,5},{5,9},{9,13},{14,2},{2,6},{... | collective-permute-start | bytes 294920 | tf_op jit(solution)/shard_map/ppermute | solution.py:20
  118.2 2.3 %collective-permute-done.19 = bf16[2,96,256]{2,1,0:T(8,128)(2,1)S(1)} collective-permute-done((bf16[2,96,256]{2,1,0:T(8,128)(2,1)S(1)}, bf16[2,96,256]{2,1,0:T(8,128)(2,1)S(1)}, u32[]{:S(2)}, u32[]{:S(2)}) %collective-permute-start.19) | collective-permute-done | bytes 98336 | tf_op jit(solution)/shard_map/ppermute | solution.py:20
  120.5 3.4 %collective-permute-done.20 = bf16[2,96,256]{2,1,0:T(8,128)(2,1)S(1)} collective-permute-done((bf16[2,96,256]{2,1,0:T(8,128)(2,1)S(1)}, bf16[2,96,256]{2,1,0:T(8,128)(2,1)S(1)}, u32[]{:S(2)}, u32[]{:S(2)}) %collective-permute-start.20) | collective-permute-done | bytes 98336 | tf_op jit(solution)/shard_map/ppermute | solution.py:20
  127.8 7.7 %collective-permute-done.22 = bf16[4,2,96,256]{3,2,1,0:T(8,128)(2,1)S(1)} collective-permute-done((bf16[4,2,96,256]{3,2,1,0:T(8,128)(2,1)S(1)}, bf16[4,2,96,256]{3,2,1,0:T(8,128)(2,1)S(1)}, u32[]{:S(2)}, u32[]{:S(2)}) %collective-permute-start.22) | collective-permute-done | bytes 393248 | tf_op jit(solution)/shard_map/ppermute | solution.py:20
  136.8 6.8 %collective-permute-done.24 = bf16[4,2,96,256]{3,2,1,0:T(8,128)(2,1)S(1)} collective-permute-done((bf16[4,2,96,256]{3,2,1,0:T(8,128)(2,1)S(1)}, bf16[4,2,96,256]{3,2,1,0:T(8,128)(2,1)S(1)}, u32[]{:S(2)}, u32[]{:S(2)}) %collective-permute-start.24) | collective-permute-done | bytes 393248 | tf_op jit(solution)/shard_map/ppermute | solution.py:20
  145.9 6.6 %shard_map.81 = f32[3,2,256]{2,1,0:T(2,128)} custom-call(bf16[2,3,2,256,256]{4,3,2,1,0:T(8,128)(2,1)} %bitcast.121, bf16[2,3,2,256,256]{4,3,2,1,0:T(8,128)(2,1)} %bitcast.122, bf16[512,1024]{1,0:T(8,128)(2,1)} %bitcast.130, bf16[2048,512]{1,0:T(8,128)(2,1)} %maximum_maximum_fusion.wide_ref), custom_call_target="tpu_custom_call" | custom-call | tf_op jit(solution)/shard_map/pallas_call | solution.py:193
  (120 shorter events, 44.6 us)
Async XLA Ops:
  3.4 15.5 %collective-permute-start.1 = (bf16[6,2,3,256,8]{3,4,2,1,0:T(8,128)(2,1)}, bf16[6,2,3,256,8]{3,4,2,1,0:T(8,128)(2,1)S(1)}, u32[]{:S(2)}, u32[]{:S(2)}) collective-permute-start(bf16[6,2,3,256,8]{3,4,2,1,0:T(8,128)(2,1)} %copy.46), channel_id=1, source_target_pairs={{0,1},{1,0},{2,3},{3,2},{4,5},{5,4},{6,7},{7,6},{8,9},{9,8},{10,11... | collective-permute-start | bytes 442376 | tf_op jit(solution)/shard_map/ppermute | solution.py:24
  5.3 27.9 %collective-permute-start = (bf16[2,2,3,256,128]{4,3,2,1,0:T(8,128)(2,1)S(1)}, bf16[2,2,3,256,128]{4,3,2,1,0:T(8,128)(2,1)}, u32[]{:S(2)}, u32[]{:S(2)}) collective-permute-start(bf16[2,2,3,256,128]{4,3,2,1,0:T(8,128)(2,1)S(1)} %get-tuple-element.30), channel_id=1, source_target_pairs={{2,0},{3,1},{4,2},{5,3},{6,4},{7,5},{8,6},{9,7},{10,8},{11,9},{12,... | collective-permute-start | bytes 2359304 | tf_op jit(solution)/shard_map/ppermute | solution.py:20
  10.9 34.8 %collective-permute-start.7 = (bf16[2,2,3,256,128]{4,3,2,1,0:T(8,128)(2,1)}, bf16[2,2,3,256,128]{4,3,2,1,0:T(8,128)(2,1)}, u32[]{:S(2)}, u32[]{:S(2)}) collective-permute-start(bf16[2,2,3,256,128]{4,3,2,1,0:T(8,128)(2,1)} %get-tuple-element.31), channel_id=1, source_target_pairs={{2,0},{3,1},{4,2},{5,3},{6,4},{7,5},{8,6},{9,7},{10,8},{11,9},{12,... | collective-permute-start | bytes 2359304 | tf_op jit(solution)/shard_map/ppermute | solution.py:20
  11.4 50.8 %collective-permute-start.13 = (bf16[2,2,3,256,128]{4,3,2,1,0:T(8,128)(2,1)}, bf16[2,2,3,256,128]{4,3,2,1,0:T(8,128)(2,1)}, u32[]{:S(2)}, u32[]{:S(2)}) collective-permute-start(bf16[2,2,3,256,128]{4,3,2,1,0:T(8,128)(2,1)} %get-tuple-element.32), channel_id=1, source_target_pairs={{2,0},{3,1},{4,2},{5,3},{6,4},{7,5},{8,6},{9,7},{10,8},{11,9},{12,... | collective-permute-start | bytes 2359304 | tf_op jit(solution)/shard_map/ppermute | solution.py:20
  52.3 16.1 %collective-permute-start.8 = (bf16[2,4,2,96,256]{4,3,2,1,0:T(8,128)(2,1)}, bf16[2,4,2,96,256]{4,3,2,1,0:T(8,128)(2,1)}, u32[]{:S(2)}, u32[]{:S(2)}) collective-permute-start(bf16[2,4,2,96,256]{4,3,2,1,0:T(8,128)(2,1)} %dynamic-slice_bitcast_fusion.1), channel_id=1, source_target_pairs={{0,1},{1,0},{2,3},{3,2},{4,5},{5,4},{6,7},{7,6},{8,9},{9,8},{10,11... | collective-permute-start | bytes 2359304 | tf_op jit(solution)/shard_map/ppermute | solution.py:24
  54.5 14.0 %collective-permute-start.3 = (bf16[2,4,96,256]{3,2,1,0:T(8,128)(2,1)}, bf16[2,4,96,256]{3,2,1,0:T(8,128)(2,1)S(1)}, u32[]{:S(2)}, u32[]{:S(2)}) collective-permute-start(bf16[2,4,96,256]{3,2,1,0:T(8,128)(2,1)} %fusion), channel_id=1, source_target_pairs={{0,2},{1,3},{2,0},{3,1},{4,6},{5,7},{6,4},{7,5},{8,10},{9,11},{10,... | collective-permute-start | bytes 1179656 | tf_op jit(solution)/shard_map/ppermute | solution.py:24
  74.0 10.3 %collective-permute-start.14 = (bf16[2,4,2,96,256]{4,3,2,1,0:T(8,128)(2,1)S(1)}, bf16[2,4,2,96,256]{4,3,2,1,0:T(8,128)(2,1)S(1)}, u32[]{:S(2)}, u32[]{:S(2)}) collective-permute-start(bf16[2,4,2,96,256]{4,3,2,1,0:T(8,128)(2,1)S(1)} %dynamic-slice_bitcast_fusion), channel_id=1, source_target_pairs={{0,1},{1,0},{2,3},{3,2},{4,5},{5,4},{6,7},{7,6},{8,9},{9,8},{10,11... | collective-permute-start | bytes 2359304 | tf_op jit(solution)/shard_map/ppermute | solution.py:24
  74.3 10.4 %collective-permute-start.4 = (bf16[2,96,256]{2,1,0:T(8,128)(2,1)S(1)}, bf16[2,96,256]{2,1,0:T(8,128)(2,1)S(1)}, u32[]{:S(2)}, u32[]{:S(2)}) collective-permute-start(bf16[2,96,256]{2,1,0:T(8,128)(2,1)S(1)} %get-tuple-element.39), channel_id=1, source_target_pairs={{12,0},{0,4},{4,8},{8,12},{13,1},{1,5},{5,9},{9,13},{14,2},{2,6},{... | collective-permute-start | bytes 294920 | tf_op jit(solution)/shard_map/ppermute | solution.py:20
  75.9 11.5 %collective-permute-start.5 = (bf16[2,96,256]{2,1,0:T(8,128)(2,1)S(1)}, bf16[2,96,256]{2,1,0:T(8,128)(2,1)S(1)}, u32[]{:S(2)}, u32[]{:S(2)}) collective-permute-start(bf16[2,96,256]{2,1,0:T(8,128)(2,1)S(1)} %get-tuple-element.41), channel_id=1, source_target_pairs={{8,0},{12,4},{0,8},{4,12},{9,1},{13,5},{1,9},{5,13},{10,2},{14,6},... | collective-permute-start | bytes 294920 | tf_op jit(solution)/shard_map/ppermute | solution.py:20
  80.3 7.1 %collective-permute-start.6 = (bf16[2,96,256]{2,1,0:T(8,128)(2,1)S(1)}, bf16[2,96,256]{2,1,0:T(8,128)(2,1)S(1)}, u32[]{:S(2)}, u32[]{:S(2)}) collective-permute-start(bf16[2,96,256]{2,1,0:T(8,128)(2,1)S(1)} %get-tuple-element.40), channel_id=1, source_target_pairs={{4,0},{8,4},{12,8},{0,12},{5,1},{9,5},{13,9},{1,13},{6,2},{10,6},{... | collective-permute-start | bytes 294920 | tf_op jit(solution)/shard_map/ppermute | solution.py:20
  81.8 12.4 %collective-permute-start.9 = (bf16[2,4,96,256]{3,2,1,0:T(8,128)(2,1)S(1)}, bf16[2,4,96,256]{3,2,1,0:T(8,128)(2,1)S(1)}, u32[]{:S(2)}, u32[]{:S(2)}) collective-permute-start(bf16[2,4,96,256]{3,2,1,0:T(8,128)(2,1)S(1)} %fusion.1), channel_id=1, source_target_pairs={{0,2},{1,3},{2,0},{3,1},{4,6},{5,7},{6,4},{7,5},{8,10},{9,11},{10,... | collective-permute-start | bytes 1179656 | tf_op jit(solution)/shard_map/ppermute | solution.py:24
  84.6 17.3 %collective-permute-start.15 = (bf16[2,4,96,256]{3,2,1,0:T(8,128)(2,1)S(1)}, bf16[2,4,96,256]{3,2,1,0:T(8,128)(2,1)S(1)}, u32[]{:S(2)}, u32[]{:S(2)}) collective-permute-start(bf16[2,4,96,256]{3,2,1,0:T(8,128)(2,1)S(1)} %fusion.2), channel_id=1, source_target_pairs={{0,2},{1,3},{2,0},{3,1},{4,6},{5,7},{6,4},{7,5},{8,10},{9,11},{10,... | collective-permute-start | bytes 1179656 | tf_op jit(solution)/shard_map/ppermute | solution.py:24
  94.4 9.6 %collective-permute-start.10 = (bf16[2,96,256]{2,1,0:T(8,128)(2,1)S(1)}, bf16[2,96,256]{2,1,0:T(8,128)(2,1)S(1)}, u32[]{:S(2)}, u32[]{:S(2)}) collective-permute-start(bf16[2,96,256]{2,1,0:T(8,128)(2,1)S(1)} %get-tuple-element.42), channel_id=1, source_target_pairs={{12,0},{0,4},{4,8},{8,12},{13,1},{1,5},{5,9},{9,13},{14,2},{2,6},{... | collective-permute-start | bytes 294920 | tf_op jit(solution)/shard_map/ppermute | solution.py:20
  96.4 10.1 %collective-permute-start.11 = (bf16[2,96,256]{2,1,0:T(8,128)(2,1)S(1)}, bf16[2,96,256]{2,1,0:T(8,128)(2,1)S(1)}, u32[]{:S(2)}, u32[]{:S(2)}) collective-permute-start(bf16[2,96,256]{2,1,0:T(8,128)(2,1)S(1)} %get-tuple-element.44), channel_id=1, source_target_pairs={{8,0},{12,4},{0,8},{4,12},{9,1},{13,5},{1,9},{5,13},{10,2},{14,6},... | collective-permute-start | bytes 294920 | tf_op jit(solution)/shard_map/ppermute | solution.py:20
  96.4 10.1 %collective-permute-start.12 = (bf16[2,96,256]{2,1,0:T(8,128)(2,1)S(1)}, bf16[2,96,256]{2,1,0:T(8,128)(2,1)S(1)}, u32[]{:S(2)}, u32[]{:S(2)}) collective-permute-start(bf16[2,96,256]{2,1,0:T(8,128)(2,1)S(1)} %get-tuple-element.43), channel_id=1, source_target_pairs={{4,0},{8,4},{12,8},{0,12},{5,1},{9,5},{13,9},{1,13},{6,2},{10,6},{... | collective-permute-start | bytes 294920 | tf_op jit(solution)/shard_map/ppermute | solution.py:20
  102.0 7.7 %collective-permute-start.16 = (bf16[2,96,256]{2,1,0:T(8,128)(2,1)S(1)}, bf16[2,96,256]{2,1,0:T(8,128)(2,1)S(1)}, u32[]{:S(2)}, u32[]{:S(2)}) collective-permute-start(bf16[2,96,256]{2,1,0:T(8,128)(2,1)S(1)} %get-tuple-element.45), channel_id=1, source_target_pairs={{12,0},{0,4},{4,8},{8,12},{13,1},{1,5},{5,9},{9,13},{14,2},{2,6},{... | collective-permute-start | bytes 294920 | tf_op jit(solution)/shard_map/ppermute | solution.py:20
  103.7 8.5 %collective-permute-start.17 = (bf16[2,96,256]{2,1,0:T(8,128)(2,1)S(1)}, bf16[2,96,256]{2,1,0:T(8,128)(2,1)S(1)}, u32[]{:S(2)}, u32[]{:S(2)}) collective-permute-start(bf16[2,96,256]{2,1,0:T(8,128)(2,1)S(1)} %get-tuple-element.47), channel_id=1, source_target_pairs={{8,0},{12,4},{0,8},{4,12},{9,1},{13,5},{1,9},{5,13},{10,2},{14,6},... | collective-permute-start | bytes 294920 | tf_op jit(solution)/shard_map/ppermute | solution.py:20
  104.0 8.3 %collective-permute-start.18 = (bf16[2,96,256]{2,1,0:T(8,128)(2,1)S(1)}, bf16[2,96,256]{2,1,0:T(8,128)(2,1)S(1)}, u32[]{:S(2)}, u32[]{:S(2)}) collective-permute-start(bf16[2,96,256]{2,1,0:T(8,128)(2,1)S(1)} %get-tuple-element.46), channel_id=1, source_target_pairs={{4,0},{8,4},{12,8},{0,12},{5,1},{9,5},{13,9},{1,13},{6,2},{10,6},{... | collective-permute-start | bytes 294920 | tf_op jit(solution)/shard_map/ppermute | solution.py:20
  113.2 7.4 %collective-permute-start.19 = (bf16[2,96,256]{2,1,0:T(8,128)(2,1)S(1)}, bf16[2,96,256]{2,1,0:T(8,128)(2,1)S(1)}, u32[]{:S(2)}, u32[]{:S(2)}) collective-permute-start(bf16[2,96,256]{2,1,0:T(8,128)(2,1)S(1)} %get-tuple-element.38), channel_id=1, source_target_pairs={{12,0},{0,4},{4,8},{8,12},{13,1},{1,5},{5,9},{9,13},{14,2},{2,6},{... | collective-permute-start | bytes 294920 | tf_op jit(solution)/shard_map/ppermute | solution.py:20
  115.8 8.2 %collective-permute-start.20 = (bf16[2,96,256]{2,1,0:T(8,128)(2,1)S(1)}, bf16[2,96,256]{2,1,0:T(8,128)(2,1)S(1)}, u32[]{:S(2)}, u32[]{:S(2)}) collective-permute-start(bf16[2,96,256]{2,1,0:T(8,128)(2,1)S(1)} %get-tuple-element.37), channel_id=1, source_target_pairs={{8,0},{12,4},{0,8},{4,12},{9,1},{13,5},{1,9},{5,13},{10,2},{14,6},... | collective-permute-start | bytes 294920 | tf_op jit(solution)/shard_map/ppermute | solution.py:20
  117.0 6.9 %collective-permute-start.21 = (bf16[2,96,256]{2,1,0:T(8,128)(2,1)S(1)}, bf16[2,96,256]{2,1,0:T(8,128)(2,1)S(1)}, u32[]{:S(2)}, u32[]{:S(2)}) collective-permute-start(bf16[2,96,256]{2,1,0:T(8,128)(2,1)S(1)} %get-tuple-element.36), channel_id=1, source_target_pairs={{4,0},{8,4},{12,8},{0,12},{5,1},{9,5},{13,9},{1,13},{6,2},{10,6},{... | collective-permute-start | bytes 294920 | tf_op jit(solution)/shard_map/ppermute | solution.py:20
  124.7 10.9 %collective-permute-start.22 = (bf16[4,2,96,256]{3,2,1,0:T(8,128)(2,1)S(1)}, bf16[4,2,96,256]{3,2,1,0:T(8,128)(2,1)S(1)}, u32[]{:S(2)}, u32[]{:S(2)}) collective-permute-start(bf16[4,2,96,256]{3,2,1,0:T(8,128)(2,1)S(1)} %broadcast_select_fusion), channel_id=1, source_target_pairs={{3,0},{0,1},{1,2},{2,3},{7,4},{4,5},{5,6},{6,7},{11,8},{8,9},{9,10... | collective-permute-start | bytes 1179656 | tf_op jit(solution)/shard_map/ppermute | solution.py:20
  124.8 12.0 %collective-permute-start.23 = (bf16[4,2,96,256]{3,2,1,0:T(8,128)(2,1)S(1)}, bf16[4,2,96,256]{3,2,1,0:T(8,128)(2,1)S(1)}, u32[]{:S(2)}, u32[]{:S(2)}) collective-permute-start(bf16[4,2,96,256]{3,2,1,0:T(8,128)(2,1)S(1)} %broadcast_select_fusion), channel_id=1, source_target_pairs={{2,0},{3,1},{0,2},{1,3},{6,4},{7,5},{4,6},{5,7},{10,8},{11,9},{8,1... | collective-permute-start | bytes 1179656 | tf_op jit(solution)/shard_map/ppermute | solution.py:20
  126.3 17.3 %collective-permute-start.24 = (bf16[4,2,96,256]{3,2,1,0:T(8,128)(2,1)S(1)}, bf16[4,2,96,256]{3,2,1,0:T(8,128)(2,1)S(1)}, u32[]{:S(2)}, u32[]{:S(2)}) collective-permute-start(bf16[4,2,96,256]{3,2,1,0:T(8,128)(2,1)S(1)} %broadcast_select_fusion), channel_id=1, source_target_pairs={{1,0},{2,1},{3,2},{0,3},{5,4},{6,5},{7,6},{4,7},{9,8},{10,9},{11,1... | collective-permute-start | bytes 1179656 | tf_op jit(solution)/shard_map/ppermute | solution.py:20
  (14 other events, 113.2 us)

commit v20 on v18

--- a/solution.py
+++ b/solution.py
@@ -220,7 +220,7 @@
     coord_y = device % 2 * half_rows + column // LZ
     coord_z = column % LZ
     angle = phase_angles(momenta, (coord_x, coord_y, coord_z), (extent_x, LY, LZ))[0]
-    halves = 3 if time_count % 3 == 0 else (2 if time_count % 2 == 0 else 1)
+    halves = time_count
     span = time_count // halves
     far_tile = [(h * span, shifted(eigenvectors[h * span : (h + 1) * span], SPACE, -2)) for h in range(halves)]
     row_in = swapped(eigenvectors[..., :LZ], SPACE, 0)

time: 148 us -> 181 us (1.22)
  starting transfers between devices: 33.6 us -> 52.2 us
  Pallas kernels: 30.7 us -> 40 us
  local copies, waits for them, and re-layouts: 21.2 us -> 25.6 us
  waiting for transfers between devices: 50.6 us -> 53.4 us
  other arithmetic: 9.33 us -> 6.87 us
    ppermute x18 -> x30, starting transfers between devices: 30.1 us -> 45 us  [shifted(): return lax.ppermute(block, axis, route)]
    ppermute x7 -> x13, waiting for transfers between devices: 10.4 us -> 23.1 us  [swapped(): lax.ppermute(value, axis, [(i, i ^ 1 << bit) for i in range(lax.axis_size...]
    ppermute x18 -> x30, waiting for transfers between devices: 40.3 us -> 30.3 us  [shifted(): return lax.ppermute(block, axis, route)]
    pallas_call x3 -> x6, Pallas kernels: 13.1 us -> 22.4 us  [second_pass(): pl.pallas_call(functools.partial(sums_kernel, scale=scale, course_list=(0...]
    ppermute x7 -> x13, starting transfers between devices: 3.56 us -> 7.23 us  [swapped(): lax.ppermute(value, axis, [(i, i ^ 1 << bit) for i in range(lax.axis_size...]
    add x3 -> x6, other arithmetic: 2.97 us -> 0.54 us  [body(): chunk = keep + swapped_chunks[half].astype(jnp.float32)]
    squeeze x3 -> x6, local copies, waits for them, and re-layouts: 4.66 us -> 6.4 us  [body(): send = lax.dynamic_index_in_dim(part_blocks, 1 - core, 3, keepdims=False)]
    unnamed x24 -> x38, local copies, waits for them, and re-layouts: 3.79 us -> 3.69 us
  transfers between devices with their start and end apart: 25 -> 43, of which waited for: 13 -> 16; matrix products, arithmetic and copies ran while one was open for 15% -> 13% of each run, Pallas kernels for 16% -> 19%
where the time goes in v20:
time: 181 us; the launch traced here: 180 us
  waiting for transfers between devices  53.4 us (30%)
  starting transfers between devices  52.2 us (29%)
  Pallas kernels  40 us (22%)
  local copies, waits for them, and re-layouts  25.6 us (14%)
  other arithmetic  6.87 us (4%)
  between operations  2.06 us (1%)
    ppermute x30, starting transfers between devices, shifted(): return lax.ppermute(block, axis, route)  45 us
    ppermute x30, waiting for transfers between devices, shifted(): return lax.ppermute(block, axis, route)  30.3 us
    ppermute x13, waiting for transfers between devices, swapped(): lax.ppermute(value, axis, [(i, i ^ 1 << bit) for i in range(lax.axis_size...  23.1 us
    pallas_call x6, Pallas kernels, second_pass(): pl.pallas_call(functools.partial(sums_kernel, scale=scale, course_list=(0...  22.4 us
    pallas_call x1, Pallas kernels, local_sums(): pl.pallas_call(functools.partial(sums_kernel, scale=scale, course_list=ne...  11 us
    ppermute x13, starting transfers between devices, swapped(): lax.ppermute(value, axis, [(i, i ^ 1 << bit) for i in range(lax.axis_size...  7.23 us
    pallas_call x1, Pallas kernels, contract_panel(): pl.pallas_call(panel_kernel, grid=(count_ops,), in_specs=[pl.BlockSpec((1...  6.63 us
    squeeze x6, local copies, waits for them, and re-layouts, body(): send = lax.dynamic_index_in_dim(part_blocks, 1 - core, 3, keepdims=False)  6.4 us
  transfers between devices with their start and end apart: 43, of which 16 were waited for; matrix products, arithmetic and copies ran while one was open for 13% of the time, Pallas kernels for 19%

profile of v20, /device:TPU:0, one launch (start us, length us, event | category | flops | bytes accessed | tf_op | source)
XLA Modules:
  0.0 180.2 jit_solution(129137012881115918)
XLA Ops:
  0.7 3.2 %fusion.57 = (bf16[1,2,3,256,128]{4,3,2,1,0:T(8,128)(2,1)}, bf16[1,2,3,256,128]{4,3,2,1,0:T(8,128)(2,1)}, bf16[1,2,3,256,128]{4,3,2,1,0:T(8,128)(2,1)}, bf16[1,2...) fusion(bf16[6,2,3,256,128]{4,3,2,1,0:T(8,128)(2,1)} %field_ref.13), kind=kLoop, calls=%fused_computation.162 | loop fusion | bytes 4718592 | tf_op jit(solution)/shard_map/slice | solution.py:225
  3.8 6.1 %collective-permute-start = (bf16[1,2,3,256,128]{4,3,2,1,0:T(8,128)(2,1)}, bf16[1,2,3,256,128]{4,3,2,1,0:T(8,128)(2,1)}, u32[]{:S(2)}, u32[]{:S(2)}) collective-permute-start(bf16[1,2,3,256,128]{4,3,2,1,0:T(8,128)(2,1)} %get-tuple-element.47), channel_id=1, source_target_pairs={{2,0},{3,1},{4,2},{5,3},{6,4},{7,5},{8,6},{9,7},{10,8},{11,9},{12,... | collective-permute-start | bytes 1179656 | tf_op jit(solution)/shard_map/ppermute | solution.py:20
  28.2 11.0 %shard_map.77 = (bf16[6,1536,256]{2,1,0:T(8,128)(2,1)}, bf16[6,512,768]{2,1,0:T(8,128)(2,1)}) custom-call(s32[3]{0:T(128)} %select_reduce_fusion.slot_ref, bf16[6,2,3,256,128]{4,3,2,1,0:T(8,128)(2,1)} %field_ref.13, bf16[6,2,3,256,128]{4,3,2,1,0:T(8,128)(2,1)} %pad.6.near_ref, f32[6,3,2,3,3,128]{5,4,3,2,1,0:T(4,128)} %copy.47.link_ref, ...), custom_call_target="tpu_custom_call" | custom-call | tf_op jit(solution)/shard_map/pallas_call | solution.py:118
  39.2 3.9 %shard_map.78 = bf16[1,1536,256]{2,1,0:T(8,128)(2,1)} custom-call(s32[3]{0:T(128)} %select_reduce_fusion.slot_ref, bf16[6,2,3,256,128]{4,3,2,1,0:T(8,128)(2,1)} %field_ref.13, bf16[1,2,3,256,128]{4,3,2,1,0:T(8,128)(2,1)} %collective-permute-done.near_ref, f32[6,3,2,3,3,128]{5,4,3,2,1,0:T(4,128)} %copy.47.link_ref, ...), custom_call_target="tpu_custom_call" | custom-call | tf_op jit(solution)/shard_map/pallas_call | solution.py:147
  46.8 3.7 %shard_map.79 = bf16[1,1536,256]{2,1,0:T(8,128)(2,1)} custom-call(s32[3]{0:T(128)} %select_reduce_fusion.slot_ref, bf16[6,2,3,256,128]{4,3,2,1,0:T(8,128)(2,1)} %field_ref.13, bf16[1,2,3,256,128]{4,3,2,1,0:T(8,128)(2,1)} %collective-permute-done.7.near_ref, f32[6,3,2,3,3,128]{5,4,3,2,1,0:T(4,128)} %copy.47.link_ref, ...), custom_call_target="tpu_custom_call" | custom-call | tf_op jit(solution)/shard_map/pallas_call | solution.py:147
  54.4 5.5 %collective-permute-start.6 = (bf16[1,96,256]{2,1,0:T(8,128)(2,1)S(1)}, bf16[1,96,256]{2,1,0:T(8,128)(2,1)S(1)}, u32[]{:S(2)}, u32[]{:S(2)}) collective-permute-start(bf16[1,96,256]{2,1,0:T(8,128)(2,1)S(1)} %get-tuple-element.70), channel_id=1, source_target_pairs={{4,0},{8,4},{12,8},{0,12},{5,1},{9,5},{13,9},{1,13},{6,2},{10,6},{... | collective-permute-start | bytes 147464 | tf_op jit(solution)/shard_map/ppermute | solution.py:20
  60.5 3.7 %shard_map.80 = bf16[1,1536,256]{2,1,0:T(8,128)(2,1)} custom-call(s32[3]{0:T(128)} %select_reduce_fusion.slot_ref, bf16[6,2,3,256,128]{4,3,2,1,0:T(8,128)(2,1)} %field_ref.13, bf16[1,2,3,256,128]{4,3,2,1,0:T(8,128)(2,1)} %collective-permute-done.13.near_ref, f32[6,3,2,3,3,128]{5,4,3,2,1,0:T(4,128)} %copy.47.link_ref, ...), custom_call_target="tpu_custom_call" | custom-call | tf_op jit(solution)/shard_map/pallas_call | solution.py:147
  65.5 5.2 %collective-permute-start.31 = (bf16[1,2,3,256,128]{4,3,2,1,0:T(8,128)(2,1)S(1)}, bf16[1,2,3,256,128]{4,3,2,1,0:T(8,128)(2,1)S(1)}, u32[]{:S(2)}, u32[]{:S(2)}) collective-permute-start(bf16[1,2,3,256,128]{4,3,2,1,0:T(8,128)(2,1)S(1)} %copy-done.12), channel_id=1, source_target_pairs={{2,0},{3,1},{4,2},{5,3},{6,4},{7,5},{8,6},{9,7},{10,8},{11,9},{12,... | collective-permute-start | bytes 1179656 | tf_op jit(solution)/shard_map/ppermute | solution.py:20
  70.8 10.3 %collective-permute-done.9 = bf16[1,4,96,256]{3,2,1,0:T(8,128)(2,1)S(1)} collective-permute-done((bf16[1,4,96,256]{3,2,1,0:T(8,128)(2,1)S(1)}, bf16[1,4,96,256]{3,2,1,0:T(8,128)(2,1)S(1)}, u32[]{:S(2)}, u32[]{:S(2)}) %collective-permute-start.9) | collective-permute-done | bytes 196640 | tf_op jit(solution)/shard_map/ppermute | solution.py:24
  81.2 3.1 %collective-permute-start.12 = (bf16[1,96,256]{2,1,0:T(8,128)(2,1)S(1)}, bf16[1,96,256]{2,1,0:T(8,128)(2,1)S(1)}, u32[]{:S(2)}, u32[]{:S(2)}) collective-permute-start(bf16[1,96,256]{2,1,0:T(8,128)(2,1)S(1)} %get-tuple-element.67), channel_id=1, source_target_pairs={{4,0},{8,4},{12,8},{0,12},{5,1},{9,5},{13,9},{1,13},{6,2},{10,6},{... | collective-permute-start | bytes 147464 | tf_op jit(solution)/shard_map/ppermute | solution.py:20
  85.7 3.7 %shard_map.81 = bf16[1,1536,256]{2,1,0:T(8,128)(2,1)} custom-call(s32[3]{0:T(128)} %select_reduce_fusion.slot_ref, bf16[6,2,3,256,128]{4,3,2,1,0:T(8,128)(2,1)} %field_ref.13, bf16[1,2,3,256,128]{4,3,2,1,0:T(8,128)(2,1)} %collective-permute-done.19.near_ref, f32[6,3,2,3,3,128]{5,4,3,2,1,0:T(4,128)} %copy.47.link_ref, ...), custom_call_target="tpu_custom_call" | custom-call | tf_op jit(solution)/shard_map/pallas_call | solution.py:147
  90.7 2.5 %collective-permute-start.15 = (bf16[1,4,96,256]{3,2,1,0:T(8,128)(2,1)S(1)}, bf16[1,4,96,256]{3,2,1,0:T(8,128)(2,1)S(1)}, u32[]{:S(2)}, u32[]{:S(2)}) collective-permute-start(bf16[1,4,96,256]{3,2,1,0:T(8,128)(2,1)S(1)} %fusion.2), channel_id=1, source_target_pairs={{0,2},{1,3},{2,0},{3,1},{4,6},{5,7},{6,4},{7,5},{8,10},{9,11},{10,... | collective-permute-start | bytes 589832 | tf_op jit(solution)/shard_map/ppermute | solution.py:24
  93.2 4.2 %collective-permute-done.15 = bf16[1,4,96,256]{3,2,1,0:T(8,128)(2,1)S(1)} collective-permute-done((bf16[1,4,96,256]{3,2,1,0:T(8,128)(2,1)S(1)}, bf16[1,4,96,256]{3,2,1,0:T(8,128)(2,1)S(1)}, u32[]{:S(2)}, u32[]{:S(2)}) %collective-permute-start.15) | collective-permute-done | bytes 196640 | tf_op jit(solution)/shard_map/ppermute | solution.py:24
  102.5 3.7 %shard_map.82 = bf16[1,1536,256]{2,1,0:T(8,128)(2,1)} custom-call(s32[3]{0:T(128)} %select_reduce_fusion.slot_ref, bf16[6,2,3,256,128]{4,3,2,1,0:T(8,128)(2,1)} %field_ref.13, bf16[1,2,3,256,128]{4,3,2,1,0:T(8,128)(2,1)} %collective-permute-done.25.near_ref, f32[6,3,2,3,3,128]{5,4,3,2,1,0:T(4,128)} %copy.47.link_ref, ...), custom_call_target="tpu_custom_call" | custom-call | tf_op jit(solution)/shard_map/pallas_call | solution.py:147
  107.5 3.6 %collective-permute-start.24 = (bf16[1,96,256]{2,1,0:T(8,128)(2,1)S(1)}, bf16[1,96,256]{2,1,0:T(8,128)(2,1)S(1)}, u32[]{:S(2)}, u32[]{:S(2)}) collective-permute-start(bf16[1,96,256]{2,1,0:T(8,128)(2,1)S(1)} %get-tuple-element.61), channel_id=1, source_target_pairs={{4,0},{8,4},{12,8},{0,12},{5,1},{9,5},{13,9},{1,13},{6,2},{10,6},{... | collective-permute-start | bytes 147464 | tf_op jit(solution)/shard_map/ppermute | solution.py:20
  112.6 3.7 %shard_map.83 = bf16[1,1536,256]{2,1,0:T(8,128)(2,1)} custom-call(s32[3]{0:T(128)} %select_reduce_fusion.slot_ref, bf16[6,2,3,256,128]{4,3,2,1,0:T(8,128)(2,1)} %field_ref.13, bf16[1,2,3,256,128]{4,3,2,1,0:T(8,128)(2,1)} %copy-done.11, f32[6,3,2,3,3,128]{5,4,3,2,1,0:T(4,128)} %copy.47.link_ref, bf16[6,512,768]{2,1,0:T(8,128)(2,1)} %get-tuple-element.10.trig_ref, ...), custom_call_target="tpu_custom_call" | custom-call | tf_op jit(solution)/shard_map/pallas_call | solution.py:147
  120.2 5.5 %collective-permute-done.27 = bf16[1,4,96,256]{3,2,1,0:T(8,128)(2,1)S(1)} collective-permute-done((bf16[1,4,96,256]{3,2,1,0:T(8,128)(2,1)S(1)}, bf16[1,4,96,256]{3,2,1,0:T(8,128)(2,1)S(1)}, u32[]{:S(2)}, u32[]{:S(2)}) %collective-permute-start.27) | collective-permute-done | bytes 196640 | tf_op jit(solution)/shard_map/ppermute | solution.py:24
  125.8 3.6 %collective-permute-start.30 = (bf16[1,96,256]{2,1,0:T(8,128)(2,1)S(1)}, bf16[1,96,256]{2,1,0:T(8,128)(2,1)S(1)}, u32[]{:S(2)}, u32[]{:S(2)}) collective-permute-start(bf16[1,96,256]{2,1,0:T(8,128)(2,1)S(1)} %get-tuple-element.58), channel_id=1, source_target_pairs={{4,0},{8,4},{12,8},{0,12},{5,1},{9,5},{13,9},{1,13},{6,2},{10,6},{... | collective-permute-start | bytes 147464 | tf_op jit(solution)/shard_map/ppermute | solution.py:20
  130.2 3.6 %collective-permute-start.36 = (bf16[1,96,256]{2,1,0:T(8,128)(2,1)S(1)}, bf16[1,96,256]{2,1,0:T(8,128)(2,1)S(1)}, u32[]{:S(2)}, u32[]{:S(2)}) collective-permute-start(bf16[1,96,256]{2,1,0:T(8,128)(2,1)S(1)} %get-tuple-element.55), channel_id=1, source_target_pairs={{4,0},{8,4},{12,8},{0,12},{5,1},{9,5},{13,9},{1,13},{6,2},{10,6},{... | collective-permute-start | bytes 147464 | tf_op jit(solution)/shard_map/ppermute | solution.py:20
  136.0 2.8 %collective-permute-done.35 = bf16[1,96,256]{2,1,0:T(8,128)(2,1)S(1)} collective-permute-done((bf16[1,96,256]{2,1,0:T(8,128)(2,1)S(1)}, bf16[1,96,256]{2,1,0:T(8,128)(2,1)S(1)}, u32[]{:S(2)}, u32[]{:S(2)}) %collective-permute-start.35) | collective-permute-done | bytes 49184 | tf_op jit(solution)/shard_map/ppermute | solution.py:20
  143.6 3.8 %collective-permute-done.39 = bf16[2,96,256]{2,1,0:T(8,128)(2,1)S(1)} collective-permute-done((bf16[2,96,256]{2,1,0:T(8,128)(2,1)S(1)}, bf16[2,96,256]{2,1,0:T(8,128)(2,1)S(1)}, u32[]{:S(2)}, u32[]{:S(2)}) %collective-permute-start.39) | collective-permute-done | bytes 98336 | tf_op jit(solution)/shard_map/ppermute | solution.py:20
  151.7 8.1 %collective-permute-done.42 = bf16[4,2,96,256]{3,2,1,0:T(8,128)(2,1)S(1)} collective-permute-done((bf16[4,2,96,256]{3,2,1,0:T(8,128)(2,1)S(1)}, bf16[4,2,96,256]{3,2,1,0:T(8,128)(2,1)S(1)}, u32[]{:S(2)}, u32[]{:S(2)}) %collective-permute-start.42) | collective-permute-done | bytes 393248 | tf_op jit(solution)/shard_map/ppermute | solution.py:20
  159.8 9.1 %collective-permute-done.41 = bf16[4,2,96,256]{3,2,1,0:T(8,128)(2,1)S(1)} collective-permute-done((bf16[4,2,96,256]{3,2,1,0:T(8,128)(2,1)S(1)}, bf16[4,2,96,256]{3,2,1,0:T(8,128)(2,1)S(1)}, u32[]{:S(2)}, u32[]{:S(2)}) %collective-permute-start.41) | collective-permute-done | bytes 393248 | tf_op jit(solution)/shard_map/ppermute | solution.py:20
  172.1 6.6 %shard_map.84 = f32[3,2,256]{2,1,0:T(2,128)} custom-call(bf16[2,3,2,256,256]{4,3,2,1,0:T(8,128)(2,1)} %bitcast.208, bf16[2,3,2,256,256]{4,3,2,1,0:T(8,128)(2,1)} %bitcast.209, bf16[512,1024]{1,0:T(8,128)(2,1)} %bitcast.211, bf16[2048,512]{1,0:T(8,128)(2,1)} %maximum_maximum_fusion.wide_ref), custom_call_target="tpu_custom_call" | custom-call | tf_op jit(solution)/shard_map/pallas_call | solution.py:193
  (186 shorter events, 58.0 us)
Async XLA Ops:
  3.8 35.4 %collective-permute-start = (bf16[1,2,3,256,128]{4,3,2,1,0:T(8,128)(2,1)}, bf16[1,2,3,256,128]{4,3,2,1,0:T(8,128)(2,1)}, u32[]{:S(2)}, u32[]{:S(2)}) collective-permute-start(bf16[1,2,3,256,128]{4,3,2,1,0:T(8,128)(2,1)} %get-tuple-element.47), channel_id=1, source_target_pairs={{2,0},{3,1},{4,2},{5,3},{6,4},{7,5},{8,6},{9,7},{10,8},{11,9},{12,... | collective-permute-start | bytes 1179656 | tf_op jit(solution)/shard_map/ppermute | solution.py:20
  11.4 10.5 %collective-permute-start.1 = (bf16[6,2,3,256,8]{3,4,2,1,0:T(8,128)(2,1)}, bf16[6,2,3,256,8]{3,4,2,1,0:T(8,128)(2,1)S(1)}, u32[]{:S(2)}, u32[]{:S(2)}) collective-permute-start(bf16[6,2,3,256,8]{3,4,2,1,0:T(8,128)(2,1)} %copy.58), channel_id=1, source_target_pairs={{0,1},{1,0},{2,3},{3,2},{4,5},{5,4},{6,7},{7,6},{8,9},{9,8},{10,11... | collective-permute-start | bytes 442376 | tf_op jit(solution)/shard_map/ppermute | solution.py:24
  11.4 35.4 %collective-permute-start.7 = (bf16[1,2,3,256,128]{4,3,2,1,0:T(8,128)(2,1)}, bf16[1,2,3,256,128]{4,3,2,1,0:T(8,128)(2,1)}, u32[]{:S(2)}, u32[]{:S(2)}) collective-permute-start(bf16[1,2,3,256,128]{4,3,2,1,0:T(8,128)(2,1)} %get-tuple-element.46), channel_id=1, source_target_pairs={{2,0},{3,1},{4,2},{5,3},{6,4},{7,5},{8,6},{9,7},{10,8},{11,9},{12,... | collective-permute-start | bytes 1179656 | tf_op jit(solution)/shard_map/ppermute | solution.py:20
  11.9 47.9 %collective-permute-start.13 = (bf16[1,2,3,256,128]{4,3,2,1,0:T(8,128)(2,1)}, bf16[1,2,3,256,128]{4,3,2,1,0:T(8,128)(2,1)}, u32[]{:S(2)}, u32[]{:S(2)}) collective-permute-start(bf16[1,2,3,256,128]{4,3,2,1,0:T(8,128)(2,1)} %get-tuple-element.45), channel_id=1, source_target_pairs={{2,0},{3,1},{4,2},{5,3},{6,4},{7,5},{8,6},{9,7},{10,8},{11,9},{12,... | collective-permute-start | bytes 1179656 | tf_op jit(solution)/shard_map/ppermute | solution.py:20
  13.3 71.0 %collective-permute-start.19 = (bf16[1,2,3,256,128]{4,3,2,1,0:T(8,128)(2,1)}, bf16[1,2,3,256,128]{4,3,2,1,0:T(8,128)(2,1)}, u32[]{:S(2)}, u32[]{:S(2)}) collective-permute-start(bf16[1,2,3,256,128]{4,3,2,1,0:T(8,128)(2,1)} %get-tuple-element.44), channel_id=1, source_target_pairs={{2,0},{3,1},{4,2},{5,3},{6,4},{7,5},{8,6},{9,7},{10,8},{11,9},{12,... | collective-permute-start | bytes 1179656 | tf_op jit(solution)/shard_map/ppermute | solution.py:20
  22.5 78.0 %collective-permute-start.25 = (bf16[1,2,3,256,128]{4,3,2,1,0:T(8,128)(2,1)}, bf16[1,2,3,256,128]{4,3,2,1,0:T(8,128)(2,1)}, u32[]{:S(2)}, u32[]{:S(2)}) collective-permute-start(bf16[1,2,3,256,128]{4,3,2,1,0:T(8,128)(2,1)} %get-tuple-element.43), channel_id=1, source_target_pairs={{2,0},{3,1},{4,2},{5,3},{6,4},{7,5},{8,6},{9,7},{10,8},{11,9},{12,... | collective-permute-start | bytes 1179656 | tf_op jit(solution)/shard_map/ppermute | solution.py:20
  46.1 8.2 %collective-permute-start.3 = (bf16[1,4,96,256]{3,2,1,0:T(8,128)(2,1)S(1)}, bf16[1,4,96,256]{3,2,1,0:T(8,128)(2,1)S(1)}, u32[]{:S(2)}, u32[]{:S(2)}) collective-permute-start(bf16[1,4,96,256]{3,2,1,0:T(8,128)(2,1)S(1)} %fusion), channel_id=1, source_target_pairs={{0,2},{1,3},{2,0},{3,1},{4,6},{5,7},{6,4},{7,5},{8,10},{9,11},{10,... | collective-permute-start | bytes 589832 | tf_op jit(solution)/shard_map/ppermute | solution.py:24
  51.5 8.3 %collective-permute-start.8 = (bf16[1,4,2,96,256]{4,3,2,1,0:T(8,128)(2,1)S(1)}, bf16[1,4,2,96,256]{4,3,2,1,0:T(8,128)(2,1)S(1)}, u32[]{:S(2)}, u32[]{:S(2)}) collective-permute-start(bf16[1,4,2,96,256]{4,3,2,1,0:T(8,128)(2,1)S(1)} %dynamic-slice_bitcast_fusion.4), channel_id=1, source_target_pairs={{0,1},{1,0},{2,3},{3,2},{4,5},{5,4},{6,7},{7,6},{8,9},{9,8},{10,11... | collective-permute-start | bytes 1179656 | tf_op jit(solution)/shard_map/ppermute | solution.py:24
  54.4 11.1 %collective-permute-start.6 = (bf16[1,96,256]{2,1,0:T(8,128)(2,1)S(1)}, bf16[1,96,256]{2,1,0:T(8,128)(2,1)S(1)}, u32[]{:S(2)}, u32[]{:S(2)}) collective-permute-start(bf16[1,96,256]{2,1,0:T(8,128)(2,1)S(1)} %get-tuple-element.70), channel_id=1, source_target_pairs={{4,0},{8,4},{12,8},{0,12},{5,1},{9,5},{13,9},{1,13},{6,2},{10,6},{... | collective-permute-start | bytes 147464 | tf_op jit(solution)/shard_map/ppermute | solution.py:20
  59.8 10.8 %collective-permute-start.5 = (bf16[1,96,256]{2,1,0:T(8,128)(2,1)S(1)}, bf16[1,96,256]{2,1,0:T(8,128)(2,1)S(1)}, u32[]{:S(2)}, u32[]{:S(2)}) collective-permute-start(bf16[1,96,256]{2,1,0:T(8,128)(2,1)S(1)} %get-tuple-element.71), channel_id=1, source_target_pairs={{8,0},{12,4},{0,8},{4,12},{9,1},{13,5},{1,9},{5,13},{10,2},{14,6},... | collective-permute-start | bytes 147464 | tf_op jit(solution)/shard_map/ppermute | solution.py:20
  59.8 10.8 %collective-permute-start.4 = (bf16[1,96,256]{2,1,0:T(8,128)(2,1)S(1)}, bf16[1,96,256]{2,1,0:T(8,128)(2,1)S(1)}, u32[]{:S(2)}, u32[]{:S(2)}) collective-permute-start(bf16[1,96,256]{2,1,0:T(8,128)(2,1)S(1)} %get-tuple-element.69), channel_id=1, source_target_pairs={{12,0},{0,4},{4,8},{8,12},{13,1},{1,5},{5,9},{9,13},{14,2},{2,6},{... | collective-permute-start | bytes 147464 | tf_op jit(solution)/shard_map/ppermute | solution.py:20
  65.5 46.4 %collective-permute-start.31 = (bf16[1,2,3,256,128]{4,3,2,1,0:T(8,128)(2,1)S(1)}, bf16[1,2,3,256,128]{4,3,2,1,0:T(8,128)(2,1)S(1)}, u32[]{:S(2)}, u32[]{:S(2)}) collective-permute-start(bf16[1,2,3,256,128]{4,3,2,1,0:T(8,128)(2,1)S(1)} %copy-done.12), channel_id=1, source_target_pairs={{2,0},{3,1},{4,2},{5,3},{6,4},{7,5},{8,6},{9,7},{10,8},{11,9},{12,... | collective-permute-start | bytes 1179656 | tf_op jit(solution)/shard_map/ppermute | solution.py:20
  70.6 10.5 %collective-permute-start.9 = (bf16[1,4,96,256]{3,2,1,0:T(8,128)(2,1)S(1)}, bf16[1,4,96,256]{3,2,1,0:T(8,128)(2,1)S(1)}, u32[]{:S(2)}, u32[]{:S(2)}) collective-permute-start(bf16[1,4,96,256]{3,2,1,0:T(8,128)(2,1)S(1)} %fusion.1), channel_id=1, source_target_pairs={{0,2},{1,3},{2,0},{3,1},{4,6},{5,7},{6,4},{7,5},{8,10},{9,11},{10,... | collective-permute-start | bytes 589832 | tf_op jit(solution)/shard_map/ppermute | solution.py:24
  70.7 14.5 %collective-permute-start.14 = (bf16[1,4,2,96,256]{4,3,2,1,0:T(8,128)(2,1)S(1)}, bf16[1,4,2,96,256]{4,3,2,1,0:T(8,128)(2,1)S(1)}, u32[]{:S(2)}, u32[]{:S(2)}) collective-permute-start(bf16[1,4,2,96,256]{4,3,2,1,0:T(8,128)(2,1)S(1)} %dynamic-slice_bitcast_fusion.3), channel_id=1, source_target_pairs={{0,1},{1,0},{2,3},{3,2},{4,5},{5,4},{6,7},{7,6},{8,9},{9,8},{10,11... | collective-permute-start | bytes 1179656 | tf_op jit(solution)/shard_map/ppermute | solution.py:24
  81.2 9.4 %collective-permute-start.12 = (bf16[1,96,256]{2,1,0:T(8,128)(2,1)S(1)}, bf16[1,96,256]{2,1,0:T(8,128)(2,1)S(1)}, u32[]{:S(2)}, u32[]{:S(2)}) collective-permute-start(bf16[1,96,256]{2,1,0:T(8,128)(2,1)S(1)} %get-tuple-element.67), channel_id=1, source_target_pairs={{4,0},{8,4},{12,8},{0,12},{5,1},{9,5},{13,9},{1,13},{6,2},{10,6},{... | collective-permute-start | bytes 147464 | tf_op jit(solution)/shard_map/ppermute | solution.py:20
  84.3 8.9 %collective-permute-start.11 = (bf16[1,96,256]{2,1,0:T(8,128)(2,1)S(1)}, bf16[1,96,256]{2,1,0:T(8,128)(2,1)S(1)}, u32[]{:S(2)}, u32[]{:S(2)}) collective-permute-start(bf16[1,96,256]{2,1,0:T(8,128)(2,1)S(1)} %get-tuple-element.68), channel_id=1, source_target_pairs={{8,0},{12,4},{0,8},{4,12},{9,1},{13,5},{1,9},{5,13},{10,2},{14,6},... | collective-permute-start | bytes 147464 | tf_op jit(solution)/shard_map/ppermute | solution.py:20
  97.5 9.7 %collective-permute-start.18 = (bf16[1,96,256]{2,1,0:T(8,128)(2,1)S(1)}, bf16[1,96,256]{2,1,0:T(8,128)(2,1)S(1)}, u32[]{:S(2)}, u32[]{:S(2)}) collective-permute-start(bf16[1,96,256]{2,1,0:T(8,128)(2,1)S(1)} %get-tuple-element.64), channel_id=1, source_target_pairs={{4,0},{8,4},{12,8},{0,12},{5,1},{9,5},{13,9},{1,13},{6,2},{10,6},{... | collective-permute-start | bytes 147464 | tf_op jit(solution)/shard_map/ppermute | solution.py:20
  107.5 10.0 %collective-permute-start.24 = (bf16[1,96,256]{2,1,0:T(8,128)(2,1)S(1)}, bf16[1,96,256]{2,1,0:T(8,128)(2,1)S(1)}, u32[]{:S(2)}, u32[]{:S(2)}) collective-permute-start(bf16[1,96,256]{2,1,0:T(8,128)(2,1)S(1)} %get-tuple-element.61), channel_id=1, source_target_pairs={{4,0},{8,4},{12,8},{0,12},{5,1},{9,5},{13,9},{1,13},{6,2},{10,6},{... | collective-permute-start | bytes 147464 | tf_op jit(solution)/shard_map/ppermute | solution.py:20
  119.3 10.7 %collective-permute-start.33 = (bf16[1,4,96,256]{3,2,1,0:T(8,128)(2,1)S(1)}, bf16[1,4,96,256]{3,2,1,0:T(8,128)(2,1)S(1)}, u32[]{:S(2)}, u32[]{:S(2)}) collective-permute-start(bf16[1,4,96,256]{3,2,1,0:T(8,128)(2,1)S(1)} %fusion.5), channel_id=1, source_target_pairs={{0,2},{1,3},{2,0},{3,1},{4,6},{5,7},{6,4},{7,5},{8,10},{9,11},{10,... | collective-permute-start | bytes 589832 | tf_op jit(solution)/shard_map/ppermute | solution.py:24
  125.8 8.7 %collective-permute-start.30 = (bf16[1,96,256]{2,1,0:T(8,128)(2,1)S(1)}, bf16[1,96,256]{2,1,0:T(8,128)(2,1)S(1)}, u32[]{:S(2)}, u32[]{:S(2)}) collective-permute-start(bf16[1,96,256]{2,1,0:T(8,128)(2,1)S(1)} %get-tuple-element.58), channel_id=1, source_target_pairs={{4,0},{8,4},{12,8},{0,12},{5,1},{9,5},{13,9},{1,13},{6,2},{10,6},{... | collective-permute-start | bytes 147464 | tf_op jit(solution)/shard_map/ppermute | solution.py:20
  141.3 8.5 %collective-permute-start.38 = (bf16[2,96,256]{2,1,0:T(8,128)(2,1)S(1)}, bf16[2,96,256]{2,1,0:T(8,128)(2,1)S(1)}, u32[]{:S(2)}, u32[]{:S(2)}) collective-permute-start(bf16[2,96,256]{2,1,0:T(8,128)(2,1)S(1)} %get-tuple-element.52), channel_id=1, source_target_pairs={{8,0},{12,4},{0,8},{4,12},{9,1},{13,5},{1,9},{5,13},{10,2},{14,6},... | collective-permute-start | bytes 294920 | tf_op jit(solution)/shard_map/ppermute | solution.py:20
  150.5 9.3 %collective-permute-start.42 = (bf16[4,2,96,256]{3,2,1,0:T(8,128)(2,1)S(1)}, bf16[4,2,96,256]{3,2,1,0:T(8,128)(2,1)S(1)}, u32[]{:S(2)}, u32[]{:S(2)}) collective-permute-start(bf16[4,2,96,256]{3,2,1,0:T(8,128)(2,1)S(1)} %broadcast_select_fusion), channel_id=1, source_target_pairs={{1,0},{2,1},{3,2},{0,3},{5,4},{6,5},{7,6},{4,7},{9,8},{10,9},{11,1... | collective-permute-start | bytes 1179656 | tf_op jit(solution)/shard_map/ppermute | solution.py:20
  150.6 18.3 %collective-permute-start.41 = (bf16[4,2,96,256]{3,2,1,0:T(8,128)(2,1)S(1)}, bf16[4,2,96,256]{3,2,1,0:T(8,128)(2,1)S(1)}, u32[]{:S(2)}, u32[]{:S(2)}) collective-permute-start(bf16[4,2,96,256]{3,2,1,0:T(8,128)(2,1)S(1)} %broadcast_select_fusion), channel_id=1, source_target_pairs={{2,0},{3,1},{0,2},{1,3},{6,4},{7,5},{4,6},{5,7},{10,8},{11,9},{8,1... | collective-permute-start | bytes 1179656 | tf_op jit(solution)/shard_map/ppermute | solution.py:20
  151.4 18.3 %collective-permute-start.40 = (bf16[4,2,96,256]{3,2,1,0:T(8,128)(2,1)S(1)}, bf16[4,2,96,256]{3,2,1,0:T(8,128)(2,1)S(1)}, u32[]{:S(2)}, u32[]{:S(2)}) collective-permute-start(bf16[4,2,96,256]{3,2,1,0:T(8,128)(2,1)S(1)} %broadcast_select_fusion), channel_id=1, source_target_pairs={{3,0},{0,1},{1,2},{2,3},{7,4},{4,5},{5,6},{6,7},{11,8},{8,9},{9,10... | collective-permute-start | bytes 1179656 | tf_op jit(solution)/shard_map/ppermute | solution.py:20
  (37 other events, 230.8 us)

commit v21 on v20

--- a/solution.py
+++ b/solution.py
@@ -220,7 +220,7 @@
     coord_y = device % 2 * half_rows + column // LZ
     coord_z = column % LZ
     angle = phase_angles(momenta, (coord_x, coord_y, coord_z), (extent_x, LY, LZ))[0]
-    halves = time_count
+    halves = 2 if time_count % 2 == 0 else 1
     span = time_count // halves
     far_tile = [(h * span, shifted(eigenvectors[h * span : (h + 1) * span], SPACE, -2)) for h in range(halves)]
     row_in = swapped(eigenvectors[..., :LZ], SPACE, 0)

time: 181 us -> 163 us (0.901)
  starting transfers between devices: 52.2 us -> 24.2 us
  waiting for transfers between devices: 53.4 us -> 74 us
  Pallas kernels: 40 us -> 30.4 us
    ppermute x30 -> x14, starting transfers between devices: 45 us -> 22 us  [shifted(): return lax.ppermute(block, axis, route)]
    ppermute x30 -> x14, waiting for transfers between devices: 30.3 us -> 52.8 us  [shifted(): return lax.ppermute(block, axis, route)]
    pallas_call x6 -> x2, Pallas kernels: 22.4 us -> 12.8 us  [second_pass(): pl.pallas_call(functools.partial(sums_kernel, scale=scale, course_list=(0...]
    ppermute x13 -> x5, starting transfers between devices: 7.23 us -> 2.23 us  [swapped(): lax.ppermute(value, axis, [(i, i ^ 1 << bit) for i in range(lax.axis_size...]
    squeeze x6 -> x2, local copies, waits for them, and re-layouts: 6.4 us -> 3.81 us  [body(): send = lax.dynamic_index_in_dim(part_blocks, 1 - core, 3, keepdims=False)]
    ppermute x13 -> x5, waiting for transfers between devices: 23.1 us -> 21.2 us  [swapped(): lax.ppermute(value, axis, [(i, i ^ 1 << bit) for i in range(lax.axis_size...]
    unnamed x38 -> x22, local copies, waits for them, and re-layouts: 3.69 us -> 5.09 us
  transfers between devices with their start and end apart: 43 -> 19, of which waited for: 16 -> 12; matrix products, arithmetic and copies ran while one was open for 13% -> 12% of each run, Pallas kernels for 19% -> 11%
where the time goes in v21:
time: 163 us
  waiting for transfers between devices  74 us (45%)
  Pallas kernels  30.4 us (19%)
  starting transfers between devices  24.2 us (15%)
  local copies, waits for them, and re-layouts  24 us (15%)
  other arithmetic  8.42 us (5%)
  between operations  1.65 us (1%)
    ppermute x14, waiting for transfers between devices, shifted(): return lax.ppermute(block, axis, route)  52.8 us
    ppermute x14, starting transfers between devices, shifted(): return lax.ppermute(block, axis, route)  22 us
    ppermute x5, waiting for transfers between devices, swapped(): lax.ppermute(value, axis, [(i, i ^ 1 << bit) for i in range(lax.axis_size...  21.2 us
    pallas_call x2, Pallas kernels, second_pass(): pl.pallas_call(functools.partial(sums_kernel, scale=scale, course_list=(0...  12.8 us
    pallas_call x1, Pallas kernels, local_sums(): pl.pallas_call(functools.partial(sums_kernel, scale=scale, course_list=ne...  11 us
    pallas_call x1, Pallas kernels, contract_panel(): pl.pallas_call(panel_kernel, grid=(count_ops,), in_specs=[pl.BlockSpec((1...  6.63 us
    unnamed x22, local copies, waits for them, and re-layouts  5.09 us
    squeeze x2, local copies, waits for them, and re-layouts, body(): send = lax.dynamic_index_in_dim(part_blocks, 1 - core, 3, keepdims=False)  3.81 us
  transfers between devices with their start and end apart: 19, of which 12 were waited for; matrix products, arithmetic and copies ran while one was open for 12% of the time, Pallas kernels for 11%

profile of v21, /device:TPU:0, one launch (start us, length us, event | category | flops | bytes accessed | tf_op | source)
XLA Modules:
  0.0 162.7 jit_solution(680585961893765354)
XLA Ops:
  0.7 3.5 %fusion.31 = (bf16[3,2,3,256,128]{4,3,2,1,0:T(8,128)(2,1)}, bf16[3,2,3,256,128]{4,3,2,1,0:T(8,128)(2,1)}) fusion(bf16[6,2,3,256,128]{4,3,2,1,0:T(8,128)(2,1)} %field_ref.5), kind=kLoop, calls=%fused_computation.105 | loop fusion | bytes 4718592 | tf_op jit(solution)/shard_map/slice | solution.py:225
  4.1 6.0 %collective-permute-start = (bf16[3,2,3,256,128]{4,3,2,1,0:T(8,128)(2,1)}, bf16[3,2,3,256,128]{4,3,2,1,0:T(8,128)(2,1)}, u32[]{:S(2)}, u32[]{:S(2)}) collective-permute-start(bf16[3,2,3,256,128]{4,3,2,1,0:T(8,128)(2,1)} %get-tuple-element.26), channel_id=1, source_target_pairs={{2,0},{3,1},{4,2},{5,3},{6,4},{7,5},{8,6},{9,7},{10,8},{11,9},{12,... | collective-permute-start | bytes 3538952 | tf_op jit(solution)/shard_map/ppermute | solution.py:20
  15.4 1.7 %copy.35.link_ref = f32[6,3,2,3,3,128]{5,4,3,2,1,0:T(4,128)} copy(f32[6,3,2,3,3,128]{5,2,4,3,1,0:T(2,128)} %param.9) | data formatting | bytes 331776 | tf_op args[1]
  17.7 2.2 %copy.33 = bf16[6,2,3,256,8]{4,3,2,1,0:T(8,128)(2,1)S(1)} copy(bf16[6,2,3,256,8]{3,4,2,1,0:T(8,128)(2,1)} %collective-permute-done.1) | data formatting | bytes 294912 | tf_op jit(solution)/shard_map/ppermute | solution.py:24
  19.8 2.3 %pad.6.near_ref = bf16[6,2,3,256,128]{4,3,2,1,0:T(8,128)(2,1)} pad(bf16[6,2,3,256,8]{4,3,2,1,0:T(8,128)(2,1)S(1)} %copy.33, bf16[]{:T(256)} %constant.245.clone.1), padding=0_0x0_0x0_0x0_0x120_0 | pad | bytes 2506754 | tf_op jit(solution)/shard_map/jit(_pad)/pad | solution.py:103
  22.1 11.0 %shard_map.77 = (bf16[6,1536,256]{2,1,0:T(8,128)(2,1)}, bf16[6,512,768]{2,1,0:T(8,128)(2,1)}) custom-call(s32[3]{0:T(128)} %select_reduce_fusion.slot_ref, bf16[6,2,3,256,128]{4,3,2,1,0:T(8,128)(2,1)} %field_ref.5, bf16[6,2,3,256,128]{4,3,2,1,0:T(8,128)(2,1)} %pad.6.near_ref, f32[6,3,2,3,3,128]{5,4,3,2,1,0:T(4,128)} %copy.35.link_ref, ...), custom_call_target="tpu_custom_call" | custom-call | tf_op jit(solution)/shard_map/pallas_call | solution.py:118
  33.1 3.8 %collective-permute-done.near_ref = bf16[3,2,3,256,128]{4,3,2,1,0:T(8,128)(2,1)} collective-permute-done((bf16[3,2,3,256,128]{4,3,2,1,0:T(8,128)(2,1)}, bf16[3,2,3,256,128]{4,3,2,1,0:T(8,128)(2,1)}, u32[]{:S(2)}, u32[]{:S(2)}) %collective-permute-start) | collective-permute-done | bytes 1179680 | tf_op jit(solution)/shard_map/ppermute | solution.py:20
  36.8 6.4 %shard_map.78 = bf16[3,1536,256]{2,1,0:T(8,128)(2,1)} custom-call(s32[3]{0:T(128)} %select_reduce_fusion.slot_ref, bf16[6,2,3,256,128]{4,3,2,1,0:T(8,128)(2,1)} %field_ref.5, bf16[3,2,3,256,128]{4,3,2,1,0:T(8,128)(2,1)} %collective-permute-done.near_ref, f32[6,3,2,3,3,128]{5,4,3,2,1,0:T(4,128)} %copy.35.link_ref, ...), custom_call_target="tpu_custom_call" | custom-call | tf_op jit(solution)/shard_map/pallas_call | solution.py:147
  43.2 2.5 %dynamic-slice_bitcast_fusion.1 = bf16[3,4,2,96,256]{4,3,2,1,0:T(8,128)(2,1)} fusion(bf16[3,4,2,2,96,256]{5,4,3,2,1,0:T(8,128)(2,1)} %bitcast.98, s32[]{:T(128)S(6)} %select_n.291), kind=kLoop, calls=%fused_computation.15 | loop fusion | bytes 2359300 | tf_op jit(solution)/shard_map/jit(dynamic_index_in_dim)/squeeze | solution.py:240
  48.3 12.6 %collective-permute-done.7.near_ref = bf16[3,2,3,256,128]{4,3,2,1,0:T(8,128)(2,1)S(1)} collective-permute-done((bf16[3,2,3,256,128]{4,3,2,1,0:T(8,128)(2,1)}, bf16[3,2,3,256,128]{4,3,2,1,0:T(8,128)(2,1)S(1)}, u32[]{:S(2)}, u32[]{:S(2)}) %collective-permute-start.7) | collective-permute-done | bytes 1179680 | tf_op jit(solution)/shard_map/ppermute | solution.py:20
  62.0 6.4 %shard_map.79 = bf16[3,1536,256]{2,1,0:T(8,128)(2,1)} custom-call(s32[3]{0:T(128)} %select_reduce_fusion.slot_ref, bf16[6,2,3,256,128]{4,3,2,1,0:T(8,128)(2,1)} %field_ref.5, bf16[3,2,3,256,128]{4,3,2,1,0:T(8,128)(2,1)} %copy-done.6, f32[6,3,2,3,3,128]{5,4,3,2,1,0:T(4,128)} %copy.35.link_ref, bf16[6,512,768]{2,1,0:T(8,128)(2,1)} %get-tuple-element.6.trig_ref, ...), custom_call_target="tpu_custom_call" | custom-call | tf_op jit(solution)/shard_map/pallas_call | solution.py:147
  72.4 1.7 %convert_add_fusion.1 = f32[3,4,2,96,256]{4,3,2,1,0:T(8,128)S(1)} fusion(bf16[3,4,2,96,256]{4,3,2,1,0:T(8,128)(2,1)} %collective-permute-done.2, bf16[3,4,2,2,96,256]{5,4,3,2,1,0:T(8,128)(2,1)S(1)} %bitcast.99, s32[]{:T(128)S(6)} %select_n.290), kind=kLoop, calls=%fused_computation.6 | loop fusion | flops 1769472 | bytes 4718596 | tf_op jit(solution)/shard_map/add | solution.py:251
  75.0 1.9 %collective-permute-start.9 = (bf16[3,4,96,256]{3,2,1,0:T(8,128)(2,1)S(1)}, bf16[3,4,96,256]{3,2,1,0:T(8,128)(2,1)S(1)}, u32[]{:S(2)}, u32[]{:S(2)}) collective-permute-start(bf16[3,4,96,256]{3,2,1,0:T(8,128)(2,1)S(1)} %fusion.1), channel_id=1, source_target_pairs={{0,2},{1,3},{2,0},{3,1},{4,6},{5,7},{6,4},{7,5},{8,10},{9,11},{10,... | collective-permute-start | bytes 1769480 | tf_op jit(solution)/shard_map/ppermute | solution.py:24
  76.9 13.6 %collective-permute-done.3 = bf16[3,4,96,256]{3,2,1,0:T(8,128)(2,1)S(1)} collective-permute-done((bf16[3,4,96,256]{3,2,1,0:T(8,128)(2,1)S(1)}, bf16[3,4,96,256]{3,2,1,0:T(8,128)(2,1)S(1)}, u32[]{:S(2)}, u32[]{:S(2)}) %collective-permute-start.3) | collective-permute-done | bytes 589856 | tf_op jit(solution)/shard_map/ppermute | solution.py:24
  90.7 3.7 %collective-permute-start.6 = (bf16[3,96,256]{2,1,0:T(8,128)(2,1)S(1)}, bf16[3,96,256]{2,1,0:T(8,128)(2,1)S(1)}, u32[]{:S(2)}, u32[]{:S(2)}) collective-permute-start(bf16[3,96,256]{2,1,0:T(8,128)(2,1)S(1)} %get-tuple-element.31), channel_id=1, source_target_pairs={{4,0},{8,4},{12,8},{0,12},{5,1},{9,5},{13,9},{1,13},{6,2},{10,6},{... | collective-permute-start | bytes 442376 | tf_op jit(solution)/shard_map/ppermute | solution.py:20
  95.1 7.6 %collective-permute-done.9 = bf16[3,4,96,256]{3,2,1,0:T(8,128)(2,1)S(1)} collective-permute-done((bf16[3,4,96,256]{3,2,1,0:T(8,128)(2,1)S(1)}, bf16[3,4,96,256]{3,2,1,0:T(8,128)(2,1)S(1)}, u32[]{:S(2)}, u32[]{:S(2)}) %collective-permute-start.9) | collective-permute-done | bytes 589856 | tf_op jit(solution)/shard_map/ppermute | solution.py:24
  102.9 3.9 %collective-permute-start.12 = (bf16[3,96,256]{2,1,0:T(8,128)(2,1)S(1)}, bf16[3,96,256]{2,1,0:T(8,128)(2,1)S(1)}, u32[]{:S(2)}, u32[]{:S(2)}) collective-permute-start(bf16[3,96,256]{2,1,0:T(8,128)(2,1)S(1)} %get-tuple-element.34), channel_id=1, source_target_pairs={{4,0},{8,4},{12,8},{0,12},{5,1},{9,5},{13,9},{1,13},{6,2},{10,6},{... | collective-permute-start | bytes 442376 | tf_op jit(solution)/shard_map/ppermute | solution.py:20
  107.7 3.5 %collective-permute-done.12 = bf16[3,96,256]{2,1,0:T(8,128)(2,1)S(1)} collective-permute-done((bf16[3,96,256]{2,1,0:T(8,128)(2,1)S(1)}, bf16[3,96,256]{2,1,0:T(8,128)(2,1)S(1)}, u32[]{:S(2)}, u32[]{:S(2)}) %collective-permute-start.12) | collective-permute-done | bytes 147488 | tf_op jit(solution)/shard_map/ppermute | solution.py:20
  111.2 8.3 %collective-permute-done.11 = bf16[3,96,256]{2,1,0:T(8,128)(2,1)S(1)} collective-permute-done((bf16[3,96,256]{2,1,0:T(8,128)(2,1)S(1)}, bf16[3,96,256]{2,1,0:T(8,128)(2,1)S(1)}, u32[]{:S(2)}, u32[]{:S(2)}) %collective-permute-start.11) | collective-permute-done | bytes 147488 | tf_op jit(solution)/shard_map/ppermute | solution.py:20
  123.2 1.9 %collective-permute-start.13 = (bf16[2,96,256]{2,1,0:T(8,128)(2,1)S(1)}, bf16[2,96,256]{2,1,0:T(8,128)(2,1)S(1)}, u32[]{:S(2)}, u32[]{:S(2)}) collective-permute-start(bf16[2,96,256]{2,1,0:T(8,128)(2,1)S(1)} %get-tuple-element.39), channel_id=1, source_target_pairs={{12,0},{0,4},{4,8},{8,12},{13,1},{1,5},{5,9},{9,13},{14,2},{2,6},{... | collective-permute-start | bytes 294920 | tf_op jit(solution)/shard_map/ppermute | solution.py:20
  125.9 5.7 %collective-permute-done.14 = bf16[2,96,256]{2,1,0:T(8,128)(2,1)S(1)} collective-permute-done((bf16[2,96,256]{2,1,0:T(8,128)(2,1)S(1)}, bf16[2,96,256]{2,1,0:T(8,128)(2,1)S(1)}, u32[]{:S(2)}, u32[]{:S(2)}) %collective-permute-start.14) | collective-permute-done | bytes 98336 | tf_op jit(solution)/shard_map/ppermute | solution.py:20
  134.2 6.7 %collective-permute-done.18 = bf16[4,2,96,256]{3,2,1,0:T(8,128)(2,1)S(1)} collective-permute-done((bf16[4,2,96,256]{3,2,1,0:T(8,128)(2,1)S(1)}, bf16[4,2,96,256]{3,2,1,0:T(8,128)(2,1)S(1)}, u32[]{:S(2)}, u32[]{:S(2)}) %collective-permute-start.18) | collective-permute-done | bytes 393248 | tf_op jit(solution)/shard_map/ppermute | solution.py:20
  141.0 11.1 %collective-permute-done.17 = bf16[4,2,96,256]{3,2,1,0:T(8,128)(2,1)S(1)} collective-permute-done((bf16[4,2,96,256]{3,2,1,0:T(8,128)(2,1)S(1)}, bf16[4,2,96,256]{3,2,1,0:T(8,128)(2,1)S(1)}, u32[]{:S(2)}, u32[]{:S(2)}) %collective-permute-start.17) | collective-permute-done | bytes 393248 | tf_op jit(solution)/shard_map/ppermute | solution.py:20
  154.6 6.6 %shard_map.80 = f32[3,2,256]{2,1,0:T(2,128)} custom-call(bf16[2,3,2,256,256]{4,3,2,1,0:T(8,128)(2,1)} %bitcast.96, bf16[2,3,2,256,256]{4,3,2,1,0:T(8,128)(2,1)} %bitcast.97, bf16[512,1024]{1,0:T(8,128)(2,1)} %bitcast.103, bf16[2048,512]{1,0:T(8,128)(2,1)} %maximum_maximum_fusion.wide_ref), custom_call_target="tpu_custom_call" | custom-call | tf_op jit(solution)/shard_map/pallas_call | solution.py:193
  (95 shorter events, 26.4 us)
Async XLA Ops:
  0.6 45.1 %copy-start = (s32[4,2]{0,1:T(2,128)S(1)}, s32[4,2]{0,1:T(2,128)}, u32[]{:S(2)}) copy-start(s32[4,2]{0,1:T(2,128)} %param.13) | copy-start | bytes 100
  0.6 10.0 %copy-start.1 = (bf16[6,2,3,256,128]{4,3,2,1,0:T(8,128)(2,1)S(1)}, bf16[6,2,3,256,128]{4,3,2,1,0:T(8,128)(2,1)}, u32[]{:S(2)}) copy-start(bf16[6,2,3,256,128]{4,3,2,1,0:T(8,128)(2,1)} %field_ref.5) | copy-start | bytes 7077892
  4.1 8.0 %copy-start.8 = (s32[1,3]{1,0:T(1,128)S(1)}, s32[1,3]{1,0:T(1,128)}, u32[]{:S(2)}) copy-start(s32[1,3]{1,0:T(1,128)} %param.12) | copy-start | bytes 40
  4.1 12.9 %copy-start.9 = (s32[3]{0:T(128)S(1)}, s32[3]{0:T(128)}, u32[]{:S(2)}) copy-start(s32[3]{0:T(128)} %param.11) | copy-start | bytes 40
  4.1 32.7 %collective-permute-start = (bf16[3,2,3,256,128]{4,3,2,1,0:T(8,128)(2,1)}, bf16[3,2,3,256,128]{4,3,2,1,0:T(8,128)(2,1)}, u32[]{:S(2)}, u32[]{:S(2)}) collective-permute-start(bf16[3,2,3,256,128]{4,3,2,1,0:T(8,128)(2,1)} %get-tuple-element.26), channel_id=1, source_target_pairs={{2,0},{3,1},{4,2},{5,3},{6,4},{7,5},{8,6},{9,7},{10,8},{11,9},{12,... | collective-permute-start | bytes 3538952 | tf_op jit(solution)/shard_map/ppermute | solution.py:20
  10.1 50.8 %collective-permute-start.7 = (bf16[3,2,3,256,128]{4,3,2,1,0:T(8,128)(2,1)}, bf16[3,2,3,256,128]{4,3,2,1,0:T(8,128)(2,1)S(1)}, u32[]{:S(2)}, u32[]{:S(2)}) collective-permute-start(bf16[3,2,3,256,128]{4,3,2,1,0:T(8,128)(2,1)} %get-tuple-element.27), channel_id=1, source_target_pairs={{2,0},{3,1},{4,2},{5,3},{6,4},{7,5},{8,6},{9,7},{10,8},{11,9},{12,... | collective-permute-start | bytes 3538952 | tf_op jit(solution)/shard_map/ppermute | solution.py:20
  12.1 5.5 %collective-permute-start.1 = (bf16[6,2,3,256,8]{3,4,2,1,0:T(8,128)(2,1)}, bf16[6,2,3,256,8]{3,4,2,1,0:T(8,128)(2,1)}, u32[]{:S(2)}, u32[]{:S(2)}) collective-permute-start(bf16[6,2,3,256,8]{3,4,2,1,0:T(8,128)(2,1)} %copy.42), channel_id=1, source_target_pairs={{0,1},{1,0},{2,3},{3,2},{4,5},{5,4},{6,7},{7,6},{8,9},{9,8},{10,11... | collective-permute-start | bytes 442376 | tf_op jit(solution)/shard_map/ppermute | solution.py:24
  45.7 15.3 %collective-permute-start.2 = (bf16[3,4,2,96,256]{4,3,2,1,0:T(8,128)(2,1)}, bf16[3,4,2,96,256]{4,3,2,1,0:T(8,128)(2,1)}, u32[]{:S(2)}, u32[]{:S(2)}) collective-permute-start(bf16[3,4,2,96,256]{4,3,2,1,0:T(8,128)(2,1)} %dynamic-slice_bitcast_fusion.1), channel_id=1, source_target_pairs={{0,1},{1,0},{2,3},{3,2},{4,5},{5,4},{6,7},{7,6},{8,9},{9,8},{10,11... | collective-permute-start | bytes 3538952 | tf_op jit(solution)/shard_map/ppermute | solution.py:24
  69.7 4.8 %collective-permute-start.8 = (bf16[3,4,2,96,256]{4,3,2,1,0:T(8,128)(2,1)S(1)}, bf16[3,4,2,96,256]{4,3,2,1,0:T(8,128)(2,1)S(1)}, u32[]{:S(2)}, u32[]{:S(2)}) collective-permute-start(bf16[3,4,2,96,256]{4,3,2,1,0:T(8,128)(2,1)S(1)} %dynamic-slice_bitcast_fusion), channel_id=1, source_target_pairs={{0,1},{1,0},{2,3},{3,2},{4,5},{5,4},{6,7},{7,6},{8,9},{9,8},{10,11... | collective-permute-start | bytes 3538952 | tf_op jit(solution)/shard_map/ppermute | solution.py:24
  74.2 16.2 %collective-permute-start.3 = (bf16[3,4,96,256]{3,2,1,0:T(8,128)(2,1)S(1)}, bf16[3,4,96,256]{3,2,1,0:T(8,128)(2,1)S(1)}, u32[]{:S(2)}, u32[]{:S(2)}) collective-permute-start(bf16[3,4,96,256]{3,2,1,0:T(8,128)(2,1)S(1)} %fusion), channel_id=1, source_target_pairs={{0,2},{1,3},{2,0},{3,1},{4,6},{5,7},{6,4},{7,5},{8,10},{9,11},{10,... | collective-permute-start | bytes 1769480 | tf_op jit(solution)/shard_map/ppermute | solution.py:24
  75.0 27.7 %collective-permute-start.9 = (bf16[3,4,96,256]{3,2,1,0:T(8,128)(2,1)S(1)}, bf16[3,4,96,256]{3,2,1,0:T(8,128)(2,1)S(1)}, u32[]{:S(2)}, u32[]{:S(2)}) collective-permute-start(bf16[3,4,96,256]{3,2,1,0:T(8,128)(2,1)S(1)} %fusion.1), channel_id=1, source_target_pairs={{0,2},{1,3},{2,0},{3,1},{4,6},{5,7},{6,4},{7,5},{8,10},{9,11},{10,... | collective-permute-start | bytes 1769480 | tf_op jit(solution)/shard_map/ppermute | solution.py:24
  90.7 16.2 %collective-permute-start.6 = (bf16[3,96,256]{2,1,0:T(8,128)(2,1)S(1)}, bf16[3,96,256]{2,1,0:T(8,128)(2,1)S(1)}, u32[]{:S(2)}, u32[]{:S(2)}) collective-permute-start(bf16[3,96,256]{2,1,0:T(8,128)(2,1)S(1)} %get-tuple-element.31), channel_id=1, source_target_pairs={{4,0},{8,4},{12,8},{0,12},{5,1},{9,5},{13,9},{1,13},{6,2},{10,6},{... | collective-permute-start | bytes 442376 | tf_op jit(solution)/shard_map/ppermute | solution.py:20
  94.4 13.2 %collective-permute-start.5 = (bf16[3,96,256]{2,1,0:T(8,128)(2,1)S(1)}, bf16[3,96,256]{2,1,0:T(8,128)(2,1)S(1)}, u32[]{:S(2)}, u32[]{:S(2)}) collective-permute-start(bf16[3,96,256]{2,1,0:T(8,128)(2,1)S(1)} %get-tuple-element.32), channel_id=1, source_target_pairs={{8,0},{12,4},{0,8},{4,12},{9,1},{13,5},{1,9},{5,13},{10,2},{14,6},... | collective-permute-start | bytes 442376 | tf_op jit(solution)/shard_map/ppermute | solution.py:20
  94.4 13.2 %collective-permute-start.4 = (bf16[3,96,256]{2,1,0:T(8,128)(2,1)S(1)}, bf16[3,96,256]{2,1,0:T(8,128)(2,1)S(1)}, u32[]{:S(2)}, u32[]{:S(2)}) collective-permute-start(bf16[3,96,256]{2,1,0:T(8,128)(2,1)S(1)} %get-tuple-element.30), channel_id=1, source_target_pairs={{12,0},{0,4},{4,8},{8,12},{13,1},{1,5},{5,9},{9,13},{14,2},{2,6},{... | collective-permute-start | bytes 442376 | tf_op jit(solution)/shard_map/ppermute | solution.py:20
  102.9 8.2 %collective-permute-start.12 = (bf16[3,96,256]{2,1,0:T(8,128)(2,1)S(1)}, bf16[3,96,256]{2,1,0:T(8,128)(2,1)S(1)}, u32[]{:S(2)}, u32[]{:S(2)}) collective-permute-start(bf16[3,96,256]{2,1,0:T(8,128)(2,1)S(1)} %get-tuple-element.34), channel_id=1, source_target_pairs={{4,0},{8,4},{12,8},{0,12},{5,1},{9,5},{13,9},{1,13},{6,2},{10,6},{... | collective-permute-start | bytes 442376 | tf_op jit(solution)/shard_map/ppermute | solution.py:20
  106.9 12.6 %collective-permute-start.11 = (bf16[3,96,256]{2,1,0:T(8,128)(2,1)S(1)}, bf16[3,96,256]{2,1,0:T(8,128)(2,1)S(1)}, u32[]{:S(2)}, u32[]{:S(2)}) collective-permute-start(bf16[3,96,256]{2,1,0:T(8,128)(2,1)S(1)} %get-tuple-element.35), channel_id=1, source_target_pairs={{8,0},{12,4},{0,8},{4,12},{9,1},{13,5},{1,9},{5,13},{10,2},{14,6},... | collective-permute-start | bytes 442376 | tf_op jit(solution)/shard_map/ppermute | solution.py:20
  106.9 12.6 %collective-permute-start.10 = (bf16[3,96,256]{2,1,0:T(8,128)(2,1)S(1)}, bf16[3,96,256]{2,1,0:T(8,128)(2,1)S(1)}, u32[]{:S(2)}, u32[]{:S(2)}) collective-permute-start(bf16[3,96,256]{2,1,0:T(8,128)(2,1)S(1)} %get-tuple-element.33), channel_id=1, source_target_pairs={{12,0},{0,4},{4,8},{8,12},{13,1},{1,5},{5,9},{9,13},{14,2},{2,6},{... | collective-permute-start | bytes 442376 | tf_op jit(solution)/shard_map/ppermute | solution.py:20
  119.6 12.1 %copy-start.5 = (bf16[6,96,256]{2,1,0:T(8,128)(2,1)}, bf16[6,96,256]{2,1,0:T(8,128)(2,1)S(1)}, u32[]{:S(2)}) copy-start(bf16[6,96,256]{2,1,0:T(8,128)(2,1)S(1)} %pad_maximum_fusion.2) | copy-start | bytes 884740
  120.4 5.5 %collective-permute-start.15 = (bf16[2,96,256]{2,1,0:T(8,128)(2,1)S(1)}, bf16[2,96,256]{2,1,0:T(8,128)(2,1)S(1)}, u32[]{:S(2)}, u32[]{:S(2)}) collective-permute-start(bf16[2,96,256]{2,1,0:T(8,128)(2,1)S(1)} %get-tuple-element.37), channel_id=1, source_target_pairs={{4,0},{8,4},{12,8},{0,12},{5,1},{9,5},{13,9},{1,13},{6,2},{10,6},{... | collective-permute-start | bytes 294920 | tf_op jit(solution)/shard_map/ppermute | solution.py:20
  121.7 9.9 %collective-permute-start.14 = (bf16[2,96,256]{2,1,0:T(8,128)(2,1)S(1)}, bf16[2,96,256]{2,1,0:T(8,128)(2,1)S(1)}, u32[]{:S(2)}, u32[]{:S(2)}) collective-permute-start(bf16[2,96,256]{2,1,0:T(8,128)(2,1)S(1)} %get-tuple-element.38), channel_id=1, source_target_pairs={{8,0},{12,4},{0,8},{4,12},{9,1},{13,5},{1,9},{5,13},{10,2},{14,6},... | collective-permute-start | bytes 294920 | tf_op jit(solution)/shard_map/ppermute | solution.py:20
  123.2 8.4 %collective-permute-start.13 = (bf16[2,96,256]{2,1,0:T(8,128)(2,1)S(1)}, bf16[2,96,256]{2,1,0:T(8,128)(2,1)S(1)}, u32[]{:S(2)}, u32[]{:S(2)}) collective-permute-start(bf16[2,96,256]{2,1,0:T(8,128)(2,1)S(1)} %get-tuple-element.39), channel_id=1, source_target_pairs={{12,0},{0,4},{4,8},{8,12},{13,1},{1,5},{5,9},{9,13},{14,2},{2,6},{... | collective-permute-start | bytes 294920 | tf_op jit(solution)/shard_map/ppermute | solution.py:20
  132.4 8.6 %collective-permute-start.18 = (bf16[4,2,96,256]{3,2,1,0:T(8,128)(2,1)S(1)}, bf16[4,2,96,256]{3,2,1,0:T(8,128)(2,1)S(1)}, u32[]{:S(2)}, u32[]{:S(2)}) collective-permute-start(bf16[4,2,96,256]{3,2,1,0:T(8,128)(2,1)S(1)} %broadcast_select_fusion), channel_id=1, source_target_pairs={{1,0},{2,1},{3,2},{0,3},{5,4},{6,5},{7,6},{4,7},{9,8},{10,9},{11,1... | collective-permute-start | bytes 1179656 | tf_op jit(solution)/shard_map/ppermute | solution.py:20
  132.4 19.7 %collective-permute-start.17 = (bf16[4,2,96,256]{3,2,1,0:T(8,128)(2,1)S(1)}, bf16[4,2,96,256]{3,2,1,0:T(8,128)(2,1)S(1)}, u32[]{:S(2)}, u32[]{:S(2)}) collective-permute-start(bf16[4,2,96,256]{3,2,1,0:T(8,128)(2,1)S(1)} %broadcast_select_fusion), channel_id=1, source_target_pairs={{2,0},{3,1},{0,2},{1,3},{6,4},{7,5},{4,6},{5,7},{10,8},{11,9},{8,1... | collective-permute-start | bytes 1179656 | tf_op jit(solution)/shard_map/ppermute | solution.py:20
  133.9 18.3 %collective-permute-start.16 = (bf16[4,2,96,256]{3,2,1,0:T(8,128)(2,1)S(1)}, bf16[4,2,96,256]{3,2,1,0:T(8,128)(2,1)S(1)}, u32[]{:S(2)}, u32[]{:S(2)}) collective-permute-start(bf16[4,2,96,256]{3,2,1,0:T(8,128)(2,1)S(1)} %broadcast_select_fusion), channel_id=1, source_target_pairs={{3,0},{0,1},{1,2},{2,3},{7,4},{4,5},{5,6},{6,7},{11,8},{8,9},{9,10... | collective-permute-start | bytes 1179656 | tf_op jit(solution)/shard_map/ppermute | solution.py:20
  (5 other events, 12.8 us)

commit v22 on v21

--- a/solution.py
+++ b/solution.py
@@ -220,9 +220,12 @@
     coord_y = device % 2 * half_rows + column // LZ
     coord_z = column % LZ
     angle = phase_angles(momenta, (coord_x, coord_y, coord_z), (extent_x, LY, LZ))[0]
-    halves = 2 if time_count % 2 == 0 else 1
-    span = time_count // halves
-    far_tile = [(h * span, shifted(eigenvectors[h * span : (h + 1) * span], SPACE, -2)) for h in range(halves)]
+    lead = (time_count + 1) // 2
+    middle = (time_count - lead + 1) // 2
+    sizes = [size for size in (lead, middle, time_count - lead - middle) if size > 0]
+    starts = [sum(sizes[:h]) for h in range(len(sizes))]
+    halves = len(sizes)
+    far_tile = [(starts[h], shifted(eigenvectors[starts[h] : starts[h] + sizes[h]], SPACE, -2)) for h in range(halves)]
     row_in = swapped(eigenvectors[..., :LZ], SPACE, 0)
     scale = 1.0 / math.sqrt(3.0 * extent_x * LY * LZ)
     slot_of, left, first_partial = local_sums(eigenvectors, gauge_links, row_in, directions, angle, scale)
@@ -236,7 +239,7 @@
         chunk_partial = second_pass(slot_of, eigenvectors, gauge_links, left, first_partial, first, far_part, scale)
         partial_chunks.append(chunk_partial)
         if count_slabs <= 8:
-            part_blocks = chunk_partial.reshape(span, count_slabs, 2, 2, -1, count_ev)
+            part_blocks = chunk_partial.reshape(sizes[half], count_slabs, 2, 2, -1, count_ev)
             send = lax.dynamic_index_in_dim(part_blocks, 1 - core, 3, keepdims=False)
             swapped_chunks.append(swapped(send, "member", 0))
     partial = jnp.concatenate(partial_chunks, 0)
@@ -246,7 +249,7 @@
         side = member // 2
         own_parts = []
         for half in range(halves):
-            part_blocks = partial_chunks[half].reshape(span, count_slabs, 2, 2, rows, count_ev)
+            part_blocks = partial_chunks[half].reshape(sizes[half], count_slabs, 2, 2, rows, count_ev)
             keep = lax.dynamic_index_in_dim(part_blocks, core, 3, keepdims=False).astype(jnp.float32)
             chunk = keep + swapped_chunks[half].astype(jnp.float32)
             keep = lax.dynamic_index_in_dim(chunk, side, 2, keepdims=False)

time: 163 us -> 173 us (1.061)
  starting transfers between devices: 24.2 us -> 40.1 us
  waiting for transfers between devices: 74 us -> 59.5 us
  local copies, waits for them, and re-layouts: 24 us -> 28 us
  other arithmetic: 8.42 us -> 10.5 us
  Pallas kernels: 30.4 us -> 32.2 us
    ppermute x14 -> x18, starting transfers between devices: 22 us -> 32.8 us  [shifted(): return lax.ppermute(block, axis, route)]
    ppermute x14 -> x18, waiting for transfers between devices: 52.8 us -> 42.7 us  [shifted(): return lax.ppermute(block, axis, route)]
    ppermute x5 -> x7, starting transfers between devices: 2.23 us -> 7.26 us  [swapped(): lax.ppermute(value, axis, [(i, i ^ 1 << bit) for i in range(lax.axis_size...]
    ppermute x5 -> x7, waiting for transfers between devices: 21.2 us -> 16.9 us  [swapped(): lax.ppermute(value, axis, [(i, i ^ 1 << bit) for i in range(lax.axis_size...]
    pallas_call x2 -> x3, Pallas kernels: 12.8 us -> 14.6 us  [second_pass(): pl.pallas_call(functools.partial(sums_kernel, scale=scale, course_list=(0...]
    squeeze x2 -> x3, local copies, waits for them, and re-layouts: 3.81 us -> 4.8 us  [body(): send = lax.dynamic_index_in_dim(part_blocks, 1 - core, 3, keepdims=False)]
    slice x1 -> x3, local copies, waits for them, and re-layouts: 3.47 us -> 4.26 us  [body(): eigenvectors[starts[h]:starts[h] + sizes[h]]]
    unnamed x22 -> x28, local copies, waits for them, and re-layouts: 5.09 us -> 5.09 us
  transfers between devices with their start and end apart: 19 -> 25, of which waited for: 12 -> 14; matrix products, arithmetic and copies ran while one was open for 12% -> 15% of each run, Pallas kernels for 11% -> 11%
where the time goes in v22:
time: 173 us; the launch traced here: 172 us
  waiting for transfers between devices  59.5 us (34%)
  starting transfers between devices  40.1 us (23%)
  Pallas kernels  32.2 us (19%)
  local copies, waits for them, and re-layouts  28 us (16%)
  other arithmetic  10.5 us (6%)
  between operations  1.74 us (1%)
    ppermute x18, waiting for transfers between devices, shifted(): return lax.ppermute(block, axis, route)  42.7 us
    ppermute x18, starting transfers between devices, shifted(): return lax.ppermute(block, axis, route)  32.8 us
    ppermute x7, waiting for transfers between devices, swapped(): lax.ppermute(value, axis, [(i, i ^ 1 << bit) for i in range(lax.axis_size...  16.9 us
    pallas_call x3, Pallas kernels, second_pass(): pl.pallas_call(functools.partial(sums_kernel, scale=scale, course_list=(0...  14.6 us
    pallas_call x1, Pallas kernels, local_sums(): pl.pallas_call(functools.partial(sums_kernel, scale=scale, course_list=ne...  10.9 us
    ppermute x7, starting transfers between devices, swapped(): lax.ppermute(value, axis, [(i, i ^ 1 << bit) for i in range(lax.axis_size...  7.26 us
    pallas_call x1, Pallas kernels, contract_panel(): pl.pallas_call(panel_kernel, grid=(count_ops,), in_specs=[pl.BlockSpec((1...  6.64 us
    unnamed x28, local copies, waits for them, and re-layouts  5.09 us
  transfers between devices with their start and end apart: 25, of which 14 were waited for; matrix products, arithmetic and copies ran while one was open for 15% of the time, Pallas kernels for 11%

profile of v22, /device:TPU:0, one launch (start us, length us, event | category | flops | bytes accessed | tf_op | source)
XLA Modules:
  0.0 172.0 jit_solution(13242857618842464956)
XLA Ops:
  0.7 2.5 %slice.31 = bf16[3,2,3,256,128]{4,3,2,1,0:T(8,128)(2,1)} slice(bf16[6,2,3,256,128]{4,3,2,1,0:T(8,128)(2,1)} %field_ref.7), slice={[0:3], [0:2], [0:3], [0:256], [0:128]} | slice | bytes 2359296 | tf_op jit(solution)/shard_map/slice | solution.py:228
  3.2 6.0 %collective-permute-start = (bf16[3,2,3,256,128]{4,3,2,1,0:T(8,128)(2,1)}, bf16[3,2,3,256,128]{4,3,2,1,0:T(8,128)(2,1)S(1)}, u32[]{:S(2)}, u32[]{:S(2)}) collective-permute-start(bf16[3,2,3,256,128]{4,3,2,1,0:T(8,128)(2,1)} %slice.31), channel_id=1, source_target_pairs={{2,0},{3,1},{4,2},{5,3},{6,4},{7,5},{8,6},{9,7},{10,8},{11,9},{12,... | collective-permute-start | bytes 3538952 | tf_op jit(solution)/shard_map/ppermute | solution.py:20
  18.2 2.4 %pad.6.near_ref = bf16[6,2,3,256,128]{4,3,2,1,0:T(8,128)(2,1)} pad(bf16[6,2,3,256,8]{4,3,2,1,0:T(8,128)(2,1)S(1)} %copy.36, bf16[]{:T(256)} %constant.283.clone.1), padding=0_0x0_0x0_0x0_0x120_0 | pad | bytes 2506754 | tf_op jit(solution)/shard_map/jit(_pad)/pad | solution.py:103
  20.5 10.9 %shard_map.77 = (bf16[6,1536,256]{2,1,0:T(8,128)(2,1)}, bf16[6,512,768]{2,1,0:T(8,128)(2,1)}) custom-call(s32[3]{0:T(128)} %select_reduce_fusion.slot_ref, bf16[6,2,3,256,128]{4,3,2,1,0:T(8,128)(2,1)} %field_ref.7, bf16[6,2,3,256,128]{4,3,2,1,0:T(8,128)(2,1)} %pad.6.near_ref, f32[6,3,2,3,3,128]{5,4,3,2,1,0:T(4,128)} %copy.38.link_ref, ...), custom_call_target="tpu_custom_call" | custom-call | tf_op jit(solution)/shard_map/pallas_call | solution.py:118
  31.5 3.2 %collective-permute-done.near_ref = bf16[3,2,3,256,128]{4,3,2,1,0:T(8,128)(2,1)S(1)} collective-permute-done((bf16[3,2,3,256,128]{4,3,2,1,0:T(8,128)(2,1)}, bf16[3,2,3,256,128]{4,3,2,1,0:T(8,128)(2,1)S(1)}, u32[]{:S(2)}, u32[]{:S(2)}) %collective-permute-start) | collective-permute-done | bytes 1179680 | tf_op jit(solution)/shard_map/ppermute | solution.py:20
  35.8 6.4 %shard_map.78 = bf16[3,1536,256]{2,1,0:T(8,128)(2,1)} custom-call(s32[3]{0:T(128)} %select_reduce_fusion.slot_ref, bf16[6,2,3,256,128]{4,3,2,1,0:T(8,128)(2,1)} %field_ref.7, bf16[3,2,3,256,128]{4,3,2,1,0:T(8,128)(2,1)} %copy-done.9, f32[6,3,2,3,3,128]{5,4,3,2,1,0:T(4,128)} %copy.38.link_ref, bf16[6,512,768]{2,1,0:T(8,128)(2,1)} %get-tuple-element.7.trig_ref, ...), custom_call_target="tpu_custom_call" | custom-call | tf_op jit(solution)/shard_map/pallas_call | solution.py:147
  42.2 2.5 %dynamic-slice_bitcast_fusion = bf16[3,4,2,96,256]{4,3,2,1,0:T(8,128)(2,1)} fusion(bf16[3,4,2,2,96,256]{5,4,3,2,1,0:T(8,128)(2,1)} %bitcast.123, s32[]{:T(128)S(6)} %select_n.313), kind=kLoop, calls=%fused_computation.12 | loop fusion | bytes 2359300 | tf_op jit(solution)/shard_map/jit(dynamic_index_in_dim)/squeeze | solution.py:243
  45.7 5.1 %collective-permute-start.7 = (bf16[2,2,3,256,128]{4,3,2,1,0:T(8,128)(2,1)}, bf16[2,2,3,256,128]{4,3,2,1,0:T(8,128)(2,1)}, u32[]{:S(2)}, u32[]{:S(2)}) collective-permute-start(bf16[2,2,3,256,128]{4,3,2,1,0:T(8,128)(2,1)} %slice.36), channel_id=1, source_target_pairs={{2,0},{3,1},{4,2},{5,3},{6,4},{7,5},{8,6},{9,7},{10,8},{11,9},{12,... | collective-permute-start | bytes 2359304 | tf_op jit(solution)/shard_map/ppermute | solution.py:20
  60.6 8.3 %collective-permute-done.7.near_ref = bf16[2,2,3,256,128]{4,3,2,1,0:T(8,128)(2,1)} collective-permute-done((bf16[2,2,3,256,128]{4,3,2,1,0:T(8,128)(2,1)}, bf16[2,2,3,256,128]{4,3,2,1,0:T(8,128)(2,1)}, u32[]{:S(2)}, u32[]{:S(2)}) %collective-permute-start.7) | collective-permute-done | bytes 786464 | tf_op jit(solution)/shard_map/ppermute | solution.py:20
  68.9 4.4 %shard_map.79 = bf16[2,1536,256]{2,1,0:T(8,128)(2,1)} custom-call(s32[3]{0:T(128)} %select_reduce_fusion.slot_ref, bf16[6,2,3,256,128]{4,3,2,1,0:T(8,128)(2,1)} %field_ref.7, bf16[2,2,3,256,128]{4,3,2,1,0:T(8,128)(2,1)} %collective-permute-done.7.near_ref, f32[6,3,2,3,3,128]{5,4,3,2,1,0:T(4,128)} %copy.38.link_ref, ...), custom_call_target="tpu_custom_call" | custom-call | tf_op jit(solution)/shard_map/pallas_call | solution.py:147
  76.1 10.9 %collective-permute-done.3 = bf16[3,4,96,256]{3,2,1,0:T(8,128)(2,1)} collective-permute-done((bf16[3,4,96,256]{3,2,1,0:T(8,128)(2,1)}, bf16[3,4,96,256]{3,2,1,0:T(8,128)(2,1)}, u32[]{:S(2)}, u32[]{:S(2)}) %collective-permute-start.3) | collective-permute-done | bytes 589856 | tf_op jit(solution)/shard_map/ppermute | solution.py:24
  89.2 6.2 %collective-permute-start.5 = (bf16[3,96,256]{2,1,0:T(8,128)(2,1)S(1)}, bf16[3,96,256]{2,1,0:T(8,128)(2,1)S(1)}, u32[]{:S(2)}, u32[]{:S(2)}) collective-permute-start(bf16[3,96,256]{2,1,0:T(8,128)(2,1)S(1)} %get-tuple-element.34), channel_id=1, source_target_pairs={{8,0},{12,4},{0,8},{4,12},{9,1},{13,5},{1,9},{5,13},{10,2},{14,6},... | collective-permute-start | bytes 442376 | tf_op jit(solution)/shard_map/ppermute | solution.py:20
  95.4 3.8 %shard_map.80 = bf16[1,1536,256]{2,1,0:T(8,128)(2,1)} custom-call(s32[3]{0:T(128)} %select_reduce_fusion.slot_ref, bf16[6,2,3,256,128]{4,3,2,1,0:T(8,128)(2,1)} %field_ref.7, bf16[1,2,3,256,128]{4,3,2,1,0:T(8,128)(2,1)} %collective-permute-done.13.near_ref, f32[6,3,2,3,3,128]{5,4,3,2,1,0:T(4,128)} %copy.38.link_ref, ...), custom_call_target="tpu_custom_call" | custom-call | tf_op jit(solution)/shard_map/pallas_call | solution.py:147
  101.7 2.5 %collective-permute-start.9 = (bf16[2,4,96,256]{3,2,1,0:T(8,128)(2,1)S(1)}, bf16[2,4,96,256]{3,2,1,0:T(8,128)(2,1)S(1)}, u32[]{:S(2)}, u32[]{:S(2)}) collective-permute-start(bf16[2,4,96,256]{3,2,1,0:T(8,128)(2,1)S(1)} %fusion.1), channel_id=1, source_target_pairs={{0,2},{1,3},{2,0},{3,1},{4,6},{5,7},{6,4},{7,5},{8,10},{9,11},{10,... | collective-permute-start | bytes 1179656 | tf_op jit(solution)/shard_map/ppermute | solution.py:24
  105.7 2.5 %collective-permute-start.15 = (bf16[1,4,96,256]{3,2,1,0:T(8,128)(2,1)S(1)}, bf16[1,4,96,256]{3,2,1,0:T(8,128)(2,1)S(1)}, u32[]{:S(2)}, u32[]{:S(2)}) collective-permute-start(bf16[1,4,96,256]{3,2,1,0:T(8,128)(2,1)S(1)} %fusion.5), channel_id=1, source_target_pairs={{0,2},{1,3},{2,0},{3,1},{4,6},{5,7},{6,4},{7,5},{8,10},{9,11},{10,... | collective-permute-start | bytes 589832 | tf_op jit(solution)/shard_map/ppermute | solution.py:24
  108.3 6.0 %collective-permute-done.9 = bf16[2,4,96,256]{3,2,1,0:T(8,128)(2,1)S(1)} collective-permute-done((bf16[2,4,96,256]{3,2,1,0:T(8,128)(2,1)S(1)}, bf16[2,4,96,256]{3,2,1,0:T(8,128)(2,1)S(1)}, u32[]{:S(2)}, u32[]{:S(2)}) %collective-permute-start.9) | collective-permute-done | bytes 393248 | tf_op jit(solution)/shard_map/ppermute | solution.py:24
  116.3 2.4 %collective-permute-start.12 = (bf16[2,96,256]{2,1,0:T(8,128)(2,1)S(1)}, bf16[2,96,256]{2,1,0:T(8,128)(2,1)S(1)}, u32[]{:S(2)}, u32[]{:S(2)}) collective-permute-start(bf16[2,96,256]{2,1,0:T(8,128)(2,1)S(1)} %get-tuple-element.40), channel_id=1, source_target_pairs={{4,0},{8,4},{12,8},{0,12},{5,1},{9,5},{13,9},{1,13},{6,2},{10,6},{... | collective-permute-start | bytes 294920 | tf_op jit(solution)/shard_map/ppermute | solution.py:20
  123.4 2.6 %collective-permute-done.11 = bf16[2,96,256]{2,1,0:T(8,128)(2,1)S(1)} collective-permute-done((bf16[2,96,256]{2,1,0:T(8,128)(2,1)S(1)}, bf16[2,96,256]{2,1,0:T(8,128)(2,1)S(1)}, u32[]{:S(2)}, u32[]{:S(2)}) %collective-permute-start.11) | collective-permute-done | bytes 98336 | tf_op jit(solution)/shard_map/ppermute | solution.py:20
  127.1 3.1 %collective-permute-done.17 = bf16[1,96,256]{2,1,0:T(8,128)(2,1)S(1)} collective-permute-done((bf16[1,96,256]{2,1,0:T(8,128)(2,1)S(1)}, bf16[1,96,256]{2,1,0:T(8,128)(2,1)S(1)}, u32[]{:S(2)}, u32[]{:S(2)}) %collective-permute-start.17) | collective-permute-done | bytes 49184 | tf_op jit(solution)/shard_map/ppermute | solution.py:20
  135.1 3.6 %collective-permute-done.19 = bf16[2,96,256]{2,1,0:T(8,128)(2,1)S(1)} collective-permute-done((bf16[2,96,256]{2,1,0:T(8,128)(2,1)S(1)}, bf16[2,96,256]{2,1,0:T(8,128)(2,1)S(1)}, u32[]{:S(2)}, u32[]{:S(2)}) %collective-permute-start.19) | collective-permute-done | bytes 98336 | tf_op jit(solution)/shard_map/ppermute | solution.py:20
  138.7 3.2 %collective-permute-done.20 = bf16[2,96,256]{2,1,0:T(8,128)(2,1)S(1)} collective-permute-done((bf16[2,96,256]{2,1,0:T(8,128)(2,1)S(1)}, bf16[2,96,256]{2,1,0:T(8,128)(2,1)S(1)}, u32[]{:S(2)}, u32[]{:S(2)}) %collective-permute-start.20) | collective-permute-done | bytes 98336 | tf_op jit(solution)/shard_map/ppermute | solution.py:20
  145.8 7.7 %collective-permute-done.22 = bf16[4,2,96,256]{3,2,1,0:T(8,128)(2,1)S(1)} collective-permute-done((bf16[4,2,96,256]{3,2,1,0:T(8,128)(2,1)S(1)}, bf16[4,2,96,256]{3,2,1,0:T(8,128)(2,1)S(1)}, u32[]{:S(2)}, u32[]{:S(2)}) %collective-permute-start.22) | collective-permute-done | bytes 393248 | tf_op jit(solution)/shard_map/ppermute | solution.py:20
  154.7 6.9 %collective-permute-done.24 = bf16[4,2,96,256]{3,2,1,0:T(8,128)(2,1)S(1)} collective-permute-done((bf16[4,2,96,256]{3,2,1,0:T(8,128)(2,1)S(1)}, bf16[4,2,96,256]{3,2,1,0:T(8,128)(2,1)S(1)}, u32[]{:S(2)}, u32[]{:S(2)}) %collective-permute-start.24) | collective-permute-done | bytes 393248 | tf_op jit(solution)/shard_map/ppermute | solution.py:20
  163.9 6.6 %shard_map.81 = f32[3,2,256]{2,1,0:T(2,128)} custom-call(bf16[2,3,2,256,256]{4,3,2,1,0:T(8,128)(2,1)} %bitcast.121, bf16[2,3,2,256,256]{4,3,2,1,0:T(8,128)(2,1)} %bitcast.122, bf16[512,1024]{1,0:T(8,128)(2,1)} %bitcast.128, bf16[2048,512]{1,0:T(8,128)(2,1)} %maximum_maximum_fusion.wide_ref), custom_call_target="tpu_custom_call" | custom-call | tf_op jit(solution)/shard_map/pallas_call | solution.py:193
  (122 shorter events, 50.4 us)
Async XLA Ops:
  3.2 31.5 %collective-permute-start = (bf16[3,2,3,256,128]{4,3,2,1,0:T(8,128)(2,1)}, bf16[3,2,3,256,128]{4,3,2,1,0:T(8,128)(2,1)S(1)}, u32[]{:S(2)}, u32[]{:S(2)}) collective-permute-start(bf16[3,2,3,256,128]{4,3,2,1,0:T(8,128)(2,1)} %slice.31), channel_id=1, source_target_pairs={{2,0},{3,1},{4,2},{5,3},{6,4},{7,5},{8,6},{9,7},{10,8},{11,9},{12,... | collective-permute-start | bytes 3538952 | tf_op jit(solution)/shard_map/ppermute | solution.py:20
  10.7 5.5 %collective-permute-start.1 = (bf16[6,2,3,256,8]{3,4,2,1,0:T(8,128)(2,1)}, bf16[6,2,3,256,8]{3,4,2,1,0:T(8,128)(2,1)}, u32[]{:S(2)}, u32[]{:S(2)}) collective-permute-start(bf16[6,2,3,256,8]{3,4,2,1,0:T(8,128)(2,1)} %copy.46), channel_id=1, source_target_pairs={{0,1},{1,0},{2,3},{3,2},{4,5},{5,4},{6,7},{7,6},{8,9},{9,8},{10,11... | collective-permute-start | bytes 442376 | tf_op jit(solution)/shard_map/ppermute | solution.py:24
  44.7 10.4 %collective-permute-start.2 = (bf16[3,4,2,96,256]{4,3,2,1,0:T(8,128)(2,1)}, bf16[3,4,2,96,256]{4,3,2,1,0:T(8,128)(2,1)}, u32[]{:S(2)}, u32[]{:S(2)}) collective-permute-start(bf16[3,4,2,96,256]{4,3,2,1,0:T(8,128)(2,1)} %dynamic-slice_bitcast_fusion), channel_id=1, source_target_pairs={{0,1},{1,0},{2,3},{3,2},{4,5},{5,4},{6,7},{7,6},{8,9},{9,8},{10,11... | collective-permute-start | bytes 3538952 | tf_op jit(solution)/shard_map/ppermute | solution.py:24
  45.7 23.2 %collective-permute-start.7 = (bf16[2,2,3,256,128]{4,3,2,1,0:T(8,128)(2,1)}, bf16[2,2,3,256,128]{4,3,2,1,0:T(8,128)(2,1)}, u32[]{:S(2)}, u32[]{:S(2)}) collective-permute-start(bf16[2,2,3,256,128]{4,3,2,1,0:T(8,128)(2,1)} %slice.36), channel_id=1, source_target_pairs={{2,0},{3,1},{4,2},{5,3},{6,4},{7,5},{8,6},{9,7},{10,8},{11,9},{12,... | collective-permute-start | bytes 2359304 | tf_op jit(solution)/shard_map/ppermute | solution.py:20
  51.5 43.9 %collective-permute-start.13 = (bf16[1,2,3,256,128]{4,3,2,1,0:T(8,128)(2,1)}, bf16[1,2,3,256,128]{4,3,2,1,0:T(8,128)(2,1)}, u32[]{:S(2)}, u32[]{:S(2)}) collective-permute-start(bf16[1,2,3,256,128]{4,3,2,1,0:T(8,128)(2,1)} %slice.37), channel_id=1, source_target_pairs={{2,0},{3,1},{4,2},{5,3},{6,4},{7,5},{8,6},{9,7},{10,8},{11,9},{12,... | collective-permute-start | bytes 1179656 | tf_op jit(solution)/shard_map/ppermute | solution.py:20
  58.5 28.4 %collective-permute-start.3 = (bf16[3,4,96,256]{3,2,1,0:T(8,128)(2,1)}, bf16[3,4,96,256]{3,2,1,0:T(8,128)(2,1)}, u32[]{:S(2)}, u32[]{:S(2)}) collective-permute-start(bf16[3,4,96,256]{3,2,1,0:T(8,128)(2,1)} %fusion), channel_id=1, source_target_pairs={{0,2},{1,3},{2,0},{3,1},{4,6},{5,7},{6,4},{7,5},{8,10},{9,11},{10,... | collective-permute-start | bytes 1769480 | tf_op jit(solution)/shard_map/ppermute | solution.py:24
  74.5 20.9 %collective-permute-start.8 = (bf16[2,4,2,96,256]{4,3,2,1,0:T(8,128)(2,1)S(1)}, bf16[2,4,2,96,256]{4,3,2,1,0:T(8,128)(2,1)}, u32[]{:S(2)}, u32[]{:S(2)}) collective-permute-start(bf16[2,4,2,96,256]{4,3,2,1,0:T(8,128)(2,1)S(1)} %dynamic-slice_bitcast_fusion.1), channel_id=1, source_target_pairs={{0,1},{1,0},{2,3},{3,2},{4,5},{5,4},{6,7},{7,6},{8,9},{9,8},{10,11... | collective-permute-start | bytes 2359304 | tf_op jit(solution)/shard_map/ppermute | solution.py:24
  89.0 15.3 %collective-permute-start.4 = (bf16[3,96,256]{2,1,0:T(8,128)(2,1)}, bf16[3,96,256]{2,1,0:T(8,128)(2,1)S(1)}, u32[]{:S(2)}, u32[]{:S(2)}) collective-permute-start(bf16[3,96,256]{2,1,0:T(8,128)(2,1)} %get-tuple-element.32), channel_id=1, source_target_pairs={{12,0},{0,4},{4,8},{8,12},{13,1},{1,5},{5,9},{9,13},{14,2},{2,6},{... | collective-permute-start | bytes 442376 | tf_op jit(solution)/shard_map/ppermute | solution.py:20
  89.2 16.3 %collective-permute-start.5 = (bf16[3,96,256]{2,1,0:T(8,128)(2,1)S(1)}, bf16[3,96,256]{2,1,0:T(8,128)(2,1)S(1)}, u32[]{:S(2)}, u32[]{:S(2)}) collective-permute-start(bf16[3,96,256]{2,1,0:T(8,128)(2,1)S(1)} %get-tuple-element.34), channel_id=1, source_target_pairs={{8,0},{12,4},{0,8},{4,12},{9,1},{13,5},{1,9},{5,13},{10,2},{14,6},... | collective-permute-start | bytes 442376 | tf_op jit(solution)/shard_map/ppermute | solution.py:20
  95.4 10.1 %collective-permute-start.6 = (bf16[3,96,256]{2,1,0:T(8,128)(2,1)S(1)}, bf16[3,96,256]{2,1,0:T(8,128)(2,1)S(1)}, u32[]{:S(2)}, u32[]{:S(2)}) collective-permute-start(bf16[3,96,256]{2,1,0:T(8,128)(2,1)S(1)} %get-tuple-element.33), channel_id=1, source_target_pairs={{4,0},{8,4},{12,8},{0,12},{5,1},{9,5},{13,9},{1,13},{6,2},{10,6},{... | collective-permute-start | bytes 442376 | tf_op jit(solution)/shard_map/ppermute | solution.py:20
  101.7 12.5 %collective-permute-start.9 = (bf16[2,4,96,256]{3,2,1,0:T(8,128)(2,1)S(1)}, bf16[2,4,96,256]{3,2,1,0:T(8,128)(2,1)S(1)}, u32[]{:S(2)}, u32[]{:S(2)}) collective-permute-start(bf16[2,4,96,256]{3,2,1,0:T(8,128)(2,1)S(1)} %fusion.1), channel_id=1, source_target_pairs={{0,2},{1,3},{2,0},{3,1},{4,6},{5,7},{6,4},{7,5},{8,10},{9,11},{10,... | collective-permute-start | bytes 1179656 | tf_op jit(solution)/shard_map/ppermute | solution.py:24
  105.7 13.1 %collective-permute-start.15 = (bf16[1,4,96,256]{3,2,1,0:T(8,128)(2,1)S(1)}, bf16[1,4,96,256]{3,2,1,0:T(8,128)(2,1)S(1)}, u32[]{:S(2)}, u32[]{:S(2)}) collective-permute-start(bf16[1,4,96,256]{3,2,1,0:T(8,128)(2,1)S(1)} %fusion.5), channel_id=1, source_target_pairs={{0,2},{1,3},{2,0},{3,1},{4,6},{5,7},{6,4},{7,5},{8,10},{9,11},{10,... | collective-permute-start | bytes 589832 | tf_op jit(solution)/shard_map/ppermute | solution.py:24
  114.4 7.6 %collective-permute-start.10 = (bf16[2,96,256]{2,1,0:T(8,128)(2,1)S(1)}, bf16[2,96,256]{2,1,0:T(8,128)(2,1)S(1)}, u32[]{:S(2)}, u32[]{:S(2)}) collective-permute-start(bf16[2,96,256]{2,1,0:T(8,128)(2,1)S(1)} %get-tuple-element.39), channel_id=1, source_target_pairs={{12,0},{0,4},{4,8},{8,12},{13,1},{1,5},{5,9},{9,13},{14,2},{2,6},{... | collective-permute-start | bytes 294920 | tf_op jit(solution)/shard_map/ppermute | solution.py:20
  116.3 9.7 %collective-permute-start.11 = (bf16[2,96,256]{2,1,0:T(8,128)(2,1)S(1)}, bf16[2,96,256]{2,1,0:T(8,128)(2,1)S(1)}, u32[]{:S(2)}, u32[]{:S(2)}) collective-permute-start(bf16[2,96,256]{2,1,0:T(8,128)(2,1)S(1)} %get-tuple-element.41), channel_id=1, source_target_pairs={{8,0},{12,4},{0,8},{4,12},{9,1},{13,5},{1,9},{5,13},{10,2},{14,6},... | collective-permute-start | bytes 294920 | tf_op jit(solution)/shard_map/ppermute | solution.py:20
  116.3 9.7 %collective-permute-start.12 = (bf16[2,96,256]{2,1,0:T(8,128)(2,1)S(1)}, bf16[2,96,256]{2,1,0:T(8,128)(2,1)S(1)}, u32[]{:S(2)}, u32[]{:S(2)}) collective-permute-start(bf16[2,96,256]{2,1,0:T(8,128)(2,1)S(1)} %get-tuple-element.40), channel_id=1, source_target_pairs={{4,0},{8,4},{12,8},{0,12},{5,1},{9,5},{13,9},{1,13},{6,2},{10,6},{... | collective-permute-start | bytes 294920 | tf_op jit(solution)/shard_map/ppermute | solution.py:20
  118.9 8.3 %collective-permute-start.16 = (bf16[1,96,256]{2,1,0:T(8,128)(2,1)S(1)}, bf16[1,96,256]{2,1,0:T(8,128)(2,1)S(1)}, u32[]{:S(2)}, u32[]{:S(2)}) collective-permute-start(bf16[1,96,256]{2,1,0:T(8,128)(2,1)S(1)} %get-tuple-element.42), channel_id=1, source_target_pairs={{12,0},{0,4},{4,8},{8,12},{13,1},{1,5},{5,9},{9,13},{14,2},{2,6},{... | collective-permute-start | bytes 147464 | tf_op jit(solution)/shard_map/ppermute | solution.py:20
  120.3 10.0 %collective-permute-start.17 = (bf16[1,96,256]{2,1,0:T(8,128)(2,1)S(1)}, bf16[1,96,256]{2,1,0:T(8,128)(2,1)S(1)}, u32[]{:S(2)}, u32[]{:S(2)}) collective-permute-start(bf16[1,96,256]{2,1,0:T(8,128)(2,1)S(1)} %get-tuple-element.44), channel_id=1, source_target_pairs={{8,0},{12,4},{0,8},{4,12},{9,1},{13,5},{1,9},{5,13},{10,2},{14,6},... | collective-permute-start | bytes 147464 | tf_op jit(solution)/shard_map/ppermute | solution.py:20
  122.0 8.2 %collective-permute-start.18 = (bf16[1,96,256]{2,1,0:T(8,128)(2,1)S(1)}, bf16[1,96,256]{2,1,0:T(8,128)(2,1)S(1)}, u32[]{:S(2)}, u32[]{:S(2)}) collective-permute-start(bf16[1,96,256]{2,1,0:T(8,128)(2,1)S(1)} %get-tuple-element.43), channel_id=1, source_target_pairs={{4,0},{8,4},{12,8},{0,12},{5,1},{9,5},{13,9},{1,13},{6,2},{10,6},{... | collective-permute-start | bytes 147464 | tf_op jit(solution)/shard_map/ppermute | solution.py:20
  131.1 7.6 %collective-permute-start.19 = (bf16[2,96,256]{2,1,0:T(8,128)(2,1)S(1)}, bf16[2,96,256]{2,1,0:T(8,128)(2,1)S(1)}, u32[]{:S(2)}, u32[]{:S(2)}) collective-permute-start(bf16[2,96,256]{2,1,0:T(8,128)(2,1)S(1)} %get-tuple-element.38), channel_id=1, source_target_pairs={{12,0},{0,4},{4,8},{8,12},{13,1},{1,5},{5,9},{9,13},{14,2},{2,6},{... | collective-permute-start | bytes 294920 | tf_op jit(solution)/shard_map/ppermute | solution.py:20
  132.6 9.2 %collective-permute-start.20 = (bf16[2,96,256]{2,1,0:T(8,128)(2,1)S(1)}, bf16[2,96,256]{2,1,0:T(8,128)(2,1)S(1)}, u32[]{:S(2)}, u32[]{:S(2)}) collective-permute-start(bf16[2,96,256]{2,1,0:T(8,128)(2,1)S(1)} %get-tuple-element.37), channel_id=1, source_target_pairs={{8,0},{12,4},{0,8},{4,12},{9,1},{13,5},{1,9},{5,13},{10,2},{14,6},... | collective-permute-start | bytes 294920 | tf_op jit(solution)/shard_map/ppermute | solution.py:20
  133.4 8.5 %collective-permute-start.21 = (bf16[2,96,256]{2,1,0:T(8,128)(2,1)S(1)}, bf16[2,96,256]{2,1,0:T(8,128)(2,1)S(1)}, u32[]{:S(2)}, u32[]{:S(2)}) collective-permute-start(bf16[2,96,256]{2,1,0:T(8,128)(2,1)S(1)} %get-tuple-element.36), channel_id=1, source_target_pairs={{4,0},{8,4},{12,8},{0,12},{5,1},{9,5},{13,9},{1,13},{6,2},{10,6},{... | collective-permute-start | bytes 294920 | tf_op jit(solution)/shard_map/ppermute | solution.py:20
  142.6 10.9 %collective-permute-start.22 = (bf16[4,2,96,256]{3,2,1,0:T(8,128)(2,1)S(1)}, bf16[4,2,96,256]{3,2,1,0:T(8,128)(2,1)S(1)}, u32[]{:S(2)}, u32[]{:S(2)}) collective-permute-start(bf16[4,2,96,256]{3,2,1,0:T(8,128)(2,1)S(1)} %broadcast_select_fusion), channel_id=1, source_target_pairs={{3,0},{0,1},{1,2},{2,3},{7,4},{4,5},{5,6},{6,7},{11,8},{8,9},{9,10... | collective-permute-start | bytes 1179656 | tf_op jit(solution)/shard_map/ppermute | solution.py:20
  142.7 12.0 %collective-permute-start.23 = (bf16[4,2,96,256]{3,2,1,0:T(8,128)(2,1)S(1)}, bf16[4,2,96,256]{3,2,1,0:T(8,128)(2,1)S(1)}, u32[]{:S(2)}, u32[]{:S(2)}) collective-permute-start(bf16[4,2,96,256]{3,2,1,0:T(8,128)(2,1)S(1)} %broadcast_select_fusion), channel_id=1, source_target_pairs={{2,0},{3,1},{0,2},{1,3},{6,4},{7,5},{4,6},{5,7},{10,8},{11,9},{8,1... | collective-permute-start | bytes 1179656 | tf_op jit(solution)/shard_map/ppermute | solution.py:20
  144.3 17.3 %collective-permute-start.24 = (bf16[4,2,96,256]{3,2,1,0:T(8,128)(2,1)S(1)}, bf16[4,2,96,256]{3,2,1,0:T(8,128)(2,1)S(1)}, u32[]{:S(2)}, u32[]{:S(2)}) collective-permute-start(bf16[4,2,96,256]{3,2,1,0:T(8,128)(2,1)S(1)} %broadcast_select_fusion), channel_id=1, source_target_pairs={{1,0},{2,1},{3,2},{0,3},{5,4},{6,5},{7,6},{4,7},{9,8},{10,9},{11,1... | collective-permute-start | bytes 1179656 | tf_op jit(solution)/shard_map/ppermute | solution.py:20
  (14 other events, 127.8 us)

commit v23 on v18

--- a/solution.py
+++ b/solution.py
@@ -271,9 +271,11 @@
         across = jnp.take(arrived, (slab - jnp.arange(count_slabs, dtype=jnp.int32)) % count_slabs, axis=0)
     else:
         across = lax.all_to_all(outgoing, "slab", 0, 0, tiled=True)
-    shared = [across] + [shifted(across, "member", shift) for shift in range(1, NSPIN)]
-    shared = jnp.stack(shared, 0)
-    within = jnp.take(shared, (member - jnp.arange(NSPIN, dtype=jnp.int32)) % NSPIN, axis=0)
+    pair = jnp.stack([across, swapped(across, "member", 0)], 0)
+    by_core = jnp.take(pair, (jnp.arange(2, dtype=jnp.int32) + member % 2) % 2, axis=0)
+    both = jnp.stack([by_core, swapped(by_core, "member", 1)], 0)
+    within = jnp.take(both, (jnp.arange(2, dtype=jnp.int32) + member // 2) % 2, axis=0)
+    within = within.reshape((NSPIN,) + across.shape)
     incoming = within.transpose(1, 0, 2, 3, 4).reshape(nspace, 2, rows, count_ev)
     count_ops = partial.shape[1] // (2 * count_ev)
     gathered = incoming.transpose(1, 0, 2, 3).reshape(2, count_ops, 2, count_ev, count_ev)

time: 148 us -> 150 us (1.014)
  other arithmetic: 9.33 us -> 11.8 us
  starting transfers between devices: 33.6 us -> 31.4 us
  local copies, waits for them, and re-layouts: 21.2 us -> 23.3 us
    ppermute x18 -> x15, waiting for transfers between devices: 40.3 us -> 21.1 us  [shifted(): return lax.ppermute(block, axis, route)]
    ppermute x7 -> x9, waiting for transfers between devices: 10.4 us -> 29.3 us  [swapped(): lax.ppermute(value, axis, [(i, i ^ 1 << bit) for i in range(lax.axis_size...]
    ppermute x18 -> x15, starting transfers between devices: 30.1 us -> 26.6 us  [shifted(): return lax.ppermute(block, axis, route)]
    slice x1, local copies, waits for them, and re-layouts: 1.37 us -> 3.18 us  [body(): eigenvectors[h * span:(h + 1) * span]]
    select_n x2 -> x5, other arithmetic: 0.23 us -> 1.91 us  [the longest x2 1.62 us: body(): jnp.take(both, (jnp.arange(2, dtype=jnp.int32) + member // 2) % 2, axis=0)]
    ppermute x7 -> x9, starting transfers between devices: 3.56 us -> 4.74 us  [swapped(): lax.ppermute(value, axis, [(i, i ^ 1 << bit) for i in range(lax.axis_size...]
    unnamed x24 -> x34, local copies, waits for them, and re-layouts: 3.79 us -> 2.97 us
  transfers between devices with their start and end apart: 25 -> 24, of which waited for: 13 -> 12; matrix products, arithmetic and copies ran while one was open for 15% -> 17% of each run, Pallas kernels for 16% -> 16%
where the time goes in v23:
time: 150 us; the launch traced here: 149 us
  waiting for transfers between devices  50.4 us (34%)
  starting transfers between devices  31.4 us (21%)
  Pallas kernels  30.7 us (20%)
  local copies, waits for them, and re-layouts  23.3 us (16%)
  other arithmetic  11.8 us (8%)
  between operations  1.84 us (1%)
    ppermute x9, waiting for transfers between devices, swapped(): lax.ppermute(value, axis, [(i, i ^ 1 << bit) for i in range(lax.axis_size...  29.3 us
    ppermute x15, starting transfers between devices, shifted(): return lax.ppermute(block, axis, route)  26.6 us
    ppermute x15, waiting for transfers between devices, shifted(): return lax.ppermute(block, axis, route)  21.1 us
    pallas_call x3, Pallas kernels, second_pass(): pl.pallas_call(functools.partial(sums_kernel, scale=scale, course_list=(0...  13.1 us
    pallas_call x1, Pallas kernels, local_sums(): pl.pallas_call(functools.partial(sums_kernel, scale=scale, course_list=ne...  11 us
    pallas_call x1, Pallas kernels, contract_panel(): pl.pallas_call(panel_kernel, grid=(count_ops,), in_specs=[pl.BlockSpec((1...  6.63 us
    ppermute x9, starting transfers between devices, swapped(): lax.ppermute(value, axis, [(i, i ^ 1 << bit) for i in range(lax.axis_size...  4.74 us
    squeeze x3, local copies, waits for them, and re-layouts, body(): send = lax.dynamic_index_in_dim(part_blocks, 1 - core, 3, keepdims=False)  4.55 us
  transfers between devices with their start and end apart: 24, of which 12 were waited for; matrix products, arithmetic and copies ran while one was open for 17% of the time, Pallas kernels for 16%

profile of v23, /device:TPU:0, one launch (start us, length us, event | category | flops | bytes accessed | tf_op | source)
XLA Modules:
  0.0 149.4 jit_solution(3040177685111665129)
XLA Ops:
  0.7 3.2 %fusion.39 = (bf16[2,2,3,256,128]{4,3,2,1,0:T(8,128)(2,1)}, bf16[2,2,3,256,128]{4,3,2,1,0:T(8,128)(2,1)S(1)}, bf16[2,2,3,256,128]{4,3,2,1,0:T(8,128)(2,1)}) fusion(bf16[6,2,3,256,128]{4,3,2,1,0:T(8,128)(2,1)} %field_ref.7), kind=kLoop, calls=%fused_computation.135 | loop fusion | bytes 4718592 | tf_op jit(solution)/shard_map/slice | solution.py:225
  3.8 6.0 %collective-permute-start = (bf16[2,2,3,256,128]{4,3,2,1,0:T(8,128)(2,1)}, bf16[2,2,3,256,128]{4,3,2,1,0:T(8,128)(2,1)}, u32[]{:S(2)}, u32[]{:S(2)}) collective-permute-start(bf16[2,2,3,256,128]{4,3,2,1,0:T(8,128)(2,1)} %get-tuple-element.30), channel_id=1, source_target_pairs={{2,0},{3,1},{4,2},{5,3},{6,4},{7,5},{8,6},{9,7},{10,8},{11,9},{12,... | collective-permute-start | bytes 2359304 | tf_op jit(solution)/shard_map/ppermute | solution.py:20
  20.6 2.2 %pad.6.near_ref = bf16[6,2,3,256,128]{4,3,2,1,0:T(8,128)(2,1)} pad(bf16[6,2,3,256,8]{4,3,2,1,0:T(8,128)(2,1)S(1)} %copy.36, bf16[]{:T(256)} %constant.293.clone.1), padding=0_0x0_0x0_0x0_0x120_0 | pad | bytes 2506754 | tf_op jit(solution)/shard_map/jit(_pad)/pad | solution.py:103
  22.9 11.0 %shard_map.77 = (bf16[6,1536,256]{2,1,0:T(8,128)(2,1)}, bf16[6,512,768]{2,1,0:T(8,128)(2,1)}) custom-call(s32[3]{0:T(128)} %select_reduce_fusion.slot_ref, bf16[6,2,3,256,128]{4,3,2,1,0:T(8,128)(2,1)} %field_ref.7, bf16[6,2,3,256,128]{4,3,2,1,0:T(8,128)(2,1)} %pad.6.near_ref, f32[6,3,2,3,3,128]{5,4,3,2,1,0:T(4,128)} %copy.38.link_ref, ...), custom_call_target="tpu_custom_call" | custom-call | tf_op jit(solution)/shard_map/pallas_call | solution.py:118
  33.8 4.4 %shard_map.78 = bf16[2,1536,256]{2,1,0:T(8,128)(2,1)} custom-call(s32[3]{0:T(128)} %select_reduce_fusion.slot_ref, bf16[6,2,3,256,128]{4,3,2,1,0:T(8,128)(2,1)} %field_ref.7, bf16[2,2,3,256,128]{4,3,2,1,0:T(8,128)(2,1)} %collective-permute-done.near_ref, f32[6,3,2,3,3,128]{5,4,3,2,1,0:T(4,128)} %copy.38.link_ref, ...), custom_call_target="tpu_custom_call" | custom-call | tf_op jit(solution)/shard_map/pallas_call | solution.py:147
  40.3 4.5 %collective-permute-done.7.near_ref = bf16[2,2,3,256,128]{4,3,2,1,0:T(8,128)(2,1)} collective-permute-done((bf16[2,2,3,256,128]{4,3,2,1,0:T(8,128)(2,1)S(1)}, bf16[2,2,3,256,128]{4,3,2,1,0:T(8,128)(2,1)}, u32[]{:S(2)}, u32[]{:S(2)}) %collective-permute-start.7) | collective-permute-done | bytes 786464 | tf_op jit(solution)/shard_map/ppermute | solution.py:20
  44.9 4.4 %shard_map.79 = bf16[2,1536,256]{2,1,0:T(8,128)(2,1)} custom-call(s32[3]{0:T(128)} %select_reduce_fusion.slot_ref, bf16[6,2,3,256,128]{4,3,2,1,0:T(8,128)(2,1)} %field_ref.7, bf16[2,2,3,256,128]{4,3,2,1,0:T(8,128)(2,1)} %collective-permute-done.7.near_ref, f32[6,3,2,3,3,128]{5,4,3,2,1,0:T(4,128)} %copy.38.link_ref, ...), custom_call_target="tpu_custom_call" | custom-call | tf_op jit(solution)/shard_map/pallas_call | solution.py:147
  49.2 2.2 %dynamic-slice_bitcast_fusion.1 = bf16[2,4,2,96,256]{4,3,2,1,0:T(8,128)(2,1)} fusion(bf16[2,4,2,2,96,256]{5,4,3,2,1,0:T(8,128)(2,1)} %bitcast.129, s32[]{:T(128)S(6)} %select_n.351), kind=kLoop, calls=%fused_computation.21 | loop fusion | bytes 1572868 | tf_op jit(solution)/shard_map/jit(dynamic_index_in_dim)/squeeze | solution.py:240
  57.6 3.0 %collective-permute-done.13.near_ref = bf16[2,2,3,256,128]{4,3,2,1,0:T(8,128)(2,1)} collective-permute-done((bf16[2,2,3,256,128]{4,3,2,1,0:T(8,128)(2,1)}, bf16[2,2,3,256,128]{4,3,2,1,0:T(8,128)(2,1)}, u32[]{:S(2)}, u32[]{:S(2)}) %collective-permute-start.13) | collective-permute-done | bytes 786464 | tf_op jit(solution)/shard_map/ppermute | solution.py:20
  60.7 4.4 %shard_map.80 = bf16[2,1536,256]{2,1,0:T(8,128)(2,1)} custom-call(s32[3]{0:T(128)} %select_reduce_fusion.slot_ref, bf16[6,2,3,256,128]{4,3,2,1,0:T(8,128)(2,1)} %field_ref.7, bf16[2,2,3,256,128]{4,3,2,1,0:T(8,128)(2,1)} %collective-permute-done.13.near_ref, f32[6,3,2,3,3,128]{5,4,3,2,1,0:T(4,128)} %copy.38.link_ref, ...), custom_call_target="tpu_custom_call" | custom-call | tf_op jit(solution)/shard_map/pallas_call | solution.py:147
  68.7 4.3 %collective-permute-start.5 = (bf16[2,96,256]{2,1,0:T(8,128)(2,1)S(1)}, bf16[2,96,256]{2,1,0:T(8,128)(2,1)S(1)}, u32[]{:S(2)}, u32[]{:S(2)}) collective-permute-start(bf16[2,96,256]{2,1,0:T(8,128)(2,1)S(1)} %get-tuple-element.41), channel_id=1, source_target_pairs={{8,0},{12,4},{0,8},{4,12},{9,1},{13,5},{1,9},{5,13},{10,2},{14,6},... | collective-permute-start | bytes 294920 | tf_op jit(solution)/shard_map/ppermute | solution.py:20
  74.6 2.5 %collective-permute-start.9 = (bf16[2,4,96,256]{3,2,1,0:T(8,128)(2,1)S(1)}, bf16[2,4,96,256]{3,2,1,0:T(8,128)(2,1)S(1)}, u32[]{:S(2)}, u32[]{:S(2)}) collective-permute-start(bf16[2,4,96,256]{3,2,1,0:T(8,128)(2,1)S(1)} %fusion.1), channel_id=1, source_target_pairs={{0,2},{1,3},{2,0},{3,1},{4,6},{5,7},{6,4},{7,5},{8,10},{9,11},{10,... | collective-permute-start | bytes 1179656 | tf_op jit(solution)/shard_map/ppermute | solution.py:24
  77.5 2.3 %collective-permute-done.5 = bf16[2,96,256]{2,1,0:T(8,128)(2,1)S(1)} collective-permute-done((bf16[2,96,256]{2,1,0:T(8,128)(2,1)S(1)}, bf16[2,96,256]{2,1,0:T(8,128)(2,1)S(1)}, u32[]{:S(2)}, u32[]{:S(2)}) %collective-permute-start.5) | collective-permute-done | bytes 98336 | tf_op jit(solution)/shard_map/ppermute | solution.py:20
  79.9 7.2 %collective-permute-done.9 = bf16[2,4,96,256]{3,2,1,0:T(8,128)(2,1)S(1)} collective-permute-done((bf16[2,4,96,256]{3,2,1,0:T(8,128)(2,1)S(1)}, bf16[2,4,96,256]{3,2,1,0:T(8,128)(2,1)S(1)}, u32[]{:S(2)}, u32[]{:S(2)}) %collective-permute-start.9) | collective-permute-done | bytes 393248 | tf_op jit(solution)/shard_map/ppermute | solution.py:24
  89.2 2.4 %collective-permute-start.12 = (bf16[2,96,256]{2,1,0:T(8,128)(2,1)S(1)}, bf16[2,96,256]{2,1,0:T(8,128)(2,1)S(1)}, u32[]{:S(2)}, u32[]{:S(2)}) collective-permute-start(bf16[2,96,256]{2,1,0:T(8,128)(2,1)S(1)} %get-tuple-element.43), channel_id=1, source_target_pairs={{4,0},{8,4},{12,8},{0,12},{5,1},{9,5},{13,9},{1,13},{6,2},{10,6},{... | collective-permute-start | bytes 294920 | tf_op jit(solution)/shard_map/ppermute | solution.py:20
  91.7 2.6 %collective-permute-done.15 = bf16[2,4,96,256]{3,2,1,0:T(8,128)(2,1)S(1)} collective-permute-done((bf16[2,4,96,256]{3,2,1,0:T(8,128)(2,1)S(1)}, bf16[2,4,96,256]{3,2,1,0:T(8,128)(2,1)S(1)}, u32[]{:S(2)}, u32[]{:S(2)}) %collective-permute-start.15) | collective-permute-done | bytes 393248 | tf_op jit(solution)/shard_map/ppermute | solution.py:24
  96.4 2.4 %collective-permute-start.18 = (bf16[2,96,256]{2,1,0:T(8,128)(2,1)S(1)}, bf16[2,96,256]{2,1,0:T(8,128)(2,1)S(1)}, u32[]{:S(2)}, u32[]{:S(2)}) collective-permute-start(bf16[2,96,256]{2,1,0:T(8,128)(2,1)S(1)} %get-tuple-element.46), channel_id=1, source_target_pairs={{4,0},{8,4},{12,8},{0,12},{5,1},{9,5},{13,9},{1,13},{6,2},{10,6},{... | collective-permute-start | bytes 294920 | tf_op jit(solution)/shard_map/ppermute | solution.py:20
  98.9 3.2 %collective-permute-done.16 = bf16[2,96,256]{2,1,0:T(8,128)(2,1)S(1)} collective-permute-done((bf16[2,96,256]{2,1,0:T(8,128)(2,1)S(1)}, bf16[2,96,256]{2,1,0:T(8,128)(2,1)S(1)}, u32[]{:S(2)}, u32[]{:S(2)}) %collective-permute-start.16) | collective-permute-done | bytes 98336 | tf_op jit(solution)/shard_map/ppermute | solution.py:20
  102.2 2.4 %collective-permute-done.17 = bf16[2,96,256]{2,1,0:T(8,128)(2,1)S(1)} collective-permute-done((bf16[2,96,256]{2,1,0:T(8,128)(2,1)S(1)}, bf16[2,96,256]{2,1,0:T(8,128)(2,1)S(1)}, u32[]{:S(2)}, u32[]{:S(2)}) %collective-permute-start.17) | collective-permute-done | bytes 98336 | tf_op jit(solution)/shard_map/ppermute | solution.py:20
  105.4 2.4 %collective-permute-start.19 = (bf16[2,96,256]{2,1,0:T(8,128)(2,1)S(1)}, bf16[2,96,256]{2,1,0:T(8,128)(2,1)S(1)}, u32[]{:S(2)}, u32[]{:S(2)}) collective-permute-start(bf16[2,96,256]{2,1,0:T(8,128)(2,1)S(1)} %get-tuple-element.38), channel_id=1, source_target_pairs={{12,0},{0,4},{4,8},{8,12},{13,1},{1,5},{5,9},{9,13},{14,2},{2,6},{... | collective-permute-start | bytes 294920 | tf_op jit(solution)/shard_map/ppermute | solution.py:20
  110.2 2.7 %collective-permute-done.19 = bf16[2,96,256]{2,1,0:T(8,128)(2,1)S(1)} collective-permute-done((bf16[2,96,256]{2,1,0:T(8,128)(2,1)S(1)}, bf16[2,96,256]{2,1,0:T(8,128)(2,1)S(1)}, u32[]{:S(2)}, u32[]{:S(2)}) %collective-permute-start.19) | collective-permute-done | bytes 98336 | tf_op jit(solution)/shard_map/ppermute | solution.py:20
  113.0 3.0 %collective-permute-done.20 = bf16[2,96,256]{2,1,0:T(8,128)(2,1)S(1)} collective-permute-done((bf16[2,96,256]{2,1,0:T(8,128)(2,1)S(1)}, bf16[2,96,256]{2,1,0:T(8,128)(2,1)S(1)}, u32[]{:S(2)}, u32[]{:S(2)}) %collective-permute-start.20) | collective-permute-done | bytes 98336 | tf_op jit(solution)/shard_map/ppermute | solution.py:20
  122.4 16.5 %collective-permute-done.23 = bf16[2,4,2,96,256]{4,3,2,1,0:T(8,128)(2,1)S(1)} collective-permute-done((bf16[2,4,2,96,256]{4,3,2,1,0:T(8,128)(2,1)S(1)}, bf16[2,4,2,96,256]{4,3,2,1,0:T(8,128)(2,1)S(1)}, u32[]{:S(2)}, u32[]{:S(2)}) %collective-permute-start.23) | collective-permute-done | bytes 786464 | tf_op jit(solution)/shard_map/ppermute | solution.py:24
  141.4 6.6 %shard_map.81 = f32[3,2,256]{2,1,0:T(2,128)} custom-call(bf16[2,3,2,256,256]{4,3,2,1,0:T(8,128)(2,1)} %bitcast.127, bf16[2,3,2,256,256]{4,3,2,1,0:T(8,128)(2,1)} %bitcast.128, bf16[512,1024]{1,0:T(8,128)(2,1)} %bitcast.136, bf16[2048,512]{1,0:T(8,128)(2,1)} %maximum_maximum_fusion.wide_ref), custom_call_target="tpu_custom_call" | custom-call | tf_op jit(solution)/shard_map/pallas_call | solution.py:193
  (132 shorter events, 41.7 us)
Async XLA Ops:
  3.8 30.0 %collective-permute-start = (bf16[2,2,3,256,128]{4,3,2,1,0:T(8,128)(2,1)}, bf16[2,2,3,256,128]{4,3,2,1,0:T(8,128)(2,1)}, u32[]{:S(2)}, u32[]{:S(2)}) collective-permute-start(bf16[2,2,3,256,128]{4,3,2,1,0:T(8,128)(2,1)} %get-tuple-element.30), channel_id=1, source_target_pairs={{2,0},{3,1},{4,2},{5,3},{6,4},{7,5},{8,6},{9,7},{10,8},{11,9},{12,... | collective-permute-start | bytes 2359304 | tf_op jit(solution)/shard_map/ppermute | solution.py:20
  11.3 7.9 %collective-permute-start.1 = (bf16[6,2,3,256,8]{3,4,2,1,0:T(8,128)(2,1)}, bf16[6,2,3,256,8]{3,4,2,1,0:T(8,128)(2,1)S(1)}, u32[]{:S(2)}, u32[]{:S(2)}) collective-permute-start(bf16[6,2,3,256,8]{3,4,2,1,0:T(8,128)(2,1)} %copy.46), channel_id=1, source_target_pairs={{0,1},{1,0},{2,3},{3,2},{4,5},{5,4},{6,7},{7,6},{8,9},{9,8},{10,11... | collective-permute-start | bytes 442376 | tf_op jit(solution)/shard_map/ppermute | solution.py:24
  11.3 33.5 %collective-permute-start.7 = (bf16[2,2,3,256,128]{4,3,2,1,0:T(8,128)(2,1)S(1)}, bf16[2,2,3,256,128]{4,3,2,1,0:T(8,128)(2,1)}, u32[]{:S(2)}, u32[]{:S(2)}) collective-permute-start(bf16[2,2,3,256,128]{4,3,2,1,0:T(8,128)(2,1)S(1)} %get-tuple-element.31), channel_id=1, source_target_pairs={{2,0},{3,1},{4,2},{5,3},{6,4},{7,5},{8,6},{9,7},{10,8},{11,9},{12,... | collective-permute-start | bytes 2359304 | tf_op jit(solution)/shard_map/ppermute | solution.py:20
  11.9 48.8 %collective-permute-start.13 = (bf16[2,2,3,256,128]{4,3,2,1,0:T(8,128)(2,1)}, bf16[2,2,3,256,128]{4,3,2,1,0:T(8,128)(2,1)}, u32[]{:S(2)}, u32[]{:S(2)}) collective-permute-start(bf16[2,2,3,256,128]{4,3,2,1,0:T(8,128)(2,1)} %get-tuple-element.32), channel_id=1, source_target_pairs={{2,0},{3,1},{4,2},{5,3},{6,4},{7,5},{8,6},{9,7},{10,8},{11,9},{12,... | collective-permute-start | bytes 2359304 | tf_op jit(solution)/shard_map/ppermute | solution.py:20
  39.4 5.4 %collective-permute-start.2 = (bf16[2,4,2,96,256]{4,3,2,1,0:T(8,128)(2,1)S(1)}, bf16[2,4,2,96,256]{4,3,2,1,0:T(8,128)(2,1)}, u32[]{:S(2)}, u32[]{:S(2)}) collective-permute-start(bf16[2,4,2,96,256]{4,3,2,1,0:T(8,128)(2,1)S(1)} %dynamic-slice_bitcast_fusion.2), channel_id=1, source_target_pairs={{0,1},{1,0},{2,3},{3,2},{4,5},{5,4},{6,7},{7,6},{8,9},{9,8},{10,11... | collective-permute-start | bytes 2359304 | tf_op jit(solution)/shard_map/ppermute | solution.py:24
  51.4 9.3 %collective-permute-start.8 = (bf16[2,4,2,96,256]{4,3,2,1,0:T(8,128)(2,1)}, bf16[2,4,2,96,256]{4,3,2,1,0:T(8,128)(2,1)}, u32[]{:S(2)}, u32[]{:S(2)}) collective-permute-start(bf16[2,4,2,96,256]{4,3,2,1,0:T(8,128)(2,1)} %dynamic-slice_bitcast_fusion.1), channel_id=1, source_target_pairs={{0,1},{1,0},{2,3},{3,2},{4,5},{5,4},{6,7},{7,6},{8,9},{9,8},{10,11... | collective-permute-start | bytes 2359304 | tf_op jit(solution)/shard_map/ppermute | solution.py:24
  56.2 11.6 %collective-permute-start.3 = (bf16[2,4,96,256]{3,2,1,0:T(8,128)(2,1)S(1)}, bf16[2,4,96,256]{3,2,1,0:T(8,128)(2,1)S(1)}, u32[]{:S(2)}, u32[]{:S(2)}) collective-permute-start(bf16[2,4,96,256]{3,2,1,0:T(8,128)(2,1)S(1)} %fusion), channel_id=1, source_target_pairs={{0,2},{1,3},{2,0},{3,1},{4,6},{5,7},{6,4},{7,5},{8,10},{9,11},{10,... | collective-permute-start | bytes 1179656 | tf_op jit(solution)/shard_map/ppermute | solution.py:24
  66.3 10.8 %collective-permute-start.14 = (bf16[2,4,2,96,256]{4,3,2,1,0:T(8,128)(2,1)S(1)}, bf16[2,4,2,96,256]{4,3,2,1,0:T(8,128)(2,1)S(1)}, u32[]{:S(2)}, u32[]{:S(2)}) collective-permute-start(bf16[2,4,2,96,256]{4,3,2,1,0:T(8,128)(2,1)S(1)} %dynamic-slice_bitcast_fusion), channel_id=1, source_target_pairs={{0,1},{1,0},{2,3},{3,2},{4,5},{5,4},{6,7},{7,6},{8,9},{9,8},{10,11... | collective-permute-start | bytes 2359304 | tf_op jit(solution)/shard_map/ppermute | solution.py:24
  68.0 9.5 %collective-permute-start.4 = (bf16[2,96,256]{2,1,0:T(8,128)(2,1)S(1)}, bf16[2,96,256]{2,1,0:T(8,128)(2,1)S(1)}, u32[]{:S(2)}, u32[]{:S(2)}) collective-permute-start(bf16[2,96,256]{2,1,0:T(8,128)(2,1)S(1)} %get-tuple-element.39), channel_id=1, source_target_pairs={{12,0},{0,4},{4,8},{8,12},{13,1},{1,5},{5,9},{9,13},{14,2},{2,6},{... | collective-permute-start | bytes 294920 | tf_op jit(solution)/shard_map/ppermute | solution.py:20
  68.7 11.1 %collective-permute-start.5 = (bf16[2,96,256]{2,1,0:T(8,128)(2,1)S(1)}, bf16[2,96,256]{2,1,0:T(8,128)(2,1)S(1)}, u32[]{:S(2)}, u32[]{:S(2)}) collective-permute-start(bf16[2,96,256]{2,1,0:T(8,128)(2,1)S(1)} %get-tuple-element.41), channel_id=1, source_target_pairs={{8,0},{12,4},{0,8},{4,12},{9,1},{13,5},{1,9},{5,13},{10,2},{14,6},... | collective-permute-start | bytes 294920 | tf_op jit(solution)/shard_map/ppermute | solution.py:20
  73.0 6.8 %collective-permute-start.6 = (bf16[2,96,256]{2,1,0:T(8,128)(2,1)S(1)}, bf16[2,96,256]{2,1,0:T(8,128)(2,1)S(1)}, u32[]{:S(2)}, u32[]{:S(2)}) collective-permute-start(bf16[2,96,256]{2,1,0:T(8,128)(2,1)S(1)} %get-tuple-element.40), channel_id=1, source_target_pairs={{4,0},{8,4},{12,8},{0,12},{5,1},{9,5},{13,9},{1,13},{6,2},{10,6},{... | collective-permute-start | bytes 294920 | tf_op jit(solution)/shard_map/ppermute | solution.py:20
  74.6 12.5 %collective-permute-start.9 = (bf16[2,4,96,256]{3,2,1,0:T(8,128)(2,1)S(1)}, bf16[2,4,96,256]{3,2,1,0:T(8,128)(2,1)S(1)}, u32[]{:S(2)}, u32[]{:S(2)}) collective-permute-start(bf16[2,4,96,256]{3,2,1,0:T(8,128)(2,1)S(1)} %fusion.1), channel_id=1, source_target_pairs={{0,2},{1,3},{2,0},{3,1},{4,6},{5,7},{6,4},{7,5},{8,10},{9,11},{10,... | collective-permute-start | bytes 1179656 | tf_op jit(solution)/shard_map/ppermute | solution.py:24
  77.4 16.9 %collective-permute-start.15 = (bf16[2,4,96,256]{3,2,1,0:T(8,128)(2,1)S(1)}, bf16[2,4,96,256]{3,2,1,0:T(8,128)(2,1)S(1)}, u32[]{:S(2)}, u32[]{:S(2)}) collective-permute-start(bf16[2,4,96,256]{3,2,1,0:T(8,128)(2,1)S(1)} %fusion.2), channel_id=1, source_target_pairs={{0,2},{1,3},{2,0},{3,1},{4,6},{5,7},{6,4},{7,5},{8,10},{9,11},{10,... | collective-permute-start | bytes 1179656 | tf_op jit(solution)/shard_map/ppermute | solution.py:24
  87.2 9.2 %collective-permute-start.10 = (bf16[2,96,256]{2,1,0:T(8,128)(2,1)S(1)}, bf16[2,96,256]{2,1,0:T(8,128)(2,1)S(1)}, u32[]{:S(2)}, u32[]{:S(2)}) collective-permute-start(bf16[2,96,256]{2,1,0:T(8,128)(2,1)S(1)} %get-tuple-element.42), channel_id=1, source_target_pairs={{12,0},{0,4},{4,8},{8,12},{13,1},{1,5},{5,9},{9,13},{14,2},{2,6},{... | collective-permute-start | bytes 294920 | tf_op jit(solution)/shard_map/ppermute | solution.py:20
  89.2 9.6 %collective-permute-start.11 = (bf16[2,96,256]{2,1,0:T(8,128)(2,1)S(1)}, bf16[2,96,256]{2,1,0:T(8,128)(2,1)S(1)}, u32[]{:S(2)}, u32[]{:S(2)}) collective-permute-start(bf16[2,96,256]{2,1,0:T(8,128)(2,1)S(1)} %get-tuple-element.44), channel_id=1, source_target_pairs={{8,0},{12,4},{0,8},{4,12},{9,1},{13,5},{1,9},{5,13},{10,2},{14,6},... | collective-permute-start | bytes 294920 | tf_op jit(solution)/shard_map/ppermute | solution.py:20
  89.2 9.6 %collective-permute-start.12 = (bf16[2,96,256]{2,1,0:T(8,128)(2,1)S(1)}, bf16[2,96,256]{2,1,0:T(8,128)(2,1)S(1)}, u32[]{:S(2)}, u32[]{:S(2)}) collective-permute-start(bf16[2,96,256]{2,1,0:T(8,128)(2,1)S(1)} %get-tuple-element.43), channel_id=1, source_target_pairs={{4,0},{8,4},{12,8},{0,12},{5,1},{9,5},{13,9},{1,13},{6,2},{10,6},{... | collective-permute-start | bytes 294920 | tf_op jit(solution)/shard_map/ppermute | solution.py:20
  94.5 7.7 %collective-permute-start.16 = (bf16[2,96,256]{2,1,0:T(8,128)(2,1)S(1)}, bf16[2,96,256]{2,1,0:T(8,128)(2,1)S(1)}, u32[]{:S(2)}, u32[]{:S(2)}) collective-permute-start(bf16[2,96,256]{2,1,0:T(8,128)(2,1)S(1)} %get-tuple-element.45), channel_id=1, source_target_pairs={{12,0},{0,4},{4,8},{8,12},{13,1},{1,5},{5,9},{9,13},{14,2},{2,6},{... | collective-permute-start | bytes 294920 | tf_op jit(solution)/shard_map/ppermute | solution.py:20
  96.2 8.4 %collective-permute-start.17 = (bf16[2,96,256]{2,1,0:T(8,128)(2,1)S(1)}, bf16[2,96,256]{2,1,0:T(8,128)(2,1)S(1)}, u32[]{:S(2)}, u32[]{:S(2)}) collective-permute-start(bf16[2,96,256]{2,1,0:T(8,128)(2,1)S(1)} %get-tuple-element.47), channel_id=1, source_target_pairs={{8,0},{12,4},{0,8},{4,12},{9,1},{13,5},{1,9},{5,13},{10,2},{14,6},... | collective-permute-start | bytes 294920 | tf_op jit(solution)/shard_map/ppermute | solution.py:20
  96.4 8.1 %collective-permute-start.18 = (bf16[2,96,256]{2,1,0:T(8,128)(2,1)S(1)}, bf16[2,96,256]{2,1,0:T(8,128)(2,1)S(1)}, u32[]{:S(2)}, u32[]{:S(2)}) collective-permute-start(bf16[2,96,256]{2,1,0:T(8,128)(2,1)S(1)} %get-tuple-element.46), channel_id=1, source_target_pairs={{4,0},{8,4},{12,8},{0,12},{5,1},{9,5},{13,9},{1,13},{6,2},{10,6},{... | collective-permute-start | bytes 294920 | tf_op jit(solution)/shard_map/ppermute | solution.py:20
  105.4 7.6 %collective-permute-start.19 = (bf16[2,96,256]{2,1,0:T(8,128)(2,1)S(1)}, bf16[2,96,256]{2,1,0:T(8,128)(2,1)S(1)}, u32[]{:S(2)}, u32[]{:S(2)}) collective-permute-start(bf16[2,96,256]{2,1,0:T(8,128)(2,1)S(1)} %get-tuple-element.38), channel_id=1, source_target_pairs={{12,0},{0,4},{4,8},{8,12},{13,1},{1,5},{5,9},{9,13},{14,2},{2,6},{... | collective-permute-start | bytes 294920 | tf_op jit(solution)/shard_map/ppermute | solution.py:20
  107.8 8.1 %collective-permute-start.20 = (bf16[2,96,256]{2,1,0:T(8,128)(2,1)S(1)}, bf16[2,96,256]{2,1,0:T(8,128)(2,1)S(1)}, u32[]{:S(2)}, u32[]{:S(2)}) collective-permute-start(bf16[2,96,256]{2,1,0:T(8,128)(2,1)S(1)} %get-tuple-element.37), channel_id=1, source_target_pairs={{8,0},{12,4},{0,8},{4,12},{9,1},{13,5},{1,9},{5,13},{10,2},{14,6},... | collective-permute-start | bytes 294920 | tf_op jit(solution)/shard_map/ppermute | solution.py:20
  109.1 6.8 %collective-permute-start.21 = (bf16[2,96,256]{2,1,0:T(8,128)(2,1)S(1)}, bf16[2,96,256]{2,1,0:T(8,128)(2,1)S(1)}, u32[]{:S(2)}, u32[]{:S(2)}) collective-permute-start(bf16[2,96,256]{2,1,0:T(8,128)(2,1)S(1)} %get-tuple-element.36), channel_id=1, source_target_pairs={{4,0},{8,4},{12,8},{0,12},{5,1},{9,5},{13,9},{1,13},{6,2},{10,6},{... | collective-permute-start | bytes 294920 | tf_op jit(solution)/shard_map/ppermute | solution.py:20
  116.7 1.8 %collective-permute-start.22 = (bf16[4,2,96,256]{3,2,1,0:T(8,128)(2,1)S(1)}, bf16[4,2,96,256]{3,2,1,0:T(8,128)(2,1)S(1)}, u32[]{:S(2)}, u32[]{:S(2)}) collective-permute-start(bf16[4,2,96,256]{3,2,1,0:T(8,128)(2,1)S(1)} %broadcast_select_fusion.1), channel_id=1, source_target_pairs={{0,1},{1,0},{2,3},{3,2},{4,5},{5,4},{6,7},{7,6},{8,9},{9,8},{10,11... | collective-permute-start | bytes 1179656 | tf_op jit(solution)/shard_map/ppermute | solution.py:24
  119.3 19.6 %collective-permute-start.23 = (bf16[2,4,2,96,256]{4,3,2,1,0:T(8,128)(2,1)S(1)}, bf16[2,4,2,96,256]{4,3,2,1,0:T(8,128)(2,1)S(1)}, u32[]{:S(2)}, u32[]{:S(2)}) collective-permute-start(bf16[2,4,2,96,256]{4,3,2,1,0:T(8,128)(2,1)S(1)} %broadcast_select_fusion), channel_id=1, source_target_pairs={{0,2},{1,3},{2,0},{3,1},{4,6},{5,7},{6,4},{7,5},{8,10},{9,11},{10,... | collective-permute-start | bytes 2359304 | tf_op jit(solution)/shard_map/ppermute | solution.py:24
  (16 other events, 118.3 us)
